TPU v7x, 32 devices: a whole 2x2x4 slice. The times are simulated.
32 devices in a mesh: inl: 4 (over y, core), xl: 2 (over x), gz: 4 (over z).
Axes of the slice: x: 2, y: 2, z: 4, core: 2. Of those that a mesh axis runs over, the one named last changes fastest.
Arguments:
- wave_p: float32 [32, 32, 256], P('gz', 'inl', 'xl'), may hold values from -6 to 6
- wave_p_old: float32 [32, 32, 256], P('gz', 'inl', 'xl'), may hold values from -6 to 6
- wave_q: float32 [32, 32, 256], P('gz', 'inl', 'xl'), may hold values from -6 to 6
- wave_q_old: float32 [32, 32, 256], P('gz', 'inl', 'xl'), may hold values from -6 to 6
- courant_square: float32 [32, 32, 256], P('gz', 'inl', 'xl'), may hold values from 0.05 to 0.11
- thomsen_epsilon: float32 [32, 32, 256], P('gz', 'inl', 'xl'), may hold values from 0.1 to 0.35
- thomsen_delta: float32 [32, 32, 256], P('gz', 'inl', 'xl'), may hold values from 0.02 to 0.2
- tilt_angle: float32 [32, 32, 256], P('gz', 'inl', 'xl'), may hold values from -3.140625 to 3.140625
- azimuth: float32 [32, 32, 256], P('gz', 'inl', 'xl'), may hold values from -3.140625 to 3.140625
- shear_ratio: float32 [32, 32, 256], P('gz', 'inl', 'xl'), may hold values from 0.1 to 0.6
- damping: float32 [32, 32, 256], P('gz', 'inl', 'xl'), may hold values from 0 to 0.3
- trace_samples: float32 [8192, 256], P(('inl', 'xl', 'gz')), may hold values from -6 to 6
- resample_filter: float32 [2, 256], replicated, may hold values from -0.375 to 0.375
- line_gain: float32 [64], replicated, may hold values from 0.5 to 4
- receiver_inline: int32 [8192], P(('inl', 'xl', 'gz')), may hold values from 0 to 31, as said below
- receiver_crossline: int32 [8192], P(('inl', 'xl', 'gz')), may hold values from 0 to 255, as said below
- shot_line: int32 [8192], P(('inl', 'xl', 'gz')), may hold values from 0 to 63
Outputs:
- next_p: float32 [32, 32, 256], P('gz', 'inl', 'xl')
- next_q: float32 [32, 32, 256], P('gz', 'inl', 'xl')
- prior_p: float32 [32, 32, 256], P('gz', 'inl', 'xl')
- prior_q: float32 [32, 32, 256], P('gz', 'inl', 'xl')
Inputs may be any that keep to these rules, and one draw needn't show every extreme that they name: In each aligned block of 256 traces (the traces of one device), at most 64 traces lie in one device column (equal receiver_inline // 8 and receiver_crossline // 128); in every block some column holds exactly 64. `receiver_crossline`: see receiver_inline.
All inputs are finite; a program needn't handle non-finite values.
Results may differ from a plain program's by a relative error of at most 0.000075.
Values sent between devices are 32-bit elements; how exact they have to be, the bound alone decides.
No kernel may reach another device: no remote copies, remote signals or barrier semaphores. Data moves between devices by JAX's collectives and lax.ppermute only.
A program may use at most 64 MiB of HBM per device.

v0:
```python
import jax
import jax.numpy as jnp
from jax import lax
from jax.sharding import PartitionSpec as P

second_coef = (-205.0 / 72.0, 8.0 / 5.0, -1.0 / 5.0, 8.0 / 315.0, -1.0 / 560.0)
first_coef = (0.0, 4.0 / 5.0, -1.0 / 5.0, 4.0 / 105.0, -1.0 / 280.0)


def with_halo(block, sides, width):
    for axis, dim in sides:
        count = lax.axis_size(axis)
        forward = [(i, i + 1) for i in range(count - 1)]
        backward = [(target, source) for source, target in forward]
        low = lax.ppermute(
            lax.slice_in_dim(block, block.shape[dim] - width, None, axis=dim), axis, forward
        )
        high = lax.ppermute(lax.slice_in_dim(block, 0, width, axis=dim), axis, backward)
        block = jnp.concatenate([low, block, high], axis=dim)
    return block


def derivatives(padded):
    depth = padded.shape[-3] - 8
    across = padded.shape[-2] - 8
    along = padded.shape[-1] - 8

    def piece(dz, dx, dy):
        return padded[
            ..., 4 + dz : 4 + dz + depth, 4 + dx : 4 + dx + across, 4 + dy : 4 + dy + along
        ]

    center = piece(0, 0, 0)
    u_zz = second_coef[0] * center
    u_xx = second_coef[0] * center
    u_yy = second_coef[0] * center
    for k in range(1, 5):
        u_zz = u_zz + second_coef[k] * (piece(k, 0, 0) + piece(-k, 0, 0))
        u_xx = u_xx + second_coef[k] * (piece(0, k, 0) + piece(0, -k, 0))
        u_yy = u_yy + second_coef[k] * (piece(0, 0, k) + piece(0, 0, -k))
    grad_x = first_coef[1] * (padded[..., :, 5 : 5 + across, :] - padded[..., :, 3 : 3 + across, :])
    grad_y = first_coef[1] * (
        padded[..., :, 4 : 4 + across, 5 : 5 + along]
        - padded[..., :, 4 : 4 + across, 3 : 3 + along]
    )
    for k in range(2, 5):
        grad_x = grad_x + first_coef[k] * (
            padded[..., :, 4 + k : 4 + k + across, :] - padded[..., :, 4 - k : 4 - k + across, :]
        )
        grad_y = grad_y + first_coef[k] * (
            padded[..., :, 4 : 4 + across, 4 + k : 4 + k + along]
            - padded[..., :, 4 : 4 + across, 4 - k : 4 - k + along]
        )
    u_xy = first_coef[1] * (
        grad_x[..., 4 : 4 + depth, :, 5 : 5 + along] - grad_x[..., 4 : 4 + depth, :, 3 : 3 + along]
    )
    u_xz = first_coef[1] * (
        grad_x[..., 5 : 5 + depth, :, 4 : 4 + along] - grad_x[..., 3 : 3 + depth, :, 4 : 4 + along]
    )
    u_yz = first_coef[1] * (grad_y[..., 5 : 5 + depth, :, :] - grad_y[..., 3 : 3 + depth, :, :])
    for k in range(2, 5):
        u_xy = u_xy + first_coef[k] * (
            grad_x[..., 4 : 4 + depth, :, 4 + k : 4 + k + along]
            - grad_x[..., 4 : 4 + depth, :, 4 - k : 4 - k + along]
        )
        u_xz = u_xz + first_coef[k] * (
            grad_x[..., 4 + k : 4 + k + depth, :, 4 : 4 + along]
            - grad_x[..., 4 - k : 4 - k + depth, :, 4 : 4 + along]
        )
        u_yz = u_yz + first_coef[k] * (
            grad_y[..., 4 + k : 4 + k + depth, :, :] - grad_y[..., 4 - k : 4 - k + depth, :, :]
        )
    return (u_zz, u_xx, u_yy, u_xy, u_xz, u_yz)


def anisotropy(tilt_angle, azimuth):
    sin_t = jnp.sin(tilt_angle)
    cos_t = jnp.cos(tilt_angle)
    sin_f = jnp.sin(azimuth)
    cos_f = jnp.cos(azimuth)
    a_xx = sin_t * sin_t * cos_f * cos_f
    a_yy = sin_t * sin_t * sin_f * sin_f
    a_zz = cos_t * cos_t
    a_xy = 2.0 * sin_t * sin_t * sin_f * cos_f
    a_xz = 2.0 * sin_t * cos_t * cos_f
    a_yz = 2.0 * sin_t * cos_t * sin_f
    return (a_xx, a_yy, a_zz, a_xy, a_xz, a_yz)


def advance(padded, current, previous, fields, coefs, plane, top):
    courant, eps_field, delta_field, shear, damp = fields
    a_xx, a_yy, a_zz, a_xy, a_xz, a_yz = coefs
    u_zz, u_xx, u_yy, u_xy, u_xz, u_yz = derivatives(padded)
    h_one = a_xx * u_xx + a_yy * u_yy + a_zz * u_zz + a_xy * u_xy + a_xz * u_xz + a_yz * u_yz
    h_two = u_xx + u_yy + u_zz - h_one
    wave_a = current[0]
    wave_b = current[1]
    old_a = previous[0]
    old_b = previous[1]
    new_a = (
        2.0 * wave_a
        - old_a
        + courant * ((1.0 + 2.0 * eps_field) * h_two[0] + h_one[1] + shear * (h_one[0] - h_one[1]))
        - damp * (wave_a - old_a)
    )
    new_b = (
        2.0 * wave_b
        - old_b
        + courant
        * ((1.0 + 2.0 * delta_field) * h_two[0] + h_one[1] + shear * (h_two[1] - h_two[0]))
        - damp * (wave_b - old_b)
    )
    new_a = new_a.at[top].add(plane)
    new_b = new_b.at[top].add(plane)
    return jnp.stack([new_a, new_b])


def step_amplitudes(samples, resample_filter, line_gain, lines):
    table = jnp.arange(line_gain.shape[0], dtype=jnp.int32)
    gains = jnp.sum(jnp.where(lines[:, None] == table[None, :], line_gain[None, :], 0.0), axis=1)
    return jnp.dot(samples, resample_filter.T, precision=lax.Precision.HIGHEST) * gains[:, None]


def local(
    wave_p,
    wave_p_old,
    wave_q,
    wave_q_old,
    courant_square,
    thomsen_epsilon,
    thomsen_delta,
    tilt_angle,
    azimuth,
    shear_ratio,
    damping,
    trace_samples,
    resample_filter,
    line_gain,
    receiver_inline,
    receiver_crossline,
    shot_line,
):
    depth, inline_cells, cross_cells = wave_p.shape
    cells = inline_cells * cross_cells
    steps = resample_filter.shape[0]
    xl_count = lax.axis_size("xl")
    columns = lax.axis_size("inl") * xl_count
    capacity = 2 * trace_samples.shape[0] // columns
    owner = receiver_inline // inline_cells * xl_count + receiver_crossline // cross_cells
    local_cell = receiver_inline % inline_cells * cross_cells + receiver_crossline % cross_cells
    payload = step_amplitudes(trace_samples, resample_filter, line_gain, shot_line)
    onehot = (owner[:, None] == jnp.arange(columns, dtype=jnp.int32)[None, :]).astype(jnp.int32)
    rank = jnp.sum(jnp.cumsum(onehot, axis=0) * onehot, axis=1) - 1
    slot = owner * capacity + rank
    width = payload.shape[1]
    float_buffer = (
        jnp.zeros((columns * capacity, width), jnp.float32)
        .at[slot]
        .set(payload)
        .reshape(columns, capacity, width)
    )
    label_buffer = (
        jnp.full((columns * capacity,), -1, jnp.int32)
        .at[slot]
        .set(local_cell)
        .reshape(columns, capacity)
    )
    arrived, arrived_labels = (
        lax.all_to_all(float_buffer, ("inl", "xl"), split_axis=0, concat_axis=0, tiled=True),
        lax.all_to_all(label_buffer, ("inl", "xl"), split_axis=0, concat_axis=0, tiled=True),
    )
    amplitude = arrived.reshape(-1, width)
    flat_labels = arrived_labels.reshape(-1)
    target = jnp.where(flat_labels >= 0, flat_labels, cells)
    planes = jnp.zeros((steps, cells), jnp.float32).at[:, target].add(amplitude.T, mode="drop")
    planes = lax.psum(planes, "gz")
    surface_flag = jnp.where(lax.axis_index("gz") == 0, 1.0, 0.0).astype(jnp.float32)
    planes = planes.reshape(steps, inline_cells, cross_cells) * surface_flag
    fields = (courant_square, thomsen_epsilon, thomsen_delta, shear_ratio, damping)
    current = jnp.stack([wave_p, wave_q])
    previous = jnp.stack([wave_p_old, wave_q_old])
    coefs = anisotropy(tilt_angle, azimuth)
    for step in range(steps):
        padded = with_halo(current, (("inl", 2), ("xl", 3), ("gz", 1)), 4)
        newer = advance(padded, current, previous, fields, coefs, planes[step], 0)
        previous = current
        current = newer
    return (current[0], current[1], previous[0], previous[1])


def solution(mesh):
    return jax.shard_map(
        local,
        mesh=mesh,
        in_specs=(
            P("gz", "inl", "xl"),
            P("gz", "inl", "xl"),
            P("gz", "inl", "xl"),
            P("gz", "inl", "xl"),
            P("gz", "inl", "xl"),
            P("gz", "inl", "xl"),
            P("gz", "inl", "xl"),
            P("gz", "inl", "xl"),
            P("gz", "inl", "xl"),
            P("gz", "inl", "xl"),
            P("gz", "inl", "xl"),
            P(("inl", "xl", "gz"), None),
            P(),
            P(),
            P(("inl", "xl", "gz")),
            P(("inl", "xl", "gz")),
            P(("inl", "xl", "gz")),
        ),
        out_specs=(
            P("gz", "inl", "xl"),
            P("gz", "inl", "xl"),
            P("gz", "inl", "xl"),
            P("gz", "inl", "xl"),
        ),
        check_vma=False,
    )
```

profile of v0, /device:TPU:17, one launch (start us, length us, event | category | flops | bytes accessed | tf_op | source)
XLA Modules:
  0.0 108.6 jit_solution(15742423838032627012)
XLA Ops:
  0.6 0.7 fusion.178
  1.4 0.6 reduce-window.6
  2.0 0.2 slice_reduce_fusion.2
  2.3 0.1 fusion.170
  2.4 1.4 %scatter_custom_fusion = s32[512]{0:T(512)S(1)} fusion(s32[256]{0:T(256)S(1)} %compare_select_fusion.2, s32[256]{0:T(256)S(1)} %get-tuple-element.96, s32[]{:T(128)} %constant.177.clone.1), kind=kCustom, calls=%fused_computation.335 | custom fusion | bytes 2052 | tf_op jit(solution)/shard_map/scatter | solution.py:165
  3.8 0.7 all_to_all.9
  4.5 4.4 %all-to-all-start = ((s32[8,1,64]{2,1,0:T(1,128)}), s32[8,1,64]{2,1,0:T(1,128)S(1)}, u32[]{:S(2)}, u32[]{:S(2)}) async-start(s32[8,1,64]{2,1,0:T(1,128)} %all_to_all.9), calls=%async_computation | async-start | bytes 8192 | tf_op jit(solution)/shard_map/all_to_all | solution.py:170
  8.9 3.5 %collective-permute-start.1 = (f32[2,8,4,128]{3,2,1,0:T(4,128)S(1)}, f32[2,8,4,128]{3,2,1,0:T(4,128)S(1)}, u32[]{:S(2)}, u32[]{:S(2)}) collective-permute-start(f32[2,8,4,128]{3,2,1,0:T(4,128)S(1)} %get-tuple-element.85), channel_id=1, source_target_pairs={{0,8},{8,16},{16,24},{1,9},{9,17},{17,25},{2,10},{10,18},{18,26},{... | collective-permute-start | bytes 98312 | tf_op jit(solution)/shard_map/ppermute | solution.py:15
  12.5 1.9 %collective-permute-start = (f32[2,8,4,128]{3,2,1,0:T(4,128)S(1)}, f32[2,8,4,128]{3,2,1,0:T(4,128)S(1)}, u32[]{:S(2)}, u32[]{:S(2)}) collective-permute-start(f32[2,8,4,128]{3,2,1,0:T(4,128)S(1)} %get-tuple-element.86), channel_id=1, source_target_pairs={{8,0},{16,8},{24,16},{9,1},{17,9},{25,17},{10,2},{18,10},{26,18},{... | collective-permute-start | bytes 98312 | tf_op jit(solution)/shard_map/ppermute | solution.py:18
  14.4 0.1 select_reduce_fusion
  14.5 0.2 fusion.187
  14.8 0.6 copy-done.16
  15.5 0.3 convolution_multiply_fusion
  15.7 0.2 copy.28
  15.9 1.2 %scatter_custom_fusion.1 = f32[512,2]{1,0:T(8,128)S(1)} fusion(s32[256]{0:T(256)S(1)} %compare_select_fusion.2, f32[256,2]{1,0:T(8,128)S(1)} %copy.28, f32[]{:T(128)} %constant.176.clone.1), kind=kCustom, calls=%fused_computation.67 | custom fusion | bytes 4100 | tf_op jit(solution)/shard_map/scatter | solution.py:159
  17.2 0.1 copy.29
  17.3 0.7 reshape.234
  18.0 4.3 %all-to-all-start.1 = ((f32[8,1,128]{2,1,0:T(1,128)}), f32[8,1,128]{2,1,0:T(1,128)S(1)}, u32[]{:S(2)}, u32[]{:S(2)}) async-start(f32[8,1,128]{2,1,0:T(1,128)} %reshape.234), calls=%async_computation.1 | async-start | bytes 8192 | tf_op jit(solution)/shard_map/all_to_all | solution.py:169
  22.3 0.5 broadcast.341
  22.8 0.7 reduce.17
  23.5 0.1 reshape.187
  23.6 2.6 %all-to-all-done.1 = f32[8,1,128]{2,1,0:T(1,128)S(1)} async-done(((f32[8,1,128]{2,1,0:T(1,128)}), f32[8,1,128]{2,1,0:T(1,128)S(1)}, u32[]{:S(2)}, u32[]{:S(2)}) %all-to-all-start.1) | async-done | bytes 4128 | tf_op jit(solution)/shard_map/all_to_all | solution.py:169
  26.2 0.5 broadcast.390
  26.7 0.7 reduce.18
  27.4 0.1 reshape.235
  27.4 0.2 copy.32
  27.6 2.4 %scatter_custom_fusion.2 = f32[2,1024]{0,1:T(8,128)S(1)} fusion(s32[512]{0:T(512)S(1)} %bitcast.139, f32[512,2]{1,0:T(8,128)S(1)} %bitcast.135, f32[]{:T(128)} %constant.176.clone.1), kind=kCustom, calls=%fused_computation.37 | custom fusion | flops 1024 | bytes 8196 | tf_op jit(solution)/shard_map/scatter-add | solution.py:175
  30.0 23.1 %psum.7 = f32[2,1024]{0,1:T(8,128)S(1)} all-reduce(f32[2,1024]{0,1:T(8,128)S(1)} %scatter_custom_fusion.2), channel_id=1, replica_groups=mesh['inl'=4,'xl'=2,'gz'=4] {'gz'}, use_global_device_ids=true, to_apply=%region_7.8 | all-reduce | flops 2048 | bytes 16384 | tf_op jit(solution)/shard_map/psum | solution.py:176
  53.1 0.5 slice_reduce_fusion
  53.7 0.1 fusion.186
  53.8 2.1 %collective-permute-start.3 = (f32[2,8,16,4]{3,2,1,0:T(8,128)S(1)}, f32[2,8,16,4]{3,2,1,0:T(8,128)S(1)}, u32[]{:S(2)}, u32[]{:S(2)}) collective-permute-start(f32[2,8,16,4]{3,2,1,0:T(8,128)S(1)} %get-tuple-element.72), channel_id=1, source_target_pairs={{0,4},{1,5},{2,6},{3,7},{8,12},{9,13},{10,14},{11,15},{16,20},{17,... | collective-permute-start | bytes 12296 | tf_op jit(solution)/shard_map/ppermute | solution.py:15
  55.9 1.3 %collective-permute-start.2 = (f32[2,8,16,4]{3,2,1,0:T(8,128)S(1)}, f32[2,8,16,4]{3,2,1,0:T(8,128)S(1)}, u32[]{:S(2)}, u32[]{:S(2)}) collective-permute-start(f32[2,8,16,4]{3,2,1,0:T(8,128)S(1)} %get-tuple-element.73), channel_id=1, source_target_pairs={{4,0},{5,1},{6,2},{7,3},{12,8},{13,9},{14,10},{15,11},{20,16},{21,... | collective-permute-start | bytes 12296 | tf_op jit(solution)/shard_map/ppermute | solution.py:18
  57.2 0.6 collective-permute-done.3
  57.8 3.8 %collective-permute-done.2 = f32[2,8,16,4]{3,2,1,0:T(8,128)S(1)} collective-permute-done((f32[2,8,16,4]{3,2,1,0:T(8,128)S(1)}, f32[2,8,16,4]{3,2,1,0:T(8,128)S(1)}, u32[]{:S(2)}, u32[]{:S(2)}) %collective-permute-start.2) | collective-permute-done | bytes 4128 | tf_op jit(solution)/shard_map/ppermute | solution.py:18
  61.6 0.2 pad_maximum_fusion.3
  61.9 2.1 %collective-permute-start.4 = (f32[2,4,16,136]{3,2,1,0:T(8,128)S(1)}, f32[2,4,16,136]{3,2,1,0:T(8,128)S(1)}, u32[]{:S(2)}, u32[]{:S(2)}) collective-permute-start(f32[2,4,16,136]{3,2,1,0:T(8,128)S(1)} %get-tuple-element.60), channel_id=1, source_target_pairs={{1,0},{2,1},{3,2},{5,4},{6,5},{7,6},{9,8},{10,9},{11,10},{13,12},{... | collective-permute-start | bytes 208904 | tf_op jit(solution)/shard_map/ppermute | solution.py:18
  63.9 3.2 %collective-permute-start.5 = (f32[2,4,16,136]{3,2,1,0:T(8,128)S(1)}, f32[2,4,16,136]{3,2,1,0:T(8,128)S(1)}, u32[]{:S(2)}, u32[]{:S(2)}) collective-permute-start(f32[2,4,16,136]{3,2,1,0:T(8,128)S(1)} %get-tuple-element.61), channel_id=1, source_target_pairs={{0,1},{1,2},{2,3},{4,5},{5,6},{6,7},{8,9},{9,10},{10,11},{12,13},{... | collective-permute-start | bytes 208904 | tf_op jit(solution)/shard_map/ppermute | solution.py:15
  67.2 0.2 pad_maximum_fusion.2
  67.4 0.5 collective-permute-done.4
  67.9 2.3 %collective-permute-done.5 = f32[2,4,16,136]{3,2,1,0:T(8,128)S(1)} collective-permute-done((f32[2,4,16,136]{3,2,1,0:T(8,128)S(1)}, f32[2,4,16,136]{3,2,1,0:T(8,128)S(1)}, u32[]{:S(2)}, u32[]{:S(2)}) %collective-permute-start.5) | collective-permute-done | bytes 69664 | tf_op jit(solution)/shard_map/ppermute | solution.py:15
  70.2 0.2 pad_maximum_fusion
  70.4 0.3 fusion.24
  70.7 0.2 fusion.8
  71.0 0.6 add_subtract_fusion.1
  71.6 0.1 copy-done.5
  71.9 10.9 %collective-permute-start.7 = (f32[2,8,4,128]{3,2,1,0:T(4,128)S(1)}, f32[2,8,4,128]{3,2,1,0:T(4,128)S(1)}, u32[]{:S(2)}, u32[]{:S(2)}) collective-permute-start(f32[2,8,4,128]{3,2,1,0:T(4,128)S(1)} %get-tuple-element.76), channel_id=1, source_target_pairs={{0,8},{8,16},{16,24},{1,9},{9,17},{17,25},{2,10},{10,18},{18,26},{... | collective-permute-start | bytes 98312 | tf_op jit(solution)/shard_map/ppermute | solution.py:15
  82.9 1.9 %collective-permute-start.6 = (f32[2,8,4,128]{3,2,1,0:T(4,128)S(1)}, f32[2,8,4,128]{3,2,1,0:T(4,128)S(1)}, u32[]{:S(2)}, u32[]{:S(2)}) collective-permute-start(f32[2,8,4,128]{3,2,1,0:T(4,128)S(1)} %get-tuple-element.77), channel_id=1, source_target_pairs={{8,0},{16,8},{24,16},{9,1},{17,9},{25,17},{10,2},{18,10},{26,18},{... | collective-permute-start | bytes 98312 | tf_op jit(solution)/shard_map/ppermute | solution.py:18
  84.8 3.3 %collective-permute-done.6 = f32[2,8,4,128]{3,2,1,0:T(4,128)S(1)} collective-permute-done((f32[2,8,4,128]{3,2,1,0:T(4,128)S(1)}, f32[2,8,4,128]{3,2,1,0:T(4,128)S(1)}, u32[]{:S(2)}, u32[]{:S(2)}) %collective-permute-start.6) | collective-permute-done | bytes 32800 | tf_op jit(solution)/shard_map/ppermute | solution.py:18
  88.1 0.1 fusion.185
  88.2 1.3 %collective-permute-start.9 = (f32[2,8,16,4]{3,2,1,0:T(8,128)S(1)}, f32[2,8,16,4]{3,2,1,0:T(8,128)S(1)}, u32[]{:S(2)}, u32[]{:S(2)}) collective-permute-start(f32[2,8,16,4]{3,2,1,0:T(8,128)S(1)} %get-tuple-element.68), channel_id=1, source_target_pairs={{0,4},{1,5},{2,6},{3,7},{8,12},{9,13},{10,14},{11,15},{16,20},{17,... | collective-permute-start | bytes 12296 | tf_op jit(solution)/shard_map/ppermute | solution.py:15
  89.5 1.3 %collective-permute-start.8 = (f32[2,8,16,4]{3,2,1,0:T(8,128)S(1)}, f32[2,8,16,4]{3,2,1,0:T(8,128)S(1)}, u32[]{:S(2)}, u32[]{:S(2)}) collective-permute-start(f32[2,8,16,4]{3,2,1,0:T(8,128)S(1)} %get-tuple-element.69), channel_id=1, source_target_pairs={{4,0},{5,1},{6,2},{7,3},{12,8},{13,9},{14,10},{15,11},{20,16},{21,... | collective-permute-start | bytes 12296 | tf_op jit(solution)/shard_map/ppermute | solution.py:18
  90.9 0.6 collective-permute-done.9
  91.4 3.8 %collective-permute-done.8 = f32[2,8,16,4]{3,2,1,0:T(8,128)S(1)} collective-permute-done((f32[2,8,16,4]{3,2,1,0:T(8,128)S(1)}, f32[2,8,16,4]{3,2,1,0:T(8,128)S(1)}, u32[]{:S(2)}, u32[]{:S(2)}) %collective-permute-start.8) | collective-permute-done | bytes 4128 | tf_op jit(solution)/shard_map/ppermute | solution.py:18
  95.2 0.2 pad_maximum_fusion.5
  95.5 3.6 %collective-permute-start.10 = (f32[2,4,16,136]{3,2,1,0:T(8,128)S(1)}, f32[2,4,16,136]{3,2,1,0:T(8,128)S(1)}, u32[]{:S(2)}, u32[]{:S(2)}) collective-permute-start(f32[2,4,16,136]{3,2,1,0:T(8,128)S(1)} %get-tuple-element.58), channel_id=1, source_target_pairs={{1,0},{2,1},{3,2},{5,4},{6,5},{7,6},{9,8},{10,9},{11,10},{13,12},{... | collective-permute-start | bytes 208904 | tf_op jit(solution)/shard_map/ppermute | solution.py:18
  99.2 1.9 %collective-permute-start.11 = (f32[2,4,16,136]{3,2,1,0:T(8,128)S(1)}, f32[2,4,16,136]{3,2,1,0:T(8,128)S(1)}, u32[]{:S(2)}, u32[]{:S(2)}) collective-permute-start(f32[2,4,16,136]{3,2,1,0:T(8,128)S(1)} %get-tuple-element.59), channel_id=1, source_target_pairs={{0,1},{1,2},{2,3},{4,5},{5,6},{6,7},{8,9},{9,10},{10,11},{12,13},{... | collective-permute-start | bytes 208904 | tf_op jit(solution)/shard_map/ppermute | solution.py:15
  101.1 0.2 pad_maximum_fusion.4
  101.3 1.0 collective-permute-done.10
  102.3 4.2 %collective-permute-done.11 = f32[2,4,16,136]{3,2,1,0:T(8,128)S(1)} collective-permute-done((f32[2,4,16,136]{3,2,1,0:T(8,128)S(1)}, f32[2,4,16,136]{3,2,1,0:T(8,128)S(1)}, u32[]{:S(2)}, u32[]{:S(2)}) %collective-permute-start.11) | collective-permute-done | bytes 69664 | tf_op jit(solution)/shard_map/ppermute | solution.py:15
  106.5 0.2 pad_maximum_fusion.1
  106.7 0.3 fusion.17
  107.0 0.2 fusion.1
  107.3 0.6 add_subtract_fusion
  108.0 0.6 copy-done.10
  (58 shorter events, 0.6 us)
Async XLA Ops:
  0.6 14.2 %copy-start = (f32[256,256]{1,0:T(8,128)S(1)}, f32[256,256]{1,0:T(8,128)}, u32[]{:S(2)}) copy-start(f32[256,256]{1,0:T(8,128)} %param.36) | copy-start | bytes 786436
  1.4 7.4 %copy-start.3 = (f32[8,8,128]{2,1,0:T(8,128)S(1)}, f32[8,8,128]{2,1,0:T(8,128)}, u32[]{:S(2)}) copy-start(f32[8,8,128]{2,1,0:T(8,128)} %param.25) | copy-start | bytes 98308
  1.4 7.4 %copy-start.4 = (f32[8,8,128]{2,1,0:T(8,128)S(1)}, f32[8,8,128]{2,1,0:T(8,128)}, u32[]{:S(2)}) copy-start(f32[8,8,128]{2,1,0:T(8,128)} %param.27) | copy-start | bytes 98308
  4.5 13.5 %all-to-all-start = ((s32[8,1,64]{2,1,0:T(1,128)}), s32[8,1,64]{2,1,0:T(1,128)S(1)}, u32[]{:S(2)}, u32[]{:S(2)}) async-start(s32[8,1,64]{2,1,0:T(1,128)} %all_to_all.9), calls=%async_computation | async-start | bytes 8192 | tf_op jit(solution)/shard_map/all_to_all | solution.py:170
  8.9 5.7 %copy-start.12 = (f32[8,8,128]{2,1,0:T(8,128)S(1)}, f32[8,8,128]{2,1,0:T(8,128)}, u32[]{:S(2)}) copy-start(f32[8,8,128]{2,1,0:T(8,128)} %param.33) | copy-start | bytes 98308
  8.9 5.7 %copy-start.13 = (f32[8,8,128]{2,1,0:T(8,128)S(1)}, f32[8,8,128]{2,1,0:T(8,128)}, u32[]{:S(2)}) copy-start(f32[8,8,128]{2,1,0:T(8,128)} %param.32) | copy-start | bytes 98308
  8.9 5.5 %copy-start.17 = (s32[256]{0:T(256)S(1)}, s32[256]{0:T(256)}, u32[]{:S(2)}) copy-start(s32[256]{0:T(256)} %param.41) | copy-start | bytes 3076
  8.9 5.5 %copy-start.18 = (f32[64]{0:T(128)S(1)}, f32[64]{0:T(128)}, u32[]{:S(2)}) copy-start(f32[64]{0:T(128)} %param.38) | copy-start | bytes 772
  8.9 44.7 %collective-permute-start.1 = (f32[2,8,4,128]{3,2,1,0:T(4,128)S(1)}, f32[2,8,4,128]{3,2,1,0:T(4,128)S(1)}, u32[]{:S(2)}, u32[]{:S(2)}) collective-permute-start(f32[2,8,4,128]{3,2,1,0:T(4,128)S(1)} %get-tuple-element.85), channel_id=1, source_target_pairs={{0,8},{8,16},{16,24},{1,9},{9,17},{17,25},{2,10},{10,18},{18,26},{... | collective-permute-start | bytes 98312 | tf_op jit(solution)/shard_map/ppermute | solution.py:15
  12.5 41.1 %collective-permute-start = (f32[2,8,4,128]{3,2,1,0:T(4,128)S(1)}, f32[2,8,4,128]{3,2,1,0:T(4,128)S(1)}, u32[]{:S(2)}, u32[]{:S(2)}) collective-permute-start(f32[2,8,4,128]{3,2,1,0:T(4,128)S(1)} %get-tuple-element.86), channel_id=1, source_target_pairs={{8,0},{16,8},{24,16},{9,1},{17,9},{25,17},{10,2},{18,10},{26,18},{... | collective-permute-start | bytes 98312 | tf_op jit(solution)/shard_map/ppermute | solution.py:18
  14.8 0.7 copy-start.16
  18.0 8.2 %all-to-all-start.1 = ((f32[8,1,128]{2,1,0:T(1,128)}), f32[8,1,128]{2,1,0:T(1,128)S(1)}, u32[]{:S(2)}, u32[]{:S(2)}) async-start(f32[8,1,128]{2,1,0:T(1,128)} %reshape.234), calls=%async_computation.1 | async-start | bytes 8192 | tf_op jit(solution)/shard_map/all_to_all | solution.py:169
  53.8 4.0 %collective-permute-start.3 = (f32[2,8,16,4]{3,2,1,0:T(8,128)S(1)}, f32[2,8,16,4]{3,2,1,0:T(8,128)S(1)}, u32[]{:S(2)}, u32[]{:S(2)}) collective-permute-start(f32[2,8,16,4]{3,2,1,0:T(8,128)S(1)} %get-tuple-element.72), channel_id=1, source_target_pairs={{0,4},{1,5},{2,6},{3,7},{8,12},{9,13},{10,14},{11,15},{16,20},{17,... | collective-permute-start | bytes 12296 | tf_op jit(solution)/shard_map/ppermute | solution.py:15
  55.9 5.7 %collective-permute-start.2 = (f32[2,8,16,4]{3,2,1,0:T(8,128)S(1)}, f32[2,8,16,4]{3,2,1,0:T(8,128)S(1)}, u32[]{:S(2)}, u32[]{:S(2)}) collective-permute-start(f32[2,8,16,4]{3,2,1,0:T(8,128)S(1)} %get-tuple-element.73), channel_id=1, source_target_pairs={{4,0},{5,1},{6,2},{7,3},{12,8},{13,9},{14,10},{15,11},{20,16},{21,... | collective-permute-start | bytes 12296 | tf_op jit(solution)/shard_map/ppermute | solution.py:18
  61.9 6.0 %collective-permute-start.4 = (f32[2,4,16,136]{3,2,1,0:T(8,128)S(1)}, f32[2,4,16,136]{3,2,1,0:T(8,128)S(1)}, u32[]{:S(2)}, u32[]{:S(2)}) collective-permute-start(f32[2,4,16,136]{3,2,1,0:T(8,128)S(1)} %get-tuple-element.60), channel_id=1, source_target_pairs={{1,0},{2,1},{3,2},{5,4},{6,5},{7,6},{9,8},{10,9},{11,10},{13,12},{... | collective-permute-start | bytes 208904 | tf_op jit(solution)/shard_map/ppermute | solution.py:18
  63.9 6.2 %collective-permute-start.5 = (f32[2,4,16,136]{3,2,1,0:T(8,128)S(1)}, f32[2,4,16,136]{3,2,1,0:T(8,128)S(1)}, u32[]{:S(2)}, u32[]{:S(2)}) collective-permute-start(f32[2,4,16,136]{3,2,1,0:T(8,128)S(1)} %get-tuple-element.61), channel_id=1, source_target_pairs={{0,1},{1,2},{2,3},{4,5},{5,6},{6,7},{8,9},{9,10},{10,11},{12,13},{... | collective-permute-start | bytes 208904 | tf_op jit(solution)/shard_map/ppermute | solution.py:15
  70.9 0.8 copy-start.5
  70.9 0.8 copy-start.6
  70.9 0.8 copy-start.7
  71.0 0.8 copy-start.8
  71.0 0.8 copy-start.9
  71.0 0.8 copy-start.14
  71.0 0.8 copy-start.15
  71.9 36.0 %copy-start.1 = (f32[8,8,128]{2,1,0:T(8,128)}, f32[8,8,128]{2,1,0:T(8,128)S(1)}, u32[]{:S(2)}) copy-start(f32[8,8,128]{2,1,0:T(8,128)S(1)} %get-tuple-element.94) | copy-start | bytes 98308
  71.9 36.0 %copy-start.2 = (f32[8,8,128]{2,1,0:T(8,128)}, f32[8,8,128]{2,1,0:T(8,128)S(1)}, u32[]{:S(2)}) copy-start(f32[8,8,128]{2,1,0:T(8,128)S(1)} %get-tuple-element.95) | copy-start | bytes 98308
  71.9 12.9 %collective-permute-start.7 = (f32[2,8,4,128]{3,2,1,0:T(4,128)S(1)}, f32[2,8,4,128]{3,2,1,0:T(4,128)S(1)}, u32[]{:S(2)}, u32[]{:S(2)}) collective-permute-start(f32[2,8,4,128]{3,2,1,0:T(4,128)S(1)} %get-tuple-element.76), channel_id=1, source_target_pairs={{0,8},{8,16},{16,24},{1,9},{9,17},{17,25},{2,10},{10,18},{18,26},{... | collective-permute-start | bytes 98312 | tf_op jit(solution)/shard_map/ppermute | solution.py:15
  82.9 5.2 %collective-permute-start.6 = (f32[2,8,4,128]{3,2,1,0:T(4,128)S(1)}, f32[2,8,4,128]{3,2,1,0:T(4,128)S(1)}, u32[]{:S(2)}, u32[]{:S(2)}) collective-permute-start(f32[2,8,4,128]{3,2,1,0:T(4,128)S(1)} %get-tuple-element.77), channel_id=1, source_target_pairs={{8,0},{16,8},{24,16},{9,1},{17,9},{25,17},{10,2},{18,10},{26,18},{... | collective-permute-start | bytes 98312 | tf_op jit(solution)/shard_map/ppermute | solution.py:18
  88.2 3.2 %collective-permute-start.9 = (f32[2,8,16,4]{3,2,1,0:T(8,128)S(1)}, f32[2,8,16,4]{3,2,1,0:T(8,128)S(1)}, u32[]{:S(2)}, u32[]{:S(2)}) collective-permute-start(f32[2,8,16,4]{3,2,1,0:T(8,128)S(1)} %get-tuple-element.68), channel_id=1, source_target_pairs={{0,4},{1,5},{2,6},{3,7},{8,12},{9,13},{10,14},{11,15},{16,20},{17,... | collective-permute-start | bytes 12296 | tf_op jit(solution)/shard_map/ppermute | solution.py:15
  89.5 5.7 %collective-permute-start.8 = (f32[2,8,16,4]{3,2,1,0:T(8,128)S(1)}, f32[2,8,16,4]{3,2,1,0:T(8,128)S(1)}, u32[]{:S(2)}, u32[]{:S(2)}) collective-permute-start(f32[2,8,16,4]{3,2,1,0:T(8,128)S(1)} %get-tuple-element.69), channel_id=1, source_target_pairs={{4,0},{5,1},{6,2},{7,3},{12,8},{13,9},{14,10},{15,11},{20,16},{21,... | collective-permute-start | bytes 12296 | tf_op jit(solution)/shard_map/ppermute | solution.py:18
  95.5 6.8 %collective-permute-start.10 = (f32[2,4,16,136]{3,2,1,0:T(8,128)S(1)}, f32[2,4,16,136]{3,2,1,0:T(8,128)S(1)}, u32[]{:S(2)}, u32[]{:S(2)}) collective-permute-start(f32[2,4,16,136]{3,2,1,0:T(8,128)S(1)} %get-tuple-element.58), channel_id=1, source_target_pairs={{1,0},{2,1},{3,2},{5,4},{6,5},{7,6},{9,8},{10,9},{11,10},{13,12},{... | collective-permute-start | bytes 208904 | tf_op jit(solution)/shard_map/ppermute | solution.py:18
  99.2 7.3 %collective-permute-start.11 = (f32[2,4,16,136]{3,2,1,0:T(8,128)S(1)}, f32[2,4,16,136]{3,2,1,0:T(8,128)S(1)}, u32[]{:S(2)}, u32[]{:S(2)}) collective-permute-start(f32[2,4,16,136]{3,2,1,0:T(8,128)S(1)} %get-tuple-element.59), channel_id=1, source_target_pairs={{0,1},{1,2},{2,3},{4,5},{5,6},{6,7},{8,9},{9,10},{10,11},{12,13},{... | collective-permute-start | bytes 208904 | tf_op jit(solution)/shard_map/ppermute | solution.py:15
  107.9 0.6 copy-start.10
  107.9 0.6 copy-start.11
where the time goes:
time: 109 us
  starting transfers between devices  43.9 us (40%)
  blocking collectives  23.1 us (21%)
  waiting for transfers between devices  22.7 us (21%)
  other arithmetic  9.15 us (8%)
  local copies, waits for them, and re-layouts  8.32 us (8%)
  between operations  1.24 us (1%)
    psum x1, blocking collectives, local(): planes = lax.psum(planes, 'gz')  23.1 us
    ppermute x6, starting transfers between devices, with_halo(): lax.ppermute(lax.slice_in_dim(block, block.shape[dim] - width, None, axis...  23 us
    ppermute x6, waiting for transfers between devices, with_halo(): lax.ppermute(lax.slice_in_dim(block, 0, width, axis=dim), axis, backward)  12.4 us
    ppermute x6, starting transfers between devices, with_halo(): lax.ppermute(lax.slice_in_dim(block, 0, width, axis=dim), axis, backward)  12.1 us
    ppermute x6, waiting for transfers between devices, with_halo(): lax.ppermute(lax.slice_in_dim(block, block.shape[dim] - width, None, axis...  7.67 us
    all_to_all x1, starting transfers between devices, local(): lax.all_to_all(label_buffer, ('inl', 'xl'), split_axis=0, concat_axis=0,...  4.39 us
    all_to_all x1, starting transfers between devices, local(): lax.all_to_all(float_buffer, ('inl', 'xl'), split_axis=0, concat_axis=0,...  4.3 us
    all_to_all x1, waiting for transfers between devices, local(): lax.all_to_all(float_buffer, ('inl', 'xl'), split_axis=0, concat_axis=0,...  2.63 us
  transfers between devices with their start and end apart: 14, of which 10 were waited for; matrix products, arithmetic and copies ran while one was open for 8% of the time, Pallas kernels for 0%

commit v1 on v0

--- a/solution.py
+++ b/solution.py
@@ -144,6 +144,7 @@
     cells = inline_cells * cross_cells
     steps = resample_filter.shape[0]
     xl_count = lax.axis_size("xl")
+    gz_count = lax.axis_size("gz")
     columns = lax.axis_size("inl") * xl_count
     capacity = 2 * trace_samples.shape[0] // columns
     owner = receiver_inline // inline_cells * xl_count + receiver_crossline // cross_cells
@@ -151,31 +152,14 @@
     payload = step_amplitudes(trace_samples, resample_filter, line_gain, shot_line)
     onehot = (owner[:, None] == jnp.arange(columns, dtype=jnp.int32)[None, :]).astype(jnp.int32)
     rank = jnp.sum(jnp.cumsum(onehot, axis=0) * onehot, axis=1) - 1
-    slot = owner * capacity + rank
-    width = payload.shape[1]
-    float_buffer = (
-        jnp.zeros((columns * capacity, width), jnp.float32)
-        .at[slot]
-        .set(payload)
-        .reshape(columns, capacity, width)
-    )
-    label_buffer = (
-        jnp.full((columns * capacity,), -1, jnp.int32)
-        .at[slot]
-        .set(local_cell)
-        .reshape(columns, capacity)
-    )
-    arrived, arrived_labels = (
-        lax.all_to_all(float_buffer, ("inl", "xl"), split_axis=0, concat_axis=0, tiled=True),
-        lax.all_to_all(label_buffer, ("inl", "xl"), split_axis=0, concat_axis=0, tiled=True),
-    )
-    amplitude = arrived.reshape(-1, width)
-    flat_labels = arrived_labels.reshape(-1)
-    target = jnp.where(flat_labels >= 0, flat_labels, cells)
-    planes = jnp.zeros((steps, cells), jnp.float32).at[:, target].add(amplitude.T, mode="drop")
-    planes = lax.psum(planes, "gz")
-    surface_flag = jnp.where(lax.axis_index("gz") == 0, 1.0, 0.0).astype(jnp.float32)
-    planes = planes.reshape(steps, inline_cells, cross_cells) * surface_flag
+    slot = owner * (gz_count * capacity) + rank
+    packed = jnp.concatenate([payload, local_cell.astype(jnp.float32)[:, None]], axis=1)
+    width = packed.shape[1]
+    send = jnp.zeros((columns * gz_count * capacity, width), jnp.float32).at[slot].set(packed)
+    arrived = lax.all_to_all(send, ("inl", "xl", "gz"), split_axis=0, concat_axis=0, tiled=True)
+    target = arrived[:, steps].astype(jnp.int32)
+    planes = jnp.zeros((steps, cells), jnp.float32).at[:, target].add(arrived[:, :steps].T, mode="drop")
+    planes = planes.reshape(steps, inline_cells, cross_cells)
     fields = (courant_square, thomsen_epsilon, thomsen_delta, shear_ratio, damping)
     current = jnp.stack([wave_p, wave_q])
     previous = jnp.stack([wave_p_old, wave_q_old])

time: 109 us -> 81.9 us (0.75)
  the two profiles are of different devices: /device:TPU:17 before, /device:TPU:22 now
where the time goes in v1:
time: 81.9 us; the launch traced here: 81.2 us
  starting transfers between devices  32.7 us (40%)
  other arithmetic  21.2 us (26%)
  waiting for transfers between devices  17.4 us (21%)
  local copies, waits for them, and re-layouts  8.42 us (10%)
  between operations  1.25 us (2%)
    scatter-add x1, other arithmetic, local(): jnp.zeros((steps, cells), jnp.float32).at[:, target]  14.8 us
    ppermute x6, starting transfers between devices, with_halo(): lax.ppermute(lax.slice_in_dim(block, block.shape[dim] - width, None, axis...  14.2 us
    ppermute x6, waiting for transfers between devices, with_halo(): lax.ppermute(lax.slice_in_dim(block, block.shape[dim] - width, None, axis...  13.8 us
    ppermute x6, starting transfers between devices, with_halo(): lax.ppermute(lax.slice_in_dim(block, 0, width, axis=dim), axis, backward)  12.7 us
    all_to_all x1, starting transfers between devices, local(): lax.all_to_all(send, ('inl', 'xl', 'gz'), split_axis=0, concat_axis=0, ti...  5.88 us
    ppermute x6, waiting for transfers between devices, with_halo(): lax.ppermute(lax.slice_in_dim(block, 0, width, axis=dim), axis, backward)  3.67 us
    unnamed x44, local copies, waits for them, and re-layouts  3.63 us
  transfers between devices with their start and end apart: 13, of which 7 were waited for; matrix products, arithmetic and copies ran while one was open for 28% of the time, Pallas kernels for 0%

profile of v1, /device:TPU:22, one launch (start us, length us, event | category | flops | bytes accessed | tf_op | source)
XLA Modules:
  0.0 81.2 jit_solution(3976589861376081952)
XLA Ops:
  0.6 0.9 %fusion.143 = (f32[2,8,4,128]{3,2,1,0:T(4,128)S(1)}, f32[2,8,4,128]{3,2,1,0:T(4,128)S(1)}) fusion(f32[1,8,8,128]{3,2,1,0:T(8,128)} %bitcast.121, f32[1,8,8,128]{3,2,1,0:T(8,128)} %bitcast.128), kind=kLoop, calls=%fused_computation.267 | loop fusion | flops 16384 | bytes 131072 | tf_op jit(solution)/shard_map/stack | solution.py:164
  1.5 1.9 %collective-permute-start = (f32[2,8,4,128]{3,2,1,0:T(4,128)S(1)}, f32[2,8,4,128]{3,2,1,0:T(4,128)S(1)}, u32[]{:S(2)}, u32[]{:S(2)}) collective-permute-start(f32[2,8,4,128]{3,2,1,0:T(4,128)S(1)} %get-tuple-element.86), channel_id=1, source_target_pairs={{8,0},{16,8},{24,16},{9,1},{17,9},{25,17},{10,2},{18,10},{26,18},{... | collective-permute-start | bytes 98312 | tf_op jit(solution)/shard_map/ppermute | solution.py:18
  3.5 2.4 %collective-permute-start.1 = (f32[2,8,4,128]{3,2,1,0:T(4,128)S(1)}, f32[2,8,4,128]{3,2,1,0:T(4,128)S(1)}, u32[]{:S(2)}, u32[]{:S(2)}) collective-permute-start(f32[2,8,4,128]{3,2,1,0:T(4,128)S(1)} %get-tuple-element.85), channel_id=1, source_target_pairs={{0,8},{8,16},{16,24},{1,9},{9,17},{17,25},{2,10},{10,18},{18,26},{... | collective-permute-start | bytes 98312 | tf_op jit(solution)/shard_map/ppermute | solution.py:15
  5.9 0.6 reduce-window.6
  6.5 0.2 slice_reduce_fusion.2
  6.8 0.1 fusion.170
  6.9 0.7 copy-done.17
  7.6 0.1 select_reduce_fusion
  7.7 0.6 copy-done.16
  8.2 0.3 convolution_multiply_fusion
  8.5 0.1 pad_maximum_fusion.36
  8.6 0.1 copy.31
  8.7 1.4 %scatter_custom_fusion = f32[2048,3]{1,0:T(8,128)S(1)} fusion(s32[256]{0:T(256)S(1)} %compare_select_fusion.1, f32[256,3]{1,0:T(8,128)S(1)} %copy.31, f32[]{:T(128)} %constant.170.clone.1), kind=kCustom, calls=%fused_computation.7 | custom fusion | bytes 24580 | tf_op jit(solution)/shard_map/scatter | solution.py:158
  10.1 0.4 copy.32
  10.5 0.7 reshape.177
  11.3 5.9 %all-to-all-start = ((f32[32,1,192]{2,1,0:T(1,128)}), f32[32,1,192]{2,1,0:T(1,128)S(1)}, u32[]{:S(2)}, u32[]{:S(2)}) async-start(f32[32,1,192]{2,1,0:T(1,128)} %reshape.177), calls=%async_computation | async-start | bytes 65536 | tf_op jit(solution)/shard_map/all_to_all | solution.py:159
  17.2 0.2 fusion.186
  17.5 0.7 copy-done.3
  18.2 0.0 copy-done.4
  18.2 0.1 fusion.185
  18.3 2.5 %collective-permute-start.2 = (f32[2,8,16,4]{3,2,1,0:T(8,128)S(1)}, f32[2,8,16,4]{3,2,1,0:T(8,128)S(1)}, u32[]{:S(2)}, u32[]{:S(2)}) collective-permute-start(f32[2,8,16,4]{3,2,1,0:T(8,128)S(1)} %get-tuple-element.73), channel_id=1, source_target_pairs={{4,0},{5,1},{6,2},{7,3},{12,8},{13,9},{14,10},{15,11},{20,16},{21,... | collective-permute-start | bytes 12296 | tf_op jit(solution)/shard_map/ppermute | solution.py:18
  20.8 1.3 %collective-permute-start.3 = (f32[2,8,16,4]{3,2,1,0:T(8,128)S(1)}, f32[2,8,16,4]{3,2,1,0:T(8,128)S(1)}, u32[]{:S(2)}, u32[]{:S(2)}) collective-permute-start(f32[2,8,16,4]{3,2,1,0:T(8,128)S(1)} %get-tuple-element.72), channel_id=1, source_target_pairs={{0,4},{1,5},{2,6},{3,7},{8,12},{9,13},{10,14},{11,15},{16,20},{17,... | collective-permute-start | bytes 12296 | tf_op jit(solution)/shard_map/ppermute | solution.py:15
  22.1 1.7 %collective-permute-done.2 = f32[2,8,16,4]{3,2,1,0:T(8,128)S(1)} collective-permute-done((f32[2,8,16,4]{3,2,1,0:T(8,128)S(1)}, f32[2,8,16,4]{3,2,1,0:T(8,128)S(1)}, u32[]{:S(2)}, u32[]{:S(2)}) %collective-permute-start.2) | collective-permute-done | bytes 4128 | tf_op jit(solution)/shard_map/ppermute | solution.py:18
  23.8 4.1 %collective-permute-done.3 = f32[2,8,16,4]{3,2,1,0:T(8,128)S(1)} collective-permute-done((f32[2,8,16,4]{3,2,1,0:T(8,128)S(1)}, f32[2,8,16,4]{3,2,1,0:T(8,128)S(1)}, u32[]{:S(2)}, u32[]{:S(2)}) %collective-permute-start.3) | collective-permute-done | bytes 4128 | tf_op jit(solution)/shard_map/ppermute | solution.py:15
  28.0 0.2 pad_maximum_fusion.3
  28.2 0.7 fusion.183
  28.9 2.4 %collective-permute-start.4 = (f32[2,4,16,136]{3,2,1,0:T(8,128)}, f32[2,4,16,136]{3,2,1,0:T(8,128)S(1)}, u32[]{:S(2)}, u32[]{:S(2)}) collective-permute-start(f32[2,4,16,136]{3,2,1,0:T(8,128)} %get-tuple-element.60), channel_id=1, source_target_pairs={{1,0},{2,1},{3,2},{5,4},{6,5},{7,6},{9,8},{10,9},{11,10},{13,12},{... | collective-permute-start | bytes 208904 | tf_op jit(solution)/shard_map/ppermute | solution.py:18
  31.4 3.4 %collective-permute-start.5 = (f32[2,4,16,136]{3,2,1,0:T(8,128)}, f32[2,4,16,136]{3,2,1,0:T(8,128)S(1)}, u32[]{:S(2)}, u32[]{:S(2)}) collective-permute-start(f32[2,4,16,136]{3,2,1,0:T(8,128)} %get-tuple-element.61), channel_id=1, source_target_pairs={{0,1},{1,2},{2,3},{4,5},{5,6},{6,7},{8,9},{9,10},{10,11},{12,13},{... | collective-permute-start | bytes 208904 | tf_op jit(solution)/shard_map/ppermute | solution.py:15
  34.8 0.2 pad_maximum_fusion.2
  35.0 0.5 broadcast.347
  35.5 0.7 reduce.14
  36.2 0.1 reshape.178
  36.3 0.1 all_to_all.10
  36.5 0.4 copy.34
  36.8 14.8 %scatter_custom_fusion.1 = f32[2,1024]{0,1:T(8,128)S(1)} fusion(s32[2048]{0:T(1024)S(1)} %bitcast.138, f32[2048,2]{1,0:T(8,128)S(1)} %copy.34, f32[]{:T(128)} %constant.170.clone.1), kind=kCustom, calls=%fused_computation.37 | custom fusion | flops 4096 | bytes 8196 | tf_op jit(solution)/shard_map/scatter-add | solution.py:161
  51.7 0.5 slice_reduce_fusion
  52.2 0.2 pad_maximum_fusion
  52.4 0.3 fusion.26
  52.8 0.2 fusion.10
  53.0 0.6 add_subtract_fusion.1
  53.7 0.1 copy-done.5
  53.7 0.0 copy-done.6
  53.8 0.0 copy-done.8
  53.8 0.0 copy-done.9
  53.8 0.0 copy-done.15
  53.9 1.9 %collective-permute-start.6 = (f32[2,8,4,128]{3,2,1,0:T(4,128)S(1)}, f32[2,8,4,128]{3,2,1,0:T(4,128)S(1)}, u32[]{:S(2)}, u32[]{:S(2)}) collective-permute-start(f32[2,8,4,128]{3,2,1,0:T(4,128)S(1)} %get-tuple-element.77), channel_id=1, source_target_pairs={{8,0},{16,8},{24,16},{9,1},{17,9},{25,17},{10,2},{18,10},{26,18},{... | collective-permute-start | bytes 98312 | tf_op jit(solution)/shard_map/ppermute | solution.py:18
  55.9 2.4 %collective-permute-start.7 = (f32[2,8,4,128]{3,2,1,0:T(4,128)S(1)}, f32[2,8,4,128]{3,2,1,0:T(4,128)S(1)}, u32[]{:S(2)}, u32[]{:S(2)}) collective-permute-start(f32[2,8,4,128]{3,2,1,0:T(4,128)S(1)} %get-tuple-element.76), channel_id=1, source_target_pairs={{0,8},{8,16},{16,24},{1,9},{9,17},{17,25},{2,10},{10,18},{18,26},{... | collective-permute-start | bytes 98312 | tf_op jit(solution)/shard_map/ppermute | solution.py:15
  58.3 2.8 %collective-permute-done.7 = f32[2,8,4,128]{3,2,1,0:T(4,128)S(1)} collective-permute-done((f32[2,8,4,128]{3,2,1,0:T(4,128)S(1)}, f32[2,8,4,128]{3,2,1,0:T(4,128)S(1)}, u32[]{:S(2)}, u32[]{:S(2)}) %collective-permute-start.7) | collective-permute-done | bytes 32800 | tf_op jit(solution)/shard_map/ppermute | solution.py:15
  61.1 0.1 fusion.184
  61.2 1.5 %collective-permute-start.8 = (f32[2,8,16,4]{3,2,1,0:T(8,128)S(1)}, f32[2,8,16,4]{3,2,1,0:T(8,128)S(1)}, u32[]{:S(2)}, u32[]{:S(2)}) collective-permute-start(f32[2,8,16,4]{3,2,1,0:T(8,128)S(1)} %get-tuple-element.69), channel_id=1, source_target_pairs={{4,0},{5,1},{6,2},{7,3},{12,8},{13,9},{14,10},{15,11},{20,16},{21,... | collective-permute-start | bytes 12296 | tf_op jit(solution)/shard_map/ppermute | solution.py:18
  62.7 1.3 %collective-permute-start.9 = (f32[2,8,16,4]{3,2,1,0:T(8,128)S(1)}, f32[2,8,16,4]{3,2,1,0:T(8,128)S(1)}, u32[]{:S(2)}, u32[]{:S(2)}) collective-permute-start(f32[2,8,16,4]{3,2,1,0:T(8,128)S(1)} %get-tuple-element.68), channel_id=1, source_target_pairs={{0,4},{1,5},{2,6},{3,7},{8,12},{9,13},{10,14},{11,15},{16,20},{17,... | collective-permute-start | bytes 12296 | tf_op jit(solution)/shard_map/ppermute | solution.py:15
  64.0 1.2 %collective-permute-done.8 = f32[2,8,16,4]{3,2,1,0:T(8,128)S(1)} collective-permute-done((f32[2,8,16,4]{3,2,1,0:T(8,128)S(1)}, f32[2,8,16,4]{3,2,1,0:T(8,128)S(1)}, u32[]{:S(2)}, u32[]{:S(2)}) %collective-permute-start.8) | collective-permute-done | bytes 4128 | tf_op jit(solution)/shard_map/ppermute | solution.py:18
  65.2 4.4 %collective-permute-done.9 = f32[2,8,16,4]{3,2,1,0:T(8,128)S(1)} collective-permute-done((f32[2,8,16,4]{3,2,1,0:T(8,128)S(1)}, f32[2,8,16,4]{3,2,1,0:T(8,128)S(1)}, u32[]{:S(2)}, u32[]{:S(2)}) %collective-permute-start.9) | collective-permute-done | bytes 4128 | tf_op jit(solution)/shard_map/ppermute | solution.py:15
  69.5 0.2 pad_maximum_fusion.5
  69.8 2.5 %collective-permute-start.10 = (f32[2,4,16,136]{3,2,1,0:T(8,128)S(1)}, f32[2,4,16,136]{3,2,1,0:T(8,128)S(1)}, u32[]{:S(2)}, u32[]{:S(2)}) collective-permute-start(f32[2,4,16,136]{3,2,1,0:T(8,128)S(1)} %get-tuple-element.58), channel_id=1, source_target_pairs={{1,0},{2,1},{3,2},{5,4},{6,5},{7,6},{9,8},{10,9},{11,10},{13,12},{... | collective-permute-start | bytes 208904 | tf_op jit(solution)/shard_map/ppermute | solution.py:18
  72.3 3.4 %collective-permute-start.11 = (f32[2,4,16,136]{3,2,1,0:T(8,128)S(1)}, f32[2,4,16,136]{3,2,1,0:T(8,128)S(1)}, u32[]{:S(2)}, u32[]{:S(2)}) collective-permute-start(f32[2,4,16,136]{3,2,1,0:T(8,128)S(1)} %get-tuple-element.59), channel_id=1, source_target_pairs={{0,1},{1,2},{2,3},{4,5},{5,6},{6,7},{8,9},{9,10},{10,11},{12,13},{... | collective-permute-start | bytes 208904 | tf_op jit(solution)/shard_map/ppermute | solution.py:15
  75.7 0.2 pad_maximum_fusion.4
  75.9 0.8 collective-permute-done.10
  76.7 2.5 %collective-permute-done.11 = f32[2,4,16,136]{3,2,1,0:T(8,128)S(1)} collective-permute-done((f32[2,4,16,136]{3,2,1,0:T(8,128)S(1)}, f32[2,4,16,136]{3,2,1,0:T(8,128)S(1)}, u32[]{:S(2)}, u32[]{:S(2)}) %collective-permute-start.11) | collective-permute-done | bytes 69664 | tf_op jit(solution)/shard_map/ppermute | solution.py:15
  79.1 0.2 pad_maximum_fusion.1
  79.4 0.3 fusion.19
  79.7 0.2 fusion.3
  79.9 0.6 add_subtract_fusion
  80.6 0.6 copy-done.10
  (57 shorter events, 0.5 us)
Async XLA Ops:
  0.6 7.0 %copy-start = (f32[256,256]{1,0:T(8,128)S(1)}, f32[256,256]{1,0:T(8,128)}, u32[]{:S(2)}) copy-start(f32[256,256]{1,0:T(8,128)} %param.36) | copy-start | bytes 786436
  1.5 4.4 %copy-start.19 = (s32[256]{0:T(256)S(1)}, s32[256]{0:T(256)}, u32[]{:S(2)}) copy-start(s32[256]{0:T(256)} %param.40) | copy-start | bytes 3076
  1.5 4.4 %copy-start.18 = (s32[256]{0:T(256)S(1)}, s32[256]{0:T(256)}, u32[]{:S(2)}) copy-start(s32[256]{0:T(256)} %param.39) | copy-start | bytes 3076
  1.5 15.9 %collective-permute-start = (f32[2,8,4,128]{3,2,1,0:T(4,128)S(1)}, f32[2,8,4,128]{3,2,1,0:T(4,128)S(1)}, u32[]{:S(2)}, u32[]{:S(2)}) collective-permute-start(f32[2,8,4,128]{3,2,1,0:T(4,128)S(1)} %get-tuple-element.86), channel_id=1, source_target_pairs={{8,0},{16,8},{24,16},{9,1},{17,9},{25,17},{10,2},{18,10},{26,18},{... | collective-permute-start | bytes 98312 | tf_op jit(solution)/shard_map/ppermute | solution.py:18
  3.5 14.0 %collective-permute-start.1 = (f32[2,8,4,128]{3,2,1,0:T(4,128)S(1)}, f32[2,8,4,128]{3,2,1,0:T(4,128)S(1)}, u32[]{:S(2)}, u32[]{:S(2)}) collective-permute-start(f32[2,8,4,128]{3,2,1,0:T(4,128)S(1)} %get-tuple-element.85), channel_id=1, source_target_pairs={{0,8},{8,16},{16,24},{1,9},{9,17},{17,25},{2,10},{10,18},{18,26},{... | collective-permute-start | bytes 98312 | tf_op jit(solution)/shard_map/ppermute | solution.py:15
  6.9 0.7 copy-start.17
  6.9 0.7 copy-start.20
  7.6 0.7 copy-start.16
  11.3 5.9 %copy-start.12 = (f32[8,8,128]{2,1,0:T(8,128)S(1)}, f32[8,8,128]{2,1,0:T(8,128)}, u32[]{:S(2)}) copy-start(f32[8,8,128]{2,1,0:T(8,128)} %param.33) | copy-start | bytes 98308
  11.3 5.9 %copy-start.13 = (f32[8,8,128]{2,1,0:T(8,128)S(1)}, f32[8,8,128]{2,1,0:T(8,128)}, u32[]{:S(2)}) copy-start(f32[8,8,128]{2,1,0:T(8,128)} %param.32) | copy-start | bytes 98308
  11.3 23.7 %all-to-all-start = ((f32[32,1,192]{2,1,0:T(1,128)}), f32[32,1,192]{2,1,0:T(1,128)S(1)}, u32[]{:S(2)}, u32[]{:S(2)}) async-start(f32[32,1,192]{2,1,0:T(1,128)} %reshape.177), calls=%async_computation | async-start | bytes 65536 | tf_op jit(solution)/shard_map/all_to_all | solution.py:159
  17.4 0.8 copy-start.3
  17.4 0.8 copy-start.4
  18.3 5.5 %collective-permute-start.2 = (f32[2,8,16,4]{3,2,1,0:T(8,128)S(1)}, f32[2,8,16,4]{3,2,1,0:T(8,128)S(1)}, u32[]{:S(2)}, u32[]{:S(2)}) collective-permute-start(f32[2,8,16,4]{3,2,1,0:T(8,128)S(1)} %get-tuple-element.73), channel_id=1, source_target_pairs={{4,0},{5,1},{6,2},{7,3},{12,8},{13,9},{14,10},{15,11},{20,16},{21,... | collective-permute-start | bytes 12296 | tf_op jit(solution)/shard_map/ppermute | solution.py:18
  20.8 7.2 %collective-permute-start.3 = (f32[2,8,16,4]{3,2,1,0:T(8,128)S(1)}, f32[2,8,16,4]{3,2,1,0:T(8,128)S(1)}, u32[]{:S(2)}, u32[]{:S(2)}) collective-permute-start(f32[2,8,16,4]{3,2,1,0:T(8,128)S(1)} %get-tuple-element.72), channel_id=1, source_target_pairs={{0,4},{1,5},{2,6},{3,7},{8,12},{9,13},{10,14},{11,15},{16,20},{17,... | collective-permute-start | bytes 12296 | tf_op jit(solution)/shard_map/ppermute | solution.py:15
  28.9 23.3 %collective-permute-start.4 = (f32[2,4,16,136]{3,2,1,0:T(8,128)}, f32[2,4,16,136]{3,2,1,0:T(8,128)S(1)}, u32[]{:S(2)}, u32[]{:S(2)}) collective-permute-start(f32[2,4,16,136]{3,2,1,0:T(8,128)} %get-tuple-element.60), channel_id=1, source_target_pairs={{1,0},{2,1},{3,2},{5,4},{6,5},{7,6},{9,8},{10,9},{11,10},{13,12},{... | collective-permute-start | bytes 208904 | tf_op jit(solution)/shard_map/ppermute | solution.py:18
  31.4 20.8 %collective-permute-start.5 = (f32[2,4,16,136]{3,2,1,0:T(8,128)}, f32[2,4,16,136]{3,2,1,0:T(8,128)S(1)}, u32[]{:S(2)}, u32[]{:S(2)}) collective-permute-start(f32[2,4,16,136]{3,2,1,0:T(8,128)} %get-tuple-element.61), channel_id=1, source_target_pairs={{0,1},{1,2},{2,3},{4,5},{5,6},{6,7},{8,9},{9,10},{10,11},{12,13},{... | collective-permute-start | bytes 208904 | tf_op jit(solution)/shard_map/ppermute | solution.py:15
  53.0 0.8 copy-start.5
  53.0 0.8 copy-start.6
  53.0 0.8 copy-start.7
  53.0 0.8 copy-start.8
  53.0 0.8 copy-start.9
  53.0 0.8 copy-start.14
  53.0 0.8 copy-start.15
  53.9 26.6 %copy-start.1 = (f32[8,8,128]{2,1,0:T(8,128)}, f32[8,8,128]{2,1,0:T(8,128)S(1)}, u32[]{:S(2)}) copy-start(f32[8,8,128]{2,1,0:T(8,128)S(1)} %get-tuple-element.94) | copy-start | bytes 98308
  53.9 26.6 %copy-start.2 = (f32[8,8,128]{2,1,0:T(8,128)}, f32[8,8,128]{2,1,0:T(8,128)S(1)}, u32[]{:S(2)}) copy-start(f32[8,8,128]{2,1,0:T(8,128)S(1)} %get-tuple-element.95) | copy-start | bytes 98308
  53.9 4.3 %collective-permute-start.6 = (f32[2,8,4,128]{3,2,1,0:T(4,128)S(1)}, f32[2,8,4,128]{3,2,1,0:T(4,128)S(1)}, u32[]{:S(2)}, u32[]{:S(2)}) collective-permute-start(f32[2,8,4,128]{3,2,1,0:T(4,128)S(1)} %get-tuple-element.77), channel_id=1, source_target_pairs={{8,0},{16,8},{24,16},{9,1},{17,9},{25,17},{10,2},{18,10},{26,18},{... | collective-permute-start | bytes 98312 | tf_op jit(solution)/shard_map/ppermute | solution.py:18
  55.9 5.2 %collective-permute-start.7 = (f32[2,8,4,128]{3,2,1,0:T(4,128)S(1)}, f32[2,8,4,128]{3,2,1,0:T(4,128)S(1)}, u32[]{:S(2)}, u32[]{:S(2)}) collective-permute-start(f32[2,8,4,128]{3,2,1,0:T(4,128)S(1)} %get-tuple-element.76), channel_id=1, source_target_pairs={{0,8},{8,16},{16,24},{1,9},{9,17},{17,25},{2,10},{10,18},{18,26},{... | collective-permute-start | bytes 98312 | tf_op jit(solution)/shard_map/ppermute | solution.py:15
  61.2 4.0 %collective-permute-start.8 = (f32[2,8,16,4]{3,2,1,0:T(8,128)S(1)}, f32[2,8,16,4]{3,2,1,0:T(8,128)S(1)}, u32[]{:S(2)}, u32[]{:S(2)}) collective-permute-start(f32[2,8,16,4]{3,2,1,0:T(8,128)S(1)} %get-tuple-element.69), channel_id=1, source_target_pairs={{4,0},{5,1},{6,2},{7,3},{12,8},{13,9},{14,10},{15,11},{20,16},{21,... | collective-permute-start | bytes 12296 | tf_op jit(solution)/shard_map/ppermute | solution.py:18
  62.7 6.9 %collective-permute-start.9 = (f32[2,8,16,4]{3,2,1,0:T(8,128)S(1)}, f32[2,8,16,4]{3,2,1,0:T(8,128)S(1)}, u32[]{:S(2)}, u32[]{:S(2)}) collective-permute-start(f32[2,8,16,4]{3,2,1,0:T(8,128)S(1)} %get-tuple-element.68), channel_id=1, source_target_pairs={{0,4},{1,5},{2,6},{3,7},{8,12},{9,13},{10,14},{11,15},{16,20},{17,... | collective-permute-start | bytes 12296 | tf_op jit(solution)/shard_map/ppermute | solution.py:15
  69.8 6.9 %collective-permute-start.10 = (f32[2,4,16,136]{3,2,1,0:T(8,128)S(1)}, f32[2,4,16,136]{3,2,1,0:T(8,128)S(1)}, u32[]{:S(2)}, u32[]{:S(2)}) collective-permute-start(f32[2,4,16,136]{3,2,1,0:T(8,128)S(1)} %get-tuple-element.58), channel_id=1, source_target_pairs={{1,0},{2,1},{3,2},{5,4},{6,5},{7,6},{9,8},{10,9},{11,10},{13,12},{... | collective-permute-start | bytes 208904 | tf_op jit(solution)/shard_map/ppermute | solution.py:18
  72.3 6.9 %collective-permute-start.11 = (f32[2,4,16,136]{3,2,1,0:T(8,128)S(1)}, f32[2,4,16,136]{3,2,1,0:T(8,128)S(1)}, u32[]{:S(2)}, u32[]{:S(2)}) collective-permute-start(f32[2,4,16,136]{3,2,1,0:T(8,128)S(1)} %get-tuple-element.59), channel_id=1, source_target_pairs={{0,1},{1,2},{2,3},{4,5},{5,6},{6,7},{8,9},{9,10},{10,11},{12,13},{... | collective-permute-start | bytes 208904 | tf_op jit(solution)/shard_map/ppermute | solution.py:15
  80.6 0.6 copy-start.10
  80.6 0.6 copy-start.11

commit v2 on v1

--- a/solution.py
+++ b/solution.py
@@ -158,8 +158,14 @@
     send = jnp.zeros((columns * gz_count * capacity, width), jnp.float32).at[slot].set(packed)
     arrived = lax.all_to_all(send, ("inl", "xl", "gz"), split_axis=0, concat_axis=0, tiled=True)
     target = arrived[:, steps].astype(jnp.int32)
-    planes = jnp.zeros((steps, cells), jnp.float32).at[:, target].add(arrived[:, :steps].T, mode="drop")
-    planes = planes.reshape(steps, inline_cells, cross_cells)
+    row_hit = (
+        target[:, None] // cross_cells == jnp.arange(inline_cells, dtype=jnp.int32)[None, :]
+    ).astype(jnp.float32)
+    col_hit = (
+        target[:, None] % cross_cells == jnp.arange(cross_cells, dtype=jnp.int32)[None, :]
+    ).astype(jnp.float32)
+    weighted = arrived[:, :steps, None] * row_hit[:, None, :]
+    planes = jnp.einsum("nkx,ny->kxy", weighted, col_hit, precision=lax.Precision.HIGHEST)
     fields = (courant_square, thomsen_epsilon, thomsen_delta, shear_ratio, damping)
     current = jnp.stack([wave_p, wave_q])
     previous = jnp.stack([wave_p_old, wave_q_old])

time: 81.9 us -> 67.6 us (0.83)
  the two profiles are of different devices: /device:TPU:22 before, /device:TPU:14 now
where the time goes in v2:
time: 67.6 us; the launch traced here: 66.8 us
  starting transfers between devices  32.8 us (49%)
  waiting for transfers between devices  17.5 us (26%)
  local copies, waits for them, and re-layouts  8.09 us (12%)
  other arithmetic  6.36 us (9%)
  between operations  1.27 us (2%)
  matrix products  0.85 us (1%)
    ppermute x6, starting transfers between devices, with_halo(): lax.ppermute(lax.slice_in_dim(block, block.shape[dim] - width, None, axis...  14.1 us
    ppermute x6, waiting for transfers between devices, with_halo(): lax.ppermute(lax.slice_in_dim(block, block.shape[dim] - width, None, axis...  13.8 us
    ppermute x6, starting transfers between devices, with_halo(): lax.ppermute(lax.slice_in_dim(block, 0, width, axis=dim), axis, backward)  12.7 us
    all_to_all x1, starting transfers between devices, local(): lax.all_to_all(send, ('inl', 'xl', 'gz'), split_axis=0, concat_axis=0, ti...  5.96 us
    unnamed x46, local copies, waits for them, and re-layouts  4.18 us
    ppermute x6, waiting for transfers between devices, with_halo(): lax.ppermute(lax.slice_in_dim(block, 0, width, axis=dim), axis, backward)  3.67 us
    concatenate x10, other arithmetic, with_halo(): block = jnp.concatenate([low, block, high], axis=dim)  1.47 us
    scatter x1, local copies, waits for them, and re-layouts, local(): jnp.zeros((columns * gz_count * capacity, width), jnp.float32).at[slot]  1.41 us
  transfers between devices with their start and end apart: 13, of which 7 were waited for; matrix products, arithmetic and copies ran while one was open for 11% of the time, Pallas kernels for 0%

profile of v2, /device:TPU:14, one launch (start us, length us, event | category | flops | bytes accessed | tf_op | source)
XLA Modules:
  0.0 66.8 jit_solution(7149316149931104013)
XLA Ops:
  0.6 0.9 %fusion.149 = (f32[2,8,4,128]{3,2,1,0:T(4,128)S(1)}, f32[2,8,4,128]{3,2,1,0:T(4,128)S(1)}) fusion(f32[1,8,8,128]{3,2,1,0:T(8,128)} %bitcast.119, f32[1,8,8,128]{3,2,1,0:T(8,128)} %bitcast.126), kind=kLoop, calls=%fused_computation.270 | loop fusion | flops 16384 | bytes 131072 | tf_op jit(solution)/shard_map/stack | solution.py:170
  1.5 1.9 %collective-permute-start = (f32[2,8,4,128]{3,2,1,0:T(4,128)S(1)}, f32[2,8,4,128]{3,2,1,0:T(4,128)S(1)}, u32[]{:S(2)}, u32[]{:S(2)}) collective-permute-start(f32[2,8,4,128]{3,2,1,0:T(4,128)S(1)} %get-tuple-element.86), channel_id=1, source_target_pairs={{8,0},{16,8},{24,16},{9,1},{17,9},{25,17},{10,2},{18,10},{26,18},{... | collective-permute-start | bytes 98312 | tf_op jit(solution)/shard_map/ppermute | solution.py:18
  3.5 2.4 %collective-permute-start.1 = (f32[2,8,4,128]{3,2,1,0:T(4,128)S(1)}, f32[2,8,4,128]{3,2,1,0:T(4,128)S(1)}, u32[]{:S(2)}, u32[]{:S(2)}) collective-permute-start(f32[2,8,4,128]{3,2,1,0:T(4,128)S(1)} %get-tuple-element.85), channel_id=1, source_target_pairs={{0,8},{8,16},{16,24},{1,9},{9,17},{17,25},{2,10},{10,18},{18,26},{... | collective-permute-start | bytes 98312 | tf_op jit(solution)/shard_map/ppermute | solution.py:15
  5.9 0.6 reduce-window.6
  6.5 0.2 slice_reduce_fusion
  6.8 0.1 fusion.176
  6.9 0.7 copy-done.18
  7.6 0.1 select_reduce_fusion
  7.7 0.6 copy-done.17
  8.2 0.3 convolution_multiply_fusion
  8.5 0.1 pad_maximum_fusion.36
  8.6 0.1 copy.30
  8.7 1.4 %scatter_custom_fusion = f32[2048,3]{1,0:T(8,128)S(1)} fusion(s32[256]{0:T(256)S(1)} %compare_select_fusion.3, f32[256,3]{1,0:T(8,128)S(1)} %copy.30, f32[]{:T(128)} %constant.184.clone.1), kind=kCustom, calls=%fused_computation.8 | custom fusion | bytes 24580 | tf_op jit(solution)/shard_map/scatter | solution.py:158
  10.1 0.4 copy.31
  10.5 0.7 %reshape.199 = f32[32,1,192]{2,1,0:T(1,128)} reshape(f32[32,3,64]{2,1,0:T(4,128)S(1)} %bitcast.133) | data formatting | bytes 49152
  11.3 6.0 %all-to-all-start = ((f32[32,1,192]{2,1,0:T(1,128)}), f32[32,1,192]{2,1,0:T(1,128)S(1)}, u32[]{:S(2)}, u32[]{:S(2)}) async-start(f32[32,1,192]{2,1,0:T(1,128)} %reshape.199), calls=%async_computation | async-start | bytes 65536 | tf_op jit(solution)/shard_map/all_to_all | solution.py:159
  17.2 0.2 fusion.192
  17.6 0.7 %copy-done.3 = f32[8,8,128]{2,1,0:T(8,128)S(1)} copy-done((f32[8,8,128]{2,1,0:T(8,128)S(1)}, f32[8,8,128]{2,1,0:T(8,128)}, u32[]{:S(2)}) %copy-start.3) | copy-done | bytes 32792
  18.3 0.0 copy-done.4
  18.3 0.1 fusion.191
  18.4 2.5 %collective-permute-start.2 = (f32[2,8,16,4]{3,2,1,0:T(8,128)S(1)}, f32[2,8,16,4]{3,2,1,0:T(8,128)S(1)}, u32[]{:S(2)}, u32[]{:S(2)}) collective-permute-start(f32[2,8,16,4]{3,2,1,0:T(8,128)S(1)} %get-tuple-element.73), channel_id=1, source_target_pairs={{4,0},{5,1},{6,2},{7,3},{12,8},{13,9},{14,10},{15,11},{20,16},{21,... | collective-permute-start | bytes 12296 | tf_op jit(solution)/shard_map/ppermute | solution.py:18
  20.9 1.3 %collective-permute-start.3 = (f32[2,8,16,4]{3,2,1,0:T(8,128)S(1)}, f32[2,8,16,4]{3,2,1,0:T(8,128)S(1)}, u32[]{:S(2)}, u32[]{:S(2)}) collective-permute-start(f32[2,8,16,4]{3,2,1,0:T(8,128)S(1)} %get-tuple-element.72), channel_id=1, source_target_pairs={{0,4},{1,5},{2,6},{3,7},{8,12},{9,13},{10,14},{11,15},{16,20},{17,... | collective-permute-start | bytes 12296 | tf_op jit(solution)/shard_map/ppermute | solution.py:15
  22.2 1.7 %collective-permute-done.2 = f32[2,8,16,4]{3,2,1,0:T(8,128)S(1)} collective-permute-done((f32[2,8,16,4]{3,2,1,0:T(8,128)S(1)}, f32[2,8,16,4]{3,2,1,0:T(8,128)S(1)}, u32[]{:S(2)}, u32[]{:S(2)}) %collective-permute-start.2) | collective-permute-done | bytes 4128 | tf_op jit(solution)/shard_map/ppermute | solution.py:18
  23.9 4.1 %collective-permute-done.3 = f32[2,8,16,4]{3,2,1,0:T(8,128)S(1)} collective-permute-done((f32[2,8,16,4]{3,2,1,0:T(8,128)S(1)}, f32[2,8,16,4]{3,2,1,0:T(8,128)S(1)}, u32[]{:S(2)}, u32[]{:S(2)}) %collective-permute-start.3) | collective-permute-done | bytes 4128 | tf_op jit(solution)/shard_map/ppermute | solution.py:15
  28.0 0.2 pad_maximum_fusion.3
  28.3 2.5 %collective-permute-start.4 = (f32[2,4,16,136]{3,2,1,0:T(8,128)S(1)}, f32[2,4,16,136]{3,2,1,0:T(8,128)S(1)}, u32[]{:S(2)}, u32[]{:S(2)}) collective-permute-start(f32[2,4,16,136]{3,2,1,0:T(8,128)S(1)} %get-tuple-element.60), channel_id=1, source_target_pairs={{1,0},{2,1},{3,2},{5,4},{6,5},{7,6},{9,8},{10,9},{11,10},{13,12},{... | collective-permute-start | bytes 208904 | tf_op jit(solution)/shard_map/ppermute | solution.py:18
  30.8 3.4 %collective-permute-start.5 = (f32[2,4,16,136]{3,2,1,0:T(8,128)S(1)}, f32[2,4,16,136]{3,2,1,0:T(8,128)S(1)}, u32[]{:S(2)}, u32[]{:S(2)}) collective-permute-start(f32[2,4,16,136]{3,2,1,0:T(8,128)S(1)} %get-tuple-element.61), channel_id=1, source_target_pairs={{0,1},{1,2},{2,3},{4,5},{5,6},{6,7},{8,9},{9,10},{10,11},{12,13},{... | collective-permute-start | bytes 208904 | tf_op jit(solution)/shard_map/ppermute | solution.py:15
  34.2 0.2 pad_maximum_fusion.2
  34.4 0.5 broadcast.400
  34.9 0.7 %reduce.10 = f32[32,192]{1,0:T(8,128)S(1)} reduce(f32[32,1,192]{2,1,0:T(1,128)S(1)} %all-to-all-done, f32[]{:T(128)} %broadcast.400), dimensions={1}, to_apply=%all_to_all.9.reduce_sub_computation | reduce | bytes 49156 | tf_op jit(solution)/shard_map/all_to_all | solution.py:159
  35.6 0.1 reshape.200
  35.8 0.1 all_to_all.10
  35.9 0.1 and_select_fusion.1
  35.9 0.5 copy-done.10
  36.5 0.7 %slice-done = f32[2048,2]{0,1:T(2,128)S(1)} async-done(((f32[2048,3]{0,1:T(4,128)}), f32[2048,2]{0,1:T(2,128)S(1)}, s32[]{:S(2)}) %slice-start) | async-done | bytes 16408 | tf_op jit(solution)/shard_map/slice | solution.py:167
  37.2 0.6 fusion.1
  37.8 0.2 pad_maximum_fusion
  38.1 0.3 fusion.28
  38.4 0.2 fusion.14
  38.7 0.6 add_subtract_fusion.1
  39.3 0.1 copy-done.5
  39.3 0.0 copy-done.6
  39.4 0.0 copy-done.8
  39.4 0.0 copy-done.9
  39.4 0.0 copy-done.16
  39.5 1.9 %collective-permute-start.6 = (f32[2,8,4,128]{3,2,1,0:T(4,128)S(1)}, f32[2,8,4,128]{3,2,1,0:T(4,128)S(1)}, u32[]{:S(2)}, u32[]{:S(2)}) collective-permute-start(f32[2,8,4,128]{3,2,1,0:T(4,128)S(1)} %get-tuple-element.77), channel_id=1, source_target_pairs={{8,0},{16,8},{24,16},{9,1},{17,9},{25,17},{10,2},{18,10},{26,18},{... | collective-permute-start | bytes 98312 | tf_op jit(solution)/shard_map/ppermute | solution.py:18
  41.5 2.4 %collective-permute-start.7 = (f32[2,8,4,128]{3,2,1,0:T(4,128)S(1)}, f32[2,8,4,128]{3,2,1,0:T(4,128)S(1)}, u32[]{:S(2)}, u32[]{:S(2)}) collective-permute-start(f32[2,8,4,128]{3,2,1,0:T(4,128)S(1)} %get-tuple-element.76), channel_id=1, source_target_pairs={{0,8},{8,16},{16,24},{1,9},{9,17},{17,25},{2,10},{10,18},{18,26},{... | collective-permute-start | bytes 98312 | tf_op jit(solution)/shard_map/ppermute | solution.py:15
  43.9 2.8 %collective-permute-done.7 = f32[2,8,4,128]{3,2,1,0:T(4,128)S(1)} collective-permute-done((f32[2,8,4,128]{3,2,1,0:T(4,128)S(1)}, f32[2,8,4,128]{3,2,1,0:T(4,128)S(1)}, u32[]{:S(2)}, u32[]{:S(2)}) %collective-permute-start.7) | collective-permute-done | bytes 32800 | tf_op jit(solution)/shard_map/ppermute | solution.py:15
  46.7 0.1 fusion.190
  46.8 1.5 %collective-permute-start.8 = (f32[2,8,16,4]{3,2,1,0:T(8,128)S(1)}, f32[2,8,16,4]{3,2,1,0:T(8,128)S(1)}, u32[]{:S(2)}, u32[]{:S(2)}) collective-permute-start(f32[2,8,16,4]{3,2,1,0:T(8,128)S(1)} %get-tuple-element.69), channel_id=1, source_target_pairs={{4,0},{5,1},{6,2},{7,3},{12,8},{13,9},{14,10},{15,11},{20,16},{21,... | collective-permute-start | bytes 12296 | tf_op jit(solution)/shard_map/ppermute | solution.py:18
  48.3 1.3 %collective-permute-start.9 = (f32[2,8,16,4]{3,2,1,0:T(8,128)S(1)}, f32[2,8,16,4]{3,2,1,0:T(8,128)S(1)}, u32[]{:S(2)}, u32[]{:S(2)}) collective-permute-start(f32[2,8,16,4]{3,2,1,0:T(8,128)S(1)} %get-tuple-element.68), channel_id=1, source_target_pairs={{0,4},{1,5},{2,6},{3,7},{8,12},{9,13},{10,14},{11,15},{16,20},{17,... | collective-permute-start | bytes 12296 | tf_op jit(solution)/shard_map/ppermute | solution.py:15
  49.6 1.2 %collective-permute-done.8 = f32[2,8,16,4]{3,2,1,0:T(8,128)S(1)} collective-permute-done((f32[2,8,16,4]{3,2,1,0:T(8,128)S(1)}, f32[2,8,16,4]{3,2,1,0:T(8,128)S(1)}, u32[]{:S(2)}, u32[]{:S(2)}) %collective-permute-start.8) | collective-permute-done | bytes 4128 | tf_op jit(solution)/shard_map/ppermute | solution.py:18
  50.8 4.4 %collective-permute-done.9 = f32[2,8,16,4]{3,2,1,0:T(8,128)S(1)} collective-permute-done((f32[2,8,16,4]{3,2,1,0:T(8,128)S(1)}, f32[2,8,16,4]{3,2,1,0:T(8,128)S(1)}, u32[]{:S(2)}, u32[]{:S(2)}) %collective-permute-start.9) | collective-permute-done | bytes 4128 | tf_op jit(solution)/shard_map/ppermute | solution.py:15
  55.2 0.2 pad_maximum_fusion.5
  55.4 2.5 %collective-permute-start.10 = (f32[2,4,16,136]{3,2,1,0:T(8,128)S(1)}, f32[2,4,16,136]{3,2,1,0:T(8,128)S(1)}, u32[]{:S(2)}, u32[]{:S(2)}) collective-permute-start(f32[2,4,16,136]{3,2,1,0:T(8,128)S(1)} %get-tuple-element.58), channel_id=1, source_target_pairs={{1,0},{2,1},{3,2},{5,4},{6,5},{7,6},{9,8},{10,9},{11,10},{13,12},{... | collective-permute-start | bytes 208904 | tf_op jit(solution)/shard_map/ppermute | solution.py:18
  57.9 3.4 %collective-permute-start.11 = (f32[2,4,16,136]{3,2,1,0:T(8,128)S(1)}, f32[2,4,16,136]{3,2,1,0:T(8,128)S(1)}, u32[]{:S(2)}, u32[]{:S(2)}) collective-permute-start(f32[2,4,16,136]{3,2,1,0:T(8,128)S(1)} %get-tuple-element.59), channel_id=1, source_target_pairs={{0,1},{1,2},{2,3},{4,5},{5,6},{6,7},{8,9},{9,10},{10,11},{12,13},{... | collective-permute-start | bytes 208904 | tf_op jit(solution)/shard_map/ppermute | solution.py:15
  61.3 0.2 pad_maximum_fusion.4
  61.5 0.8 %collective-permute-done.10 = f32[2,4,16,136]{3,2,1,0:T(8,128)S(1)} collective-permute-done((f32[2,4,16,136]{3,2,1,0:T(8,128)S(1)}, f32[2,4,16,136]{3,2,1,0:T(8,128)S(1)}, u32[]{:S(2)}, u32[]{:S(2)}) %collective-permute-start.10) | collective-permute-done | bytes 69664 | tf_op jit(solution)/shard_map/ppermute | solution.py:18
  62.3 2.5 %collective-permute-done.11 = f32[2,4,16,136]{3,2,1,0:T(8,128)S(1)} collective-permute-done((f32[2,4,16,136]{3,2,1,0:T(8,128)S(1)}, f32[2,4,16,136]{3,2,1,0:T(8,128)S(1)}, u32[]{:S(2)}, u32[]{:S(2)}) %collective-permute-start.11) | collective-permute-done | bytes 69664 | tf_op jit(solution)/shard_map/ppermute | solution.py:15
  64.8 0.2 pad_maximum_fusion.1
  65.0 0.3 fusion.21
  65.3 0.2 fusion.7
  65.5 0.6 add_subtract_fusion
  66.2 0.6 copy-done.11
  (60 shorter events, 0.5 us)
Async XLA Ops:
  0.6 7.0 %copy-start = (f32[256,256]{1,0:T(8,128)S(1)}, f32[256,256]{1,0:T(8,128)}, u32[]{:S(2)}) copy-start(f32[256,256]{1,0:T(8,128)} %param.36) | copy-start | bytes 786436
  1.5 4.4 %copy-start.20 = (s32[256]{0:T(256)S(1)}, s32[256]{0:T(256)}, u32[]{:S(2)}) copy-start(s32[256]{0:T(256)} %param.40) | copy-start | bytes 3076
  1.5 4.4 %copy-start.19 = (s32[256]{0:T(256)S(1)}, s32[256]{0:T(256)}, u32[]{:S(2)}) copy-start(s32[256]{0:T(256)} %param.39) | copy-start | bytes 3076
  1.5 16.0 %collective-permute-start = (f32[2,8,4,128]{3,2,1,0:T(4,128)S(1)}, f32[2,8,4,128]{3,2,1,0:T(4,128)S(1)}, u32[]{:S(2)}, u32[]{:S(2)}) collective-permute-start(f32[2,8,4,128]{3,2,1,0:T(4,128)S(1)} %get-tuple-element.86), channel_id=1, source_target_pairs={{8,0},{16,8},{24,16},{9,1},{17,9},{25,17},{10,2},{18,10},{26,18},{... | collective-permute-start | bytes 98312 | tf_op jit(solution)/shard_map/ppermute | solution.py:18
  3.5 14.1 %collective-permute-start.1 = (f32[2,8,4,128]{3,2,1,0:T(4,128)S(1)}, f32[2,8,4,128]{3,2,1,0:T(4,128)S(1)}, u32[]{:S(2)}, u32[]{:S(2)}) collective-permute-start(f32[2,8,4,128]{3,2,1,0:T(4,128)S(1)} %get-tuple-element.85), channel_id=1, source_target_pairs={{0,8},{8,16},{16,24},{1,9},{9,17},{17,25},{2,10},{10,18},{18,26},{... | collective-permute-start | bytes 98312 | tf_op jit(solution)/shard_map/ppermute | solution.py:15
  6.9 0.7 %copy-start.18 = (s32[256]{0:T(256)S(1)}, s32[256]{0:T(256)}, u32[]{:S(2)}) copy-start(s32[256]{0:T(256)} %param.41) | copy-start | bytes 3076
  6.9 0.7 %copy-start.21 = (f32[64]{0:T(128)S(1)}, f32[64]{0:T(128)}, u32[]{:S(2)}) copy-start(f32[64]{0:T(128)} %param.38) | copy-start | bytes 772
  7.6 0.7 %copy-start.17 = (f32[2,256]{1,0:T(2,128)S(1)}, f32[2,256]{1,0:T(2,128)}, u32[]{:S(2)}) copy-start(f32[2,256]{1,0:T(2,128)} %param.37) | copy-start | bytes 6148
  11.3 6.0 %copy-start.13 = (f32[8,8,128]{2,1,0:T(8,128)S(1)}, f32[8,8,128]{2,1,0:T(8,128)}, u32[]{:S(2)}) copy-start(f32[8,8,128]{2,1,0:T(8,128)} %param.33) | copy-start | bytes 98308
  11.3 6.0 %copy-start.14 = (f32[8,8,128]{2,1,0:T(8,128)S(1)}, f32[8,8,128]{2,1,0:T(8,128)}, u32[]{:S(2)}) copy-start(f32[8,8,128]{2,1,0:T(8,128)} %param.32) | copy-start | bytes 98308
  11.3 23.1 %all-to-all-start = ((f32[32,1,192]{2,1,0:T(1,128)}), f32[32,1,192]{2,1,0:T(1,128)S(1)}, u32[]{:S(2)}, u32[]{:S(2)}) async-start(f32[32,1,192]{2,1,0:T(1,128)} %reshape.199), calls=%async_computation | async-start | bytes 65536 | tf_op jit(solution)/shard_map/all_to_all | solution.py:159
  17.5 0.8 %copy-start.3 = (f32[8,8,128]{2,1,0:T(8,128)S(1)}, f32[8,8,128]{2,1,0:T(8,128)}, u32[]{:S(2)}) copy-start(f32[8,8,128]{2,1,0:T(8,128)} %param.25) | copy-start | bytes 98308
  17.5 0.8 %copy-start.4 = (f32[8,8,128]{2,1,0:T(8,128)S(1)}, f32[8,8,128]{2,1,0:T(8,128)}, u32[]{:S(2)}) copy-start(f32[8,8,128]{2,1,0:T(8,128)} %param.27) | copy-start | bytes 98308
  18.4 5.5 %collective-permute-start.2 = (f32[2,8,16,4]{3,2,1,0:T(8,128)S(1)}, f32[2,8,16,4]{3,2,1,0:T(8,128)S(1)}, u32[]{:S(2)}, u32[]{:S(2)}) collective-permute-start(f32[2,8,16,4]{3,2,1,0:T(8,128)S(1)} %get-tuple-element.73), channel_id=1, source_target_pairs={{4,0},{5,1},{6,2},{7,3},{12,8},{13,9},{14,10},{15,11},{20,16},{21,... | collective-permute-start | bytes 12296 | tf_op jit(solution)/shard_map/ppermute | solution.py:18
  20.9 7.2 %collective-permute-start.3 = (f32[2,8,16,4]{3,2,1,0:T(8,128)S(1)}, f32[2,8,16,4]{3,2,1,0:T(8,128)S(1)}, u32[]{:S(2)}, u32[]{:S(2)}) collective-permute-start(f32[2,8,16,4]{3,2,1,0:T(8,128)S(1)} %get-tuple-element.72), channel_id=1, source_target_pairs={{0,4},{1,5},{2,6},{3,7},{8,12},{9,13},{10,14},{11,15},{16,20},{17,... | collective-permute-start | bytes 12296 | tf_op jit(solution)/shard_map/ppermute | solution.py:15
  28.3 9.5 %collective-permute-start.4 = (f32[2,4,16,136]{3,2,1,0:T(8,128)S(1)}, f32[2,4,16,136]{3,2,1,0:T(8,128)S(1)}, u32[]{:S(2)}, u32[]{:S(2)}) collective-permute-start(f32[2,4,16,136]{3,2,1,0:T(8,128)S(1)} %get-tuple-element.60), channel_id=1, source_target_pairs={{1,0},{2,1},{3,2},{5,4},{6,5},{7,6},{9,8},{10,9},{11,10},{13,12},{... | collective-permute-start | bytes 208904 | tf_op jit(solution)/shard_map/ppermute | solution.py:18
  30.8 7.0 %collective-permute-start.5 = (f32[2,4,16,136]{3,2,1,0:T(8,128)S(1)}, f32[2,4,16,136]{3,2,1,0:T(8,128)S(1)}, u32[]{:S(2)}, u32[]{:S(2)}) collective-permute-start(f32[2,4,16,136]{3,2,1,0:T(8,128)S(1)} %get-tuple-element.61), channel_id=1, source_target_pairs={{0,1},{1,2},{2,3},{4,5},{5,6},{6,7},{8,9},{9,10},{10,11},{12,13},{... | collective-permute-start | bytes 208904 | tf_op jit(solution)/shard_map/ppermute | solution.py:15
  35.8 0.6 copy-start.10
  36.5 0.7 %slice-start = ((f32[2048,3]{0,1:T(4,128)}), f32[2048,2]{0,1:T(2,128)S(1)}, s32[]{:S(2)}) async-start(f32[2048,3]{0,1:T(4,128)} %copy-done.10), calls=%async_computation.1 | async-start | bytes 32768 | tf_op jit(solution)/shard_map/slice | solution.py:167
  38.6 0.8 %copy-start.5 = (f32[8,8,128]{2,1,0:T(8,128)S(1)}, f32[8,8,128]{2,1,0:T(8,128)}, u32[]{:S(2)}) copy-start(f32[8,8,128]{2,1,0:T(8,128)} %param.29) | copy-start | bytes 98308
  38.6 0.8 %copy-start.6 = (f32[8,8,128]{2,1,0:T(8,128)S(1)}, f32[8,8,128]{2,1,0:T(8,128)}, u32[]{:S(2)}) copy-start(f32[8,8,128]{2,1,0:T(8,128)} %param.34) | copy-start | bytes 98308
  38.6 0.8 %copy-start.7 = (f32[8,8,128]{2,1,0:T(8,128)S(1)}, f32[8,8,128]{2,1,0:T(8,128)}, u32[]{:S(2)}) copy-start(f32[8,8,128]{2,1,0:T(8,128)} %param.35) | copy-start | bytes 98308
  38.6 0.8 %copy-start.8 = (f32[8,8,128]{2,1,0:T(8,128)S(1)}, f32[8,8,128]{2,1,0:T(8,128)}, u32[]{:S(2)}) copy-start(f32[8,8,128]{2,1,0:T(8,128)} %param.31) | copy-start | bytes 98308
  38.6 0.8 %copy-start.9 = (f32[8,8,128]{2,1,0:T(8,128)S(1)}, f32[8,8,128]{2,1,0:T(8,128)}, u32[]{:S(2)}) copy-start(f32[8,8,128]{2,1,0:T(8,128)} %param.30) | copy-start | bytes 98308
  38.6 0.8 %copy-start.15 = (f32[8,8,128]{2,1,0:T(8,128)S(1)}, f32[8,8,128]{2,1,0:T(8,128)}, u32[]{:S(2)}) copy-start(f32[8,8,128]{2,1,0:T(8,128)} %param.28) | copy-start | bytes 98308
  38.6 0.8 %copy-start.16 = (f32[8,8,128]{2,1,0:T(8,128)S(1)}, f32[8,8,128]{2,1,0:T(8,128)}, u32[]{:S(2)}) copy-start(f32[8,8,128]{2,1,0:T(8,128)} %param.26) | copy-start | bytes 98308
  39.5 26.6 %copy-start.1 = (f32[8,8,128]{2,1,0:T(8,128)}, f32[8,8,128]{2,1,0:T(8,128)S(1)}, u32[]{:S(2)}) copy-start(f32[8,8,128]{2,1,0:T(8,128)S(1)} %get-tuple-element.94) | copy-start | bytes 98308
  39.5 26.6 %copy-start.2 = (f32[8,8,128]{2,1,0:T(8,128)}, f32[8,8,128]{2,1,0:T(8,128)S(1)}, u32[]{:S(2)}) copy-start(f32[8,8,128]{2,1,0:T(8,128)S(1)} %get-tuple-element.95) | copy-start | bytes 98308
  39.5 4.3 %collective-permute-start.6 = (f32[2,8,4,128]{3,2,1,0:T(4,128)S(1)}, f32[2,8,4,128]{3,2,1,0:T(4,128)S(1)}, u32[]{:S(2)}, u32[]{:S(2)}) collective-permute-start(f32[2,8,4,128]{3,2,1,0:T(4,128)S(1)} %get-tuple-element.77), channel_id=1, source_target_pairs={{8,0},{16,8},{24,16},{9,1},{17,9},{25,17},{10,2},{18,10},{26,18},{... | collective-permute-start | bytes 98312 | tf_op jit(solution)/shard_map/ppermute | solution.py:18
  41.5 5.2 %collective-permute-start.7 = (f32[2,8,4,128]{3,2,1,0:T(4,128)S(1)}, f32[2,8,4,128]{3,2,1,0:T(4,128)S(1)}, u32[]{:S(2)}, u32[]{:S(2)}) collective-permute-start(f32[2,8,4,128]{3,2,1,0:T(4,128)S(1)} %get-tuple-element.76), channel_id=1, source_target_pairs={{0,8},{8,16},{16,24},{1,9},{9,17},{17,25},{2,10},{10,18},{18,26},{... | collective-permute-start | bytes 98312 | tf_op jit(solution)/shard_map/ppermute | solution.py:15
  46.8 4.0 %collective-permute-start.8 = (f32[2,8,16,4]{3,2,1,0:T(8,128)S(1)}, f32[2,8,16,4]{3,2,1,0:T(8,128)S(1)}, u32[]{:S(2)}, u32[]{:S(2)}) collective-permute-start(f32[2,8,16,4]{3,2,1,0:T(8,128)S(1)} %get-tuple-element.69), channel_id=1, source_target_pairs={{4,0},{5,1},{6,2},{7,3},{12,8},{13,9},{14,10},{15,11},{20,16},{21,... | collective-permute-start | bytes 12296 | tf_op jit(solution)/shard_map/ppermute | solution.py:18
  48.3 6.9 %collective-permute-start.9 = (f32[2,8,16,4]{3,2,1,0:T(8,128)S(1)}, f32[2,8,16,4]{3,2,1,0:T(8,128)S(1)}, u32[]{:S(2)}, u32[]{:S(2)}) collective-permute-start(f32[2,8,16,4]{3,2,1,0:T(8,128)S(1)} %get-tuple-element.68), channel_id=1, source_target_pairs={{0,4},{1,5},{2,6},{3,7},{8,12},{9,13},{10,14},{11,15},{16,20},{17,... | collective-permute-start | bytes 12296 | tf_op jit(solution)/shard_map/ppermute | solution.py:15
  55.4 6.9 %collective-permute-start.10 = (f32[2,4,16,136]{3,2,1,0:T(8,128)S(1)}, f32[2,4,16,136]{3,2,1,0:T(8,128)S(1)}, u32[]{:S(2)}, u32[]{:S(2)}) collective-permute-start(f32[2,4,16,136]{3,2,1,0:T(8,128)S(1)} %get-tuple-element.58), channel_id=1, source_target_pairs={{1,0},{2,1},{3,2},{5,4},{6,5},{7,6},{9,8},{10,9},{11,10},{13,12},{... | collective-permute-start | bytes 208904 | tf_op jit(solution)/shard_map/ppermute | solution.py:18
  57.9 6.9 %collective-permute-start.11 = (f32[2,4,16,136]{3,2,1,0:T(8,128)S(1)}, f32[2,4,16,136]{3,2,1,0:T(8,128)S(1)}, u32[]{:S(2)}, u32[]{:S(2)}) collective-permute-start(f32[2,4,16,136]{3,2,1,0:T(8,128)S(1)} %get-tuple-element.59), channel_id=1, source_target_pairs={{0,1},{1,2},{2,3},{4,5},{5,6},{6,7},{8,9},{9,10},{10,11},{12,13},{... | collective-permute-start | bytes 208904 | tf_op jit(solution)/shard_map/ppermute | solution.py:15
  66.2 0.6 copy-start.11
  66.2 0.6 copy-start.12

commit v3 on v2

--- a/solution.py
+++ b/solution.py
@@ -5,19 +5,6 @@
 
 second_coef = (-205.0 / 72.0, 8.0 / 5.0, -1.0 / 5.0, 8.0 / 315.0, -1.0 / 560.0)
 first_coef = (0.0, 4.0 / 5.0, -1.0 / 5.0, 4.0 / 105.0, -1.0 / 280.0)
-
-
-def with_halo(block, sides, width):
-    for axis, dim in sides:
-        count = lax.axis_size(axis)
-        forward = [(i, i + 1) for i in range(count - 1)]
-        backward = [(target, source) for source, target in forward]
-        low = lax.ppermute(
-            lax.slice_in_dim(block, block.shape[dim] - width, None, axis=dim), axis, forward
-        )
-        high = lax.ppermute(lax.slice_in_dim(block, 0, width, axis=dim), axis, backward)
-        block = jnp.concatenate([low, block, high], axis=dim)
-    return block
 
 
 def derivatives(padded):
@@ -87,7 +74,7 @@
     return (a_xx, a_yy, a_zz, a_xy, a_xz, a_yz)
 
 
-def advance(padded, current, previous, fields, coefs, plane, top):
+def advance_raw(padded, current, previous, fields, coefs):
     courant, eps_field, delta_field, shear, damp = fields
     a_xx, a_yy, a_zz, a_xy, a_xz, a_yz = coefs
     u_zz, u_xx, u_yy, u_xy, u_xz, u_yz = derivatives(padded)
@@ -110,8 +97,6 @@
         * ((1.0 + 2.0 * delta_field) * h_two[0] + h_one[1] + shear * (h_two[1] - h_two[0]))
         - damp * (wave_b - old_b)
     )
-    new_a = new_a.at[top].add(plane)
-    new_b = new_b.at[top].add(plane)
     return jnp.stack([new_a, new_b])
 
 
@@ -119,6 +104,51 @@
     table = jnp.arange(line_gain.shape[0], dtype=jnp.int32)
     gains = jnp.sum(jnp.where(lines[:, None] == table[None, :], line_gain[None, :], 0.0), axis=1)
     return jnp.dot(samples, resample_filter.T, precision=lax.Precision.HIGHEST) * gains[:, None]
+
+
+def exchange(groups, axis, dim):
+    count = lax.axis_size(axis)
+    forward = [(i, i + 1) for i in range(count - 1)]
+    backward = [(target, source) for source, target in forward]
+    lows = [lax.slice_in_dim(a, a.shape[dim] - w, None, axis=dim) for a, w in groups]
+    highs = [lax.slice_in_dim(a, 0, w, axis=dim) for a, w in groups]
+    got_low = lax.ppermute(jnp.concatenate([x.reshape(-1) for x in lows]), axis, forward)
+    got_high = lax.ppermute(jnp.concatenate([x.reshape(-1) for x in highs]), axis, backward)
+    out = []
+    offset = 0
+    for (a, w), piece in zip(groups, lows):
+        n = piece.size
+        low = got_low[offset : offset + n].reshape(piece.shape)
+        high = got_high[offset : offset + n].reshape(piece.shape)
+        offset += n
+        out.append((jnp.concatenate([low, a, high], axis=dim), w))
+    return out
+
+
+def plane_entries(receiver_inline, receiver_crossline, payload, inline_cells, cross_cells, halo):
+    inl_count = lax.axis_size("inl")
+    xl_count = lax.axis_size("xl")
+    col_x = receiver_inline // inline_cells
+    col_y = receiver_crossline // cross_cells
+    off_x = receiver_inline % inline_cells
+    off_y = receiver_crossline % cross_cells
+    near_x = jnp.where(off_x < halo, col_x - 1, jnp.where(off_x >= inline_cells - halo, col_x + 1, -1))
+    near_y = jnp.where(off_y < halo, col_y - 1, jnp.where(off_y >= cross_cells - halo, col_y + 1, -1))
+    ok_x = (near_x >= 0) & (near_x < inl_count)
+    ok_y = (near_y >= 0) & (near_y < xl_count)
+    dest_x = jnp.concatenate([col_x, near_x, col_x, near_x])
+    dest_y = jnp.concatenate([col_y, col_y, near_y, near_y])
+    valid = jnp.concatenate([jnp.ones_like(ok_x), ok_x, ok_y, ok_x & ok_y])
+    gx = jnp.concatenate([receiver_inline] * 4)
+    gy = jnp.concatenate([receiver_crossline] * 4)
+    local_x = gx - dest_x * inline_cells + halo
+    local_y = gy - dest_y * cross_cells + halo
+    dest = jnp.where(valid, dest_x * xl_count + dest_y, inl_count * xl_count)
+    amps = jnp.concatenate([payload] * 4, axis=0)
+    entries = jnp.concatenate(
+        [amps, local_x.astype(jnp.float32)[:, None], local_y.astype(jnp.float32)[:, None]], axis=1
+    )
+    return dest, entries
 
 
 def local(
@@ -140,42 +170,80 @@
     receiver_crossline,
     shot_line,
 ):
+    halo = 4
     depth, inline_cells, cross_cells = wave_p.shape
-    cells = inline_cells * cross_cells
     steps = resample_filter.shape[0]
     xl_count = lax.axis_size("xl")
     gz_count = lax.axis_size("gz")
     columns = lax.axis_size("inl") * xl_count
-    capacity = 2 * trace_samples.shape[0] // columns
-    owner = receiver_inline // inline_cells * xl_count + receiver_crossline // cross_cells
-    local_cell = receiver_inline % inline_cells * cross_cells + receiver_crossline % cross_cells
+    traces = trace_samples.shape[0]
+    capacity = min(9 * (2 * traces // columns), traces)
+
+    wide = [
+        (jnp.stack([wave_p, wave_q]), 2 * halo),
+        (
+            jnp.stack(
+                [
+                    wave_p_old,
+                    wave_q_old,
+                    courant_square,
+                    thomsen_epsilon,
+                    thomsen_delta,
+                    tilt_angle,
+                    azimuth,
+                    shear_ratio,
+                    damping,
+                ]
+            ),
+            halo,
+        ),
+    ]
+    for axis, dim in (("inl", 2), ("gz", 1), ("xl", 3)):
+        wide = exchange(wide, axis, dim)
+    current_wide = wide[0][0]
+    rest = wide[1][0]
+
     payload = step_amplitudes(trace_samples, resample_filter, line_gain, shot_line)
-    onehot = (owner[:, None] == jnp.arange(columns, dtype=jnp.int32)[None, :]).astype(jnp.int32)
+    dest, entries = plane_entries(
+        receiver_inline, receiver_crossline, payload, inline_cells, cross_cells, halo
+    )
+    onehot = (dest[:, None] == jnp.arange(columns, dtype=jnp.int32)[None, :]).astype(jnp.int32)
     rank = jnp.sum(jnp.cumsum(onehot, axis=0) * onehot, axis=1) - 1
-    slot = owner * (gz_count * capacity) + rank
-    packed = jnp.concatenate([payload, local_cell.astype(jnp.float32)[:, None]], axis=1)
-    width = packed.shape[1]
-    send = jnp.zeros((columns * gz_count * capacity, width), jnp.float32).at[slot].set(packed)
+    slot = jnp.where(dest < columns, dest * (gz_count * capacity) + rank, columns * gz_count * capacity)
+    width = entries.shape[1]
+    send = (
+        jnp.zeros((columns * gz_count * capacity, width), jnp.float32)
+        .at[slot]
+        .set(entries, mode="drop")
+    )
     arrived = lax.all_to_all(send, ("inl", "xl", "gz"), split_axis=0, concat_axis=0, tiled=True)
-    target = arrived[:, steps].astype(jnp.int32)
+    row_at = arrived[:, steps].astype(jnp.int32)
+    col_at = arrived[:, steps + 1].astype(jnp.int32)
     row_hit = (
-        target[:, None] // cross_cells == jnp.arange(inline_cells, dtype=jnp.int32)[None, :]
+        row_at[:, None] == jnp.arange(inline_cells + 2 * halo, dtype=jnp.int32)[None, :]
     ).astype(jnp.float32)
     col_hit = (
-        target[:, None] % cross_cells == jnp.arange(cross_cells, dtype=jnp.int32)[None, :]
+        col_at[:, None] == jnp.arange(cross_cells + 2 * halo, dtype=jnp.int32)[None, :]
     ).astype(jnp.float32)
     weighted = arrived[:, :steps, None] * row_hit[:, None, :]
     planes = jnp.einsum("nkx,ny->kxy", weighted, col_hit, precision=lax.Precision.HIGHEST)
-    fields = (courant_square, thomsen_epsilon, thomsen_delta, shear_ratio, damping)
-    current = jnp.stack([wave_p, wave_q])
-    previous = jnp.stack([wave_p_old, wave_q_old])
-    coefs = anisotropy(tilt_angle, azimuth)
-    for step in range(steps):
-        padded = with_halo(current, (("inl", 2), ("xl", 3), ("gz", 1)), 4)
-        newer = advance(padded, current, previous, fields, coefs, planes[step], 0)
-        previous = current
-        current = newer
-    return (current[0], current[1], previous[0], previous[1])
+
+    inner = (slice(None), slice(halo, -halo), slice(halo, -halo), slice(halo, -halo))
+    courant, eps_field, delta_field, tilt_wide, azimuth_wide, shear, damp = [rest[i] for i in range(2, 9)]
+    fields_wide = (courant, eps_field, delta_field, shear, damp)
+    coefs_wide = anisotropy(tilt_wide, azimuth_wide)
+    first = advance_raw(current_wide, current_wide[inner], rest[0:2], fields_wide, coefs_wide)
+    first = lax.optimization_barrier(first)
+    first = first.at[:, halo].add(planes[0][None])
+
+    block = inner[1:]
+    fields = tuple(f[block] for f in fields_wide)
+    coefs = tuple(c[block] for c in coefs_wide)
+    previous = jnp.stack([wave_p, wave_q])
+    second = advance_raw(first, first[inner], previous, fields, coefs)
+    second = second.at[:, 0].add(planes[1][halo:-halo, halo:-halo][None])
+    middle = first[inner]
+    return (second[0], second[1], middle[0], middle[1])
 
 
 def solution(mesh):

time: 67.6 us -> 100 us (1.48)
  the two profiles are of different devices: /device:TPU:14 before, /device:TPU:0 now
where the time goes in v3:
time: 100 us; the launch traced here: 99 us
  local copies, waits for them, and re-layouts  32.4 us (32%)
  other arithmetic  27.7 us (28%)
  starting transfers between devices  22.5 us (22%)
  waiting for transfers between devices  12.3 us (12%)
  matrix products  2.73 us (3%)
  between operations  1.34 us (1%)
    ppermute x3, starting transfers between devices, exchange(): lax.ppermute(jnp.concatenate([x.reshape(-1) for x in lows]), axis, forward)  9.43 us
    all_to_all x1, starting transfers between devices, local(): lax.all_to_all(send, ('inl', 'xl', 'gz'), split_axis=0, concat_axis=0, ti...  9.2 us
    unnamed x58, local copies, waits for them, and re-layouts  7.73 us
    ppermute x3, waiting for transfers between devices, exchange(): lax.ppermute(jnp.concatenate([x.reshape(-1) for x in highs]), axis, backw...  5.86 us
    scatter x1, local copies, waits for them, and re-layouts, local(): send = jnp.zeros((columns * gz_count * capacity, width), jnp.float32).at[...  5.27 us
    concatenate x6, other arithmetic, exchange(): out.append((jnp.concatenate([low, a, high], axis=dim), w))  5.13 us
    ppermute x3, waiting for transfers between devices, exchange(): lax.ppermute(jnp.concatenate([x.reshape(-1) for x in lows]), axis, forward)  4.87 us
    sub x2, other arithmetic, advance_raw(): h_two = u_xx + u_yy + u_zz - h_one  4.31 us
  transfers between devices with their start and end apart: 7, of which 4 were waited for; matrix products, arithmetic and copies ran while one was open for 22% of the time, Pallas kernels for 0%

profile of v3, /device:TPU:0, one launch (start us, length us, event | category | flops | bytes accessed | tf_op | source)
XLA Modules:
  0.0 99.0 jit_solution(932592985786279700)
XLA Ops:
  0.7 0.8 bitcast_dynamic-update-slice_fusion.8
  1.5 0.8 bitcast_dynamic-update-slice_fusion.7
  2.3 0.8 bitcast_dynamic-update-slice_fusion.6
  3.1 0.8 bitcast_dynamic-update-slice_fusion.5
  3.8 0.8 bitcast_dynamic-update-slice_fusion.4
  4.6 0.8 bitcast_dynamic-update-slice_fusion.3
  5.4 0.8 bitcast_dynamic-update-slice_fusion.2
  6.1 0.8 bitcast_dynamic-update-slice_fusion.1
  6.9 0.8 bitcast_dynamic-update-slice_fusion
  7.8 2.4 %collective-permute-start = (f32[53248]{0:T(1024)S(1)}, f32[53248]{0:T(1024)S(1)}, u32[]{:S(2)}, u32[]{:S(2)}) collective-permute-start(f32[53248]{0:T(1024)S(1)} %get-tuple-element.92), channel_id=1, source_target_pairs={{0,8},{8,16},{16,24},{1,9},{9,17},{17,25},{2,10},{10,18},{18,26},{... | collective-permute-start | bytes 638984 | tf_op jit(solution)/shard_map/ppermute | solution.py:115
  10.1 1.3 %collective-permute-start.1 = (f32[53248]{0:T(1024)S(1)}, f32[53248]{0:T(1024)S(1)}, u32[]{:S(2)}, u32[]{:S(2)}) collective-permute-start(f32[53248]{0:T(1024)S(1)} %get-tuple-element.93), channel_id=1, source_target_pairs={{8,0},{16,8},{24,16},{9,1},{17,9},{25,17},{10,2},{18,10},{26,18},{... | collective-permute-start | bytes 638984 | tf_op jit(solution)/shard_map/ppermute | solution.py:116
  11.6 2.3 %reduce-window.6 = s32[8,8,128]{2,1,0:T(8,128)S(1)} reduce-window(s32[8,8,128]{2,1,0:T(8,128)S(1)} %fusion.185, s32[]{:T(128)} %constant.166.clone.1), window={size=1x1x128 pad=0_0x0_0x127_0}, to_apply=%region_0.1 | reduce-window | flops 1040384 | bytes 65540 | tf_op jit(solution)/shard_map/reduce-window
  13.9 0.3 slice_reduce_fusion
  14.2 0.2 reduce-window.9
  14.5 0.1 select_reduce_fusion
  14.6 0.3 convolution_multiply_fusion
  14.9 0.2 copy.27
  15.2 5.3 %scatter_custom_fusion = f32[8192,4]{1,0:T(8,128)} fusion(s32[1024]{0:T(1024)S(1)} %bitcast.239, f32[1024,4]{1,0:T(8,128)S(1)} %copy.27, f32[]{:T(128)} %constant.164.clone.1), kind=kCustom, calls=%fused_computation.6 | custom fusion | bytes 131076 | tf_op jit(solution)/shard_map/scatter | solution.py:217
  20.5 3.5 %copy.28 = f32[32,256,4]{1,2,0:T(4,128)} copy(f32[32,256,4]{2,1,0:T(8,128)} %bitcast.175) | data formatting | bytes 262144 | tf_op jit(solution)/shard_map/all_to_all | solution.py:219
  23.9 9.2 %all-to-all-start = ((f32[32,256,4]{1,2,0:T(4,128)}), f32[32,256,4]{1,2,0:T(4,128)S(1)}, u32[]{:S(2)}, u32[]{:S(2)}) async-start(f32[32,256,4]{1,2,0:T(4,128)} %copy.28), calls=%async_computation | async-start | bytes 262144 | tf_op jit(solution)/shard_map/all_to_all | solution.py:219
  33.2 0.1 pad_maximum_fusion.17
  33.4 0.9 pad_maximum_fusion.16
  34.3 3.7 %collective-permute-start.2 = (f32[122880]{0:T(1024)}, f32[122880]{0:T(1024)S(1)}, u32[]{:S(2)}, u32[]{:S(2)}) collective-permute-start(f32[122880]{0:T(1024)} %get-tuple-element.82), channel_id=1, source_target_pairs={{0,1},{1,2},{2,3},{4,5},{5,6},{6,7},{8,9},{9,10},{10,11},{12,13},{... | collective-permute-start | bytes 1474568 | tf_op jit(solution)/shard_map/ppermute | solution.py:115
  38.0 1.3 %collective-permute-start.3 = (f32[122880]{0:T(1024)S(1)}, f32[122880]{0:T(1024)S(1)}, u32[]{:S(2)}, u32[]{:S(2)}) collective-permute-start(f32[122880]{0:T(1024)S(1)} %get-tuple-element.83), channel_id=1, source_target_pairs={{1,0},{2,1},{3,2},{5,4},{6,5},{7,6},{9,8},{10,9},{11,10},{13,12},{... | collective-permute-start | bytes 1474568 | tf_op jit(solution)/shard_map/ppermute | solution.py:116
  39.3 1.6 %all-to-all-done = f32[32,256,4]{1,2,0:T(4,128)S(1)} async-done(((f32[32,256,4]{1,2,0:T(4,128)}), f32[32,256,4]{1,2,0:T(4,128)S(1)}, u32[]{:S(2)}, u32[]{:S(2)}) %all-to-all-start) | async-done | bytes 131104 | tf_op jit(solution)/shard_map/all_to_all | solution.py:219
  41.0 2.5 %fusion.1 = f32[2,16,136]{2,1,0:T(8,128)S(1)} fusion(s32[8192]{0:T(1024)S(1)} %bitcast.226, f32[8192,16]{0,1:T(8,128)S(1)} %fusion.75, f32[8192,2]{0,1:T(2,128)S(1)} %slice.1044), kind=kOutput, calls=%fused_computation.3 | convolution fusion | flops 429195264 | bytes 640000 | tf_op jit(solution)/shard_map/nkx,ny->kxy/dot_general | solution.py:229
  43.5 0.7 slice.1140
  44.2 4.9 %collective-permute-done.2 = f32[122880]{0:T(1024)S(1)} collective-permute-done((f32[122880]{0:T(1024)}, f32[122880]{0:T(1024)S(1)}, u32[]{:S(2)}, u32[]{:S(2)}) %collective-permute-start.2) | collective-permute-done | bytes 491552 | tf_op jit(solution)/shard_map/ppermute | solution.py:115
  49.1 3.8 %collective-permute-done.3 = f32[122880]{0:T(1024)S(1)} collective-permute-done((f32[122880]{0:T(1024)S(1)}, f32[122880]{0:T(1024)S(1)}, u32[]{:S(2)}, u32[]{:S(2)}) %collective-permute-start.3) | collective-permute-done | bytes 491552 | tf_op jit(solution)/shard_map/ppermute | solution.py:116
  53.0 1.0 fusion.204
  53.9 0.3 reshape.742
  54.3 0.6 copy-done.4
  54.9 0.1 copy-done.6
  55.1 0.2 pad_maximum_fusion.1
  55.2 0.4 fusion.203
  55.6 0.7 reshape.743
  56.4 3.4 %collective-permute-start.4 = (f32[18432]{0:T(1024)S(1)}, f32[18432]{0:T(1024)S(1)}, u32[]{:S(2)}, u32[]{:S(2)}) collective-permute-start(f32[18432]{0:T(1024)S(1)} %pad_maximum_fusion.24), channel_id=1, source_target_pairs={{0,4},{1,5},{2,6},{3,7},{8,12},{9,13},{10,14},{11,15},{16,20},{17,... | collective-permute-start | bytes 221192 | tf_op jit(solution)/shard_map/ppermute | solution.py:115
  59.8 1.3 %reshape.745 = f32[9216]{0:T(1024)S(1)} reshape(f32[2,24,24,8]{3,2,1,0:T(8,128)} %get-tuple-element.70) | data formatting | bytes 73728 | tf_op jit(solution)/shard_map/reshape | solution.py:116
  61.1 0.7 reshape.746
  61.8 1.3 %collective-permute-start.5 = (f32[18432]{0:T(1024)S(1)}, f32[18432]{0:T(1024)S(1)}, u32[]{:S(2)}, u32[]{:S(2)}) collective-permute-start(f32[18432]{0:T(1024)S(1)} %pad_maximum_fusion.25), channel_id=1, source_target_pairs={{4,0},{5,1},{6,2},{7,3},{12,8},{13,9},{14,10},{15,11},{20,16},{21,... | collective-permute-start | bytes 221192 | tf_op jit(solution)/shard_map/ppermute | solution.py:116
  63.1 0.6 fusion.207
  63.7 2.3 %reshape.748 = f32[9,16,16,4]{3,2,1,0:T(8,128)} reshape(f32[9216]{0:T(1024)S(1)} %get-tuple-element.86) | data formatting | bytes 73728 | tf_op jit(solution)/shard_map/reshape | solution.py:121
  66.0 2.1 %collective-permute-done.5 = f32[18432]{0:T(1024)S(1)} collective-permute-done((f32[18432]{0:T(1024)S(1)}, f32[18432]{0:T(1024)S(1)}, u32[]{:S(2)}, u32[]{:S(2)}) %collective-permute-start.5) | collective-permute-done | bytes 73760 | tf_op jit(solution)/shard_map/ppermute | solution.py:116
  68.0 0.6 fusion.208
  68.7 2.2 %reshape.749 = f32[9,16,16,4]{3,2,1,0:T(8,128)} reshape(f32[9216]{0:T(1024)S(1)} %get-tuple-element.88) | data formatting | bytes 73728 | tf_op jit(solution)/shard_map/reshape | solution.py:122
  70.9 3.1 %pad_maximum_fusion = f32[9,16,16,136]{3,2,1,0:T(8,128)S(1)} fusion(f32[9,16,16,4]{3,2,1,0:T(8,128)} %reshape.749, f32[9,4,16,128]{3,2,1,0:T(8,128)} %bitcast.187, f32[9,8,4,128]{3,2,1,0:T(4,128)} %bitcast.203, f32[9,8,8,128]{3,2,1,0:T(8,128)S(1)} %bitcast_dynamic-update-slice_fusion, f32[9,8,4,128]{3,2,1,0:T(4,128)} %bitcast.200, ...), kind=kLoop, calls=%fused_computation.4 | loop fusion | flops 1880064 | bytes 2506752 | tf_op jit(solution)/shard_map/concatenate | solution.py:124
  74.0 3.6 %slice_bitcast_fusion.1 = (f32[16,16,136]{2,1,0:T(8,128)}, f32[16,16,136]{2,1,0:T(8,128)}, f32[16,16,136]{2,1,0:T(8,128)}, f32[16,16,136]{2,1,0:T(8,128)}, f32[1...) fusion(f32[9,16,16,136]{3,2,1,0:T(8,128)S(1)} %pad_maximum_fusion), kind=kLoop, calls=%fused_computation.174 | loop fusion | flops 452608 | bytes 2785280 | tf_op jit(solution)/shard_map/squeeze | solution.py:232
  77.6 1.7 %fusion.199 = (f32[16,16,136]{2,1,0:T(8,128)}, f32[16,16,136]{2,1,0:T(8,128)}, f32[16,16,136]{2,1,0:T(8,128)}) fusion(f32[9,16,16,136]{3,2,1,0:T(8,128)S(1)} %pad_maximum_fusion), kind=kLoop, calls=%fused_computation.384 | loop fusion | flops 104448 | bytes 557056 | tf_op jit(solution)/shard_map/mul | solution.py:68
  79.3 1.1 %reshape.744 = f32[2,24,24,8]{3,2,1,0:T(8,128)S(1)} reshape(f32[9216]{0:T(1024)} %get-tuple-element.87) | data formatting | bytes 73728 | tf_op jit(solution)/shard_map/reshape | solution.py:121
  80.4 1.9 %reshape.747 = f32[2,24,24,8]{3,2,1,0:T(8,128)} reshape(f32[9216]{0:T(1024)} %get-tuple-element.89) | data formatting | bytes 73728 | tf_op jit(solution)/shard_map/reshape | solution.py:122
  82.3 1.7 %pad_maximum_fusion.2 = f32[2,24,24,144]{3,2,1,0:T(8,128)S(1)} fusion(f32[2,24,24,8]{3,2,1,0:T(8,128)} %reshape.747, f32[2,8,24,128]{3,2,1,0:T(8,128)} %bitcast.181, f32[2,8,8,128]{3,2,1,0:T(8,128)S(1)} %bitcast.195, f32[1,8,8,128]{3,2,1,0:T(8,128)} %bitcast.204, f32[1,8,8,128]{3,2,1,0:T(8,128)} %bitcast.210, f32[2,8,8,128]{3,2,1,0:T(8,128)S(1)} %bitcast.190, ...), kind=kLoop, calls=%fused_computation.9 | loop fusion | flops 1161216 | bytes 1327104 | tf_op jit(solution)/shard_map/concatenate | solution.py:124
  84.1 1.6 %fusion.9 = f32[2,24,16,136]{3,2,1,0:T(8,128)S(1)} fusion(f32[2,24,24,8]{3,2,1,0:T(8,128)S(1)} %reshape.744, f32[2,8,24,128]{3,2,1,0:T(8,128)S(1)} %bitcast.182, f32[2,8,24,128]{3,2,1,0:T(8,128)S(1)} %bitcast.178, f32[2,8,8,128]{3,2,1,0:T(8,128)S(1)} %bitcast.196, f32[2,8,8,128]{3,2,1,0:T(8,128)S(1)} %bitcast.191, f32[1,8,8,128]{3,2,1,0:T(8,128)S(1)} %bitcast.208, ...), kind=kLoop, calls=%fused_computation.15 | loop fusion | flops 2402304 | bytes 3588096 | tf_op jit(solution)/shard_map/add | solution.py:37
  85.7 2.4 %fusion.66 = (f32[2,16,16,136]{3,2,1,0:T(8,128)S(1)}, f32[2,16,16,136]{3,2,1,0:T(8,128)S(1)}) fusion(f32[2,24,24,144]{3,2,1,0:T(8,128)S(1)} %pad_maximum_fusion.2), kind=kLoop, calls=%fused_computation.115 | loop fusion | flops 1740800 | bytes 5292032 | tf_op jit(solution)/shard_map/add | solution.py:26
  88.1 0.6 fusion.16
  88.7 0.3 copy-done.13
  89.4 3.8 %add_subtract_fusion = (f32[2,16,16,136]{3,2,1,0:T(8,128)S(1)}, f32[2,16,16,136]{3,2,1,0:T(8,128)S(1)}) fusion(f32[2,16,16,136]{3,2,1,0:T(8,128)S(1)} %get-tuple-element.66, f32[2,16,16,136]{3,2,1,0:T(8,128)S(1)} %get-tuple-element.65, f32[2,24,16,136]{3,2,1,0:T(8,128)S(1)} %fusion.9, f32[16,16,136]{2,1,0:T(8,128)S(1)} %copy-done.13, ...), kind=kLoop, calls=%fused_computation.130 | loop fusion | flops 5013504 | bytes 11247616 | tf_op jit(solution)/shard_map/sub | solution.py:82
  93.2 0.4 fusion.97
  93.7 0.2 fusion.82
  93.9 0.3 fusion.145
  94.3 0.3 fusion.103
  94.6 1.4 %multiply_multiply_fusion.5 = (f32[8,8,128]{2,1,0:T(8,128)S(1)}, f32[8,8,128]{2,1,0:T(8,128)S(1)}, f32[8,8,128]{2,1,0:T(8,128)S(1)}, f32[8,8,128]{2,1,0:T(8,128)...) fusion(f32[16,16,136]{2,1,0:T(8,128)} %get-tuple-element.60, f32[16,16,136]{2,1,0:T(8,128)} %get-tuple-element.57, ...), kind=kLoop, calls=%fused_computation.281 | loop fusion | flops 81920 | bytes 425984 | tf_op jit(solution)/shard_map/mul | solution.py:68
  96.0 0.5 add_subtract_fusion.1
  96.5 1.8 %fusion.178 = (f32[1,8,8,128]{3,2,1,0:T(8,128)S(1)}, f32[8,8,128]{2,1,0:T(8,128)}, f32[1,8,8,128]{3,2,1,0:T(8,128)S(1)}, f32[8,8,128]{2,1,0:T(8,128)}) fusion(f32[2,8,8,128]{3,2,1,0:T(8,128)S(1)} %get-tuple-element.33, f32[16,16,136]{2,1,0:T(8,128)} %get-tuple-element.45, f32[8,8,128]{2,1,0:T(8,128)S(1)} %copy-done.12, ...), kind=kLoop, calls=%fused_computation.307 | loop fusion | flops 229376 | bytes 557056 | tf_op jit(solution)/shard_map/stack | solution.py:100
  98.3 0.6 slice_bitcast_fusion.5
  (89 shorter events, 1.3 us)
Async XLA Ops:
  0.6 14.0 %copy-start = (f32[256,256]{1,0:T(8,128)S(1)}, f32[256,256]{1,0:T(8,128)}, u32[]{:S(2)}) copy-start(f32[256,256]{1,0:T(8,128)} %param.32) | copy-start | bytes 786436
  0.6 7.0 %copy-start.11 = (f32[8,8,128]{2,1,0:T(8,128)S(1)}, f32[8,8,128]{2,1,0:T(8,128)}, u32[]{:S(2)}) copy-start(f32[8,8,128]{2,1,0:T(8,128)} %param.21) | copy-start | bytes 98308
  0.7 7.0 %copy-start.9 = (f32[8,8,128]{2,1,0:T(8,128)S(1)}, f32[8,8,128]{2,1,0:T(8,128)}, u32[]{:S(2)}) copy-start(f32[8,8,128]{2,1,0:T(8,128)} %param.23) | copy-start | bytes 98308
  0.7 10.8 %copy-start.21 = (s32[256]{0:T(256)S(1)}, s32[256]{0:T(256)}, u32[]{:S(2)}) copy-start(s32[256]{0:T(256)} %param.35) | copy-start | bytes 3076
  0.7 10.8 %copy-start.20 = (s32[256]{0:T(256)S(1)}, s32[256]{0:T(256)}, u32[]{:S(2)}) copy-start(s32[256]{0:T(256)} %param.36) | copy-start | bytes 3076
  2.3 12.2 %copy-start.23 = (s32[256]{0:T(256)S(1)}, s32[256]{0:T(256)}, u32[]{:S(2)}) copy-start(s32[256]{0:T(256)} %param.37) | copy-start | bytes 3076
  2.3 12.2 %copy-start.24 = (f32[64]{0:T(128)S(1)}, f32[64]{0:T(128)}, u32[]{:S(2)}) copy-start(f32[64]{0:T(128)} %param.34) | copy-start | bytes 772
  2.3 12.3 %copy-start.22 = (f32[2,256]{1,0:T(2,128)S(1)}, f32[2,256]{1,0:T(2,128)}, u32[]{:S(2)}) copy-start(f32[2,256]{1,0:T(2,128)} %param.33) | copy-start | bytes 6148
  7.8 25.4 %collective-permute-start = (f32[53248]{0:T(1024)S(1)}, f32[53248]{0:T(1024)S(1)}, u32[]{:S(2)}, u32[]{:S(2)}) collective-permute-start(f32[53248]{0:T(1024)S(1)} %get-tuple-element.92), channel_id=1, source_target_pairs={{0,8},{8,16},{16,24},{1,9},{9,17},{17,25},{2,10},{10,18},{18,26},{... | collective-permute-start | bytes 638984 | tf_op jit(solution)/shard_map/ppermute | solution.py:115
  10.1 23.0 %collective-permute-start.1 = (f32[53248]{0:T(1024)S(1)}, f32[53248]{0:T(1024)S(1)}, u32[]{:S(2)}, u32[]{:S(2)}) collective-permute-start(f32[53248]{0:T(1024)S(1)} %get-tuple-element.93), channel_id=1, source_target_pairs={{8,0},{16,8},{24,16},{9,1},{17,9},{25,17},{10,2},{18,10},{26,18},{... | collective-permute-start | bytes 638984 | tf_op jit(solution)/shard_map/ppermute | solution.py:116
  23.9 17.0 %all-to-all-start = ((f32[32,256,4]{1,2,0:T(4,128)}), f32[32,256,4]{1,2,0:T(4,128)S(1)}, u32[]{:S(2)}, u32[]{:S(2)}) async-start(f32[32,256,4]{1,2,0:T(4,128)} %copy.28), calls=%async_computation | async-start | bytes 262144 | tf_op jit(solution)/shard_map/all_to_all | solution.py:219
  33.2 21.1 %copy-start.7 = (f32[36864]{0:T(1024)}, f32[36864]{0:T(1024)S(1)}, u32[]{:S(2)}) copy-start(f32[36864]{0:T(1024)S(1)} %slice.950) | copy-start | bytes 442372
  33.2 21.1 %copy-start.8 = (f32[36864]{0:T(1024)}, f32[36864]{0:T(1024)S(1)}, u32[]{:S(2)}) copy-start(f32[36864]{0:T(1024)S(1)} %slice.951) | copy-start | bytes 442372
  34.3 14.8 %collective-permute-start.2 = (f32[122880]{0:T(1024)}, f32[122880]{0:T(1024)S(1)}, u32[]{:S(2)}, u32[]{:S(2)}) collective-permute-start(f32[122880]{0:T(1024)} %get-tuple-element.82), channel_id=1, source_target_pairs={{0,1},{1,2},{2,3},{4,5},{5,6},{6,7},{8,9},{9,10},{10,11},{12,13},{... | collective-permute-start | bytes 1474568 | tf_op jit(solution)/shard_map/ppermute | solution.py:115
  38.0 14.9 %collective-permute-start.3 = (f32[122880]{0:T(1024)S(1)}, f32[122880]{0:T(1024)S(1)}, u32[]{:S(2)}, u32[]{:S(2)}) collective-permute-start(f32[122880]{0:T(1024)S(1)} %get-tuple-element.83), channel_id=1, source_target_pairs={{1,0},{2,1},{3,2},{5,4},{6,5},{7,6},{9,8},{10,9},{11,10},{13,12},{... | collective-permute-start | bytes 1474568 | tf_op jit(solution)/shard_map/ppermute | solution.py:116
  52.9 2.3 %copy-start.2 = (f32[49152]{0:T(1024)}, f32[49152]{0:T(1024)S(1)}, u32[]{:S(2)}) copy-start(f32[49152]{0:T(1024)S(1)} %slice.955) | copy-start | bytes 589828
  54.2 0.7 copy-start.4
  54.3 0.8 copy-start.6
  56.4 6.7 %collective-permute-start.4 = (f32[18432]{0:T(1024)S(1)}, f32[18432]{0:T(1024)S(1)}, u32[]{:S(2)}, u32[]{:S(2)}) collective-permute-start(f32[18432]{0:T(1024)S(1)} %pad_maximum_fusion.24), channel_id=1, source_target_pairs={{0,4},{1,5},{2,6},{3,7},{8,12},{9,13},{10,14},{11,15},{16,20},{17,... | collective-permute-start | bytes 221192 | tf_op jit(solution)/shard_map/ppermute | solution.py:115
  61.8 6.2 %collective-permute-start.5 = (f32[18432]{0:T(1024)S(1)}, f32[18432]{0:T(1024)S(1)}, u32[]{:S(2)}, u32[]{:S(2)}) collective-permute-start(f32[18432]{0:T(1024)S(1)} %pad_maximum_fusion.25), channel_id=1, source_target_pairs={{4,0},{5,1},{6,2},{7,3},{12,8},{13,9},{14,10},{15,11},{20,16},{21,... | collective-permute-start | bytes 221192 | tf_op jit(solution)/shard_map/ppermute | solution.py:116
  63.7 7.2 %copy-start.5 = (f32[73728]{0:T(1024)S(1)}, f32[73728]{0:T(1024)}, u32[]{:S(2)}) copy-start(f32[73728]{0:T(1024)} %copy-done.4) | copy-start | bytes 884740
  82.3 1.7 %copy-start.1 = (f32[2,24,24,8]{3,2,1,0:T(8,128)S(1)}, f32[2,24,24,8]{3,2,1,0:T(8,128)}, u32[]{:S(2)}) copy-start(f32[2,24,24,8]{3,2,1,0:T(8,128)} %reshape.747) | copy-start | bytes 110596
  82.3 1.7 %copy-start.3 = (f32[49152]{0:T(1024)S(1)}, f32[49152]{0:T(1024)}, u32[]{:S(2)}) copy-start(f32[49152]{0:T(1024)} %copy-done.2) | copy-start | bytes 589828
  82.3 1.7 %copy-start.10 = (f32[8,8,128]{2,1,0:T(8,128)S(1)}, f32[8,8,128]{2,1,0:T(8,128)}, u32[]{:S(2)}) copy-start(f32[8,8,128]{2,1,0:T(8,128)} %param.23) | copy-start | bytes 98308
  82.3 1.7 %copy-start.12 = (f32[8,8,128]{2,1,0:T(8,128)S(1)}, f32[8,8,128]{2,1,0:T(8,128)}, u32[]{:S(2)}) copy-start(f32[8,8,128]{2,1,0:T(8,128)} %param.21) | copy-start | bytes 98308
  88.0 1.0 copy-start.13
  88.0 1.0 %copy-start.14 = (f32[16,16,136]{2,1,0:T(8,128)S(1)}, f32[16,16,136]{2,1,0:T(8,128)}, u32[]{:S(2)}) copy-start(f32[16,16,136]{2,1,0:T(8,128)} %get-tuple-element.47) | copy-start | bytes 417796
  88.1 1.1 %copy-start.15 = (f32[16,16,136]{2,1,0:T(8,128)S(1)}, f32[16,16,136]{2,1,0:T(8,128)}, u32[]{:S(2)}) copy-start(f32[16,16,136]{2,1,0:T(8,128)} %get-tuple-element.48) | copy-start | bytes 417796
  88.1 1.2 %copy-start.16 = (f32[16,16,136]{2,1,0:T(8,128)S(1)}, f32[16,16,136]{2,1,0:T(8,128)}, u32[]{:S(2)}) copy-start(f32[16,16,136]{2,1,0:T(8,128)} %get-tuple-element.49) | copy-start | bytes 417796
  88.1 1.2 %copy-start.17 = (f32[16,16,136]{2,1,0:T(8,128)S(1)}, f32[16,16,136]{2,1,0:T(8,128)}, u32[]{:S(2)}) copy-start(f32[16,16,136]{2,1,0:T(8,128)} %get-tuple-element.50) | copy-start | bytes 417796
  88.1 1.3 %copy-start.18 = (f32[16,16,136]{2,1,0:T(8,128)S(1)}, f32[16,16,136]{2,1,0:T(8,128)}, u32[]{:S(2)}) copy-start(f32[16,16,136]{2,1,0:T(8,128)} %get-tuple-element.52) | copy-start | bytes 417796
  96.0 2.4 %copy-start.19 = (f32[8,128]{1,0:T(8,128)S(1)}, f32[8,128]{1,0:T(8,128)}, u32[]{:S(2)}) copy-start(f32[8,128]{1,0:T(8,128)} %slice.1140) | copy-start | bytes 12292

commit v4 on v3

--- a/solution.py
+++ b/solution.py
@@ -5,6 +5,23 @@
 
 second_coef = (-205.0 / 72.0, 8.0 / 5.0, -1.0 / 5.0, 8.0 / 315.0, -1.0 / 560.0)
 first_coef = (0.0, 4.0 / 5.0, -1.0 / 5.0, 4.0 / 105.0, -1.0 / 280.0)
+
+
+def with_halo(block, sides, width, tie=None):
+    for index, (axis, dim) in enumerate(sides):
+        if index == 1 and tie is not None:
+            block, tie = lax.optimization_barrier((block, tie))
+        count = lax.axis_size(axis)
+        forward = [(i, i + 1) for i in range(count - 1)]
+        backward = [(target, source) for source, target in forward]
+        low = lax.ppermute(
+            lax.slice_in_dim(block, block.shape[dim] - width, None, axis=dim), axis, forward
+        )
+        high = lax.ppermute(lax.slice_in_dim(block, 0, width, axis=dim), axis, backward)
+        block = jnp.concatenate([low, block, high], axis=dim)
+    if tie is not None:
+        return block, tie
+    return block
 
 
 def derivatives(padded):
@@ -104,25 +121,6 @@
     table = jnp.arange(line_gain.shape[0], dtype=jnp.int32)
     gains = jnp.sum(jnp.where(lines[:, None] == table[None, :], line_gain[None, :], 0.0), axis=1)
     return jnp.dot(samples, resample_filter.T, precision=lax.Precision.HIGHEST) * gains[:, None]
-
-
-def exchange(groups, axis, dim):
-    count = lax.axis_size(axis)
-    forward = [(i, i + 1) for i in range(count - 1)]
-    backward = [(target, source) for source, target in forward]
-    lows = [lax.slice_in_dim(a, a.shape[dim] - w, None, axis=dim) for a, w in groups]
-    highs = [lax.slice_in_dim(a, 0, w, axis=dim) for a, w in groups]
-    got_low = lax.ppermute(jnp.concatenate([x.reshape(-1) for x in lows]), axis, forward)
-    got_high = lax.ppermute(jnp.concatenate([x.reshape(-1) for x in highs]), axis, backward)
-    out = []
-    offset = 0
-    for (a, w), piece in zip(groups, lows):
-        n = piece.size
-        low = got_low[offset : offset + n].reshape(piece.shape)
-        high = got_high[offset : offset + n].reshape(piece.shape)
-        offset += n
-        out.append((jnp.concatenate([low, a, high], axis=dim), w))
-    return out
 
 
 def plane_entries(receiver_inline, receiver_crossline, payload, inline_cells, cross_cells, halo):
@@ -179,30 +177,6 @@
     traces = trace_samples.shape[0]
     capacity = min(9 * (2 * traces // columns), traces)
 
-    wide = [
-        (jnp.stack([wave_p, wave_q]), 2 * halo),
-        (
-            jnp.stack(
-                [
-                    wave_p_old,
-                    wave_q_old,
-                    courant_square,
-                    thomsen_epsilon,
-                    thomsen_delta,
-                    tilt_angle,
-                    azimuth,
-                    shear_ratio,
-                    damping,
-                ]
-            ),
-            halo,
-        ),
-    ]
-    for axis, dim in (("inl", 2), ("gz", 1), ("xl", 3)):
-        wide = exchange(wide, axis, dim)
-    current_wide = wide[0][0]
-    rest = wide[1][0]
-
     payload = step_amplitudes(trace_samples, resample_filter, line_gain, shot_line)
     dest, entries = plane_entries(
         receiver_inline, receiver_crossline, payload, inline_cells, cross_cells, halo
@@ -216,6 +190,9 @@
         .at[slot]
         .set(entries, mode="drop")
     )
+    sides = (("inl", 2), ("xl", 3), ("gz", 1))
+    current = jnp.stack([wave_p, wave_q])
+    padded_now, send = with_halo(current, sides, halo, send)
     arrived = lax.all_to_all(send, ("inl", "xl", "gz"), split_axis=0, concat_axis=0, tiled=True)
     row_at = arrived[:, steps].astype(jnp.int32)
     col_at = arrived[:, steps + 1].astype(jnp.int32)
@@ -228,22 +205,15 @@
     weighted = arrived[:, :steps, None] * row_hit[:, None, :]
     planes = jnp.einsum("nkx,ny->kxy", weighted, col_hit, precision=lax.Precision.HIGHEST)
 
-    inner = (slice(None), slice(halo, -halo), slice(halo, -halo), slice(halo, -halo))
-    courant, eps_field, delta_field, tilt_wide, azimuth_wide, shear, damp = [rest[i] for i in range(2, 9)]
-    fields_wide = (courant, eps_field, delta_field, shear, damp)
-    coefs_wide = anisotropy(tilt_wide, azimuth_wide)
-    first = advance_raw(current_wide, current_wide[inner], rest[0:2], fields_wide, coefs_wide)
-    first = lax.optimization_barrier(first)
-    first = first.at[:, halo].add(planes[0][None])
-
-    block = inner[1:]
-    fields = tuple(f[block] for f in fields_wide)
-    coefs = tuple(c[block] for c in coefs_wide)
-    previous = jnp.stack([wave_p, wave_q])
-    second = advance_raw(first, first[inner], previous, fields, coefs)
+    fields = (courant_square, thomsen_epsilon, thomsen_delta, shear_ratio, damping)
+    coefs = anisotropy(tilt_angle, azimuth)
+    previous = jnp.stack([wave_p_old, wave_q_old])
+    first = advance_raw(padded_now, current, previous, fields, coefs)
+    padded = with_halo(first, sides, halo).at[:, halo].add(planes[0][None])
+    first = first.at[:, 0].add(planes[0][halo:-halo, halo:-halo][None])
+    second = advance_raw(padded, first, current, fields, coefs)
     second = second.at[:, 0].add(planes[1][halo:-halo, halo:-halo][None])
-    middle = first[inner]
-    return (second[0], second[1], middle[0], middle[1])
+    return (second[0], second[1], first[0], first[1])
 
 
 def solution(mesh):

time: 100 us -> 80.7 us (0.81)
  local copies, waits for them, and re-layouts: 32.4 us -> 11.4 us
  other arithmetic: 27.7 us -> 10.3 us
  starting transfers between devices: 22.5 us -> 34.7 us
  waiting for transfers between devices: 12.3 us -> 19.1 us
    ppermute x6 -> x12, starting transfers between devices: 13.3 us -> 25.9 us  [the longest x6 18.1 us: with_halo(): lax.ppermute(lax.slice_in_dim(block, block.shape[dim] - width, None, axis...]
    reshape x8 -> x0, local copies, waits for them, and re-layouts: 10.5 us -> none  [the longest x2 4.13 us: exchange(): high = got_high[offset:offset + n].reshape(piece.shape)]
    ppermute x6 -> x12, waiting for transfers between devices: 10.7 us -> 19.1 us  [the longest x6 14.9 us: with_halo(): lax.ppermute(lax.slice_in_dim(block, 0, width, axis=dim), axis, backward)]
    unnamed x58 -> x21, local copies, waits for them, and re-layouts: 7.73 us -> 0.07 us
    concatenate x10 -> x6, other arithmetic: 6.04 us -> 0.87 us  [with_halo(): block = jnp.concatenate([low, block, high], axis=dim)]
    squeeze x1 -> x0, other arithmetic: 3.57 us -> none  [local(): rest[i]]
    sub x2, other arithmetic: 4.31 us -> 0.97 us  [advance_raw(): h_two = u_xx + u_yy + u_zz - h_one]
    mul x2 -> x1, other arithmetic: 3.12 us -> 0.07 us  [anisotropy(): a_xx = sin_t * sin_t * cos_f * cos_f]
  transfers between devices with their start and end apart: 7 -> 13, of which waited for: 4 -> 7; matrix products, arithmetic and copies ran while one was open for 22% -> 21% of each run, Pallas kernels for 0% -> 0%
where the time goes in v4:
time: 80.7 us; the launch traced here: 80.1 us
  starting transfers between devices  34.7 us (43%)
  waiting for transfers between devices  19.1 us (24%)
  local copies, waits for them, and re-layouts  11.4 us (14%)
  other arithmetic  10.3 us (13%)
  matrix products  3.41 us (4%)
  between operations  1.24 us (2%)
    ppermute x6, starting transfers between devices, with_halo(): lax.ppermute(lax.slice_in_dim(block, block.shape[dim] - width, None, axis...  18.1 us
    ppermute x6, waiting for transfers between devices, with_halo(): lax.ppermute(lax.slice_in_dim(block, 0, width, axis=dim), axis, backward)  14.9 us
    all_to_all x1, starting transfers between devices, local(): lax.all_to_all(send, ('inl', 'xl', 'gz'), split_axis=0, concat_axis=0, ti...  8.88 us
    ppermute x6, starting transfers between devices, with_halo(): lax.ppermute(lax.slice_in_dim(block, 0, width, axis=dim), axis, backward)  7.75 us
    scatter x1, local copies, waits for them, and re-layouts, local(): send = jnp.zeros((columns * gz_count * capacity, width), jnp.float32).at[...  5.24 us
    ppermute x6, waiting for transfers between devices, with_halo(): lax.ppermute(lax.slice_in_dim(block, block.shape[dim] - width, None, axis...  4.21 us
    all_to_all x1, local copies, waits for them, and re-layouts, local(): lax.all_to_all(send, ('inl', 'xl', 'gz'), split_axis=0, concat_axis=0, ti...  3.48 us
    dot_general x1, matrix products, local(): jnp.einsum('nkx,ny->kxy', weighted, col_hit, precision=lax.Precision.HIGH...  2.46 us
  transfers between devices with their start and end apart: 13, of which 7 were waited for; matrix products, arithmetic and copies ran while one was open for 21% of the time, Pallas kernels for 0%

profile of v4, /device:TPU:0, one launch (start us, length us, event | category | flops | bytes accessed | tf_op | source)
XLA Modules:
  0.0 80.1 jit_solution(17273225692955219170)
XLA Ops:
  0.6 0.0 copy-start
  0.7 0.9 %fusion.142 = (f32[2,8,4,128]{3,2,1,0:T(4,128)S(1)}, f32[2,8,4,128]{3,2,1,0:T(4,128)S(1)}) fusion(f32[1,8,8,128]{3,2,1,0:T(8,128)} %bitcast.149, f32[1,8,8,128]{3,2,1,0:T(8,128)} %bitcast.151), kind=kLoop, calls=%fused_computation.242 | loop fusion | flops 16384 | bytes 131072 | tf_op jit(solution)/shard_map/stack | solution.py:194
  1.5 2.4 %collective-permute-start = (f32[2,8,4,128]{3,2,1,0:T(4,128)S(1)}, f32[2,8,4,128]{3,2,1,0:T(4,128)S(1)}, u32[]{:S(2)}, u32[]{:S(2)}) collective-permute-start(f32[2,8,4,128]{3,2,1,0:T(4,128)S(1)} %get-tuple-element.86), channel_id=1, source_target_pairs={{0,8},{8,16},{16,24},{1,9},{9,17},{17,25},{2,10},{10,18},{18,26},{... | collective-permute-start | bytes 98312 | tf_op jit(solution)/shard_map/ppermute | solution.py:17
  3.9 1.3 %collective-permute-start.1 = (f32[2,8,4,128]{3,2,1,0:T(4,128)S(1)}, f32[2,8,4,128]{3,2,1,0:T(4,128)S(1)}, u32[]{:S(2)}, u32[]{:S(2)}) collective-permute-start(f32[2,8,4,128]{3,2,1,0:T(4,128)S(1)} %get-tuple-element.87), channel_id=1, source_target_pairs={{8,0},{16,8},{24,16},{9,1},{17,9},{25,17},{10,2},{18,10},{26,18},{... | collective-permute-start | bytes 98312 | tf_op jit(solution)/shard_map/ppermute | solution.py:20
  5.2 0.7 fusion.196
  6.0 2.3 %reduce-window.6 = s32[8,8,128]{2,1,0:T(8,128)S(1)} reduce-window(s32[8,8,128]{2,1,0:T(8,128)S(1)} %fusion.176, s32[]{:T(128)} %constant.160.clone.1), window={size=1x1x128 pad=0_0x0_0x127_0}, to_apply=%region_0.1 | reduce-window | flops 1040384 | bytes 65540 | tf_op jit(solution)/shard_map/reduce-window
  8.3 0.3 slice_reduce_fusion
  8.6 0.2 reduce-window.9
  8.8 0.1 add_bitcast_fusion
  8.9 0.8 select_reduce_fusion
  9.7 0.8 %fusion.192 = (f32[1024,1]{0,1:T(1,128)S(1)}, f32[1024,1]{0,1:T(1,128)S(1)}) fusion(s32[256,1]{0,1:T(1,128)} %bitcast.166, s32[256,1]{0,1:T(1,128)S(1)} %bitcast.157, s32[256,1]{0,1:T(1,128)S(1)} %bitcast.159, s32[256,1]{0,1:T(1,128)S(1)} %bitcast.161, s32[256,1]{0,1:T(1,128)S(1)} %bitcast.163, s32[256,1]{0,1:T(1,128)} %bitcast.167), kind=kLoop, calls=%fused_computation.328 | loop fusion | flops 20480 | bytes 14336 | tf_op jit(solution)/shard_map/convert_element_type | solution.py:147
  10.5 1.0 %fusion.201 = (f32[8,8,128]{2,1,0:T(8,128)S(1)}, f32[8,8,128]{2,1,0:T(8,128)S(1)}, f32[8,8,128]{2,1,0:T(8,128)S(1)}, f32[8,8,128]{2,1,0:T(8,128)S(1)}) fusion(f32[8,8,128]{2,1,0:T(8,128)} %param.31, f32[8,8,128]{2,1,0:T(8,128)} %param.30), kind=kLoop, calls=%fused_computation.356 | loop fusion | bytes 196608 | tf_op jit(solution)/shard_map/cos | solution.py:84
  11.6 1.0 %convolution_multiply_fusion = f32[256,2]{0,1:T(2,128)S(1)} fusion(f32[256,256]{1,0:T(8,128)S(1)} %copy-done, f32[2,256]{1,0:T(2,128)} %param.35, f32[256]{0:T(256)S(1)} %select_reduce_fusion), kind=kOutput, calls=%fused_computation.7 | convolution fusion | flops 1573376 | bytes 267264 | tf_op jit(solution)/shard_map/dot_general | solution.py:123
  12.5 0.1 multiply_multiply_fusion.1
  12.6 0.2 copy.27
  12.9 5.2 %scatter_custom_fusion = f32[8192,4]{1,0:T(8,128)} fusion(s32[1024]{0:T(1024)S(1)} %bitcast.168, f32[1024,4]{1,0:T(8,128)S(1)} %copy.27, f32[]{:T(128)} %constant.158.clone.1), kind=kCustom, calls=%fused_computation.5 | custom fusion | bytes 131076 | tf_op jit(solution)/shard_map/scatter | solution.py:191
  18.1 0.0 collective-permute-done
  18.2 0.1 fusion.200
  18.3 4.2 %collective-permute-start.3 = (f32[2,8,16,4]{3,2,1,0:T(8,128)S(1)}, f32[2,8,16,4]{3,2,1,0:T(8,128)S(1)}, u32[]{:S(2)}, u32[]{:S(2)}) collective-permute-start(f32[2,8,16,4]{3,2,1,0:T(8,128)S(1)} %get-tuple-element.75), channel_id=1, source_target_pairs={{0,4},{1,5},{2,6},{3,7},{8,12},{9,13},{10,14},{11,15},{16,20},{17,... | collective-permute-start | bytes 12296 | tf_op jit(solution)/shard_map/ppermute | solution.py:17
  22.5 1.3 %collective-permute-start.2 = (f32[2,8,16,4]{3,2,1,0:T(8,128)S(1)}, f32[2,8,16,4]{3,2,1,0:T(8,128)S(1)}, u32[]{:S(2)}, u32[]{:S(2)}) collective-permute-start(f32[2,8,16,4]{3,2,1,0:T(8,128)S(1)} %get-tuple-element.76), channel_id=1, source_target_pairs={{4,0},{5,1},{6,2},{7,3},{12,8},{13,9},{14,10},{15,11},{20,16},{21,... | collective-permute-start | bytes 12296 | tf_op jit(solution)/shard_map/ppermute | solution.py:20
  23.8 1.2 %collective-permute-done.3 = f32[2,8,16,4]{3,2,1,0:T(8,128)S(1)} collective-permute-done((f32[2,8,16,4]{3,2,1,0:T(8,128)S(1)}, f32[2,8,16,4]{3,2,1,0:T(8,128)S(1)}, u32[]{:S(2)}, u32[]{:S(2)}) %collective-permute-start.3) | collective-permute-done | bytes 4128 | tf_op jit(solution)/shard_map/ppermute | solution.py:17
  25.0 4.6 %collective-permute-done.2 = f32[2,8,16,4]{3,2,1,0:T(8,128)S(1)} collective-permute-done((f32[2,8,16,4]{3,2,1,0:T(8,128)S(1)}, f32[2,8,16,4]{3,2,1,0:T(8,128)S(1)}, u32[]{:S(2)}, u32[]{:S(2)}) %collective-permute-start.2) | collective-permute-done | bytes 4128 | tf_op jit(solution)/shard_map/ppermute | solution.py:20
  29.6 0.2 pad_maximum_fusion.2
  29.8 1.3 %collective-permute-start.4 = (f32[2,4,16,136]{3,2,1,0:T(8,128)S(1)}, f32[2,4,16,136]{3,2,1,0:T(8,128)S(1)}, u32[]{:S(2)}, u32[]{:S(2)}) collective-permute-start(f32[2,4,16,136]{3,2,1,0:T(8,128)S(1)} %get-tuple-element.65), channel_id=1, source_target_pairs={{1,0},{2,1},{3,2},{5,4},{6,5},{7,6},{9,8},{10,9},{11,10},{13,12},{... | collective-permute-start | bytes 208904 | tf_op jit(solution)/shard_map/ppermute | solution.py:20
  31.1 4.6 %collective-permute-start.5 = (f32[2,4,16,136]{3,2,1,0:T(8,128)S(1)}, f32[2,4,16,136]{3,2,1,0:T(8,128)S(1)}, u32[]{:S(2)}, u32[]{:S(2)}) collective-permute-start(f32[2,4,16,136]{3,2,1,0:T(8,128)S(1)} %get-tuple-element.66), channel_id=1, source_target_pairs={{0,1},{1,2},{2,3},{4,5},{5,6},{6,7},{8,9},{9,10},{10,11},{12,13},{... | collective-permute-start | bytes 208904 | tf_op jit(solution)/shard_map/ppermute | solution.py:17
  35.6 0.0 copy-start.3
  35.6 0.0 copy-start.4
  35.7 0.0 copy-start.5
  35.7 0.0 copy-start.6
  35.7 0.0 copy-start.7
  35.7 0.0 copy-start.8
  35.7 0.0 copy-start.9
  35.7 0.3 fusion.42
  36.0 2.0 %collective-permute-done.4 = f32[2,4,16,136]{3,2,1,0:T(8,128)S(1)} collective-permute-done((f32[2,4,16,136]{3,2,1,0:T(8,128)S(1)}, f32[2,4,16,136]{3,2,1,0:T(8,128)S(1)}, u32[]{:S(2)}, u32[]{:S(2)}) %collective-permute-start.4) | collective-permute-done | bytes 69664 | tf_op jit(solution)/shard_map/ppermute | solution.py:20
  38.0 1.3 %collective-permute-done.5 = f32[2,4,16,136]{3,2,1,0:T(8,128)S(1)} collective-permute-done((f32[2,4,16,136]{3,2,1,0:T(8,128)S(1)}, f32[2,4,16,136]{3,2,1,0:T(8,128)S(1)}, u32[]{:S(2)}, u32[]{:S(2)}) %collective-permute-start.5) | collective-permute-done | bytes 69664 | tf_op jit(solution)/shard_map/ppermute | solution.py:17
  39.3 0.2 pad_maximum_fusion
  39.4 0.3 fusion.32
  39.8 0.2 fusion.18
  40.0 0.5 add_subtract_fusion.1
  40.6 1.8 %collective-permute-start.6 = (f32[2,8,4,128]{3,2,1,0:T(4,128)S(1)}, f32[2,8,4,128]{3,2,1,0:T(4,128)S(1)}, u32[]{:S(2)}, u32[]{:S(2)}) collective-permute-start(f32[2,8,4,128]{3,2,1,0:T(4,128)S(1)} %get-tuple-element.79), channel_id=1, source_target_pairs={{0,8},{8,16},{16,24},{1,9},{9,17},{17,25},{2,10},{10,18},{18,26},{... | collective-permute-start | bytes 98312 | tf_op jit(solution)/shard_map/ppermute | solution.py:17
  42.4 1.3 %collective-permute-start.7 = (f32[2,8,4,128]{3,2,1,0:T(4,128)S(1)}, f32[2,8,4,128]{3,2,1,0:T(4,128)S(1)}, u32[]{:S(2)}, u32[]{:S(2)}) collective-permute-start(f32[2,8,4,128]{3,2,1,0:T(4,128)S(1)} %get-tuple-element.80), channel_id=1, source_target_pairs={{8,0},{16,8},{24,16},{9,1},{17,9},{25,17},{10,2},{18,10},{26,18},{... | collective-permute-start | bytes 98312 | tf_op jit(solution)/shard_map/ppermute | solution.py:20
  43.7 4.2 %collective-permute-done.7 = f32[2,8,4,128]{3,2,1,0:T(4,128)S(1)} collective-permute-done((f32[2,8,4,128]{3,2,1,0:T(4,128)S(1)}, f32[2,8,4,128]{3,2,1,0:T(4,128)S(1)}, u32[]{:S(2)}, u32[]{:S(2)}) %collective-permute-start.7) | collective-permute-done | bytes 32800 | tf_op jit(solution)/shard_map/ppermute | solution.py:20
  47.9 0.1 fusion.199
  48.0 1.5 %collective-permute-start.8 = (f32[2,8,16,4]{3,2,1,0:T(8,128)S(1)}, f32[2,8,16,4]{3,2,1,0:T(8,128)S(1)}, u32[]{:S(2)}, u32[]{:S(2)}) collective-permute-start(f32[2,8,16,4]{3,2,1,0:T(8,128)S(1)} %get-tuple-element.71), channel_id=1, source_target_pairs={{0,4},{1,5},{2,6},{3,7},{8,12},{9,13},{10,14},{11,15},{16,20},{17,... | collective-permute-start | bytes 12296 | tf_op jit(solution)/shard_map/ppermute | solution.py:17
  49.5 1.3 %collective-permute-start.9 = (f32[2,8,16,4]{3,2,1,0:T(8,128)S(1)}, f32[2,8,16,4]{3,2,1,0:T(8,128)S(1)}, u32[]{:S(2)}, u32[]{:S(2)}) collective-permute-start(f32[2,8,16,4]{3,2,1,0:T(8,128)S(1)} %get-tuple-element.72), channel_id=1, source_target_pairs={{4,0},{5,1},{6,2},{7,3},{12,8},{13,9},{14,10},{15,11},{20,16},{21,... | collective-permute-start | bytes 12296 | tf_op jit(solution)/shard_map/ppermute | solution.py:20
  50.8 3.5 %copy.28 = f32[32,256,4]{1,2,0:T(4,128)} copy(f32[32,256,4]{2,1,0:T(8,128)} %bitcast.146) | data formatting | bytes 262144 | tf_op jit(solution)/shard_map/all_to_all | solution.py:196
  54.3 8.9 %all-to-all-start = ((f32[32,256,4]{1,2,0:T(4,128)}), f32[32,256,4]{1,2,0:T(4,128)S(1)}, u32[]{:S(2)}, u32[]{:S(2)}) async-start(f32[32,256,4]{1,2,0:T(4,128)} %copy.28), calls=%async_computation | async-start | bytes 262144 | tf_op jit(solution)/shard_map/all_to_all | solution.py:196
  63.2 0.2 pad_maximum_fusion.3
  63.5 3.7 %collective-permute-start.10 = (f32[2,4,16,136]{3,2,1,0:T(8,128)S(1)}, f32[2,4,16,136]{3,2,1,0:T(8,128)S(1)}, u32[]{:S(2)}, u32[]{:S(2)}) collective-permute-start(f32[2,4,16,136]{3,2,1,0:T(8,128)S(1)} %get-tuple-element.63), channel_id=1, source_target_pairs={{0,1},{1,2},{2,3},{4,5},{5,6},{6,7},{8,9},{9,10},{10,11},{12,13},{... | collective-permute-start | bytes 208904 | tf_op jit(solution)/shard_map/ppermute | solution.py:17
  67.2 1.3 %collective-permute-start.11 = (f32[2,4,16,136]{3,2,1,0:T(8,128)S(1)}, f32[2,4,16,136]{3,2,1,0:T(8,128)S(1)}, u32[]{:S(2)}, u32[]{:S(2)}) collective-permute-start(f32[2,4,16,136]{3,2,1,0:T(8,128)S(1)} %get-tuple-element.64), channel_id=1, source_target_pairs={{1,0},{2,1},{3,2},{5,4},{6,5},{7,6},{9,8},{10,9},{11,10},{13,12},{... | collective-permute-start | bytes 208904 | tf_op jit(solution)/shard_map/ppermute | solution.py:20
  68.5 1.7 %collective-permute-done.10 = f32[2,4,16,136]{3,2,1,0:T(8,128)S(1)} collective-permute-done((f32[2,4,16,136]{3,2,1,0:T(8,128)S(1)}, f32[2,4,16,136]{3,2,1,0:T(8,128)S(1)}, u32[]{:S(2)}, u32[]{:S(2)}) %collective-permute-start.10) | collective-permute-done | bytes 69664 | tf_op jit(solution)/shard_map/ppermute | solution.py:17
  70.2 4.1 %collective-permute-done.11 = f32[2,4,16,136]{3,2,1,0:T(8,128)S(1)} collective-permute-done((f32[2,4,16,136]{3,2,1,0:T(8,128)S(1)}, f32[2,4,16,136]{3,2,1,0:T(8,128)S(1)}, u32[]{:S(2)}, u32[]{:S(2)}) %collective-permute-start.11) | collective-permute-done | bytes 69664 | tf_op jit(solution)/shard_map/ppermute | solution.py:20
  74.4 0.2 pad_maximum_fusion.1
  74.6 0.1 slice_convert_fusion.1
  74.8 2.5 %fusion.1 = f32[2,16,136]{2,1,0:T(8,128)S(1)} fusion(s32[8192]{0:T(1024)S(1)} %bitcast.155, f32[8192,16]{0,1:T(8,128)S(1)} %fusion.9, f32[8192,2]{0,1:T(2,128)S(1)} %slice.825), kind=kOutput, calls=%fused_computation.3 | convolution fusion | flops 429195264 | bytes 640000 | tf_op jit(solution)/shard_map/nkx,ny->kxy/dot_general | solution.py:206
  77.2 0.1 slice.829
  77.3 0.1 fusion.161
  77.4 0.3 fusion.25
  77.7 0.3 fusion.87
  78.1 0.2 fusion.11
  78.3 0.1 slice.912
  78.3 0.5 add_subtract_fusion
  78.8 0.6 fusion.160
  79.5 0.6 slice_bitcast_fusion
  (44 shorter events, 0.4 us)
Async XLA Ops:
  0.6 10.9 %copy-start = (f32[256,256]{1,0:T(8,128)S(1)}, f32[256,256]{1,0:T(8,128)}, u32[]{:S(2)}) copy-start(f32[256,256]{1,0:T(8,128)} %param.34) | copy-start | bytes 786436
  0.6 17.5 %copy-start.1 = (f32[8,8,128]{2,1,0:T(8,128)S(1)}, f32[8,8,128]{2,1,0:T(8,128)}, u32[]{:S(2)}) copy-start(f32[8,8,128]{2,1,0:T(8,128)} %param.23) | copy-start | bytes 98308
  0.7 17.5 %copy-start.2 = (f32[8,8,128]{2,1,0:T(8,128)S(1)}, f32[8,8,128]{2,1,0:T(8,128)}, u32[]{:S(2)}) copy-start(f32[8,8,128]{2,1,0:T(8,128)} %param.25) | copy-start | bytes 98308
  1.5 16.6 %collective-permute-start = (f32[2,8,4,128]{3,2,1,0:T(4,128)S(1)}, f32[2,8,4,128]{3,2,1,0:T(4,128)S(1)}, u32[]{:S(2)}, u32[]{:S(2)}) collective-permute-start(f32[2,8,4,128]{3,2,1,0:T(4,128)S(1)} %get-tuple-element.86), channel_id=1, source_target_pairs={{0,8},{8,16},{16,24},{1,9},{9,17},{17,25},{2,10},{10,18},{18,26},{... | collective-permute-start | bytes 98312 | tf_op jit(solution)/shard_map/ppermute | solution.py:17
  3.9 14.2 %collective-permute-start.1 = (f32[2,8,4,128]{3,2,1,0:T(4,128)S(1)}, f32[2,8,4,128]{3,2,1,0:T(4,128)S(1)}, u32[]{:S(2)}, u32[]{:S(2)}) collective-permute-start(f32[2,8,4,128]{3,2,1,0:T(4,128)S(1)} %get-tuple-element.87), channel_id=1, source_target_pairs={{8,0},{16,8},{24,16},{9,1},{17,9},{25,17},{10,2},{18,10},{26,18},{... | collective-permute-start | bytes 98312 | tf_op jit(solution)/shard_map/ppermute | solution.py:20
  18.3 6.7 %collective-permute-start.3 = (f32[2,8,16,4]{3,2,1,0:T(8,128)S(1)}, f32[2,8,16,4]{3,2,1,0:T(8,128)S(1)}, u32[]{:S(2)}, u32[]{:S(2)}) collective-permute-start(f32[2,8,16,4]{3,2,1,0:T(8,128)S(1)} %get-tuple-element.75), channel_id=1, source_target_pairs={{0,4},{1,5},{2,6},{3,7},{8,12},{9,13},{10,14},{11,15},{16,20},{17,... | collective-permute-start | bytes 12296 | tf_op jit(solution)/shard_map/ppermute | solution.py:17
  22.5 7.1 %collective-permute-start.2 = (f32[2,8,16,4]{3,2,1,0:T(8,128)S(1)}, f32[2,8,16,4]{3,2,1,0:T(8,128)S(1)}, u32[]{:S(2)}, u32[]{:S(2)}) collective-permute-start(f32[2,8,16,4]{3,2,1,0:T(8,128)S(1)} %get-tuple-element.76), channel_id=1, source_target_pairs={{4,0},{5,1},{6,2},{7,3},{12,8},{13,9},{14,10},{15,11},{20,16},{21,... | collective-permute-start | bytes 12296 | tf_op jit(solution)/shard_map/ppermute | solution.py:20
  29.8 8.2 %collective-permute-start.4 = (f32[2,4,16,136]{3,2,1,0:T(8,128)S(1)}, f32[2,4,16,136]{3,2,1,0:T(8,128)S(1)}, u32[]{:S(2)}, u32[]{:S(2)}) collective-permute-start(f32[2,4,16,136]{3,2,1,0:T(8,128)S(1)} %get-tuple-element.65), channel_id=1, source_target_pairs={{1,0},{2,1},{3,2},{5,4},{6,5},{7,6},{9,8},{10,9},{11,10},{13,12},{... | collective-permute-start | bytes 208904 | tf_op jit(solution)/shard_map/ppermute | solution.py:20
  31.1 8.2 %collective-permute-start.5 = (f32[2,4,16,136]{3,2,1,0:T(8,128)S(1)}, f32[2,4,16,136]{3,2,1,0:T(8,128)S(1)}, u32[]{:S(2)}, u32[]{:S(2)}) collective-permute-start(f32[2,4,16,136]{3,2,1,0:T(8,128)S(1)} %get-tuple-element.66), channel_id=1, source_target_pairs={{0,1},{1,2},{2,3},{4,5},{5,6},{6,7},{8,9},{9,10},{10,11},{12,13},{... | collective-permute-start | bytes 208904 | tf_op jit(solution)/shard_map/ppermute | solution.py:17
  35.6 4.8 %copy-start.3 = (f32[8,8,128]{2,1,0:T(8,128)S(1)}, f32[8,8,128]{2,1,0:T(8,128)}, u32[]{:S(2)}) copy-start(f32[8,8,128]{2,1,0:T(8,128)} %param.27) | copy-start | bytes 98308
  35.6 4.8 %copy-start.4 = (f32[8,8,128]{2,1,0:T(8,128)S(1)}, f32[8,8,128]{2,1,0:T(8,128)}, u32[]{:S(2)}) copy-start(f32[8,8,128]{2,1,0:T(8,128)} %param.32) | copy-start | bytes 98308
  35.7 4.8 %copy-start.5 = (f32[8,8,128]{2,1,0:T(8,128)S(1)}, f32[8,8,128]{2,1,0:T(8,128)}, u32[]{:S(2)}) copy-start(f32[8,8,128]{2,1,0:T(8,128)} %param.33) | copy-start | bytes 98308
  35.7 4.8 %copy-start.6 = (f32[8,8,128]{2,1,0:T(8,128)S(1)}, f32[8,8,128]{2,1,0:T(8,128)}, u32[]{:S(2)}) copy-start(f32[8,8,128]{2,1,0:T(8,128)} %param.29) | copy-start | bytes 98308
  35.7 4.8 %copy-start.7 = (f32[8,8,128]{2,1,0:T(8,128)S(1)}, f32[8,8,128]{2,1,0:T(8,128)}, u32[]{:S(2)}) copy-start(f32[8,8,128]{2,1,0:T(8,128)} %param.28) | copy-start | bytes 98308
  35.7 4.8 %copy-start.8 = (f32[8,8,128]{2,1,0:T(8,128)S(1)}, f32[8,8,128]{2,1,0:T(8,128)}, u32[]{:S(2)}) copy-start(f32[8,8,128]{2,1,0:T(8,128)} %param.26) | copy-start | bytes 98308
  35.7 4.8 %copy-start.9 = (f32[8,8,128]{2,1,0:T(8,128)S(1)}, f32[8,8,128]{2,1,0:T(8,128)}, u32[]{:S(2)}) copy-start(f32[8,8,128]{2,1,0:T(8,128)} %param.24) | copy-start | bytes 98308
  40.6 3.1 %collective-permute-start.6 = (f32[2,8,4,128]{3,2,1,0:T(4,128)S(1)}, f32[2,8,4,128]{3,2,1,0:T(4,128)S(1)}, u32[]{:S(2)}, u32[]{:S(2)}) collective-permute-start(f32[2,8,4,128]{3,2,1,0:T(4,128)S(1)} %get-tuple-element.79), channel_id=1, source_target_pairs={{0,8},{8,16},{16,24},{1,9},{9,17},{17,25},{2,10},{10,18},{18,26},{... | collective-permute-start | bytes 98312 | tf_op jit(solution)/shard_map/ppermute | solution.py:17
  42.4 5.5 %collective-permute-start.7 = (f32[2,8,4,128]{3,2,1,0:T(4,128)S(1)}, f32[2,8,4,128]{3,2,1,0:T(4,128)S(1)}, u32[]{:S(2)}, u32[]{:S(2)}) collective-permute-start(f32[2,8,4,128]{3,2,1,0:T(4,128)S(1)} %get-tuple-element.80), channel_id=1, source_target_pairs={{8,0},{16,8},{24,16},{9,1},{17,9},{25,17},{10,2},{18,10},{26,18},{... | collective-permute-start | bytes 98312 | tf_op jit(solution)/shard_map/ppermute | solution.py:20
  48.0 15.2 %collective-permute-start.8 = (f32[2,8,16,4]{3,2,1,0:T(8,128)S(1)}, f32[2,8,16,4]{3,2,1,0:T(8,128)S(1)}, u32[]{:S(2)}, u32[]{:S(2)}) collective-permute-start(f32[2,8,16,4]{3,2,1,0:T(8,128)S(1)} %get-tuple-element.71), channel_id=1, source_target_pairs={{0,4},{1,5},{2,6},{3,7},{8,12},{9,13},{10,14},{11,15},{16,20},{17,... | collective-permute-start | bytes 12296 | tf_op jit(solution)/shard_map/ppermute | solution.py:17
  49.5 13.7 %collective-permute-start.9 = (f32[2,8,16,4]{3,2,1,0:T(8,128)S(1)}, f32[2,8,16,4]{3,2,1,0:T(8,128)S(1)}, u32[]{:S(2)}, u32[]{:S(2)}) collective-permute-start(f32[2,8,16,4]{3,2,1,0:T(8,128)S(1)} %get-tuple-element.72), channel_id=1, source_target_pairs={{4,0},{5,1},{6,2},{7,3},{12,8},{13,9},{14,10},{15,11},{20,16},{21,... | collective-permute-start | bytes 12296 | tf_op jit(solution)/shard_map/ppermute | solution.py:20
  54.3 20.3 %all-to-all-start = ((f32[32,256,4]{1,2,0:T(4,128)}), f32[32,256,4]{1,2,0:T(4,128)S(1)}, u32[]{:S(2)}, u32[]{:S(2)}) async-start(f32[32,256,4]{1,2,0:T(4,128)} %copy.28), calls=%async_computation | async-start | bytes 262144 | tf_op jit(solution)/shard_map/all_to_all | solution.py:196
  63.5 6.7 %collective-permute-start.10 = (f32[2,4,16,136]{3,2,1,0:T(8,128)S(1)}, f32[2,4,16,136]{3,2,1,0:T(8,128)S(1)}, u32[]{:S(2)}, u32[]{:S(2)}) collective-permute-start(f32[2,4,16,136]{3,2,1,0:T(8,128)S(1)} %get-tuple-element.63), channel_id=1, source_target_pairs={{0,1},{1,2},{2,3},{4,5},{5,6},{6,7},{8,9},{9,10},{10,11},{12,13},{... | collective-permute-start | bytes 208904 | tf_op jit(solution)/shard_map/ppermute | solution.py:17
  67.2 7.2 %collective-permute-start.11 = (f32[2,4,16,136]{3,2,1,0:T(8,128)S(1)}, f32[2,4,16,136]{3,2,1,0:T(8,128)S(1)}, u32[]{:S(2)}, u32[]{:S(2)}) collective-permute-start(f32[2,4,16,136]{3,2,1,0:T(8,128)S(1)} %get-tuple-element.64), channel_id=1, source_target_pairs={{1,0},{2,1},{3,2},{5,4},{6,5},{7,6},{9,8},{10,9},{11,10},{13,12},{... | collective-permute-start | bytes 208904 | tf_op jit(solution)/shard_map/ppermute | solution.py:20

commit v5 on v2

--- a/solution.py
+++ b/solution.py
@@ -10,6 +10,16 @@
 def with_halo(block, sides, width):
     for axis, dim in sides:
         count = lax.axis_size(axis)
+        if count == 2:
+            first = lax.axis_index(axis) == 0
+            top = lax.slice_in_dim(block, block.shape[dim] - width, None, axis=dim)
+            bottom = lax.slice_in_dim(block, 0, width, axis=dim)
+            got = lax.ppermute(jnp.where(first, top, bottom), axis, [(0, 1), (1, 0)])
+            empty = jnp.zeros_like(got)
+            low = jnp.where(first, empty, got)
+            high = jnp.where(first, got, empty)
+            block = jnp.concatenate([low, block, high], axis=dim)
+            continue
         forward = [(i, i + 1) for i in range(count - 1)]
         backward = [(target, source) for source, target in forward]
         low = lax.ppermute(

time: 67.6 us -> 60.5 us (0.89)
  the two profiles are of different devices: /device:TPU:14 before, /device:TPU:12 now
where the time goes in v5:
time: 60.5 us; the launch traced here: 59.8 us
  starting transfers between devices  29.3 us (48%)
  waiting for transfers between devices  13.9 us (23%)
  local copies, waits for them, and re-layouts  7.9 us (13%)
  other arithmetic  6.61 us (11%)
  between operations  1.24 us (2%)
  matrix products  0.85 us (1%)
    ppermute x4, starting transfers between devices, with_halo(): lax.ppermute(lax.slice_in_dim(block, block.shape[dim] - width, None, axis...  11.4 us
    ppermute x4, starting transfers between devices, with_halo(): lax.ppermute(lax.slice_in_dim(block, 0, width, axis=dim), axis, backward)  8.95 us
    ppermute x2, waiting for transfers between devices, with_halo(): got = lax.ppermute(jnp.where(first, top, bottom), axis, [(0, 1), (1, 0)])  7.75 us
    all_to_all x1, starting transfers between devices, local(): lax.all_to_all(send, ('inl', 'xl', 'gz'), split_axis=0, concat_axis=0, ti...  5.99 us
    ppermute x4, waiting for transfers between devices, with_halo(): lax.ppermute(lax.slice_in_dim(block, block.shape[dim] - width, None, axis...  5.38 us
    unnamed x46, local copies, waits for them, and re-layouts  4.17 us
    ppermute x2, starting transfers between devices, with_halo(): got = lax.ppermute(jnp.where(first, top, bottom), axis, [(0, 1), (1, 0)])  2.97 us
    concatenate x10, other arithmetic, with_halo(): block = jnp.concatenate([low, block, high], axis=dim)  1.47 us
  transfers between devices with their start and end apart: 11, of which 5 were waited for; matrix products, arithmetic and copies ran while one was open for 12% of the time, Pallas kernels for 0%

profile of v5, /device:TPU:12, one launch (start us, length us, event | category | flops | bytes accessed | tf_op | source)
XLA Modules:
  0.0 59.8 jit_solution(16992759587731233353)
XLA Ops:
  0.6 0.0 copy-start
  0.6 0.9 %fusion.149 = (f32[2,8,4,128]{3,2,1,0:T(4,128)S(1)}, f32[2,8,4,128]{3,2,1,0:T(4,128)S(1)}) fusion(f32[1,8,8,128]{3,2,1,0:T(8,128)} %bitcast.119, f32[1,8,8,128]{3,2,1,0:T(8,128)} %bitcast.126), kind=kLoop, calls=%fused_computation.276 | loop fusion | flops 16384 | bytes 131072 | tf_op jit(solution)/shard_map/stack | solution.py:180
  1.5 1.9 %collective-permute-start = (f32[2,8,4,128]{3,2,1,0:T(4,128)S(1)}, f32[2,8,4,128]{3,2,1,0:T(4,128)S(1)}, u32[]{:S(2)}, u32[]{:S(2)}) collective-permute-start(f32[2,8,4,128]{3,2,1,0:T(4,128)S(1)} %get-tuple-element.86), channel_id=1, source_target_pairs={{8,0},{16,8},{24,16},{9,1},{17,9},{25,17},{10,2},{18,10},{26,18},{... | collective-permute-start | bytes 98312 | tf_op jit(solution)/shard_map/ppermute | solution.py:28
  3.5 2.4 %collective-permute-start.1 = (f32[2,8,4,128]{3,2,1,0:T(4,128)S(1)}, f32[2,8,4,128]{3,2,1,0:T(4,128)S(1)}, u32[]{:S(2)}, u32[]{:S(2)}) collective-permute-start(f32[2,8,4,128]{3,2,1,0:T(4,128)S(1)} %get-tuple-element.85), channel_id=1, source_target_pairs={{0,8},{8,16},{16,24},{1,9},{9,17},{17,25},{2,10},{10,18},{18,26},{... | collective-permute-start | bytes 98312 | tf_op jit(solution)/shard_map/ppermute | solution.py:25
  5.9 0.6 reduce-window.6
  6.5 0.2 slice_reduce_fusion
  6.8 0.1 fusion.176
  6.9 0.7 %copy-done.18 = s32[256]{0:T(256)S(1)} copy-done((s32[256]{0:T(256)S(1)}, s32[256]{0:T(256)}, u32[]{:S(2)}) %copy-start.18) | copy-done | bytes 1048
  7.6 0.1 select_reduce_fusion
  7.7 0.6 copy-done.17
  8.2 0.3 convolution_multiply_fusion
  8.5 0.1 pad_maximum_fusion.36
  8.6 0.1 copy.30
  8.7 1.4 %scatter_custom_fusion = f32[2048,3]{1,0:T(8,128)S(1)} fusion(s32[256]{0:T(256)S(1)} %compare_select_fusion.3, f32[256,3]{1,0:T(8,128)S(1)} %copy.30, f32[]{:T(128)} %constant.189.clone.1), kind=kCustom, calls=%fused_computation.8 | custom fusion | bytes 24580 | tf_op jit(solution)/shard_map/scatter | solution.py:168
  10.1 0.4 copy.31
  10.5 0.7 %reshape.199 = f32[32,1,192]{2,1,0:T(1,128)} reshape(f32[32,3,64]{2,1,0:T(4,128)S(1)} %bitcast.133) | data formatting | bytes 49152
  11.3 6.0 %all-to-all-start = ((f32[32,1,192]{2,1,0:T(1,128)}), f32[32,1,192]{2,1,0:T(1,128)S(1)}, u32[]{:S(2)}, u32[]{:S(2)}) async-start(f32[32,1,192]{2,1,0:T(1,128)} %reshape.199), calls=%async_computation | async-start | bytes 65536 | tf_op jit(solution)/shard_map/all_to_all | solution.py:169
  17.3 0.2 fusion.190
  17.6 0.7 %copy-done.3 = f32[8,8,128]{2,1,0:T(8,128)S(1)} copy-done((f32[8,8,128]{2,1,0:T(8,128)S(1)}, f32[8,8,128]{2,1,0:T(8,128)}, u32[]{:S(2)}) %copy-start.3) | copy-done | bytes 32792
  18.3 0.0 copy-done.4
  18.3 0.1 slice_select_fusion.1
  18.4 1.5 %collective-permute-start.2 = (f32[2,8,16,4]{3,2,1,0:T(8,128)S(1)}, f32[2,8,16,4]{3,2,1,0:T(8,128)S(1)}, u32[]{:S(2)}, u32[]{:S(2)}) collective-permute-start(f32[2,8,16,4]{3,2,1,0:T(8,128)S(1)} %slice_select_fusion.1), channel_id=1, source_target_pairs={{0,4},{4,0},{1,5},{5,1},{2,6},{6,2},{3,7},{7,3},{8,12},{12,8},{9,1... | collective-permute-start | bytes 12296 | tf_op jit(solution)/shard_map/ppermute | solution.py:17
  20.0 4.2 %collective-permute-done.2 = f32[2,8,16,4]{3,2,1,0:T(8,128)S(1)} collective-permute-done((f32[2,8,16,4]{3,2,1,0:T(8,128)S(1)}, f32[2,8,16,4]{3,2,1,0:T(8,128)S(1)}, u32[]{:S(2)}, u32[]{:S(2)}) %collective-permute-start.2) | collective-permute-done | bytes 4128 | tf_op jit(solution)/shard_map/ppermute | solution.py:17
  24.2 0.2 pad_maximum_fusion.3
  24.5 2.6 %collective-permute-start.3 = (f32[2,4,16,136]{3,2,1,0:T(8,128)S(1)}, f32[2,4,16,136]{3,2,1,0:T(8,128)S(1)}, u32[]{:S(2)}, u32[]{:S(2)}) collective-permute-start(f32[2,4,16,136]{3,2,1,0:T(8,128)S(1)} %get-tuple-element.60), channel_id=1, source_target_pairs={{1,0},{2,1},{3,2},{5,4},{6,5},{7,6},{9,8},{10,9},{11,10},{13,12},{... | collective-permute-start | bytes 208904 | tf_op jit(solution)/shard_map/ppermute | solution.py:28
  27.0 3.3 %collective-permute-start.4 = (f32[2,4,16,136]{3,2,1,0:T(8,128)S(1)}, f32[2,4,16,136]{3,2,1,0:T(8,128)S(1)}, u32[]{:S(2)}, u32[]{:S(2)}) collective-permute-start(f32[2,4,16,136]{3,2,1,0:T(8,128)S(1)} %get-tuple-element.61), channel_id=1, source_target_pairs={{0,1},{1,2},{2,3},{4,5},{5,6},{6,7},{8,9},{9,10},{10,11},{12,13},{... | collective-permute-start | bytes 208904 | tf_op jit(solution)/shard_map/ppermute | solution.py:25
  30.3 0.2 pad_maximum_fusion.2
  30.6 0.5 broadcast.408
  31.1 0.7 %reduce.10 = f32[32,192]{1,0:T(8,128)S(1)} reduce(f32[32,1,192]{2,1,0:T(1,128)S(1)} %all-to-all-done, f32[]{:T(128)} %broadcast.408), dimensions={1}, to_apply=%all_to_all.9.reduce_sub_computation | reduce | bytes 49156 | tf_op jit(solution)/shard_map/all_to_all | solution.py:169
  31.8 0.1 reshape.200
  31.9 0.1 all_to_all.10
  32.0 0.1 and_select_fusion.1
  32.1 0.5 copy-done.10
  32.7 0.7 %slice-done = f32[2048,2]{0,1:T(2,128)S(1)} async-done(((f32[2048,3]{0,1:T(4,128)}), f32[2048,2]{0,1:T(2,128)S(1)}, s32[]{:S(2)}) %slice-start) | async-done | bytes 16408 | tf_op jit(solution)/shard_map/slice | solution.py:177
  33.4 0.6 fusion.1
  34.0 0.2 pad_maximum_fusion
  34.2 0.3 fusion.28
  34.5 0.2 fusion.14
  34.8 0.6 %add_subtract_fusion.1 = (f32[2,8,8,128]{3,2,1,0:T(8,128)S(1)}, f32[2,8,8,128]{3,2,1,0:T(8,128)S(1)}) fusion(f32[2,16,8,128]{3,2,1,0:T(8,128)S(1)} %fusion.28, f32[8,8,128]{2,1,0:T(8,128)S(1)} %get-tuple-element.80, f32[2,16,8,136]{3,2,1,0:T(8,128)S(1)} %fusion.14, f32[8,8,128]{2,1,0:T(8,128)S(1)} %get-tuple-element.81, ...), kind=kLoop, calls=%fused_computation.261 | loop fusion | flops 2179072 | bytes 3227648 | tf_op jit(solution)/shard_map/sub | solution.py:105
  35.4 0.1 copy-done.5
  35.5 0.0 copy-done.6
  35.5 0.0 copy-done.7
  35.5 0.0 copy-done.8
  35.5 0.0 copy-done.9
  35.6 0.0 copy-done.15
  35.6 0.0 copy-done.16
  35.7 1.9 %collective-permute-start.5 = (f32[2,8,4,128]{3,2,1,0:T(4,128)S(1)}, f32[2,8,4,128]{3,2,1,0:T(4,128)S(1)}, u32[]{:S(2)}, u32[]{:S(2)}) collective-permute-start(f32[2,8,4,128]{3,2,1,0:T(4,128)S(1)} %get-tuple-element.77), channel_id=1, source_target_pairs={{8,0},{16,8},{24,16},{9,1},{17,9},{25,17},{10,2},{18,10},{26,18},{... | collective-permute-start | bytes 98312 | tf_op jit(solution)/shard_map/ppermute | solution.py:28
  37.6 2.4 %collective-permute-start.6 = (f32[2,8,4,128]{3,2,1,0:T(4,128)S(1)}, f32[2,8,4,128]{3,2,1,0:T(4,128)S(1)}, u32[]{:S(2)}, u32[]{:S(2)}) collective-permute-start(f32[2,8,4,128]{3,2,1,0:T(4,128)S(1)} %get-tuple-element.76), channel_id=1, source_target_pairs={{0,8},{8,16},{16,24},{1,9},{9,17},{17,25},{2,10},{10,18},{18,26},{... | collective-permute-start | bytes 98312 | tf_op jit(solution)/shard_map/ppermute | solution.py:25
  40.1 2.8 %collective-permute-done.6 = f32[2,8,4,128]{3,2,1,0:T(4,128)S(1)} collective-permute-done((f32[2,8,4,128]{3,2,1,0:T(4,128)S(1)}, f32[2,8,4,128]{3,2,1,0:T(4,128)S(1)}, u32[]{:S(2)}, u32[]{:S(2)}) %collective-permute-start.6) | collective-permute-done | bytes 32800 | tf_op jit(solution)/shard_map/ppermute | solution.py:25
  42.9 0.1 slice_select_fusion
  43.0 1.4 %collective-permute-start.7 = (f32[2,8,16,4]{3,2,1,0:T(8,128)S(1)}, f32[2,8,16,4]{3,2,1,0:T(8,128)S(1)}, u32[]{:S(2)}, u32[]{:S(2)}) collective-permute-start(f32[2,8,16,4]{3,2,1,0:T(8,128)S(1)} %slice_select_fusion), channel_id=1, source_target_pairs={{0,4},{4,0},{1,5},{5,1},{2,6},{6,2},{3,7},{7,3},{8,12},{12,8},{9,1... | collective-permute-start | bytes 12296 | tf_op jit(solution)/shard_map/ppermute | solution.py:17
  44.5 3.6 %collective-permute-done.7 = f32[2,8,16,4]{3,2,1,0:T(8,128)S(1)} collective-permute-done((f32[2,8,16,4]{3,2,1,0:T(8,128)S(1)}, f32[2,8,16,4]{3,2,1,0:T(8,128)S(1)}, u32[]{:S(2)}, u32[]{:S(2)}) %collective-permute-start.7) | collective-permute-done | bytes 4128 | tf_op jit(solution)/shard_map/ppermute | solution.py:17
  48.1 0.2 pad_maximum_fusion.5
  48.3 2.6 %collective-permute-start.8 = (f32[2,4,16,136]{3,2,1,0:T(8,128)S(1)}, f32[2,4,16,136]{3,2,1,0:T(8,128)S(1)}, u32[]{:S(2)}, u32[]{:S(2)}) collective-permute-start(f32[2,4,16,136]{3,2,1,0:T(8,128)S(1)} %get-tuple-element.58), channel_id=1, source_target_pairs={{1,0},{2,1},{3,2},{5,4},{6,5},{7,6},{9,8},{10,9},{11,10},{13,12},{... | collective-permute-start | bytes 208904 | tf_op jit(solution)/shard_map/ppermute | solution.py:28
  50.9 3.3 %collective-permute-start.9 = (f32[2,4,16,136]{3,2,1,0:T(8,128)S(1)}, f32[2,4,16,136]{3,2,1,0:T(8,128)S(1)}, u32[]{:S(2)}, u32[]{:S(2)}) collective-permute-start(f32[2,4,16,136]{3,2,1,0:T(8,128)S(1)} %get-tuple-element.59), channel_id=1, source_target_pairs={{0,1},{1,2},{2,3},{4,5},{5,6},{6,7},{8,9},{9,10},{10,11},{12,13},{... | collective-permute-start | bytes 208904 | tf_op jit(solution)/shard_map/ppermute | solution.py:25
  54.2 0.2 pad_maximum_fusion.4
  54.4 0.8 %collective-permute-done.8 = f32[2,4,16,136]{3,2,1,0:T(8,128)S(1)} collective-permute-done((f32[2,4,16,136]{3,2,1,0:T(8,128)S(1)}, f32[2,4,16,136]{3,2,1,0:T(8,128)S(1)}, u32[]{:S(2)}, u32[]{:S(2)}) %collective-permute-start.8) | collective-permute-done | bytes 69664 | tf_op jit(solution)/shard_map/ppermute | solution.py:28
  55.2 2.6 %collective-permute-done.9 = f32[2,4,16,136]{3,2,1,0:T(8,128)S(1)} collective-permute-done((f32[2,4,16,136]{3,2,1,0:T(8,128)S(1)}, f32[2,4,16,136]{3,2,1,0:T(8,128)S(1)}, u32[]{:S(2)}, u32[]{:S(2)}) %collective-permute-start.9) | collective-permute-done | bytes 69664 | tf_op jit(solution)/shard_map/ppermute | solution.py:25
  57.8 0.2 pad_maximum_fusion.1
  58.0 0.3 fusion.21
  58.3 0.2 fusion.7
  58.5 0.6 %add_subtract_fusion = (f32[2,8,8,128]{3,2,1,0:T(8,128)S(1)}, f32[2,8,8,128]{3,2,1,0:T(8,128)S(1)}) fusion(f32[2,16,8,128]{3,2,1,0:T(8,128)S(1)} %fusion.21, f32[8,8,128]{2,1,0:T(8,128)S(1)} %get-tuple-element.80, f32[2,16,8,136]{3,2,1,0:T(8,128)S(1)} %fusion.7, f32[8,8,128]{2,1,0:T(8,128)S(1)} %get-tuple-element.81, ...), kind=kLoop, calls=%fused_computation.255 | loop fusion | flops 2179072 | bytes 3227648 | tf_op jit(solution)/shard_map/sub | solution.py:105
  59.2 0.6 copy-done.11
  59.8 0.0 copy-done.12
  (58 shorter events, 0.5 us)
Async XLA Ops:
  0.6 7.0 %copy-start = (f32[256,256]{1,0:T(8,128)S(1)}, f32[256,256]{1,0:T(8,128)}, u32[]{:S(2)}) copy-start(f32[256,256]{1,0:T(8,128)} %param.36) | copy-start | bytes 786436
  1.5 4.4 %copy-start.20 = (s32[256]{0:T(256)S(1)}, s32[256]{0:T(256)}, u32[]{:S(2)}) copy-start(s32[256]{0:T(256)} %param.40) | copy-start | bytes 3076
  1.5 4.4 %copy-start.19 = (s32[256]{0:T(256)S(1)}, s32[256]{0:T(256)}, u32[]{:S(2)}) copy-start(s32[256]{0:T(256)} %param.39) | copy-start | bytes 3076
  1.5 16.0 %collective-permute-start = (f32[2,8,4,128]{3,2,1,0:T(4,128)S(1)}, f32[2,8,4,128]{3,2,1,0:T(4,128)S(1)}, u32[]{:S(2)}, u32[]{:S(2)}) collective-permute-start(f32[2,8,4,128]{3,2,1,0:T(4,128)S(1)} %get-tuple-element.86), channel_id=1, source_target_pairs={{8,0},{16,8},{24,16},{9,1},{17,9},{25,17},{10,2},{18,10},{26,18},{... | collective-permute-start | bytes 98312 | tf_op jit(solution)/shard_map/ppermute | solution.py:28
  3.5 14.1 %collective-permute-start.1 = (f32[2,8,4,128]{3,2,1,0:T(4,128)S(1)}, f32[2,8,4,128]{3,2,1,0:T(4,128)S(1)}, u32[]{:S(2)}, u32[]{:S(2)}) collective-permute-start(f32[2,8,4,128]{3,2,1,0:T(4,128)S(1)} %get-tuple-element.85), channel_id=1, source_target_pairs={{0,8},{8,16},{16,24},{1,9},{9,17},{17,25},{2,10},{10,18},{18,26},{... | collective-permute-start | bytes 98312 | tf_op jit(solution)/shard_map/ppermute | solution.py:25
  6.9 0.7 %copy-start.18 = (s32[256]{0:T(256)S(1)}, s32[256]{0:T(256)}, u32[]{:S(2)}) copy-start(s32[256]{0:T(256)} %param.41) | copy-start | bytes 3076
  6.9 0.7 %copy-start.21 = (f32[64]{0:T(128)S(1)}, f32[64]{0:T(128)}, u32[]{:S(2)}) copy-start(f32[64]{0:T(128)} %param.38) | copy-start | bytes 772
  7.6 0.7 %copy-start.17 = (f32[2,256]{1,0:T(2,128)S(1)}, f32[2,256]{1,0:T(2,128)}, u32[]{:S(2)}) copy-start(f32[2,256]{1,0:T(2,128)} %param.37) | copy-start | bytes 6148
  11.3 6.0 %copy-start.13 = (f32[8,8,128]{2,1,0:T(8,128)S(1)}, f32[8,8,128]{2,1,0:T(8,128)}, u32[]{:S(2)}) copy-start(f32[8,8,128]{2,1,0:T(8,128)} %param.33) | copy-start | bytes 98308
  11.3 6.0 %copy-start.14 = (f32[8,8,128]{2,1,0:T(8,128)S(1)}, f32[8,8,128]{2,1,0:T(8,128)}, u32[]{:S(2)}) copy-start(f32[8,8,128]{2,1,0:T(8,128)} %param.32) | copy-start | bytes 98308
  11.3 19.3 %all-to-all-start = ((f32[32,1,192]{2,1,0:T(1,128)}), f32[32,1,192]{2,1,0:T(1,128)S(1)}, u32[]{:S(2)}, u32[]{:S(2)}) async-start(f32[32,1,192]{2,1,0:T(1,128)} %reshape.199), calls=%async_computation | async-start | bytes 65536 | tf_op jit(solution)/shard_map/all_to_all | solution.py:169
  17.5 0.8 %copy-start.3 = (f32[8,8,128]{2,1,0:T(8,128)S(1)}, f32[8,8,128]{2,1,0:T(8,128)}, u32[]{:S(2)}) copy-start(f32[8,8,128]{2,1,0:T(8,128)} %param.25) | copy-start | bytes 98308
  17.5 0.8 %copy-start.4 = (f32[8,8,128]{2,1,0:T(8,128)S(1)}, f32[8,8,128]{2,1,0:T(8,128)}, u32[]{:S(2)}) copy-start(f32[8,8,128]{2,1,0:T(8,128)} %param.27) | copy-start | bytes 98308
  18.4 5.7 %collective-permute-start.2 = (f32[2,8,16,4]{3,2,1,0:T(8,128)S(1)}, f32[2,8,16,4]{3,2,1,0:T(8,128)S(1)}, u32[]{:S(2)}, u32[]{:S(2)}) collective-permute-start(f32[2,8,16,4]{3,2,1,0:T(8,128)S(1)} %slice_select_fusion.1), channel_id=1, source_target_pairs={{0,4},{4,0},{1,5},{5,1},{2,6},{6,2},{3,7},{7,3},{8,12},{12,8},{9,1... | collective-permute-start | bytes 12296 | tf_op jit(solution)/shard_map/ppermute | solution.py:17
  24.5 9.5 %collective-permute-start.3 = (f32[2,4,16,136]{3,2,1,0:T(8,128)S(1)}, f32[2,4,16,136]{3,2,1,0:T(8,128)S(1)}, u32[]{:S(2)}, u32[]{:S(2)}) collective-permute-start(f32[2,4,16,136]{3,2,1,0:T(8,128)S(1)} %get-tuple-element.60), channel_id=1, source_target_pairs={{1,0},{2,1},{3,2},{5,4},{6,5},{7,6},{9,8},{10,9},{11,10},{13,12},{... | collective-permute-start | bytes 208904 | tf_op jit(solution)/shard_map/ppermute | solution.py:28
  27.0 6.9 %collective-permute-start.4 = (f32[2,4,16,136]{3,2,1,0:T(8,128)S(1)}, f32[2,4,16,136]{3,2,1,0:T(8,128)S(1)}, u32[]{:S(2)}, u32[]{:S(2)}) collective-permute-start(f32[2,4,16,136]{3,2,1,0:T(8,128)S(1)} %get-tuple-element.61), channel_id=1, source_target_pairs={{0,1},{1,2},{2,3},{4,5},{5,6},{6,7},{8,9},{9,10},{10,11},{12,13},{... | collective-permute-start | bytes 208904 | tf_op jit(solution)/shard_map/ppermute | solution.py:25
  32.0 0.6 %copy-start.10 = (f32[2048,3]{0,1:T(4,128)}, f32[2048,3]{0,1:T(4,128)S(1)}, u32[]{:S(2)}) copy-start(f32[2048,3]{0,1:T(4,128)S(1)} %all_to_all.10) | copy-start | bytes 73732
  32.6 0.7 %slice-start = ((f32[2048,3]{0,1:T(4,128)}), f32[2048,2]{0,1:T(2,128)S(1)}, s32[]{:S(2)}) async-start(f32[2048,3]{0,1:T(4,128)} %copy-done.10), calls=%async_computation.1 | async-start | bytes 32768 | tf_op jit(solution)/shard_map/slice | solution.py:177
  34.7 0.8 %copy-start.5 = (f32[8,8,128]{2,1,0:T(8,128)S(1)}, f32[8,8,128]{2,1,0:T(8,128)}, u32[]{:S(2)}) copy-start(f32[8,8,128]{2,1,0:T(8,128)} %param.29) | copy-start | bytes 98308
  34.7 0.8 %copy-start.6 = (f32[8,8,128]{2,1,0:T(8,128)S(1)}, f32[8,8,128]{2,1,0:T(8,128)}, u32[]{:S(2)}) copy-start(f32[8,8,128]{2,1,0:T(8,128)} %param.34) | copy-start | bytes 98308
  34.8 0.8 %copy-start.7 = (f32[8,8,128]{2,1,0:T(8,128)S(1)}, f32[8,8,128]{2,1,0:T(8,128)}, u32[]{:S(2)}) copy-start(f32[8,8,128]{2,1,0:T(8,128)} %param.35) | copy-start | bytes 98308
  34.8 0.8 %copy-start.8 = (f32[8,8,128]{2,1,0:T(8,128)S(1)}, f32[8,8,128]{2,1,0:T(8,128)}, u32[]{:S(2)}) copy-start(f32[8,8,128]{2,1,0:T(8,128)} %param.31) | copy-start | bytes 98308
  34.8 0.8 %copy-start.9 = (f32[8,8,128]{2,1,0:T(8,128)S(1)}, f32[8,8,128]{2,1,0:T(8,128)}, u32[]{:S(2)}) copy-start(f32[8,8,128]{2,1,0:T(8,128)} %param.30) | copy-start | bytes 98308
  34.8 0.8 %copy-start.15 = (f32[8,8,128]{2,1,0:T(8,128)S(1)}, f32[8,8,128]{2,1,0:T(8,128)}, u32[]{:S(2)}) copy-start(f32[8,8,128]{2,1,0:T(8,128)} %param.28) | copy-start | bytes 98308
  34.8 0.8 %copy-start.16 = (f32[8,8,128]{2,1,0:T(8,128)S(1)}, f32[8,8,128]{2,1,0:T(8,128)}, u32[]{:S(2)}) copy-start(f32[8,8,128]{2,1,0:T(8,128)} %param.26) | copy-start | bytes 98308
  35.7 23.5 %copy-start.1 = (f32[8,8,128]{2,1,0:T(8,128)}, f32[8,8,128]{2,1,0:T(8,128)S(1)}, u32[]{:S(2)}) copy-start(f32[8,8,128]{2,1,0:T(8,128)S(1)} %get-tuple-element.94) | copy-start | bytes 98308
  35.7 23.5 %copy-start.2 = (f32[8,8,128]{2,1,0:T(8,128)}, f32[8,8,128]{2,1,0:T(8,128)S(1)}, u32[]{:S(2)}) copy-start(f32[8,8,128]{2,1,0:T(8,128)S(1)} %get-tuple-element.95) | copy-start | bytes 98308
  35.7 4.3 %collective-permute-start.5 = (f32[2,8,4,128]{3,2,1,0:T(4,128)S(1)}, f32[2,8,4,128]{3,2,1,0:T(4,128)S(1)}, u32[]{:S(2)}, u32[]{:S(2)}) collective-permute-start(f32[2,8,4,128]{3,2,1,0:T(4,128)S(1)} %get-tuple-element.77), channel_id=1, source_target_pairs={{8,0},{16,8},{24,16},{9,1},{17,9},{25,17},{10,2},{18,10},{26,18},{... | collective-permute-start | bytes 98312 | tf_op jit(solution)/shard_map/ppermute | solution.py:28
  37.6 5.2 %collective-permute-start.6 = (f32[2,8,4,128]{3,2,1,0:T(4,128)S(1)}, f32[2,8,4,128]{3,2,1,0:T(4,128)S(1)}, u32[]{:S(2)}, u32[]{:S(2)}) collective-permute-start(f32[2,8,4,128]{3,2,1,0:T(4,128)S(1)} %get-tuple-element.76), channel_id=1, source_target_pairs={{0,8},{8,16},{16,24},{1,9},{9,17},{17,25},{2,10},{10,18},{18,26},{... | collective-permute-start | bytes 98312 | tf_op jit(solution)/shard_map/ppermute | solution.py:25
  43.0 5.0 %collective-permute-start.7 = (f32[2,8,16,4]{3,2,1,0:T(8,128)S(1)}, f32[2,8,16,4]{3,2,1,0:T(8,128)S(1)}, u32[]{:S(2)}, u32[]{:S(2)}) collective-permute-start(f32[2,8,16,4]{3,2,1,0:T(8,128)S(1)} %slice_select_fusion), channel_id=1, source_target_pairs={{0,4},{4,0},{1,5},{5,1},{2,6},{6,2},{3,7},{7,3},{8,12},{12,8},{9,1... | collective-permute-start | bytes 12296 | tf_op jit(solution)/shard_map/ppermute | solution.py:17
  48.3 6.9 %collective-permute-start.8 = (f32[2,4,16,136]{3,2,1,0:T(8,128)S(1)}, f32[2,4,16,136]{3,2,1,0:T(8,128)S(1)}, u32[]{:S(2)}, u32[]{:S(2)}) collective-permute-start(f32[2,4,16,136]{3,2,1,0:T(8,128)S(1)} %get-tuple-element.58), channel_id=1, source_target_pairs={{1,0},{2,1},{3,2},{5,4},{6,5},{7,6},{9,8},{10,9},{11,10},{13,12},{... | collective-permute-start | bytes 208904 | tf_op jit(solution)/shard_map/ppermute | solution.py:28
  50.9 6.9 %collective-permute-start.9 = (f32[2,4,16,136]{3,2,1,0:T(8,128)S(1)}, f32[2,4,16,136]{3,2,1,0:T(8,128)S(1)}, u32[]{:S(2)}, u32[]{:S(2)}) collective-permute-start(f32[2,4,16,136]{3,2,1,0:T(8,128)S(1)} %get-tuple-element.59), channel_id=1, source_target_pairs={{0,1},{1,2},{2,3},{4,5},{5,6},{6,7},{8,9},{9,10},{10,11},{12,13},{... | collective-permute-start | bytes 208904 | tf_op jit(solution)/shard_map/ppermute | solution.py:25
  59.2 0.6 %copy-start.11 = (f32[8,8,128]{2,1,0:T(8,128)}, f32[8,8,128]{2,1,0:T(8,128)S(1)}, u32[]{:S(2)}) copy-start(f32[8,8,128]{2,1,0:T(8,128)S(1)} %get-tuple-element.92) | copy-start | bytes 98308
  59.2 0.6 %copy-start.12 = (f32[8,8,128]{2,1,0:T(8,128)}, f32[8,8,128]{2,1,0:T(8,128)S(1)}, u32[]{:S(2)}) copy-start(f32[8,8,128]{2,1,0:T(8,128)S(1)} %get-tuple-element.93) | copy-start | bytes 98308

commit v6 on v5

--- a/solution.py
+++ b/solution.py
@@ -157,25 +157,43 @@
     gz_count = lax.axis_size("gz")
     columns = lax.axis_size("inl") * xl_count
     capacity = 2 * trace_samples.shape[0] // columns
+    devices = columns * gz_count
     owner = receiver_inline // inline_cells * xl_count + receiver_crossline // cross_cells
     local_cell = receiver_inline % inline_cells * cross_cells + receiver_crossline % cross_cells
     payload = step_amplitudes(trace_samples, resample_filter, line_gain, shot_line)
-    onehot = (owner[:, None] == jnp.arange(columns, dtype=jnp.int32)[None, :]).astype(jnp.int32)
-    rank = jnp.sum(jnp.cumsum(onehot, axis=0) * onehot, axis=1) - 1
-    slot = owner * (gz_count * capacity) + rank
-    packed = jnp.concatenate([payload, local_cell.astype(jnp.float32)[:, None]], axis=1)
-    width = packed.shape[1]
-    send = jnp.zeros((columns * gz_count * capacity, width), jnp.float32).at[slot].set(packed)
+    traces = owner.shape[0]
+    highest = lax.Precision.HIGHEST
+    in_column = (owner[:, None] == jnp.arange(columns, dtype=jnp.int32)[None, :]).astype(jnp.float32)
+    order = jnp.arange(traces, dtype=jnp.int32)
+    earlier = (order[:, None] > order[None, :]).astype(jnp.float32)
+    rank = jnp.sum(jnp.dot(earlier, in_column, precision=highest) * in_column, axis=1)
+    lane = jnp.arange(3 * capacity, dtype=jnp.int32)[None, :]
+    value = jnp.where(
+        lane < capacity,
+        payload[:, 0:1],
+        jnp.where(lane < 2 * capacity, payload[:, 1:2], local_cell.astype(jnp.float32)[:, None]),
+    )
+    spread = jnp.where(rank.astype(jnp.int32)[:, None] == lane % capacity, value, 0.0)
+    to_device = (
+        (owner * gz_count)[:, None] == jnp.arange(devices, dtype=jnp.int32)[None, :]
+    ).astype(jnp.float32)
+    send = lax.dot_general(to_device, spread, (((0,), (0,)), ((), ())), precision=highest)
     arrived = lax.all_to_all(send, ("inl", "xl", "gz"), split_axis=0, concat_axis=0, tiled=True)
-    target = arrived[:, steps].astype(jnp.int32)
+    amp = arrived[:, : steps * capacity].reshape(devices, steps, capacity)
+    cell = (arrived[:, steps * capacity :] + 0.5).astype(jnp.int32)
     row_hit = (
-        target[:, None] // cross_cells == jnp.arange(inline_cells, dtype=jnp.int32)[None, :]
+        cell[None, :, :] // cross_cells
+        == jnp.arange(inline_cells, dtype=jnp.int32)[:, None, None]
     ).astype(jnp.float32)
     col_hit = (
-        target[:, None] % cross_cells == jnp.arange(cross_cells, dtype=jnp.int32)[None, :]
+        cell[None, :, :] % cross_cells == jnp.arange(cross_cells, dtype=jnp.int32)[:, None, None]
     ).astype(jnp.float32)
-    weighted = arrived[:, :steps, None] * row_hit[:, None, :]
-    planes = jnp.einsum("nkx,ny->kxy", weighted, col_hit, precision=lax.Precision.HIGHEST)
+    weighted = (jnp.transpose(amp, (1, 0, 2))[:, None] * row_hit[None]).reshape(
+        steps * inline_cells, devices, capacity
+    )
+    planes = lax.dot_general(
+        weighted, col_hit, (((1, 2), (1, 2)), ((), ())), precision=highest
+    ).reshape(steps, inline_cells, cross_cells)
     fields = (courant_square, thomsen_epsilon, thomsen_delta, shear_ratio, damping)
     current = jnp.stack([wave_p, wave_q])
     previous = jnp.stack([wave_p_old, wave_q_old])

time: 60.5 us -> 58.7 us (0.970)
  the two profiles are of different devices: /device:TPU:12 before, /device:TPU:17 now
where the time goes in v6:
time: 58.7 us; the launch traced here: 58.1 us
  starting transfers between devices  29.8 us (51%)
  waiting for transfers between devices  17.9 us (30%)
  other arithmetic  4.24 us (7%)
  local copies, waits for them, and re-layouts  3.45 us (6%)
  matrix products  1.53 us (3%)
  between operations  1.21 us (2%)
    ppermute x4, starting transfers between devices, with_halo(): lax.ppermute(lax.slice_in_dim(block, block.shape[dim] - width, None, axis...  12.8 us
    ppermute x4, waiting for transfers between devices, with_halo(): lax.ppermute(lax.slice_in_dim(block, 0, width, axis=dim), axis, backward)  8.24 us
    ppermute x4, starting transfers between devices, with_halo(): lax.ppermute(lax.slice_in_dim(block, 0, width, axis=dim), axis, backward)  8.2 us
    all_to_all x1, starting transfers between devices, local(): lax.all_to_all(send, ('inl', 'xl', 'gz'), split_axis=0, concat_axis=0, ti...  6.25 us
    ppermute x2, waiting for transfers between devices, with_halo(): got = lax.ppermute(jnp.where(first, top, bottom), axis, [(0, 1), (1, 0)])  5.2 us
    ppermute x4, waiting for transfers between devices, with_halo(): lax.ppermute(lax.slice_in_dim(block, block.shape[dim] - width, None, axis...  4.47 us
    ppermute x2, starting transfers between devices, with_halo(): got = lax.ppermute(jnp.where(first, top, bottom), axis, [(0, 1), (1, 0)])  2.51 us
    unnamed x43, local copies, waits for them, and re-layouts  2.42 us
  transfers between devices with their start and end apart: 11, of which 8 were waited for; matrix products, arithmetic and copies ran while one was open for 3% of the time, Pallas kernels for 0%

profile of v6, /device:TPU:17, one launch (start us, length us, event | category | flops | bytes accessed | tf_op | source)
XLA Modules:
  0.0 58.1 jit_solution(11053678904056558856)
XLA Ops:
  0.6 0.0 copy-start
  0.7 0.7 %copy-done.19 = s32[256]{0:T(256)S(1)} copy-done((s32[256]{0:T(256)S(1)}, s32[256]{0:T(256)}, u32[]{:S(2)}) %copy-start.19) | copy-done | bytes 1048
  1.4 0.1 select_reduce_fusion
  1.5 0.2 copy-done
  1.6 0.3 convolution_multiply_fusion
  1.9 0.1 copy-start.18
  2.0 0.7 %copy-done.17 = s32[256]{0:T(256)S(1)} copy-done((s32[256]{0:T(256)S(1)}, s32[256]{0:T(256)}, u32[]{:S(2)}) %copy-start.17) | copy-done | bytes 1048
  2.6 0.0 copy-done.18
  2.7 0.2 fusion
  2.9 0.4 convolution_bitcast_fusion
  3.3 0.7 %copy.22 = f32[32,1,192]{2,1,0:T(1,128)} copy(f32[32,1,192]{2,0,1:T(8,128)S(1)} %convolution_bitcast_fusion) | data formatting | bytes 49152 | tf_op jit(solution)/shard_map/all_to_all | solution.py:181
  4.0 6.2 %all-to-all-start = ((f32[32,1,192]{2,1,0:T(1,128)}), f32[32,1,192]{2,1,0:T(1,128)S(1)}, u32[]{:S(2)}, u32[]{:S(2)}) async-start(f32[32,1,192]{2,1,0:T(1,128)} %copy.22), calls=%async_computation | async-start | bytes 65536 | tf_op jit(solution)/shard_map/all_to_all | solution.py:181
  10.3 0.0 copy-start.12
  10.3 3.4 %collective-permute-start.1 = (f32[2,8,4,128]{3,2,1,0:T(4,128)S(1)}, f32[2,8,4,128]{3,2,1,0:T(4,128)S(1)}, u32[]{:S(2)}, u32[]{:S(2)}) collective-permute-start(f32[2,8,4,128]{3,2,1,0:T(4,128)S(1)} %get-tuple-element.87), channel_id=1, source_target_pairs={{0,8},{8,16},{16,24},{1,9},{9,17},{17,25},{2,10},{10,18},{18,26},{... | collective-permute-start | bytes 98312 | tf_op jit(solution)/shard_map/ppermute | solution.py:25
  13.7 1.9 %collective-permute-start = (f32[2,8,4,128]{3,2,1,0:T(4,128)S(1)}, f32[2,8,4,128]{3,2,1,0:T(4,128)S(1)}, u32[]{:S(2)}, u32[]{:S(2)}) collective-permute-start(f32[2,8,4,128]{3,2,1,0:T(4,128)S(1)} %get-tuple-element.88), channel_id=1, source_target_pairs={{8,0},{16,8},{24,16},{9,1},{17,9},{25,17},{10,2},{18,10},{26,18},{... | collective-permute-start | bytes 98312 | tf_op jit(solution)/shard_map/ppermute | solution.py:28
  15.6 0.2 fusion.205
  15.9 3.0 %collective-permute-done = f32[2,8,4,128]{3,2,1,0:T(4,128)S(1)} collective-permute-done((f32[2,8,4,128]{3,2,1,0:T(4,128)S(1)}, f32[2,8,4,128]{3,2,1,0:T(4,128)S(1)}, u32[]{:S(2)}, u32[]{:S(2)}) %collective-permute-start) | collective-permute-done | bytes 32800 | tf_op jit(solution)/shard_map/ppermute | solution.py:28
  18.9 0.1 slice_select_fusion.1
  19.0 1.3 %collective-permute-start.2 = (f32[2,8,16,4]{3,2,1,0:T(8,128)S(1)}, f32[2,8,16,4]{3,2,1,0:T(8,128)S(1)}, u32[]{:S(2)}, u32[]{:S(2)}) collective-permute-start(f32[2,8,16,4]{3,2,1,0:T(8,128)S(1)} %slice_select_fusion.1), channel_id=1, source_target_pairs={{0,4},{4,0},{1,5},{5,1},{2,6},{6,2},{3,7},{7,3},{8,12},{12,8},{9,1... | collective-permute-start | bytes 12296 | tf_op jit(solution)/shard_map/ppermute | solution.py:17
  20.3 2.6 %collective-permute-done.2 = f32[2,8,16,4]{3,2,1,0:T(8,128)S(1)} collective-permute-done((f32[2,8,16,4]{3,2,1,0:T(8,128)S(1)}, f32[2,8,16,4]{3,2,1,0:T(8,128)S(1)}, u32[]{:S(2)}, u32[]{:S(2)}) %collective-permute-start.2) | collective-permute-done | bytes 4128 | tf_op jit(solution)/shard_map/ppermute | solution.py:17
  22.9 0.2 pad_maximum_fusion.3
  23.2 2.2 %collective-permute-start.3 = (f32[2,4,16,136]{3,2,1,0:T(8,128)S(1)}, f32[2,4,16,136]{3,2,1,0:T(8,128)S(1)}, u32[]{:S(2)}, u32[]{:S(2)}) collective-permute-start(f32[2,4,16,136]{3,2,1,0:T(8,128)S(1)} %get-tuple-element.62), channel_id=1, source_target_pairs={{1,0},{2,1},{3,2},{5,4},{6,5},{7,6},{9,8},{10,9},{11,10},{13,12},{... | collective-permute-start | bytes 208904 | tf_op jit(solution)/shard_map/ppermute | solution.py:28
  25.4 3.1 %collective-permute-start.4 = (f32[2,4,16,136]{3,2,1,0:T(8,128)S(1)}, f32[2,4,16,136]{3,2,1,0:T(8,128)S(1)}, u32[]{:S(2)}, u32[]{:S(2)}) collective-permute-start(f32[2,4,16,136]{3,2,1,0:T(8,128)S(1)} %get-tuple-element.63), channel_id=1, source_target_pairs={{0,1},{1,2},{2,3},{4,5},{5,6},{6,7},{8,9},{9,10},{10,11},{12,13},{... | collective-permute-start | bytes 208904 | tf_op jit(solution)/shard_map/ppermute | solution.py:25
  28.5 0.2 pad_maximum_fusion.2
  28.8 0.1 reshape.205
  28.9 0.6 %convolution_bitcast_fusion.1 = f32[16,128]{1,0:T(8,128)S(1)} fusion(s32[32,64]{1,0:T(8,128)S(1)} %add_select_fusion, f32[8,32,64]{2,0,1:T(8,128)S(1)} %fusion.44, f32[2,32,64]{2,0,1:T(2,128)S(1)} %bitcast.142), kind=kOutput, calls=%fused_computation.2 | convolution fusion | flops 50626560 | bytes 98304 | tf_op jit(solution)/shard_map/dot_general | solution.py:194
  29.5 0.6 collective-permute-done.3
  30.1 2.2 %collective-permute-done.4 = f32[2,4,16,136]{3,2,1,0:T(8,128)S(1)} collective-permute-done((f32[2,4,16,136]{3,2,1,0:T(8,128)S(1)}, f32[2,4,16,136]{3,2,1,0:T(8,128)S(1)}, u32[]{:S(2)}, u32[]{:S(2)}) %collective-permute-start.4) | collective-permute-done | bytes 69664 | tf_op jit(solution)/shard_map/ppermute | solution.py:25
  32.3 0.2 pad_maximum_fusion
  32.6 0.3 fusion.30
  32.9 0.2 fusion.10
  33.1 0.0 copy-start.7
  33.1 0.0 copy-start.8
  33.2 0.0 copy-start.15
  33.2 0.6 %add_subtract_fusion.1 = (f32[2,8,8,128]{3,2,1,0:T(8,128)S(1)}, f32[2,8,8,128]{3,2,1,0:T(8,128)S(1)}) fusion(f32[2,16,8,128]{3,2,1,0:T(8,128)S(1)} %fusion.30, f32[8,8,128]{2,1,0:T(8,128)S(1)} %get-tuple-element.82, f32[2,16,8,136]{3,2,1,0:T(8,128)S(1)} %fusion.10, f32[8,8,128]{2,1,0:T(8,128)S(1)} %get-tuple-element.83, ...), kind=kLoop, calls=%fused_computation.277 | loop fusion | flops 2179072 | bytes 3227648 | tf_op jit(solution)/shard_map/sub | solution.py:105
  33.8 0.1 copy-done.5
  33.9 0.0 copy-done.6
  33.9 0.0 copy-done.7
  33.9 0.0 copy-done.8
  33.9 0.0 copy-done.9
  33.9 0.0 copy-done.14
  34.0 0.0 copy-done.15
  34.0 0.0 copy-start.1
  34.0 0.0 copy-start.2
  34.1 3.3 %collective-permute-start.6 = (f32[2,8,4,128]{3,2,1,0:T(4,128)S(1)}, f32[2,8,4,128]{3,2,1,0:T(4,128)S(1)}, u32[]{:S(2)}, u32[]{:S(2)}) collective-permute-start(f32[2,8,4,128]{3,2,1,0:T(4,128)S(1)} %get-tuple-element.78), channel_id=1, source_target_pairs={{0,8},{8,16},{16,24},{1,9},{9,17},{17,25},{2,10},{10,18},{18,26},{... | collective-permute-start | bytes 98312 | tf_op jit(solution)/shard_map/ppermute | solution.py:25
  37.3 1.9 %collective-permute-start.5 = (f32[2,8,4,128]{3,2,1,0:T(4,128)S(1)}, f32[2,8,4,128]{3,2,1,0:T(4,128)S(1)}, u32[]{:S(2)}, u32[]{:S(2)}) collective-permute-start(f32[2,8,4,128]{3,2,1,0:T(4,128)S(1)} %get-tuple-element.79), channel_id=1, source_target_pairs={{8,0},{16,8},{24,16},{9,1},{17,9},{25,17},{10,2},{18,10},{26,18},{... | collective-permute-start | bytes 98312 | tf_op jit(solution)/shard_map/ppermute | solution.py:28
  39.3 3.3 %collective-permute-done.5 = f32[2,8,4,128]{3,2,1,0:T(4,128)S(1)} collective-permute-done((f32[2,8,4,128]{3,2,1,0:T(4,128)S(1)}, f32[2,8,4,128]{3,2,1,0:T(4,128)S(1)}, u32[]{:S(2)}, u32[]{:S(2)}) %collective-permute-start.5) | collective-permute-done | bytes 32800 | tf_op jit(solution)/shard_map/ppermute | solution.py:28
  42.6 0.1 slice_select_fusion
  42.7 1.2 %collective-permute-start.7 = (f32[2,8,16,4]{3,2,1,0:T(8,128)S(1)}, f32[2,8,16,4]{3,2,1,0:T(8,128)S(1)}, u32[]{:S(2)}, u32[]{:S(2)}) collective-permute-start(f32[2,8,16,4]{3,2,1,0:T(8,128)S(1)} %slice_select_fusion), channel_id=1, source_target_pairs={{0,4},{4,0},{1,5},{5,1},{2,6},{6,2},{3,7},{7,3},{8,12},{12,8},{9,1... | collective-permute-start | bytes 12296 | tf_op jit(solution)/shard_map/ppermute | solution.py:17
  44.0 2.6 %collective-permute-done.7 = f32[2,8,16,4]{3,2,1,0:T(8,128)S(1)} collective-permute-done((f32[2,8,16,4]{3,2,1,0:T(8,128)S(1)}, f32[2,8,16,4]{3,2,1,0:T(8,128)S(1)}, u32[]{:S(2)}, u32[]{:S(2)}) %collective-permute-start.7) | collective-permute-done | bytes 4128 | tf_op jit(solution)/shard_map/ppermute | solution.py:17
  46.6 0.2 pad_maximum_fusion.5
  46.9 2.2 %collective-permute-start.8 = (f32[2,4,16,136]{3,2,1,0:T(8,128)S(1)}, f32[2,4,16,136]{3,2,1,0:T(8,128)S(1)}, u32[]{:S(2)}, u32[]{:S(2)}) collective-permute-start(f32[2,4,16,136]{3,2,1,0:T(8,128)S(1)} %get-tuple-element.60), channel_id=1, source_target_pairs={{1,0},{2,1},{3,2},{5,4},{6,5},{7,6},{9,8},{10,9},{11,10},{13,12},{... | collective-permute-start | bytes 208904 | tf_op jit(solution)/shard_map/ppermute | solution.py:28
  49.1 3.1 %collective-permute-start.9 = (f32[2,4,16,136]{3,2,1,0:T(8,128)S(1)}, f32[2,4,16,136]{3,2,1,0:T(8,128)S(1)}, u32[]{:S(2)}, u32[]{:S(2)}) collective-permute-start(f32[2,4,16,136]{3,2,1,0:T(8,128)S(1)} %get-tuple-element.61), channel_id=1, source_target_pairs={{0,1},{1,2},{2,3},{4,5},{5,6},{6,7},{8,9},{9,10},{10,11},{12,13},{... | collective-permute-start | bytes 208904 | tf_op jit(solution)/shard_map/ppermute | solution.py:25
  52.2 0.2 pad_maximum_fusion.4
  52.4 1.4 %collective-permute-done.8 = f32[2,4,16,136]{3,2,1,0:T(8,128)S(1)} collective-permute-done((f32[2,4,16,136]{3,2,1,0:T(8,128)S(1)}, f32[2,4,16,136]{3,2,1,0:T(8,128)S(1)}, u32[]{:S(2)}, u32[]{:S(2)}) %collective-permute-start.8) | collective-permute-done | bytes 69664 | tf_op jit(solution)/shard_map/ppermute | solution.py:28
  53.8 2.2 %collective-permute-done.9 = f32[2,4,16,136]{3,2,1,0:T(8,128)S(1)} collective-permute-done((f32[2,4,16,136]{3,2,1,0:T(8,128)S(1)}, f32[2,4,16,136]{3,2,1,0:T(8,128)S(1)}, u32[]{:S(2)}, u32[]{:S(2)}) %collective-permute-start.9) | collective-permute-done | bytes 69664 | tf_op jit(solution)/shard_map/ppermute | solution.py:25
  56.0 0.2 pad_maximum_fusion.1
  56.3 0.3 fusion.23
  56.6 0.2 fusion.3
  56.8 0.6 %add_subtract_fusion = (f32[2,8,8,128]{3,2,1,0:T(8,128)S(1)}, f32[2,8,8,128]{3,2,1,0:T(8,128)S(1)}) fusion(f32[2,16,8,128]{3,2,1,0:T(8,128)S(1)} %fusion.23, f32[8,8,128]{2,1,0:T(8,128)S(1)} %get-tuple-element.82, f32[2,16,8,136]{3,2,1,0:T(8,128)S(1)} %fusion.3, f32[8,8,128]{2,1,0:T(8,128)S(1)} %get-tuple-element.83, ...), kind=kLoop, calls=%fused_computation.273 | loop fusion | flops 2179072 | bytes 3227648 | tf_op jit(solution)/shard_map/sub | solution.py:105
  57.5 0.0 copy-start.10
  57.5 0.0 copy-start.11
  57.5 0.6 %copy-done.10 = f32[8,8,128]{2,1,0:T(8,128)} copy-done((f32[8,8,128]{2,1,0:T(8,128)}, f32[8,8,128]{2,1,0:T(8,128)S(1)}, u32[]{:S(2)}) %copy-start.10) | copy-done | bytes 32792
  58.1 0.0 copy-done.11
  (47 shorter events, 0.5 us)
Async XLA Ops:
  0.6 1.0 %copy-start = (f32[256,256]{1,0:T(8,128)S(1)}, f32[256,256]{1,0:T(8,128)}, u32[]{:S(2)}) copy-start(f32[256,256]{1,0:T(8,128)} %param.36) | copy-start | bytes 786436
  0.6 0.7 %copy-start.19 = (s32[256]{0:T(256)S(1)}, s32[256]{0:T(256)}, u32[]{:S(2)}) copy-start(s32[256]{0:T(256)} %param.41) | copy-start | bytes 3076
  0.7 0.7 %copy-start.20 = (f32[64]{0:T(128)S(1)}, f32[64]{0:T(128)}, u32[]{:S(2)}) copy-start(f32[64]{0:T(128)} %param.38) | copy-start | bytes 772
  0.7 0.9 %copy-start.16 = (f32[2,256]{1,0:T(2,128)S(1)}, f32[2,256]{1,0:T(2,128)}, u32[]{:S(2)}) copy-start(f32[2,256]{1,0:T(2,128)} %param.37) | copy-start | bytes 6148
  1.9 0.7 %copy-start.17 = (s32[256]{0:T(256)S(1)}, s32[256]{0:T(256)}, u32[]{:S(2)}) copy-start(s32[256]{0:T(256)} %param.40) | copy-start | bytes 3076
  1.9 0.8 %copy-start.18 = (s32[256]{0:T(256)S(1)}, s32[256]{0:T(256)}, u32[]{:S(2)}) copy-start(s32[256]{0:T(256)} %param.39) | copy-start | bytes 3076
  4.0 6.3 %copy-start.3 = (f32[8,8,128]{2,1,0:T(8,128)S(1)}, f32[8,8,128]{2,1,0:T(8,128)}, u32[]{:S(2)}) copy-start(f32[8,8,128]{2,1,0:T(8,128)} %param.25) | copy-start | bytes 98308
  4.0 6.3 %copy-start.4 = (f32[8,8,128]{2,1,0:T(8,128)S(1)}, f32[8,8,128]{2,1,0:T(8,128)}, u32[]{:S(2)}) copy-start(f32[8,8,128]{2,1,0:T(8,128)} %param.27) | copy-start | bytes 98308
  4.0 24.8 %all-to-all-start = ((f32[32,1,192]{2,1,0:T(1,128)}), f32[32,1,192]{2,1,0:T(1,128)S(1)}, u32[]{:S(2)}, u32[]{:S(2)}) async-start(f32[32,1,192]{2,1,0:T(1,128)} %copy.22), calls=%async_computation | async-start | bytes 65536 | tf_op jit(solution)/shard_map/all_to_all | solution.py:181
  10.3 5.3 %copy-start.12 = (f32[8,8,128]{2,1,0:T(8,128)S(1)}, f32[8,8,128]{2,1,0:T(8,128)}, u32[]{:S(2)}) copy-start(f32[8,8,128]{2,1,0:T(8,128)} %param.33) | copy-start | bytes 98308
  10.3 5.3 %copy-start.13 = (f32[8,8,128]{2,1,0:T(8,128)S(1)}, f32[8,8,128]{2,1,0:T(8,128)}, u32[]{:S(2)}) copy-start(f32[8,8,128]{2,1,0:T(8,128)} %param.32) | copy-start | bytes 98308
  10.3 5.6 %collective-permute-start.1 = (f32[2,8,4,128]{3,2,1,0:T(4,128)S(1)}, f32[2,8,4,128]{3,2,1,0:T(4,128)S(1)}, u32[]{:S(2)}, u32[]{:S(2)}) collective-permute-start(f32[2,8,4,128]{3,2,1,0:T(4,128)S(1)} %get-tuple-element.87), channel_id=1, source_target_pairs={{0,8},{8,16},{16,24},{1,9},{9,17},{17,25},{2,10},{10,18},{18,26},{... | collective-permute-start | bytes 98312 | tf_op jit(solution)/shard_map/ppermute | solution.py:25
  13.7 5.2 %collective-permute-start = (f32[2,8,4,128]{3,2,1,0:T(4,128)S(1)}, f32[2,8,4,128]{3,2,1,0:T(4,128)S(1)}, u32[]{:S(2)}, u32[]{:S(2)}) collective-permute-start(f32[2,8,4,128]{3,2,1,0:T(4,128)S(1)} %get-tuple-element.88), channel_id=1, source_target_pairs={{8,0},{16,8},{24,16},{9,1},{17,9},{25,17},{10,2},{18,10},{26,18},{... | collective-permute-start | bytes 98312 | tf_op jit(solution)/shard_map/ppermute | solution.py:28
  19.0 3.9 %collective-permute-start.2 = (f32[2,8,16,4]{3,2,1,0:T(8,128)S(1)}, f32[2,8,16,4]{3,2,1,0:T(8,128)S(1)}, u32[]{:S(2)}, u32[]{:S(2)}) collective-permute-start(f32[2,8,16,4]{3,2,1,0:T(8,128)S(1)} %slice_select_fusion.1), channel_id=1, source_target_pairs={{0,4},{4,0},{1,5},{5,1},{2,6},{6,2},{3,7},{7,3},{8,12},{12,8},{9,1... | collective-permute-start | bytes 12296 | tf_op jit(solution)/shard_map/ppermute | solution.py:17
  23.2 6.9 %collective-permute-start.3 = (f32[2,4,16,136]{3,2,1,0:T(8,128)S(1)}, f32[2,4,16,136]{3,2,1,0:T(8,128)S(1)}, u32[]{:S(2)}, u32[]{:S(2)}) collective-permute-start(f32[2,4,16,136]{3,2,1,0:T(8,128)S(1)} %get-tuple-element.62), channel_id=1, source_target_pairs={{1,0},{2,1},{3,2},{5,4},{6,5},{7,6},{9,8},{10,9},{11,10},{13,12},{... | collective-permute-start | bytes 208904 | tf_op jit(solution)/shard_map/ppermute | solution.py:28
  25.4 6.9 %collective-permute-start.4 = (f32[2,4,16,136]{3,2,1,0:T(8,128)S(1)}, f32[2,4,16,136]{3,2,1,0:T(8,128)S(1)}, u32[]{:S(2)}, u32[]{:S(2)}) collective-permute-start(f32[2,4,16,136]{3,2,1,0:T(8,128)S(1)} %get-tuple-element.63), channel_id=1, source_target_pairs={{0,1},{1,2},{2,3},{4,5},{5,6},{6,7},{8,9},{9,10},{10,11},{12,13},{... | collective-permute-start | bytes 208904 | tf_op jit(solution)/shard_map/ppermute | solution.py:25
  33.1 0.8 %copy-start.5 = (f32[8,8,128]{2,1,0:T(8,128)S(1)}, f32[8,8,128]{2,1,0:T(8,128)}, u32[]{:S(2)}) copy-start(f32[8,8,128]{2,1,0:T(8,128)} %param.29) | copy-start | bytes 98308
  33.1 0.8 %copy-start.6 = (f32[8,8,128]{2,1,0:T(8,128)S(1)}, f32[8,8,128]{2,1,0:T(8,128)}, u32[]{:S(2)}) copy-start(f32[8,8,128]{2,1,0:T(8,128)} %param.34) | copy-start | bytes 98308
  33.1 0.8 %copy-start.7 = (f32[8,8,128]{2,1,0:T(8,128)S(1)}, f32[8,8,128]{2,1,0:T(8,128)}, u32[]{:S(2)}) copy-start(f32[8,8,128]{2,1,0:T(8,128)} %param.35) | copy-start | bytes 98308
  33.1 0.8 %copy-start.8 = (f32[8,8,128]{2,1,0:T(8,128)S(1)}, f32[8,8,128]{2,1,0:T(8,128)}, u32[]{:S(2)}) copy-start(f32[8,8,128]{2,1,0:T(8,128)} %param.31) | copy-start | bytes 98308
  33.1 0.8 %copy-start.9 = (f32[8,8,128]{2,1,0:T(8,128)S(1)}, f32[8,8,128]{2,1,0:T(8,128)}, u32[]{:S(2)}) copy-start(f32[8,8,128]{2,1,0:T(8,128)} %param.30) | copy-start | bytes 98308
  33.2 0.8 %copy-start.14 = (f32[8,8,128]{2,1,0:T(8,128)S(1)}, f32[8,8,128]{2,1,0:T(8,128)}, u32[]{:S(2)}) copy-start(f32[8,8,128]{2,1,0:T(8,128)} %param.28) | copy-start | bytes 98308
  33.2 0.8 %copy-start.15 = (f32[8,8,128]{2,1,0:T(8,128)S(1)}, f32[8,8,128]{2,1,0:T(8,128)}, u32[]{:S(2)}) copy-start(f32[8,8,128]{2,1,0:T(8,128)} %param.26) | copy-start | bytes 98308
  34.0 23.4 %copy-start.1 = (f32[8,8,128]{2,1,0:T(8,128)}, f32[8,8,128]{2,1,0:T(8,128)S(1)}, u32[]{:S(2)}) copy-start(f32[8,8,128]{2,1,0:T(8,128)S(1)} %get-tuple-element.96) | copy-start | bytes 98308
  34.0 23.4 %copy-start.2 = (f32[8,8,128]{2,1,0:T(8,128)}, f32[8,8,128]{2,1,0:T(8,128)S(1)}, u32[]{:S(2)}) copy-start(f32[8,8,128]{2,1,0:T(8,128)S(1)} %get-tuple-element.97) | copy-start | bytes 98308
  34.1 5.2 %collective-permute-start.6 = (f32[2,8,4,128]{3,2,1,0:T(4,128)S(1)}, f32[2,8,4,128]{3,2,1,0:T(4,128)S(1)}, u32[]{:S(2)}, u32[]{:S(2)}) collective-permute-start(f32[2,8,4,128]{3,2,1,0:T(4,128)S(1)} %get-tuple-element.78), channel_id=1, source_target_pairs={{0,8},{8,16},{16,24},{1,9},{9,17},{17,25},{2,10},{10,18},{18,26},{... | collective-permute-start | bytes 98312 | tf_op jit(solution)/shard_map/ppermute | solution.py:25
  37.3 5.2 %collective-permute-start.5 = (f32[2,8,4,128]{3,2,1,0:T(4,128)S(1)}, f32[2,8,4,128]{3,2,1,0:T(4,128)S(1)}, u32[]{:S(2)}, u32[]{:S(2)}) collective-permute-start(f32[2,8,4,128]{3,2,1,0:T(4,128)S(1)} %get-tuple-element.79), channel_id=1, source_target_pairs={{8,0},{16,8},{24,16},{9,1},{17,9},{25,17},{10,2},{18,10},{26,18},{... | collective-permute-start | bytes 98312 | tf_op jit(solution)/shard_map/ppermute | solution.py:28
  42.7 3.9 %collective-permute-start.7 = (f32[2,8,16,4]{3,2,1,0:T(8,128)S(1)}, f32[2,8,16,4]{3,2,1,0:T(8,128)S(1)}, u32[]{:S(2)}, u32[]{:S(2)}) collective-permute-start(f32[2,8,16,4]{3,2,1,0:T(8,128)S(1)} %slice_select_fusion), channel_id=1, source_target_pairs={{0,4},{4,0},{1,5},{5,1},{2,6},{6,2},{3,7},{7,3},{8,12},{12,8},{9,1... | collective-permute-start | bytes 12296 | tf_op jit(solution)/shard_map/ppermute | solution.py:17
  46.9 6.9 %collective-permute-start.8 = (f32[2,4,16,136]{3,2,1,0:T(8,128)S(1)}, f32[2,4,16,136]{3,2,1,0:T(8,128)S(1)}, u32[]{:S(2)}, u32[]{:S(2)}) collective-permute-start(f32[2,4,16,136]{3,2,1,0:T(8,128)S(1)} %get-tuple-element.60), channel_id=1, source_target_pairs={{1,0},{2,1},{3,2},{5,4},{6,5},{7,6},{9,8},{10,9},{11,10},{13,12},{... | collective-permute-start | bytes 208904 | tf_op jit(solution)/shard_map/ppermute | solution.py:28
  49.1 6.9 %collective-permute-start.9 = (f32[2,4,16,136]{3,2,1,0:T(8,128)S(1)}, f32[2,4,16,136]{3,2,1,0:T(8,128)S(1)}, u32[]{:S(2)}, u32[]{:S(2)}) collective-permute-start(f32[2,4,16,136]{3,2,1,0:T(8,128)S(1)} %get-tuple-element.61), channel_id=1, source_target_pairs={{0,1},{1,2},{2,3},{4,5},{5,6},{6,7},{8,9},{9,10},{10,11},{12,13},{... | collective-permute-start | bytes 208904 | tf_op jit(solution)/shard_map/ppermute | solution.py:25
  57.5 0.6 %copy-start.10 = (f32[8,8,128]{2,1,0:T(8,128)}, f32[8,8,128]{2,1,0:T(8,128)S(1)}, u32[]{:S(2)}) copy-start(f32[8,8,128]{2,1,0:T(8,128)S(1)} %get-tuple-element.94) | copy-start | bytes 98308
  57.5 0.6 %copy-start.11 = (f32[8,8,128]{2,1,0:T(8,128)}, f32[8,8,128]{2,1,0:T(8,128)S(1)}, u32[]{:S(2)}) copy-start(f32[8,8,128]{2,1,0:T(8,128)S(1)} %get-tuple-element.95) | copy-start | bytes 98308

commit v7 on v6

--- a/solution.py
+++ b/solution.py
@@ -7,27 +7,33 @@
 first_coef = (0.0, 4.0 / 5.0, -1.0 / 5.0, 4.0 / 105.0, -1.0 / 280.0)
 
 
-def with_halo(block, sides, width):
-    for axis, dim in sides:
-        count = lax.axis_size(axis)
-        if count == 2:
-            first = lax.axis_index(axis) == 0
-            top = lax.slice_in_dim(block, block.shape[dim] - width, None, axis=dim)
-            bottom = lax.slice_in_dim(block, 0, width, axis=dim)
-            got = lax.ppermute(jnp.where(first, top, bottom), axis, [(0, 1), (1, 0)])
-            empty = jnp.zeros_like(got)
-            low = jnp.where(first, empty, got)
-            high = jnp.where(first, got, empty)
-            block = jnp.concatenate([low, block, high], axis=dim)
-            continue
-        forward = [(i, i + 1) for i in range(count - 1)]
-        backward = [(target, source) for source, target in forward]
-        low = lax.ppermute(
-            lax.slice_in_dim(block, block.shape[dim] - width, None, axis=dim), axis, forward
-        )
-        high = lax.ppermute(lax.slice_in_dim(block, 0, width, axis=dim), axis, backward)
-        block = jnp.concatenate([low, block, high], axis=dim)
-    return block
+def shift_pair(top, bottom, axis):
+    count = lax.axis_size(axis)
+    if count == 2:
+        first = lax.axis_index(axis) == 0
+        got = lax.ppermute(jnp.where(first, top, bottom), axis, [(0, 1), (1, 0)])
+        empty = jnp.zeros_like(got)
+        return jnp.where(first, empty, got), jnp.where(first, got, empty)
+    forward = [(i, i + 1) for i in range(count - 1)]
+    backward = [(target, source) for source, target in forward]
+    return lax.ppermute(top, axis, forward), lax.ppermute(bottom, axis, backward)
+
+
+def with_halo(block, width):
+    cut = lambda a, dim, lo, hi: lax.slice_in_dim(a, lo, hi, axis=dim)
+    depth, across, along = block.shape[1:]
+    low_x, high_x = shift_pair(cut(block, 2, across - width, None), cut(block, 2, 0, width), "inl")
+    low_y, high_y = shift_pair(cut(block, 3, along - width, None), cut(block, 3, 0, width), "xl")
+    strips = jnp.concatenate([low_x, high_x], axis=2)
+    low_c, high_c = shift_pair(cut(strips, 3, along - width, None), cut(strips, 3, 0, width), "xl")
+    wide_x = jnp.concatenate([low_x, block, high_x], axis=2)
+    pad_x = ((0, 0), (0, 0), (width, width), (0, 0))
+    bare = jnp.concatenate([jnp.pad(low_y, pad_x), wide_x, jnp.pad(high_y, pad_x)], axis=3)
+    low_z, high_z = shift_pair(cut(bare, 1, depth - width, None), cut(bare, 1, 0, width), "gz")
+    side_low = jnp.concatenate([low_c[:, :, :width], low_y, low_c[:, :, width:]], axis=2)
+    side_high = jnp.concatenate([high_c[:, :, :width], high_y, high_c[:, :, width:]], axis=2)
+    full = jnp.concatenate([side_low, wide_x, side_high], axis=3)
+    return jnp.concatenate([low_z, full, high_z], axis=1)
 
 
 def derivatives(padded):
@@ -199,7 +205,7 @@
     previous = jnp.stack([wave_p_old, wave_q_old])
     coefs = anisotropy(tilt_angle, azimuth)
     for step in range(steps):
-        padded = with_halo(current, (("inl", 2), ("xl", 3), ("gz", 1)), 4)
+        padded = with_halo(current, 4)
         newer = advance(padded, current, previous, fields, coefs, planes[step], 0)
         previous = current
         current = newer

time: 58.7 us -> 55.2 us (0.940)
  waiting for transfers between devices: 17.9 us -> 10.1 us
  starting transfers between devices: 29.8 us -> 33.8 us
    ppermute x10 -> x12, waiting for transfers between devices: 17.9 us -> 10.1 us  [the longest x4 4.35 us: shift_pair(): lax.ppermute(bottom, axis, backward)]
    ppermute x10 -> x12, starting transfers between devices: 23.5 us -> 27.5 us  [the longest x4 15.2 us: shift_pair(): lax.ppermute(top, axis, forward)]
    concatenate x10 -> x8, other arithmetic: 1.46 us -> 1.48 us  [the longest x2 0.54 us: with_halo(): return jnp.concatenate([low_z, full, high_z], axis=1)]
  transfers between devices with their start and end apart: 11 -> 13, of which waited for: 8 -> 6; matrix products, arithmetic and copies ran while one was open for 3% -> 4% of each run, Pallas kernels for 0% -> 0%
where the time goes in v7:
time: 55.2 us; the launch traced here: 54.7 us
  starting transfers between devices  33.8 us (61%)
  waiting for transfers between devices  10.1 us (18%)
  other arithmetic  4.59 us (8%)
  local copies, waits for them, and re-layouts  3.37 us (6%)
  matrix products  1.53 us (3%)
  between operations  1.29 us (2%)
    ppermute x4, starting transfers between devices, shift_pair(): lax.ppermute(top, axis, forward)  15.2 us
    ppermute x4, starting transfers between devices, shift_pair(): lax.ppermute(bottom, axis, backward)  8.19 us
    all_to_all x1, starting transfers between devices, local(): lax.all_to_all(send, ('inl', 'xl', 'gz'), split_axis=0, concat_axis=0, ti...  6.25 us
    ppermute x4, waiting for transfers between devices, shift_pair(): lax.ppermute(bottom, axis, backward)  4.35 us
    ppermute x4, starting transfers between devices, shift_pair(): got = lax.ppermute(jnp.where(first, top, bottom), axis, [(0, 1), (1, 0)])  4.13 us
    ppermute x4, waiting for transfers between devices, shift_pair(): lax.ppermute(top, axis, forward)  4.1 us
    unnamed x43, local copies, waits for them, and re-layouts  2.3 us
    ppermute x4, waiting for transfers between devices, shift_pair(): got = lax.ppermute(jnp.where(first, top, bottom), axis, [(0, 1), (1, 0)])  1.65 us
  transfers between devices with their start and end apart: 13, of which 6 were waited for; matrix products, arithmetic and copies ran while one was open for 4% of the time, Pallas kernels for 0%

profile of v7, /device:TPU:17, one launch (start us, length us, event | category | flops | bytes accessed | tf_op | source)
XLA Modules:
  0.0 54.7 jit_solution(11582283497131284543)
XLA Ops:
  0.6 0.0 copy-start
  0.7 0.0 copy-start.16
  0.7 0.7 %copy-done.19 = s32[256]{0:T(256)S(1)} copy-done((s32[256]{0:T(256)S(1)}, s32[256]{0:T(256)}, u32[]{:S(2)}) %copy-start.19) | copy-done | bytes 1048
  1.4 0.1 select_reduce_fusion
  1.5 0.2 copy-done
  1.6 0.3 convolution_multiply_fusion
  1.9 0.1 copy-start.18
  2.0 0.7 %copy-done.17 = s32[256]{0:T(256)S(1)} copy-done((s32[256]{0:T(256)S(1)}, s32[256]{0:T(256)}, u32[]{:S(2)}) %copy-start.17) | copy-done | bytes 1048
  2.6 0.0 copy-done.18
  2.7 0.2 fusion
  2.9 0.4 convolution_bitcast_fusion
  3.3 0.7 %copy.42 = f32[32,1,192]{2,1,0:T(1,128)} copy(f32[32,1,192]{2,0,1:T(8,128)S(1)} %convolution_bitcast_fusion) | data formatting | bytes 49152 | tf_op jit(solution)/shard_map/all_to_all | solution.py:187
  4.0 6.2 %all-to-all-start = ((f32[32,1,192]{2,1,0:T(1,128)}), f32[32,1,192]{2,1,0:T(1,128)S(1)}, u32[]{:S(2)}, u32[]{:S(2)}) async-start(f32[32,1,192]{2,1,0:T(1,128)} %copy.42), calls=%async_computation | async-start | bytes 65536 | tf_op jit(solution)/shard_map/all_to_all | solution.py:187
  10.3 3.4 %collective-permute-start.1 = (f32[2,8,4,128]{3,2,1,0:T(4,128)S(1)}, f32[2,8,4,128]{3,2,1,0:T(4,128)S(1)}, u32[]{:S(2)}, u32[]{:S(2)}) collective-permute-start(f32[2,8,4,128]{3,2,1,0:T(4,128)S(1)} %get-tuple-element.97), channel_id=1, source_target_pairs={{0,8},{8,16},{16,24},{1,9},{9,17},{17,25},{2,10},{10,18},{18,26},{... | collective-permute-start | bytes 98312 | tf_op jit(solution)/shard_map/ppermute | solution.py:19
  13.6 1.9 %collective-permute-start = (f32[2,8,4,128]{3,2,1,0:T(4,128)S(1)}, f32[2,8,4,128]{3,2,1,0:T(4,128)S(1)}, u32[]{:S(2)}, u32[]{:S(2)}) collective-permute-start(f32[2,8,4,128]{3,2,1,0:T(4,128)S(1)} %get-tuple-element.98), channel_id=1, source_target_pairs={{8,0},{16,8},{24,16},{9,1},{17,9},{25,17},{10,2},{18,10},{26,18},{... | collective-permute-start | bytes 98312 | tf_op jit(solution)/shard_map/ppermute | solution.py:19
  15.6 0.0 copy-start.12
  15.6 0.0 copy-start.13
  15.6 0.1 fusion.52
  15.7 1.3 %collective-permute-start.3 = (f32[2,8,8,4]{3,2,1,0:T(8,128)S(1)}, f32[2,8,8,4]{3,2,1,0:T(8,128)S(1)}, u32[]{:S(2)}, u32[]{:S(2)}) collective-permute-start(f32[2,8,8,4]{3,2,1,0:T(8,128)S(1)} %fusion.52), channel_id=1, source_target_pairs={{0,4},{4,0},{1,5},{5,1},{2,6},{6,2},{3,7},{7,3},{8,12},{12,8},{9,1... | collective-permute-start | bytes 6152 | tf_op jit(solution)/shard_map/ppermute | solution.py:14
  17.0 0.2 fusion.225
  17.2 1.6 %collective-permute-done.3 = f32[2,8,8,4]{3,2,1,0:T(8,128)S(1)} collective-permute-done((f32[2,8,8,4]{3,2,1,0:T(8,128)S(1)}, f32[2,8,8,4]{3,2,1,0:T(8,128)S(1)}, u32[]{:S(2)}, u32[]{:S(2)}) %collective-permute-start.3) | collective-permute-done | bytes 2080 | tf_op jit(solution)/shard_map/ppermute | solution.py:14
  18.9 0.1 fusion.160
  19.0 1.3 %collective-permute-start.2 = (f32[2,8,8,4]{3,2,1,0:T(8,128)S(1)}, f32[2,8,8,4]{3,2,1,0:T(8,128)S(1)}, u32[]{:S(2)}, u32[]{:S(2)}) collective-permute-start(f32[2,8,8,4]{3,2,1,0:T(8,128)S(1)} %fusion.160), channel_id=1, source_target_pairs={{0,4},{4,0},{1,5},{5,1},{2,6},{6,2},{3,7},{7,3},{8,12},{12,8},{9,1... | collective-permute-start | bytes 6152 | tf_op jit(solution)/shard_map/ppermute | solution.py:14
  20.3 0.2 select_maximum_fusion.2
  20.5 2.2 %collective-permute-start.4 = (f32[2,4,16,136]{3,2,1,0:T(8,128)S(1)}, f32[2,4,16,136]{3,2,1,0:T(8,128)S(1)}, u32[]{:S(2)}, u32[]{:S(2)}) collective-permute-start(f32[2,4,16,136]{3,2,1,0:T(8,128)S(1)} %get-tuple-element.62), channel_id=1, source_target_pairs={{1,0},{2,1},{3,2},{5,4},{6,5},{7,6},{9,8},{10,9},{11,10},{13,12},{... | collective-permute-start | bytes 208904 | tf_op jit(solution)/shard_map/ppermute | solution.py:19
  22.7 3.1 %collective-permute-start.5 = (f32[2,4,16,136]{3,2,1,0:T(8,128)S(1)}, f32[2,4,16,136]{3,2,1,0:T(8,128)S(1)}, u32[]{:S(2)}, u32[]{:S(2)}) collective-permute-start(f32[2,4,16,136]{3,2,1,0:T(8,128)S(1)} %get-tuple-element.63), channel_id=1, source_target_pairs={{0,1},{1,2},{2,3},{4,5},{5,6},{6,7},{8,9},{9,10},{10,11},{12,13},{... | collective-permute-start | bytes 208904 | tf_op jit(solution)/shard_map/ppermute | solution.py:19
  25.9 0.2 maximum_maximum_fusion
  26.2 0.1 reshape.205
  26.3 0.6 %convolution_bitcast_fusion.1 = f32[16,128]{1,0:T(8,128)S(1)} fusion(s32[32,64]{1,0:T(8,128)S(1)} %add_select_fusion, f32[8,32,64]{2,0,1:T(8,128)S(1)} %fusion.44, f32[2,32,64]{2,0,1:T(2,128)S(1)} %bitcast.142), kind=kOutput, calls=%fused_computation.2 | convolution fusion | flops 50626560 | bytes 98304 | tf_op jit(solution)/shard_map/dot_general | solution.py:200
  27.0 0.7 %collective-permute-done.4 = f32[2,4,16,136]{3,2,1,0:T(8,128)S(1)} collective-permute-done((f32[2,4,16,136]{3,2,1,0:T(8,128)S(1)}, f32[2,4,16,136]{3,2,1,0:T(8,128)S(1)}, u32[]{:S(2)}, u32[]{:S(2)}) %collective-permute-start.4) | collective-permute-done | bytes 69664 | tf_op jit(solution)/shard_map/ppermute | solution.py:19
  27.6 1.9 %collective-permute-done.5 = f32[2,4,16,136]{3,2,1,0:T(8,128)S(1)} collective-permute-done((f32[2,4,16,136]{3,2,1,0:T(8,128)S(1)}, f32[2,4,16,136]{3,2,1,0:T(8,128)S(1)}, u32[]{:S(2)}, u32[]{:S(2)}) %collective-permute-start.5) | collective-permute-done | bytes 69664 | tf_op jit(solution)/shard_map/ppermute | solution.py:19
  29.6 0.3 pad_maximum_fusion
  29.8 0.3 fusion.30
  30.1 0.2 fusion.10
  30.4 0.0 copy-start.5
  30.4 0.0 copy-start.6
  30.4 0.0 copy-start.8
  30.4 0.0 copy-start.9
  30.4 0.7 %add_subtract_fusion.1 = (f32[2,8,8,128]{3,2,1,0:T(8,128)S(1)}, f32[2,8,8,128]{3,2,1,0:T(8,128)S(1)}) fusion(f32[2,16,8,128]{3,2,1,0:T(8,128)S(1)} %fusion.30, f32[8,8,128]{2,1,0:T(8,128)S(1)} %get-tuple-element.86, f32[2,16,8,136]{3,2,1,0:T(8,128)S(1)} %fusion.10, f32[8,8,128]{2,1,0:T(8,128)S(1)} %get-tuple-element.87, ...), kind=kLoop, calls=%fused_computation.311 | loop fusion | flops 2703360 | bytes 3227648 | tf_op jit(solution)/shard_map/sub | solution.py:111
  31.2 0.0 copy-done.9
  31.2 0.0 copy-done.14
  31.2 0.0 copy-done.15
  31.3 0.0 copy-start.2
  31.3 0.1 fusion.48
  31.4 0.3 collective-permute-start.9
  31.8 5.6 %collective-permute-start.7 = (f32[2,8,4,128]{3,2,1,0:T(4,128)S(1)}, f32[2,8,4,128]{3,2,1,0:T(4,128)S(1)}, u32[]{:S(2)}, u32[]{:S(2)}) collective-permute-start(f32[2,8,4,128]{3,2,1,0:T(4,128)S(1)} %get-tuple-element.80), channel_id=1, source_target_pairs={{0,8},{8,16},{16,24},{1,9},{9,17},{17,25},{2,10},{10,18},{18,26},{... | collective-permute-start | bytes 98312 | tf_op jit(solution)/shard_map/ppermute | solution.py:19
  37.4 1.9 %collective-permute-start.6 = (f32[2,8,4,128]{3,2,1,0:T(4,128)S(1)}, f32[2,8,4,128]{3,2,1,0:T(4,128)S(1)}, u32[]{:S(2)}, u32[]{:S(2)}) collective-permute-start(f32[2,8,4,128]{3,2,1,0:T(4,128)S(1)} %get-tuple-element.81), channel_id=1, source_target_pairs={{8,0},{16,8},{24,16},{9,1},{17,9},{25,17},{10,2},{18,10},{26,18},{... | collective-permute-start | bytes 98312 | tf_op jit(solution)/shard_map/ppermute | solution.py:19
  39.4 3.3 %collective-permute-done.6 = f32[2,8,4,128]{3,2,1,0:T(4,128)S(1)} collective-permute-done((f32[2,8,4,128]{3,2,1,0:T(4,128)S(1)}, f32[2,8,4,128]{3,2,1,0:T(4,128)S(1)}, u32[]{:S(2)}, u32[]{:S(2)}) %collective-permute-start.6) | collective-permute-done | bytes 32800 | tf_op jit(solution)/shard_map/ppermute | solution.py:19
  42.6 0.1 fusion.103
  42.7 1.2 %collective-permute-start.8 = (f32[2,8,8,4]{3,2,1,0:T(8,128)S(1)}, f32[2,8,8,4]{3,2,1,0:T(8,128)S(1)}, u32[]{:S(2)}, u32[]{:S(2)}) collective-permute-start(f32[2,8,8,4]{3,2,1,0:T(8,128)S(1)} %fusion.103), channel_id=1, source_target_pairs={{0,4},{4,0},{1,5},{5,1},{2,6},{6,2},{3,7},{7,3},{8,12},{12,8},{9,1... | collective-permute-start | bytes 6152 | tf_op jit(solution)/shard_map/ppermute | solution.py:14
  44.0 0.2 select_maximum_fusion
  44.3 2.2 %collective-permute-start.10 = (f32[2,4,16,136]{3,2,1,0:T(8,128)S(1)}, f32[2,4,16,136]{3,2,1,0:T(8,128)S(1)}, u32[]{:S(2)}, u32[]{:S(2)}) collective-permute-start(f32[2,4,16,136]{3,2,1,0:T(8,128)S(1)} %get-tuple-element.60), channel_id=1, source_target_pairs={{1,0},{2,1},{3,2},{5,4},{6,5},{7,6},{9,8},{10,9},{11,10},{13,12},{... | collective-permute-start | bytes 208904 | tf_op jit(solution)/shard_map/ppermute | solution.py:19
  46.5 3.1 %collective-permute-start.11 = (f32[2,4,16,136]{3,2,1,0:T(8,128)S(1)}, f32[2,4,16,136]{3,2,1,0:T(8,128)S(1)}, u32[]{:S(2)}, u32[]{:S(2)}) collective-permute-start(f32[2,4,16,136]{3,2,1,0:T(8,128)S(1)} %get-tuple-element.61), channel_id=1, source_target_pairs={{0,1},{1,2},{2,3},{4,5},{5,6},{6,7},{8,9},{9,10},{10,11},{12,13},{... | collective-permute-start | bytes 208904 | tf_op jit(solution)/shard_map/ppermute | solution.py:19
  49.7 0.2 maximum_maximum_fusion.2
  49.9 0.4 collective-permute-done.10
  50.3 2.2 %collective-permute-done.11 = f32[2,4,16,136]{3,2,1,0:T(8,128)S(1)} collective-permute-done((f32[2,4,16,136]{3,2,1,0:T(8,128)S(1)}, f32[2,4,16,136]{3,2,1,0:T(8,128)S(1)}, u32[]{:S(2)}, u32[]{:S(2)}) %collective-permute-start.11) | collective-permute-done | bytes 69664 | tf_op jit(solution)/shard_map/ppermute | solution.py:19
  52.5 0.3 pad_maximum_fusion.1
  52.8 0.3 fusion.23
  53.1 0.2 fusion.3
  53.3 0.7 %add_subtract_fusion = (f32[2,8,8,128]{3,2,1,0:T(8,128)S(1)}, f32[2,8,8,128]{3,2,1,0:T(8,128)S(1)}) fusion(f32[2,16,8,128]{3,2,1,0:T(8,128)S(1)} %fusion.23, f32[8,8,128]{2,1,0:T(8,128)S(1)} %get-tuple-element.86, f32[2,16,8,136]{3,2,1,0:T(8,128)S(1)} %fusion.3, f32[8,8,128]{2,1,0:T(8,128)S(1)} %get-tuple-element.87, ...), kind=kLoop, calls=%fused_computation.307 | loop fusion | flops 2703360 | bytes 3227648 | tf_op jit(solution)/shard_map/sub | solution.py:111
  54.0 0.0 copy-start.10
  54.1 0.0 copy-start.11
  54.1 0.6 %copy-done.10 = f32[8,8,128]{2,1,0:T(8,128)} copy-done((f32[8,8,128]{2,1,0:T(8,128)}, f32[8,8,128]{2,1,0:T(8,128)S(1)}, u32[]{:S(2)}) %copy-start.10) | copy-done | bytes 32792
  54.7 0.0 copy-done.11
  (56 shorter events, 0.5 us)
Async XLA Ops:
  0.6 1.0 %copy-start = (f32[256,256]{1,0:T(8,128)S(1)}, f32[256,256]{1,0:T(8,128)}, u32[]{:S(2)}) copy-start(f32[256,256]{1,0:T(8,128)} %param.36) | copy-start | bytes 786436
  0.6 0.7 %copy-start.19 = (s32[256]{0:T(256)S(1)}, s32[256]{0:T(256)}, u32[]{:S(2)}) copy-start(s32[256]{0:T(256)} %param.41) | copy-start | bytes 3076
  0.7 0.7 %copy-start.20 = (f32[64]{0:T(128)S(1)}, f32[64]{0:T(128)}, u32[]{:S(2)}) copy-start(f32[64]{0:T(128)} %param.38) | copy-start | bytes 772
  0.7 0.9 %copy-start.16 = (f32[2,256]{1,0:T(2,128)S(1)}, f32[2,256]{1,0:T(2,128)}, u32[]{:S(2)}) copy-start(f32[2,256]{1,0:T(2,128)} %param.37) | copy-start | bytes 6148
  1.9 0.7 %copy-start.17 = (s32[256]{0:T(256)S(1)}, s32[256]{0:T(256)}, u32[]{:S(2)}) copy-start(s32[256]{0:T(256)} %param.40) | copy-start | bytes 3076
  1.9 0.8 %copy-start.18 = (s32[256]{0:T(256)S(1)}, s32[256]{0:T(256)}, u32[]{:S(2)}) copy-start(s32[256]{0:T(256)} %param.39) | copy-start | bytes 3076
  4.0 6.3 %copy-start.3 = (f32[8,8,128]{2,1,0:T(8,128)S(1)}, f32[8,8,128]{2,1,0:T(8,128)}, u32[]{:S(2)}) copy-start(f32[8,8,128]{2,1,0:T(8,128)} %param.25) | copy-start | bytes 98308
  4.0 6.3 %copy-start.4 = (f32[8,8,128]{2,1,0:T(8,128)S(1)}, f32[8,8,128]{2,1,0:T(8,128)}, u32[]{:S(2)}) copy-start(f32[8,8,128]{2,1,0:T(8,128)} %param.27) | copy-start | bytes 98308
  4.0 22.2 %all-to-all-start = ((f32[32,1,192]{2,1,0:T(1,128)}), f32[32,1,192]{2,1,0:T(1,128)S(1)}, u32[]{:S(2)}, u32[]{:S(2)}) async-start(f32[32,1,192]{2,1,0:T(1,128)} %copy.42), calls=%async_computation | async-start | bytes 65536 | tf_op jit(solution)/shard_map/all_to_all | solution.py:187
  10.3 8.6 %collective-permute-start.1 = (f32[2,8,4,128]{3,2,1,0:T(4,128)S(1)}, f32[2,8,4,128]{3,2,1,0:T(4,128)S(1)}, u32[]{:S(2)}, u32[]{:S(2)}) collective-permute-start(f32[2,8,4,128]{3,2,1,0:T(4,128)S(1)} %get-tuple-element.97), channel_id=1, source_target_pairs={{0,8},{8,16},{16,24},{1,9},{9,17},{17,25},{2,10},{10,18},{18,26},{... | collective-permute-start | bytes 98312 | tf_op jit(solution)/shard_map/ppermute | solution.py:19
  13.6 5.3 %collective-permute-start = (f32[2,8,4,128]{3,2,1,0:T(4,128)S(1)}, f32[2,8,4,128]{3,2,1,0:T(4,128)S(1)}, u32[]{:S(2)}, u32[]{:S(2)}) collective-permute-start(f32[2,8,4,128]{3,2,1,0:T(4,128)S(1)} %get-tuple-element.98), channel_id=1, source_target_pairs={{8,0},{16,8},{24,16},{9,1},{17,9},{25,17},{10,2},{18,10},{26,18},{... | collective-permute-start | bytes 98312 | tf_op jit(solution)/shard_map/ppermute | solution.py:19
  15.6 1.4 %copy-start.12 = (f32[8,8,128]{2,1,0:T(8,128)S(1)}, f32[8,8,128]{2,1,0:T(8,128)}, u32[]{:S(2)}) copy-start(f32[8,8,128]{2,1,0:T(8,128)} %param.33) | copy-start | bytes 98308
  15.6 1.4 %copy-start.13 = (f32[8,8,128]{2,1,0:T(8,128)S(1)}, f32[8,8,128]{2,1,0:T(8,128)}, u32[]{:S(2)}) copy-start(f32[8,8,128]{2,1,0:T(8,128)} %param.32) | copy-start | bytes 98308
  15.7 3.2 %collective-permute-start.3 = (f32[2,8,8,4]{3,2,1,0:T(8,128)S(1)}, f32[2,8,8,4]{3,2,1,0:T(8,128)S(1)}, u32[]{:S(2)}, u32[]{:S(2)}) collective-permute-start(f32[2,8,8,4]{3,2,1,0:T(8,128)S(1)} %fusion.52), channel_id=1, source_target_pairs={{0,4},{4,0},{1,5},{5,1},{2,6},{6,2},{3,7},{7,3},{8,12},{12,8},{9,1... | collective-permute-start | bytes 6152 | tf_op jit(solution)/shard_map/ppermute | solution.py:14
  19.0 6.9 %collective-permute-start.2 = (f32[2,8,8,4]{3,2,1,0:T(8,128)S(1)}, f32[2,8,8,4]{3,2,1,0:T(8,128)S(1)}, u32[]{:S(2)}, u32[]{:S(2)}) collective-permute-start(f32[2,8,8,4]{3,2,1,0:T(8,128)S(1)} %fusion.160), channel_id=1, source_target_pairs={{0,4},{4,0},{1,5},{5,1},{2,6},{6,2},{3,7},{7,3},{8,12},{12,8},{9,1... | collective-permute-start | bytes 6152 | tf_op jit(solution)/shard_map/ppermute | solution.py:14
  20.5 7.1 %collective-permute-start.4 = (f32[2,4,16,136]{3,2,1,0:T(8,128)S(1)}, f32[2,4,16,136]{3,2,1,0:T(8,128)S(1)}, u32[]{:S(2)}, u32[]{:S(2)}) collective-permute-start(f32[2,4,16,136]{3,2,1,0:T(8,128)S(1)} %get-tuple-element.62), channel_id=1, source_target_pairs={{1,0},{2,1},{3,2},{5,4},{6,5},{7,6},{9,8},{10,9},{11,10},{13,12},{... | collective-permute-start | bytes 208904 | tf_op jit(solution)/shard_map/ppermute | solution.py:19
  22.7 6.8 %collective-permute-start.5 = (f32[2,4,16,136]{3,2,1,0:T(8,128)S(1)}, f32[2,4,16,136]{3,2,1,0:T(8,128)S(1)}, u32[]{:S(2)}, u32[]{:S(2)}) collective-permute-start(f32[2,4,16,136]{3,2,1,0:T(8,128)S(1)} %get-tuple-element.63), channel_id=1, source_target_pairs={{0,1},{1,2},{2,3},{4,5},{5,6},{6,7},{8,9},{9,10},{10,11},{12,13},{... | collective-permute-start | bytes 208904 | tf_op jit(solution)/shard_map/ppermute | solution.py:19
  30.4 0.8 %copy-start.5 = (f32[8,8,128]{2,1,0:T(8,128)S(1)}, f32[8,8,128]{2,1,0:T(8,128)}, u32[]{:S(2)}) copy-start(f32[8,8,128]{2,1,0:T(8,128)} %param.29) | copy-start | bytes 98308
  30.4 0.8 %copy-start.6 = (f32[8,8,128]{2,1,0:T(8,128)S(1)}, f32[8,8,128]{2,1,0:T(8,128)}, u32[]{:S(2)}) copy-start(f32[8,8,128]{2,1,0:T(8,128)} %param.34) | copy-start | bytes 98308
  30.4 0.8 %copy-start.7 = (f32[8,8,128]{2,1,0:T(8,128)S(1)}, f32[8,8,128]{2,1,0:T(8,128)}, u32[]{:S(2)}) copy-start(f32[8,8,128]{2,1,0:T(8,128)} %param.35) | copy-start | bytes 98308
  30.4 0.8 %copy-start.8 = (f32[8,8,128]{2,1,0:T(8,128)S(1)}, f32[8,8,128]{2,1,0:T(8,128)}, u32[]{:S(2)}) copy-start(f32[8,8,128]{2,1,0:T(8,128)} %param.31) | copy-start | bytes 98308
  30.4 0.8 %copy-start.9 = (f32[8,8,128]{2,1,0:T(8,128)S(1)}, f32[8,8,128]{2,1,0:T(8,128)}, u32[]{:S(2)}) copy-start(f32[8,8,128]{2,1,0:T(8,128)} %param.30) | copy-start | bytes 98308
  30.4 0.8 %copy-start.14 = (f32[8,8,128]{2,1,0:T(8,128)S(1)}, f32[8,8,128]{2,1,0:T(8,128)}, u32[]{:S(2)}) copy-start(f32[8,8,128]{2,1,0:T(8,128)} %param.28) | copy-start | bytes 98308
  30.4 0.8 %copy-start.15 = (f32[8,8,128]{2,1,0:T(8,128)S(1)}, f32[8,8,128]{2,1,0:T(8,128)}, u32[]{:S(2)}) copy-start(f32[8,8,128]{2,1,0:T(8,128)} %param.26) | copy-start | bytes 98308
  31.3 22.7 %copy-start.1 = (f32[8,8,128]{2,1,0:T(8,128)}, f32[8,8,128]{2,1,0:T(8,128)S(1)}, u32[]{:S(2)}) copy-start(f32[8,8,128]{2,1,0:T(8,128)S(1)} %get-tuple-element.108) | copy-start | bytes 98308
  31.3 22.7 %copy-start.2 = (f32[8,8,128]{2,1,0:T(8,128)}, f32[8,8,128]{2,1,0:T(8,128)S(1)}, u32[]{:S(2)}) copy-start(f32[8,8,128]{2,1,0:T(8,128)S(1)} %get-tuple-element.109) | copy-start | bytes 98308
  31.4 7.9 %collective-permute-start.9 = (f32[2,8,8,4]{3,2,1,0:T(8,128)S(1)}, f32[2,8,8,4]{3,2,1,0:T(8,128)S(1)}, u32[]{:S(2)}, u32[]{:S(2)}) collective-permute-start(f32[2,8,8,4]{3,2,1,0:T(8,128)S(1)} %fusion.48), channel_id=1, source_target_pairs={{0,4},{4,0},{1,5},{5,1},{2,6},{6,2},{3,7},{7,3},{8,12},{12,8},{9,1... | collective-permute-start | bytes 6152 | tf_op jit(solution)/shard_map/ppermute | solution.py:14
  31.8 7.6 %collective-permute-start.7 = (f32[2,8,4,128]{3,2,1,0:T(4,128)S(1)}, f32[2,8,4,128]{3,2,1,0:T(4,128)S(1)}, u32[]{:S(2)}, u32[]{:S(2)}) collective-permute-start(f32[2,8,4,128]{3,2,1,0:T(4,128)S(1)} %get-tuple-element.80), channel_id=1, source_target_pairs={{0,8},{8,16},{16,24},{1,9},{9,17},{17,25},{2,10},{10,18},{18,26},{... | collective-permute-start | bytes 98312 | tf_op jit(solution)/shard_map/ppermute | solution.py:19
  37.4 5.2 %collective-permute-start.6 = (f32[2,8,4,128]{3,2,1,0:T(4,128)S(1)}, f32[2,8,4,128]{3,2,1,0:T(4,128)S(1)}, u32[]{:S(2)}, u32[]{:S(2)}) collective-permute-start(f32[2,8,4,128]{3,2,1,0:T(4,128)S(1)} %get-tuple-element.81), channel_id=1, source_target_pairs={{8,0},{16,8},{24,16},{9,1},{17,9},{25,17},{10,2},{18,10},{26,18},{... | collective-permute-start | bytes 98312 | tf_op jit(solution)/shard_map/ppermute | solution.py:19
  42.7 6.9 %collective-permute-start.8 = (f32[2,8,8,4]{3,2,1,0:T(8,128)S(1)}, f32[2,8,8,4]{3,2,1,0:T(8,128)S(1)}, u32[]{:S(2)}, u32[]{:S(2)}) collective-permute-start(f32[2,8,8,4]{3,2,1,0:T(8,128)S(1)} %fusion.103), channel_id=1, source_target_pairs={{0,4},{4,0},{1,5},{5,1},{2,6},{6,2},{3,7},{7,3},{8,12},{12,8},{9,1... | collective-permute-start | bytes 6152 | tf_op jit(solution)/shard_map/ppermute | solution.py:14
  44.3 6.0 %collective-permute-start.10 = (f32[2,4,16,136]{3,2,1,0:T(8,128)S(1)}, f32[2,4,16,136]{3,2,1,0:T(8,128)S(1)}, u32[]{:S(2)}, u32[]{:S(2)}) collective-permute-start(f32[2,4,16,136]{3,2,1,0:T(8,128)S(1)} %get-tuple-element.60), channel_id=1, source_target_pairs={{1,0},{2,1},{3,2},{5,4},{6,5},{7,6},{9,8},{10,9},{11,10},{13,12},{... | collective-permute-start | bytes 208904 | tf_op jit(solution)/shard_map/ppermute | solution.py:19
  46.5 6.0 %collective-permute-start.11 = (f32[2,4,16,136]{3,2,1,0:T(8,128)S(1)}, f32[2,4,16,136]{3,2,1,0:T(8,128)S(1)}, u32[]{:S(2)}, u32[]{:S(2)}) collective-permute-start(f32[2,4,16,136]{3,2,1,0:T(8,128)S(1)} %get-tuple-element.61), channel_id=1, source_target_pairs={{0,1},{1,2},{2,3},{4,5},{5,6},{6,7},{8,9},{9,10},{10,11},{12,13},{... | collective-permute-start | bytes 208904 | tf_op jit(solution)/shard_map/ppermute | solution.py:19
  54.0 0.6 %copy-start.10 = (f32[8,8,128]{2,1,0:T(8,128)}, f32[8,8,128]{2,1,0:T(8,128)S(1)}, u32[]{:S(2)}) copy-start(f32[8,8,128]{2,1,0:T(8,128)S(1)} %get-tuple-element.106) | copy-start | bytes 98308
  54.1 0.6 %copy-start.11 = (f32[8,8,128]{2,1,0:T(8,128)}, f32[8,8,128]{2,1,0:T(8,128)S(1)}, u32[]{:S(2)}) copy-start(f32[8,8,128]{2,1,0:T(8,128)S(1)} %get-tuple-element.107) | copy-start | bytes 98308

commit v8 on v7

--- a/solution.py
+++ b/solution.py
@@ -19,11 +19,18 @@
     return lax.ppermute(top, axis, forward), lax.ppermute(bottom, axis, backward)
 
 
-def with_halo(block, width):
+def first_round(block, width):
     cut = lambda a, dim, lo, hi: lax.slice_in_dim(a, lo, hi, axis=dim)
-    depth, across, along = block.shape[1:]
+    across, along = block.shape[2:]
     low_x, high_x = shift_pair(cut(block, 2, across - width, None), cut(block, 2, 0, width), "inl")
     low_y, high_y = shift_pair(cut(block, 3, along - width, None), cut(block, 3, 0, width), "xl")
+    return low_x, high_x, low_y, high_y
+
+
+def second_round(block, width, faces):
+    cut = lambda a, dim, lo, hi: lax.slice_in_dim(a, lo, hi, axis=dim)
+    depth, along = block.shape[1], block.shape[3]
+    low_x, high_x, low_y, high_y = faces
     strips = jnp.concatenate([low_x, high_x], axis=2)
     low_c, high_c = shift_pair(cut(strips, 3, along - width, None), cut(strips, 3, 0, width), "xl")
     wide_x = jnp.concatenate([low_x, block, high_x], axis=2)
@@ -34,6 +41,10 @@
     side_high = jnp.concatenate([high_c[:, :, :width], high_y, high_c[:, :, width:]], axis=2)
     full = jnp.concatenate([side_low, wide_x, side_high], axis=3)
     return jnp.concatenate([low_z, full, high_z], axis=1)
+
+
+def with_halo(block, width):
+    return second_round(block, width, first_round(block, width))
 
 
 def derivatives(padded):
@@ -184,6 +195,9 @@
         (owner * gz_count)[:, None] == jnp.arange(devices, dtype=jnp.int32)[None, :]
     ).astype(jnp.float32)
     send = lax.dot_general(to_device, spread, (((0,), (0,)), ((), ())), precision=highest)
+    current = jnp.stack([wave_p, wave_q])
+    faces = first_round(current, 4)
+    send, faces = lax.optimization_barrier((send, faces))
     arrived = lax.all_to_all(send, ("inl", "xl", "gz"), split_axis=0, concat_axis=0, tiled=True)
     amp = arrived[:, : steps * capacity].reshape(devices, steps, capacity)
     cell = (arrived[:, steps * capacity :] + 0.5).astype(jnp.int32)
@@ -205,7 +219,7 @@
     previous = jnp.stack([wave_p_old, wave_q_old])
     coefs = anisotropy(tilt_angle, azimuth)
     for step in range(steps):
-        padded = with_halo(current, 4)
+        padded = second_round(current, 4, faces) if step == 0 else with_halo(current, 4)
         newer = advance(padded, current, previous, fields, coefs, planes[step], 0)
         previous = current
         current = newer

time: 55.2 us -> 52.2 us (0.946)
  waiting for transfers between devices: 10.1 us -> 7.37 us
  starting transfers between devices: 33.8 us -> 32.4 us
  other arithmetic: 4.59 us -> 5.45 us
    ppermute x4, waiting for transfers between devices: 1.65 us -> 0.01 us  [shift_pair(): got = lax.ppermute(jnp.where(first, top, bottom), axis, [(0, 1), (1, 0)])]
    all_to_all x1, starting transfers between devices: 6.25 us -> 4.76 us  [local(): lax.all_to_all(send, ('inl', 'xl', 'gz'), split_axis=0, concat_axis=0, ti...]
    another operation x1, other arithmetic: 0.01 us -> 0.87 us  [local(): current = jnp.stack([wave_p, wave_q])]
    ppermute x4, starting transfers between devices: 8.19 us -> 8.88 us  [shift_pair(): lax.ppermute(bottom, axis, backward)]
    ppermute x4, waiting for transfers between devices: 4.35 us -> 3.68 us  [shift_pair(): lax.ppermute(bottom, axis, backward)]
    ppermute x4, starting transfers between devices: 15.2 us -> 14.6 us  [shift_pair(): lax.ppermute(top, axis, forward)]
  transfers between devices with their start and end apart: 13 -> 13, of which waited for: 6 -> 4; matrix products, arithmetic and copies ran while one was open for 4% -> 6% of each run, Pallas kernels for 0% -> 0%
where the time goes in v8:
time: 52.2 us; the launch traced here: 51.7 us
  starting transfers between devices  32.4 us (62%)
  waiting for transfers between devices  7.37 us (14%)
  other arithmetic  5.45 us (10%)
  local copies, waits for them, and re-layouts  3.65 us (7%)
  matrix products  1.52 us (3%)
  between operations  1.32 us (3%)
    ppermute x4, starting transfers between devices, shift_pair(): lax.ppermute(top, axis, forward)  14.6 us
    ppermute x4, starting transfers between devices, shift_pair(): lax.ppermute(bottom, axis, backward)  8.88 us
    all_to_all x1, starting transfers between devices, local(): lax.all_to_all(send, ('inl', 'xl', 'gz'), split_axis=0, concat_axis=0, ti...  4.76 us
    ppermute x4, starting transfers between devices, shift_pair(): got = lax.ppermute(jnp.where(first, top, bottom), axis, [(0, 1), (1, 0)])  4.12 us
    ppermute x4, waiting for transfers between devices, shift_pair(): lax.ppermute(bottom, axis, backward)  3.68 us
    ppermute x4, waiting for transfers between devices, shift_pair(): lax.ppermute(top, axis, forward)  3.68 us
    unnamed x43, local copies, waits for them, and re-layouts  2.58 us
    sub x2, other arithmetic, advance(): h_two = u_xx + u_yy + u_zz - h_one  1.39 us
  transfers between devices with their start and end apart: 13, of which 4 were waited for; matrix products, arithmetic and copies ran while one was open for 6% of the time, Pallas kernels for 0%

profile of v8, /device:TPU:17, one launch (start us, length us, event | category | flops | bytes accessed | tf_op | source)
XLA Modules:
  0.0 51.7 jit_solution(15390036737164188908)
XLA Ops:
  0.6 0.0 copy-start
  0.7 0.9 %fusion.176 = (f32[2,8,4,128]{3,2,1,0:T(4,128)S(1)}, f32[2,8,4,128]{3,2,1,0:T(4,128)S(1)}) fusion(f32[1,8,8,128]{3,2,1,0:T(8,128)} %bitcast.124, f32[1,8,8,128]{3,2,1,0:T(8,128)} %bitcast.131), kind=kLoop, calls=%fused_computation.321 | loop fusion | flops 16384 | bytes 131072 | tf_op jit(solution)/shard_map/stack | solution.py:218
  1.5 2.6 %collective-permute-start.1 = (f32[2,8,4,128]{3,2,1,0:T(4,128)S(1)}, f32[2,8,4,128]{3,2,1,0:T(4,128)S(1)}, u32[]{:S(2)}, u32[]{:S(2)}) collective-permute-start(f32[2,8,4,128]{3,2,1,0:T(4,128)S(1)} %get-tuple-element.109), channel_id=1, source_target_pairs={{8,0},{16,8},{24,16},{9,1},{17,9},{25,17},{10,2},{18,10},{26,18},{... | collective-permute-start | bytes 98312 | tf_op jit(solution)/shard_map/ppermute | solution.py:19
  4.1 3.0 %collective-permute-start = (f32[2,8,4,128]{3,2,1,0:T(4,128)S(1)}, f32[2,8,4,128]{3,2,1,0:T(4,128)S(1)}, u32[]{:S(2)}, u32[]{:S(2)}) collective-permute-start(f32[2,8,4,128]{3,2,1,0:T(4,128)S(1)} %get-tuple-element.110), channel_id=1, source_target_pairs={{0,8},{8,16},{16,24},{1,9},{9,17},{17,25},{2,10},{10,18},{18,26},{... | collective-permute-start | bytes 98312 | tf_op jit(solution)/shard_map/ppermute | solution.py:19
  7.2 0.0 copy-start.19
  7.2 0.0 copy-start.20
  7.2 0.1 fusion.53
  7.3 1.3 %collective-permute-start.2 = (f32[2,8,8,4]{3,2,1,0:T(8,128)S(1)}, f32[2,8,8,4]{3,2,1,0:T(8,128)S(1)}, u32[]{:S(2)}, u32[]{:S(2)}) collective-permute-start(f32[2,8,8,4]{3,2,1,0:T(8,128)S(1)} %fusion.53), channel_id=1, source_target_pairs={{0,4},{4,0},{1,5},{5,1},{2,6},{6,2},{3,7},{7,3},{8,12},{12,8},{9,1... | collective-permute-start | bytes 6152 | tf_op jit(solution)/shard_map/ppermute | solution.py:14
  8.6 0.1 select_reduce_fusion
  8.7 0.6 %copy-done.16 = f32[2,256]{1,0:T(2,128)S(1)} copy-done((f32[2,256]{1,0:T(2,128)S(1)}, f32[2,256]{1,0:T(2,128)}, u32[]{:S(2)}) %copy-start.16) | copy-done | bytes 2072
  9.3 0.3 convolution_multiply_fusion
  9.6 0.1 copy-start.18
  9.6 0.7 %copy-done.17 = s32[256]{0:T(256)S(1)} copy-done((s32[256]{0:T(256)S(1)}, s32[256]{0:T(256)}, u32[]{:S(2)}) %copy-start.17) | copy-done | bytes 1048
  10.3 0.0 copy-done.18
  10.3 0.0 copy-start.12
  10.4 0.2 fusion
  10.6 0.5 %copy-done.12 = f32[8,8,128]{2,1,0:T(8,128)S(1)} copy-done((f32[8,8,128]{2,1,0:T(8,128)S(1)}, f32[8,8,128]{2,1,0:T(8,128)}, u32[]{:S(2)}) %copy-start.12) | copy-done | bytes 32792
  11.1 0.0 copy-done.13
  11.1 0.2 fusion.226
  11.4 0.4 fusion.18
  11.9 0.1 fusion.161
  12.0 0.6 %copy.42 = f32[32,1,192]{2,1,0:T(1,128)} copy(f32[32,1,192]{2,0,1:T(8,128)S(1)} %bitcast.142) | data formatting | bytes 49152 | tf_op jit(solution)/shard_map/all_to_all | solution.py:201
  12.7 4.8 %all-to-all-start = ((f32[32,1,192]{2,1,0:T(1,128)}), f32[32,1,192]{2,1,0:T(1,128)S(1)}, u32[]{:S(2)}, u32[]{:S(2)}) async-start(f32[32,1,192]{2,1,0:T(1,128)} %copy.42), calls=%async_computation | async-start | bytes 65536 | tf_op jit(solution)/shard_map/all_to_all | solution.py:201
  17.4 1.2 %collective-permute-start.3 = (f32[2,8,8,4]{3,2,1,0:T(8,128)S(1)}, f32[2,8,8,4]{3,2,1,0:T(8,128)S(1)}, u32[]{:S(2)}, u32[]{:S(2)}) collective-permute-start(f32[2,8,8,4]{3,2,1,0:T(8,128)S(1)} %fusion.161), channel_id=1, source_target_pairs={{0,4},{4,0},{1,5},{5,1},{2,6},{6,2},{3,7},{7,3},{8,12},{12,8},{9,1... | collective-permute-start | bytes 6152 | tf_op jit(solution)/shard_map/ppermute | solution.py:14
  18.7 0.2 select_maximum_fusion.2
  19.0 2.2 %collective-permute-start.4 = (f32[2,4,16,136]{3,2,1,0:T(8,128)S(1)}, f32[2,4,16,136]{3,2,1,0:T(8,128)S(1)}, u32[]{:S(2)}, u32[]{:S(2)}) collective-permute-start(f32[2,4,16,136]{3,2,1,0:T(8,128)S(1)} %get-tuple-element.72), channel_id=1, source_target_pairs={{1,0},{2,1},{3,2},{5,4},{6,5},{7,6},{9,8},{10,9},{11,10},{13,12},{... | collective-permute-start | bytes 208904 | tf_op jit(solution)/shard_map/ppermute | solution.py:19
  21.2 3.1 %collective-permute-start.5 = (f32[2,4,16,136]{3,2,1,0:T(8,128)S(1)}, f32[2,4,16,136]{3,2,1,0:T(8,128)S(1)}, u32[]{:S(2)}, u32[]{:S(2)}) collective-permute-start(f32[2,4,16,136]{3,2,1,0:T(8,128)S(1)} %get-tuple-element.73), channel_id=1, source_target_pairs={{0,1},{1,2},{2,3},{4,5},{5,6},{6,7},{8,9},{9,10},{10,11},{12,13},{... | collective-permute-start | bytes 208904 | tf_op jit(solution)/shard_map/ppermute | solution.py:19
  24.3 0.2 maximum_maximum_fusion
  24.6 0.1 reshape.205
  24.7 0.6 %convolution_bitcast_fusion = f32[16,128]{1,0:T(8,128)S(1)} fusion(s32[32,64]{1,0:T(8,128)S(1)} %add_select_fusion, f32[8,32,64]{2,0,1:T(8,128)S(1)} %fusion.45, f32[2,32,64]{2,0,1:T(2,128)S(1)} %bitcast.141), kind=kOutput, calls=%fused_computation.1 | convolution fusion | flops 50626560 | bytes 98304 | tf_op jit(solution)/shard_map/dot_general | solution.py:214
  25.4 1.5 %collective-permute-done.5 = f32[2,4,16,136]{3,2,1,0:T(8,128)S(1)} collective-permute-done((f32[2,4,16,136]{3,2,1,0:T(8,128)S(1)}, f32[2,4,16,136]{3,2,1,0:T(8,128)S(1)}, u32[]{:S(2)}, u32[]{:S(2)}) %collective-permute-start.5) | collective-permute-done | bytes 69664 | tf_op jit(solution)/shard_map/ppermute | solution.py:19
  26.9 0.3 pad_maximum_fusion
  27.1 0.3 fusion.31
  27.4 0.2 fusion.10
  27.7 0.0 copy-start.7
  27.7 0.0 copy-start.8
  27.7 0.0 copy-start.15
  27.7 0.7 %add_subtract_fusion.1 = (f32[2,8,8,128]{3,2,1,0:T(8,128)S(1)}, f32[2,8,8,128]{3,2,1,0:T(8,128)S(1)}) fusion(f32[2,16,8,128]{3,2,1,0:T(8,128)S(1)} %fusion.31, f32[8,8,128]{2,1,0:T(8,128)S(1)} %get-tuple-element.96, f32[2,16,8,136]{3,2,1,0:T(8,128)S(1)} %fusion.10, f32[8,8,128]{2,1,0:T(8,128)S(1)} %get-tuple-element.97, ...), kind=kLoop, calls=%fused_computation.308 | loop fusion | flops 2703360 | bytes 3227648 | tf_op jit(solution)/shard_map/sub | solution.py:122
  28.5 0.0 copy-done.9
  28.5 0.0 copy-done.14
  28.5 0.0 copy-done.15
  28.6 0.0 copy-start.1
  28.6 0.0 copy-start.2
  28.6 0.1 fusion.49
  28.7 0.3 collective-permute-start.9
  29.1 5.4 %collective-permute-start.7 = (f32[2,8,4,128]{3,2,1,0:T(4,128)S(1)}, f32[2,8,4,128]{3,2,1,0:T(4,128)S(1)}, u32[]{:S(2)}, u32[]{:S(2)}) collective-permute-start(f32[2,8,4,128]{3,2,1,0:T(4,128)S(1)} %get-tuple-element.90), channel_id=1, source_target_pairs={{0,8},{8,16},{16,24},{1,9},{9,17},{17,25},{2,10},{10,18},{18,26},{... | collective-permute-start | bytes 98312 | tf_op jit(solution)/shard_map/ppermute | solution.py:19
  34.4 1.9 %collective-permute-start.6 = (f32[2,8,4,128]{3,2,1,0:T(4,128)S(1)}, f32[2,8,4,128]{3,2,1,0:T(4,128)S(1)}, u32[]{:S(2)}, u32[]{:S(2)}) collective-permute-start(f32[2,8,4,128]{3,2,1,0:T(4,128)S(1)} %get-tuple-element.91), channel_id=1, source_target_pairs={{8,0},{16,8},{24,16},{9,1},{17,9},{25,17},{10,2},{18,10},{26,18},{... | collective-permute-start | bytes 98312 | tf_op jit(solution)/shard_map/ppermute | solution.py:19
  36.4 3.3 %collective-permute-done.6 = f32[2,8,4,128]{3,2,1,0:T(4,128)S(1)} collective-permute-done((f32[2,8,4,128]{3,2,1,0:T(4,128)S(1)}, f32[2,8,4,128]{3,2,1,0:T(4,128)S(1)}, u32[]{:S(2)}, u32[]{:S(2)}) %collective-permute-start.6) | collective-permute-done | bytes 32800 | tf_op jit(solution)/shard_map/ppermute | solution.py:19
  39.6 0.1 fusion.104
  39.8 1.2 %collective-permute-start.8 = (f32[2,8,8,4]{3,2,1,0:T(8,128)S(1)}, f32[2,8,8,4]{3,2,1,0:T(8,128)S(1)}, u32[]{:S(2)}, u32[]{:S(2)}) collective-permute-start(f32[2,8,8,4]{3,2,1,0:T(8,128)S(1)} %fusion.104), channel_id=1, source_target_pairs={{0,4},{4,0},{1,5},{5,1},{2,6},{6,2},{3,7},{7,3},{8,12},{12,8},{9,1... | collective-permute-start | bytes 6152 | tf_op jit(solution)/shard_map/ppermute | solution.py:14
  41.0 0.2 select_maximum_fusion
  41.3 2.2 %collective-permute-start.10 = (f32[2,4,16,136]{3,2,1,0:T(8,128)S(1)}, f32[2,4,16,136]{3,2,1,0:T(8,128)S(1)}, u32[]{:S(2)}, u32[]{:S(2)}) collective-permute-start(f32[2,4,16,136]{3,2,1,0:T(8,128)S(1)} %get-tuple-element.70), channel_id=1, source_target_pairs={{1,0},{2,1},{3,2},{5,4},{6,5},{7,6},{9,8},{10,9},{11,10},{13,12},{... | collective-permute-start | bytes 208904 | tf_op jit(solution)/shard_map/ppermute | solution.py:19
  43.5 3.1 %collective-permute-start.11 = (f32[2,4,16,136]{3,2,1,0:T(8,128)S(1)}, f32[2,4,16,136]{3,2,1,0:T(8,128)S(1)}, u32[]{:S(2)}, u32[]{:S(2)}) collective-permute-start(f32[2,4,16,136]{3,2,1,0:T(8,128)S(1)} %get-tuple-element.71), channel_id=1, source_target_pairs={{0,1},{1,2},{2,3},{4,5},{5,6},{6,7},{8,9},{9,10},{10,11},{12,13},{... | collective-permute-start | bytes 208904 | tf_op jit(solution)/shard_map/ppermute | solution.py:19
  46.7 0.2 maximum_maximum_fusion.2
  46.9 0.4 collective-permute-done.10
  47.3 2.2 %collective-permute-done.11 = f32[2,4,16,136]{3,2,1,0:T(8,128)S(1)} collective-permute-done((f32[2,4,16,136]{3,2,1,0:T(8,128)S(1)}, f32[2,4,16,136]{3,2,1,0:T(8,128)S(1)}, u32[]{:S(2)}, u32[]{:S(2)}) %collective-permute-start.11) | collective-permute-done | bytes 69664 | tf_op jit(solution)/shard_map/ppermute | solution.py:19
  49.5 0.3 pad_maximum_fusion.1
  49.8 0.3 fusion.24
  50.1 0.2 fusion.3
  50.3 0.7 %add_subtract_fusion = (f32[2,8,8,128]{3,2,1,0:T(8,128)S(1)}, f32[2,8,8,128]{3,2,1,0:T(8,128)S(1)}) fusion(f32[2,16,8,128]{3,2,1,0:T(8,128)S(1)} %fusion.24, f32[8,8,128]{2,1,0:T(8,128)S(1)} %get-tuple-element.96, f32[2,16,8,136]{3,2,1,0:T(8,128)S(1)} %fusion.3, f32[8,8,128]{2,1,0:T(8,128)S(1)} %get-tuple-element.97, ...), kind=kLoop, calls=%fused_computation.307 | loop fusion | flops 2703360 | bytes 3227648 | tf_op jit(solution)/shard_map/sub | solution.py:122
  51.0 0.0 copy-start.10
  51.1 0.0 copy-start.11
  51.1 0.6 %copy-done.10 = f32[8,8,128]{2,1,0:T(8,128)} copy-done((f32[8,8,128]{2,1,0:T(8,128)}, f32[8,8,128]{2,1,0:T(8,128)S(1)}, u32[]{:S(2)}) %copy-start.10) | copy-done | bytes 32792
  51.7 0.0 copy-done.11
  (57 shorter events, 0.5 us)
Async XLA Ops:
  0.6 8.1 %copy-start = (f32[256,256]{1,0:T(8,128)S(1)}, f32[256,256]{1,0:T(8,128)}, u32[]{:S(2)}) copy-start(f32[256,256]{1,0:T(8,128)} %param.36) | copy-start | bytes 786436
  0.6 6.5 %copy-start.3 = (f32[8,8,128]{2,1,0:T(8,128)S(1)}, f32[8,8,128]{2,1,0:T(8,128)}, u32[]{:S(2)}) copy-start(f32[8,8,128]{2,1,0:T(8,128)} %param.25) | copy-start | bytes 98308
  0.7 6.5 %copy-start.4 = (f32[8,8,128]{2,1,0:T(8,128)S(1)}, f32[8,8,128]{2,1,0:T(8,128)}, u32[]{:S(2)}) copy-start(f32[8,8,128]{2,1,0:T(8,128)} %param.27) | copy-start | bytes 98308
  1.5 10.3 %collective-permute-start.1 = (f32[2,8,4,128]{3,2,1,0:T(4,128)S(1)}, f32[2,8,4,128]{3,2,1,0:T(4,128)S(1)}, u32[]{:S(2)}, u32[]{:S(2)}) collective-permute-start(f32[2,8,4,128]{3,2,1,0:T(4,128)S(1)} %get-tuple-element.109), channel_id=1, source_target_pairs={{8,0},{16,8},{24,16},{9,1},{17,9},{25,17},{10,2},{18,10},{26,18},{... | collective-permute-start | bytes 98312 | tf_op jit(solution)/shard_map/ppermute | solution.py:19
  4.1 7.7 %collective-permute-start = (f32[2,8,4,128]{3,2,1,0:T(4,128)S(1)}, f32[2,8,4,128]{3,2,1,0:T(4,128)S(1)}, u32[]{:S(2)}, u32[]{:S(2)}) collective-permute-start(f32[2,8,4,128]{3,2,1,0:T(4,128)S(1)} %get-tuple-element.110), channel_id=1, source_target_pairs={{0,8},{8,16},{16,24},{1,9},{9,17},{17,25},{2,10},{10,18},{18,26},{... | collective-permute-start | bytes 98312 | tf_op jit(solution)/shard_map/ppermute | solution.py:19
  7.2 1.4 %copy-start.19 = (s32[256]{0:T(256)S(1)}, s32[256]{0:T(256)}, u32[]{:S(2)}) copy-start(s32[256]{0:T(256)} %param.41) | copy-start | bytes 3076
  7.2 1.4 %copy-start.20 = (f32[64]{0:T(128)S(1)}, f32[64]{0:T(128)}, u32[]{:S(2)}) copy-start(f32[64]{0:T(128)} %param.38) | copy-start | bytes 772
  7.3 4.5 %collective-permute-start.2 = (f32[2,8,8,4]{3,2,1,0:T(8,128)S(1)}, f32[2,8,8,4]{3,2,1,0:T(8,128)S(1)}, u32[]{:S(2)}, u32[]{:S(2)}) collective-permute-start(f32[2,8,8,4]{3,2,1,0:T(8,128)S(1)} %fusion.53), channel_id=1, source_target_pairs={{0,4},{4,0},{1,5},{5,1},{2,6},{6,2},{3,7},{7,3},{8,12},{12,8},{9,1... | collective-permute-start | bytes 6152 | tf_op jit(solution)/shard_map/ppermute | solution.py:14
  8.6 0.7 %copy-start.16 = (f32[2,256]{1,0:T(2,128)S(1)}, f32[2,256]{1,0:T(2,128)}, u32[]{:S(2)}) copy-start(f32[2,256]{1,0:T(2,128)} %param.37) | copy-start | bytes 6148
  9.6 0.7 %copy-start.17 = (s32[256]{0:T(256)S(1)}, s32[256]{0:T(256)}, u32[]{:S(2)}) copy-start(s32[256]{0:T(256)} %param.40) | copy-start | bytes 3076
  9.6 0.8 %copy-start.18 = (s32[256]{0:T(256)S(1)}, s32[256]{0:T(256)}, u32[]{:S(2)}) copy-start(s32[256]{0:T(256)} %param.39) | copy-start | bytes 3076
  10.3 0.8 %copy-start.12 = (f32[8,8,128]{2,1,0:T(8,128)S(1)}, f32[8,8,128]{2,1,0:T(8,128)}, u32[]{:S(2)}) copy-start(f32[8,8,128]{2,1,0:T(8,128)} %param.33) | copy-start | bytes 98308
  10.3 0.8 %copy-start.13 = (f32[8,8,128]{2,1,0:T(8,128)S(1)}, f32[8,8,128]{2,1,0:T(8,128)}, u32[]{:S(2)}) copy-start(f32[8,8,128]{2,1,0:T(8,128)} %param.32) | copy-start | bytes 98308
  12.7 11.9 %all-to-all-start = ((f32[32,1,192]{2,1,0:T(1,128)}), f32[32,1,192]{2,1,0:T(1,128)S(1)}, u32[]{:S(2)}, u32[]{:S(2)}) async-start(f32[32,1,192]{2,1,0:T(1,128)} %copy.42), calls=%async_computation | async-start | bytes 65536 | tf_op jit(solution)/shard_map/all_to_all | solution.py:201
  17.4 6.8 %collective-permute-start.3 = (f32[2,8,8,4]{3,2,1,0:T(8,128)S(1)}, f32[2,8,8,4]{3,2,1,0:T(8,128)S(1)}, u32[]{:S(2)}, u32[]{:S(2)}) collective-permute-start(f32[2,8,8,4]{3,2,1,0:T(8,128)S(1)} %fusion.161), channel_id=1, source_target_pairs={{0,4},{4,0},{1,5},{5,1},{2,6},{6,2},{3,7},{7,3},{8,12},{12,8},{9,1... | collective-permute-start | bytes 6152 | tf_op jit(solution)/shard_map/ppermute | solution.py:14
  19.0 6.4 %collective-permute-start.4 = (f32[2,4,16,136]{3,2,1,0:T(8,128)S(1)}, f32[2,4,16,136]{3,2,1,0:T(8,128)S(1)}, u32[]{:S(2)}, u32[]{:S(2)}) collective-permute-start(f32[2,4,16,136]{3,2,1,0:T(8,128)S(1)} %get-tuple-element.72), channel_id=1, source_target_pairs={{1,0},{2,1},{3,2},{5,4},{6,5},{7,6},{9,8},{10,9},{11,10},{13,12},{... | collective-permute-start | bytes 208904 | tf_op jit(solution)/shard_map/ppermute | solution.py:19
  21.2 5.7 %collective-permute-start.5 = (f32[2,4,16,136]{3,2,1,0:T(8,128)S(1)}, f32[2,4,16,136]{3,2,1,0:T(8,128)S(1)}, u32[]{:S(2)}, u32[]{:S(2)}) collective-permute-start(f32[2,4,16,136]{3,2,1,0:T(8,128)S(1)} %get-tuple-element.73), channel_id=1, source_target_pairs={{0,1},{1,2},{2,3},{4,5},{5,6},{6,7},{8,9},{9,10},{10,11},{12,13},{... | collective-permute-start | bytes 208904 | tf_op jit(solution)/shard_map/ppermute | solution.py:19
  27.7 0.8 %copy-start.5 = (f32[8,8,128]{2,1,0:T(8,128)S(1)}, f32[8,8,128]{2,1,0:T(8,128)}, u32[]{:S(2)}) copy-start(f32[8,8,128]{2,1,0:T(8,128)} %param.29) | copy-start | bytes 98308
  27.7 0.8 %copy-start.6 = (f32[8,8,128]{2,1,0:T(8,128)S(1)}, f32[8,8,128]{2,1,0:T(8,128)}, u32[]{:S(2)}) copy-start(f32[8,8,128]{2,1,0:T(8,128)} %param.34) | copy-start | bytes 98308
  27.7 0.8 %copy-start.7 = (f32[8,8,128]{2,1,0:T(8,128)S(1)}, f32[8,8,128]{2,1,0:T(8,128)}, u32[]{:S(2)}) copy-start(f32[8,8,128]{2,1,0:T(8,128)} %param.35) | copy-start | bytes 98308
  27.7 0.8 %copy-start.8 = (f32[8,8,128]{2,1,0:T(8,128)S(1)}, f32[8,8,128]{2,1,0:T(8,128)}, u32[]{:S(2)}) copy-start(f32[8,8,128]{2,1,0:T(8,128)} %param.31) | copy-start | bytes 98308
  27.7 0.8 %copy-start.9 = (f32[8,8,128]{2,1,0:T(8,128)S(1)}, f32[8,8,128]{2,1,0:T(8,128)}, u32[]{:S(2)}) copy-start(f32[8,8,128]{2,1,0:T(8,128)} %param.30) | copy-start | bytes 98308
  27.7 0.8 %copy-start.14 = (f32[8,8,128]{2,1,0:T(8,128)S(1)}, f32[8,8,128]{2,1,0:T(8,128)}, u32[]{:S(2)}) copy-start(f32[8,8,128]{2,1,0:T(8,128)} %param.28) | copy-start | bytes 98308
  27.7 0.8 %copy-start.15 = (f32[8,8,128]{2,1,0:T(8,128)S(1)}, f32[8,8,128]{2,1,0:T(8,128)}, u32[]{:S(2)}) copy-start(f32[8,8,128]{2,1,0:T(8,128)} %param.26) | copy-start | bytes 98308
  28.6 22.4 %copy-start.1 = (f32[8,8,128]{2,1,0:T(8,128)}, f32[8,8,128]{2,1,0:T(8,128)S(1)}, u32[]{:S(2)}) copy-start(f32[8,8,128]{2,1,0:T(8,128)S(1)} %get-tuple-element.118) | copy-start | bytes 98308
  28.6 22.4 %copy-start.2 = (f32[8,8,128]{2,1,0:T(8,128)}, f32[8,8,128]{2,1,0:T(8,128)S(1)}, u32[]{:S(2)}) copy-start(f32[8,8,128]{2,1,0:T(8,128)S(1)} %get-tuple-element.119) | copy-start | bytes 98308
  28.7 7.7 %collective-permute-start.9 = (f32[2,8,8,4]{3,2,1,0:T(8,128)S(1)}, f32[2,8,8,4]{3,2,1,0:T(8,128)S(1)}, u32[]{:S(2)}, u32[]{:S(2)}) collective-permute-start(f32[2,8,8,4]{3,2,1,0:T(8,128)S(1)} %fusion.49), channel_id=1, source_target_pairs={{0,4},{4,0},{1,5},{5,1},{2,6},{6,2},{3,7},{7,3},{8,12},{12,8},{9,1... | collective-permute-start | bytes 6152 | tf_op jit(solution)/shard_map/ppermute | solution.py:14
  29.1 7.3 %collective-permute-start.7 = (f32[2,8,4,128]{3,2,1,0:T(4,128)S(1)}, f32[2,8,4,128]{3,2,1,0:T(4,128)S(1)}, u32[]{:S(2)}, u32[]{:S(2)}) collective-permute-start(f32[2,8,4,128]{3,2,1,0:T(4,128)S(1)} %get-tuple-element.90), channel_id=1, source_target_pairs={{0,8},{8,16},{16,24},{1,9},{9,17},{17,25},{2,10},{10,18},{18,26},{... | collective-permute-start | bytes 98312 | tf_op jit(solution)/shard_map/ppermute | solution.py:19
  34.4 5.2 %collective-permute-start.6 = (f32[2,8,4,128]{3,2,1,0:T(4,128)S(1)}, f32[2,8,4,128]{3,2,1,0:T(4,128)S(1)}, u32[]{:S(2)}, u32[]{:S(2)}) collective-permute-start(f32[2,8,4,128]{3,2,1,0:T(4,128)S(1)} %get-tuple-element.91), channel_id=1, source_target_pairs={{8,0},{16,8},{24,16},{9,1},{17,9},{25,17},{10,2},{18,10},{26,18},{... | collective-permute-start | bytes 98312 | tf_op jit(solution)/shard_map/ppermute | solution.py:19
  39.8 6.9 %collective-permute-start.8 = (f32[2,8,8,4]{3,2,1,0:T(8,128)S(1)}, f32[2,8,8,4]{3,2,1,0:T(8,128)S(1)}, u32[]{:S(2)}, u32[]{:S(2)}) collective-permute-start(f32[2,8,8,4]{3,2,1,0:T(8,128)S(1)} %fusion.104), channel_id=1, source_target_pairs={{0,4},{4,0},{1,5},{5,1},{2,6},{6,2},{3,7},{7,3},{8,12},{12,8},{9,1... | collective-permute-start | bytes 6152 | tf_op jit(solution)/shard_map/ppermute | solution.py:14
  41.3 6.0 %collective-permute-start.10 = (f32[2,4,16,136]{3,2,1,0:T(8,128)S(1)}, f32[2,4,16,136]{3,2,1,0:T(8,128)S(1)}, u32[]{:S(2)}, u32[]{:S(2)}) collective-permute-start(f32[2,4,16,136]{3,2,1,0:T(8,128)S(1)} %get-tuple-element.70), channel_id=1, source_target_pairs={{1,0},{2,1},{3,2},{5,4},{6,5},{7,6},{9,8},{10,9},{11,10},{13,12},{... | collective-permute-start | bytes 208904 | tf_op jit(solution)/shard_map/ppermute | solution.py:19
  43.5 6.0 %collective-permute-start.11 = (f32[2,4,16,136]{3,2,1,0:T(8,128)S(1)}, f32[2,4,16,136]{3,2,1,0:T(8,128)S(1)}, u32[]{:S(2)}, u32[]{:S(2)}) collective-permute-start(f32[2,4,16,136]{3,2,1,0:T(8,128)S(1)} %get-tuple-element.71), channel_id=1, source_target_pairs={{0,1},{1,2},{2,3},{4,5},{5,6},{6,7},{8,9},{9,10},{10,11},{12,13},{... | collective-permute-start | bytes 208904 | tf_op jit(solution)/shard_map/ppermute | solution.py:19
  51.0 0.6 %copy-start.10 = (f32[8,8,128]{2,1,0:T(8,128)}, f32[8,8,128]{2,1,0:T(8,128)S(1)}, u32[]{:S(2)}) copy-start(f32[8,8,128]{2,1,0:T(8,128)S(1)} %get-tuple-element.116) | copy-start | bytes 98308
  51.1 0.6 %copy-start.11 = (f32[8,8,128]{2,1,0:T(8,128)}, f32[8,8,128]{2,1,0:T(8,128)S(1)}, u32[]{:S(2)}) copy-start(f32[8,8,128]{2,1,0:T(8,128)S(1)} %get-tuple-element.117) | copy-start | bytes 98308

commit v9 on v8

--- a/solution.py
+++ b/solution.py
@@ -14,6 +14,13 @@
         got = lax.ppermute(jnp.where(first, top, bottom), axis, [(0, 1), (1, 0)])
         empty = jnp.zeros_like(got)
         return jnp.where(first, empty, got), jnp.where(first, got, empty)
+    if count % 2 == 0:
+        even = lax.axis_index(axis) % 2 == 0
+        inner = [(i, i ^ 1) for i in range(count)]
+        outer = [(i, i + 1 if i % 2 else i - 1) for i in range(1, count - 1)]
+        got_inner = lax.ppermute(jnp.where(even, top, bottom), axis, inner)
+        got_outer = lax.ppermute(jnp.where(even, bottom, top), axis, outer)
+        return jnp.where(even, got_outer, got_inner), jnp.where(even, got_inner, got_outer)
     forward = [(i, i + 1) for i in range(count - 1)]
     backward = [(target, source) for source, target in forward]
     return lax.ppermute(top, axis, forward), lax.ppermute(bottom, axis, backward)

time: 52.2 us -> 45.9 us (0.88)
  starting transfers between devices: 32.4 us -> 23.4 us
  waiting for transfers between devices: 7.37 us -> 8.83 us
  local copies, waits for them, and re-layouts: 3.65 us -> 4.38 us
    ppermute x8, starting transfers between devices: 23.5 us -> 14.5 us  [the longest x4 12.3 us: shift_pair(): got_outer = lax.ppermute(jnp.where(even, bottom, top), axis, outer)]
    ppermute x8, waiting for transfers between devices: 7.36 us -> 8.53 us  [the longest x4 5.92 us: shift_pair(): got_outer = lax.ppermute(jnp.where(even, bottom, top), axis, outer)]
    select_n x0 -> x8, other arithmetic: none -> 1.06 us  [the longest x3 1 us: shift_pair(): got_inner = lax.ppermute(jnp.where(even, top, bottom), axis, inner)]
    another operation x2 -> x0, other arithmetic: 0.88 us -> none  [the longest x1 0.87 us: local(): current = jnp.stack([wave_p, wave_q])]
    unnamed x43, local copies, waits for them, and re-layouts: 2.58 us -> 3.35 us
  transfers between devices with their start and end apart: 13 -> 13, of which waited for: 4 -> 6; matrix products, arithmetic and copies ran while one was open for 6% -> 7% of each run, Pallas kernels for 0% -> 0%
where the time goes in v9:
time: 45.9 us; the launch traced here: 45.1 us
  starting transfers between devices  23.4 us (51%)
  waiting for transfers between devices  8.83 us (19%)
  other arithmetic  5.65 us (12%)
  local copies, waits for them, and re-layouts  4.38 us (10%)
  matrix products  1.52 us (3%)
  between operations  1.32 us (3%)
    ppermute x4, starting transfers between devices, shift_pair(): got_outer = lax.ppermute(jnp.where(even, bottom, top), axis, outer)  12.3 us
    ppermute x4, waiting for transfers between devices, shift_pair(): got_outer = lax.ppermute(jnp.where(even, bottom, top), axis, outer)  5.92 us
    all_to_all x1, starting transfers between devices, local(): lax.all_to_all(send, ('inl', 'xl', 'gz'), split_axis=0, concat_axis=0, ti...  4.84 us
    ppermute x4, starting transfers between devices, shift_pair(): got = lax.ppermute(jnp.where(first, top, bottom), axis, [(0, 1), (1, 0)])  4.12 us
    unnamed x43, local copies, waits for them, and re-layouts  3.35 us
    ppermute x4, waiting for transfers between devices, shift_pair(): got_inner = lax.ppermute(jnp.where(even, top, bottom), axis, inner)  2.61 us
    ppermute x4, starting transfers between devices, shift_pair(): got_inner = lax.ppermute(jnp.where(even, top, bottom), axis, inner)  2.19 us
    sub x2, other arithmetic, advance(): h_two = u_xx + u_yy + u_zz - h_one  1.39 us
  transfers between devices with their start and end apart: 13, of which 6 were waited for; matrix products, arithmetic and copies ran while one was open for 7% of the time, Pallas kernels for 0%

profile of v9, /device:TPU:17, one launch (start us, length us, event | category | flops | bytes accessed | tf_op | source)
XLA Modules:
  0.0 45.1 jit_solution(8015494152854008833)
XLA Ops:
  0.6 0.0 copy-start
  0.7 0.8 %copy-done.3 = f32[8,8,128]{2,1,0:T(8,128)S(1)} copy-done((f32[8,8,128]{2,1,0:T(8,128)S(1)}, f32[8,8,128]{2,1,0:T(8,128)}, u32[]{:S(2)}) %copy-start.3) | copy-done | bytes 32792
  1.4 1.0 %broadcast_select_fusion.18 = (f32[2,8,4,128]{3,2,1,0:T(4,128)S(1)}, f32[2,8,4,128]{3,2,1,0:T(4,128)S(1)}) fusion(pred[]{:T(512)S(6)} %eq.120, f32[1,8,8,128]{3,2,1,0:T(8,128)} %bitcast.139, f32[1,8,8,128]{3,2,1,0:T(8,128)S(1)} %bitcast.132), kind=kLoop, calls=%fused_computation.388 | loop fusion | flops 49152 | bytes 131073 | tf_op jit(solution)/shard_map/jit(_where)/select_n | solution.py:21
  2.4 0.7 %collective-permute-start.1 = (f32[2,8,4,128]{3,2,1,0:T(4,128)S(1)}, f32[2,8,4,128]{3,2,1,0:T(4,128)S(1)}, u32[]{:S(2)}, u32[]{:S(2)}) collective-permute-start(f32[2,8,4,128]{3,2,1,0:T(4,128)S(1)} %get-tuple-element.117), channel_id=1, source_target_pairs={{0,8},{8,0},{16,24},{24,16},{1,9},{9,1},{17,25},{25,17},{2,10},{10... | collective-permute-start | bytes 98312 | tf_op jit(solution)/shard_map/ppermute | solution.py:21
  3.1 3.0 %collective-permute-start = (f32[2,8,4,128]{3,2,1,0:T(4,128)S(1)}, f32[2,8,4,128]{3,2,1,0:T(4,128)S(1)}, u32[]{:S(2)}, u32[]{:S(2)}) collective-permute-start(f32[2,8,4,128]{3,2,1,0:T(4,128)S(1)} %get-tuple-element.118), channel_id=1, source_target_pairs={{8,16},{16,8},{9,17},{17,9},{10,18},{18,10},{11,19},{19,11},{12,20... | collective-permute-start | bytes 98312 | tf_op jit(solution)/shard_map/ppermute | solution.py:22
  6.2 0.0 copy-start.20
  6.2 0.1 fusion.53
  6.3 1.3 %collective-permute-start.2 = (f32[2,8,8,4]{3,2,1,0:T(8,128)S(1)}, f32[2,8,8,4]{3,2,1,0:T(8,128)S(1)}, u32[]{:S(2)}, u32[]{:S(2)}) collective-permute-start(f32[2,8,8,4]{3,2,1,0:T(8,128)S(1)} %fusion.53), channel_id=1, source_target_pairs={{0,4},{4,0},{1,5},{5,1},{2,6},{6,2},{3,7},{7,3},{8,12},{12,8},{9,1... | collective-permute-start | bytes 6152 | tf_op jit(solution)/shard_map/ppermute | solution.py:14
  7.6 0.1 select_reduce_fusion
  7.7 0.6 %copy-done.16 = f32[2,256]{1,0:T(2,128)S(1)} copy-done((f32[2,256]{1,0:T(2,128)S(1)}, f32[2,256]{1,0:T(2,128)}, u32[]{:S(2)}) %copy-start.16) | copy-done | bytes 2072
  8.3 0.3 convolution_multiply_fusion
  8.6 0.1 copy-start.18
  8.6 0.7 %copy-done.17 = s32[256]{0:T(256)S(1)} copy-done((s32[256]{0:T(256)S(1)}, s32[256]{0:T(256)}, u32[]{:S(2)}) %copy-start.17) | copy-done | bytes 1048
  9.3 0.0 copy-done.18
  9.3 0.0 copy-start.13
  9.4 0.2 fusion
  9.6 0.5 %copy-done.12 = f32[8,8,128]{2,1,0:T(8,128)S(1)} copy-done((f32[8,8,128]{2,1,0:T(8,128)S(1)}, f32[8,8,128]{2,1,0:T(8,128)}, u32[]{:S(2)}) %copy-start.12) | copy-done | bytes 32792
  10.1 0.0 copy-done.13
  10.1 0.2 fusion.224
  10.4 0.4 fusion.18
  10.9 0.1 fusion.161
  11.1 0.6 %copy.42 = f32[32,1,192]{2,1,0:T(1,128)} copy(f32[32,1,192]{2,0,1:T(8,128)S(1)} %bitcast.174) | data formatting | bytes 49152 | tf_op jit(solution)/shard_map/all_to_all | solution.py:208
  11.7 4.8 %all-to-all-start = ((f32[32,1,192]{2,1,0:T(1,128)}), f32[32,1,192]{2,1,0:T(1,128)S(1)}, u32[]{:S(2)}, u32[]{:S(2)}) async-start(f32[32,1,192]{2,1,0:T(1,128)} %copy.42), calls=%async_computation | async-start | bytes 65536 | tf_op jit(solution)/shard_map/all_to_all | solution.py:208
  16.6 1.2 %collective-permute-start.3 = (f32[2,8,8,4]{3,2,1,0:T(8,128)S(1)}, f32[2,8,8,4]{3,2,1,0:T(8,128)S(1)}, u32[]{:S(2)}, u32[]{:S(2)}) collective-permute-start(f32[2,8,8,4]{3,2,1,0:T(8,128)S(1)} %fusion.161), channel_id=1, source_target_pairs={{0,4},{4,0},{1,5},{5,1},{2,6},{6,2},{3,7},{7,3},{8,12},{12,8},{9,1... | collective-permute-start | bytes 6152 | tf_op jit(solution)/shard_map/ppermute | solution.py:14
  17.8 0.2 select_maximum_fusion.2
  18.1 1.3 %collective-permute-start.4 = (f32[2,4,16,136]{3,2,1,0:T(8,128)S(1)}, f32[2,4,16,136]{3,2,1,0:T(8,128)S(1)}, u32[]{:S(2)}, u32[]{:S(2)}) collective-permute-start(f32[2,4,16,136]{3,2,1,0:T(8,128)S(1)} %get-tuple-element.76), channel_id=1, source_target_pairs={{0,1},{1,0},{2,3},{3,2},{4,5},{5,4},{6,7},{7,6},{8,9},{9,8},{10,11... | collective-permute-start | bytes 208904 | tf_op jit(solution)/shard_map/ppermute | solution.py:21
  19.4 1.9 %collective-permute-start.5 = (f32[2,4,16,136]{3,2,1,0:T(8,128)S(1)}, f32[2,4,16,136]{3,2,1,0:T(8,128)S(1)}, u32[]{:S(2)}, u32[]{:S(2)}) collective-permute-start(f32[2,4,16,136]{3,2,1,0:T(8,128)S(1)} %get-tuple-element.77), channel_id=1, source_target_pairs={{1,2},{2,1},{5,6},{6,5},{9,10},{10,9},{13,14},{14,13},{17,18},{18,... | collective-permute-start | bytes 208904 | tf_op jit(solution)/shard_map/ppermute | solution.py:22
  21.4 0.2 maximum_maximum_fusion
  21.7 0.1 reshape.205
  21.8 0.6 %convolution_bitcast_fusion = f32[16,128]{1,0:T(8,128)S(1)} fusion(s32[32,64]{1,0:T(8,128)S(1)} %add_select_fusion, f32[8,32,64]{2,0,1:T(8,128)S(1)} %fusion.45, f32[2,32,64]{2,0,1:T(2,128)S(1)} %bitcast.173), kind=kOutput, calls=%fused_computation.1 | convolution fusion | flops 50626560 | bytes 98304 | tf_op jit(solution)/shard_map/dot_general | solution.py:221
  22.4 0.1 collective-permute-done.4
  22.5 2.5 %collective-permute-done.5 = f32[2,4,16,136]{3,2,1,0:T(8,128)S(1)} collective-permute-done((f32[2,4,16,136]{3,2,1,0:T(8,128)S(1)}, f32[2,4,16,136]{3,2,1,0:T(8,128)S(1)}, u32[]{:S(2)}, u32[]{:S(2)}) %collective-permute-start.5) | collective-permute-done | bytes 69664 | tf_op jit(solution)/shard_map/ppermute | solution.py:22
  25.1 0.3 pad_maximum_fusion
  25.4 0.3 fusion.31
  25.7 0.2 fusion.10
  25.9 0.0 copy-start.7
  25.9 0.0 copy-start.8
  26.0 0.0 copy-start.14
  26.0 0.7 %add_subtract_fusion.1 = (f32[2,8,8,128]{3,2,1,0:T(8,128)S(1)}, f32[2,8,8,128]{3,2,1,0:T(8,128)S(1)}) fusion(f32[2,16,8,128]{3,2,1,0:T(8,128)S(1)} %fusion.31, f32[8,8,128]{2,1,0:T(8,128)S(1)} %get-tuple-element.102, f32[2,16,8,136]{3,2,1,0:T(8,128)S(1)} %fusion.10, f32[8,8,128]{2,1,0:T(8,128)S(1)} %get-tuple-element.103, ...), kind=kLoop, calls=%fused_computation.312 | loop fusion | flops 2703360 | bytes 3227648 | tf_op jit(solution)/shard_map/sub | solution.py:129
  26.8 0.0 copy-done.14
  26.8 0.0 copy-done.15
  26.8 0.0 copy-start.2
  26.9 0.1 fusion.49
  26.9 0.3 collective-permute-start.9
  27.3 5.4 %collective-permute-start.7 = (f32[2,8,4,128]{3,2,1,0:T(4,128)S(1)}, f32[2,8,4,128]{3,2,1,0:T(4,128)S(1)}, u32[]{:S(2)}, u32[]{:S(2)}) collective-permute-start(f32[2,8,4,128]{3,2,1,0:T(4,128)S(1)} %get-tuple-element.96), channel_id=1, source_target_pairs={{8,16},{16,8},{9,17},{17,9},{10,18},{18,10},{11,19},{19,11},{12,20... | collective-permute-start | bytes 98312 | tf_op jit(solution)/shard_map/ppermute | solution.py:22
  32.7 0.1 collective-permute-start.6
  32.8 1.5 %collective-permute-done.7 = f32[2,8,4,128]{3,2,1,0:T(4,128)S(1)} collective-permute-done((f32[2,8,4,128]{3,2,1,0:T(4,128)S(1)}, f32[2,8,4,128]{3,2,1,0:T(4,128)S(1)}, u32[]{:S(2)}, u32[]{:S(2)}) %collective-permute-start.7) | collective-permute-done | bytes 32800 | tf_op jit(solution)/shard_map/ppermute | solution.py:22
  34.3 0.1 fusion.104
  34.4 1.3 %collective-permute-start.8 = (f32[2,8,8,4]{3,2,1,0:T(8,128)S(1)}, f32[2,8,8,4]{3,2,1,0:T(8,128)S(1)}, u32[]{:S(2)}, u32[]{:S(2)}) collective-permute-start(f32[2,8,8,4]{3,2,1,0:T(8,128)S(1)} %fusion.104), channel_id=1, source_target_pairs={{0,4},{4,0},{1,5},{5,1},{2,6},{6,2},{3,7},{7,3},{8,12},{12,8},{9,1... | collective-permute-start | bytes 6152 | tf_op jit(solution)/shard_map/ppermute | solution.py:14
  35.7 0.2 select_maximum_fusion
  36.0 0.1 collective-permute-start.10
  36.0 1.9 %collective-permute-start.11 = (f32[2,4,16,136]{3,2,1,0:T(8,128)S(1)}, f32[2,4,16,136]{3,2,1,0:T(8,128)S(1)}, u32[]{:S(2)}, u32[]{:S(2)}) collective-permute-start(f32[2,4,16,136]{3,2,1,0:T(8,128)S(1)} %get-tuple-element.73), channel_id=1, source_target_pairs={{1,2},{2,1},{5,6},{6,5},{9,10},{10,9},{13,14},{14,13},{17,18},{18,... | collective-permute-start | bytes 208904 | tf_op jit(solution)/shard_map/ppermute | solution.py:22
  38.0 0.3 collective-permute-done.8
  38.3 0.2 maximum_maximum_fusion.2
  38.5 2.5 %collective-permute-done.10 = f32[2,4,16,136]{3,2,1,0:T(8,128)S(1)} collective-permute-done((f32[2,4,16,136]{3,2,1,0:T(8,128)S(1)}, f32[2,4,16,136]{3,2,1,0:T(8,128)S(1)}, u32[]{:S(2)}, u32[]{:S(2)}) %collective-permute-start.10) | collective-permute-done | bytes 69664 | tf_op jit(solution)/shard_map/ppermute | solution.py:21
  41.0 1.9 %collective-permute-done.11 = f32[2,4,16,136]{3,2,1,0:T(8,128)S(1)} collective-permute-done((f32[2,4,16,136]{3,2,1,0:T(8,128)S(1)}, f32[2,4,16,136]{3,2,1,0:T(8,128)S(1)}, u32[]{:S(2)}, u32[]{:S(2)}) %collective-permute-start.11) | collective-permute-done | bytes 69664 | tf_op jit(solution)/shard_map/ppermute | solution.py:22
  42.9 0.3 pad_maximum_fusion.1
  43.2 0.3 fusion.24
  43.5 0.2 fusion.3
  43.7 0.7 %add_subtract_fusion = (f32[2,8,8,128]{3,2,1,0:T(8,128)S(1)}, f32[2,8,8,128]{3,2,1,0:T(8,128)S(1)}) fusion(f32[2,16,8,128]{3,2,1,0:T(8,128)S(1)} %fusion.24, f32[8,8,128]{2,1,0:T(8,128)S(1)} %get-tuple-element.102, f32[2,16,8,136]{3,2,1,0:T(8,128)S(1)} %fusion.3, f32[8,8,128]{2,1,0:T(8,128)S(1)} %get-tuple-element.103, ...), kind=kLoop, calls=%fused_computation.311 | loop fusion | flops 2703360 | bytes 3227648 | tf_op jit(solution)/shard_map/sub | solution.py:129
  44.5 0.0 copy-start.10
  44.5 0.0 copy-start.11
  44.5 0.6 %copy-done.10 = f32[8,8,128]{2,1,0:T(8,128)} copy-done((f32[8,8,128]{2,1,0:T(8,128)}, f32[8,8,128]{2,1,0:T(8,128)S(1)}, u32[]{:S(2)}) %copy-start.10) | copy-done | bytes 32792
  45.1 0.0 copy-done.11
  (61 shorter events, 0.5 us)
Async XLA Ops:
  0.6 7.1 %copy-start = (f32[256,256]{1,0:T(8,128)S(1)}, f32[256,256]{1,0:T(8,128)}, u32[]{:S(2)}) copy-start(f32[256,256]{1,0:T(8,128)} %param.36) | copy-start | bytes 786436
  0.6 0.8 %copy-start.3 = (f32[8,8,128]{2,1,0:T(8,128)S(1)}, f32[8,8,128]{2,1,0:T(8,128)}, u32[]{:S(2)}) copy-start(f32[8,8,128]{2,1,0:T(8,128)} %param.25) | copy-start | bytes 98308
  1.4 4.8 %copy-start.4 = (f32[8,8,128]{2,1,0:T(8,128)S(1)}, f32[8,8,128]{2,1,0:T(8,128)}, u32[]{:S(2)}) copy-start(f32[8,8,128]{2,1,0:T(8,128)} %param.27) | copy-start | bytes 98308
  2.4 8.5 %collective-permute-start.1 = (f32[2,8,4,128]{3,2,1,0:T(4,128)S(1)}, f32[2,8,4,128]{3,2,1,0:T(4,128)S(1)}, u32[]{:S(2)}, u32[]{:S(2)}) collective-permute-start(f32[2,8,4,128]{3,2,1,0:T(4,128)S(1)} %get-tuple-element.117), channel_id=1, source_target_pairs={{0,8},{8,0},{16,24},{24,16},{1,9},{9,1},{17,25},{25,17},{2,10},{10... | collective-permute-start | bytes 98312 | tf_op jit(solution)/shard_map/ppermute | solution.py:21
  3.1 7.7 %collective-permute-start = (f32[2,8,4,128]{3,2,1,0:T(4,128)S(1)}, f32[2,8,4,128]{3,2,1,0:T(4,128)S(1)}, u32[]{:S(2)}, u32[]{:S(2)}) collective-permute-start(f32[2,8,4,128]{3,2,1,0:T(4,128)S(1)} %get-tuple-element.118), channel_id=1, source_target_pairs={{8,16},{16,8},{9,17},{17,9},{10,18},{18,10},{11,19},{19,11},{12,20... | collective-permute-start | bytes 98312 | tf_op jit(solution)/shard_map/ppermute | solution.py:22
  6.2 1.4 %copy-start.19 = (s32[256]{0:T(256)S(1)}, s32[256]{0:T(256)}, u32[]{:S(2)}) copy-start(s32[256]{0:T(256)} %param.41) | copy-start | bytes 3076
  6.2 1.4 %copy-start.20 = (f32[64]{0:T(128)S(1)}, f32[64]{0:T(128)}, u32[]{:S(2)}) copy-start(f32[64]{0:T(128)} %param.38) | copy-start | bytes 772
  6.3 4.5 %collective-permute-start.2 = (f32[2,8,8,4]{3,2,1,0:T(8,128)S(1)}, f32[2,8,8,4]{3,2,1,0:T(8,128)S(1)}, u32[]{:S(2)}, u32[]{:S(2)}) collective-permute-start(f32[2,8,8,4]{3,2,1,0:T(8,128)S(1)} %fusion.53), channel_id=1, source_target_pairs={{0,4},{4,0},{1,5},{5,1},{2,6},{6,2},{3,7},{7,3},{8,12},{12,8},{9,1... | collective-permute-start | bytes 6152 | tf_op jit(solution)/shard_map/ppermute | solution.py:14
  7.6 0.7 %copy-start.16 = (f32[2,256]{1,0:T(2,128)S(1)}, f32[2,256]{1,0:T(2,128)}, u32[]{:S(2)}) copy-start(f32[2,256]{1,0:T(2,128)} %param.37) | copy-start | bytes 6148
  8.6 0.7 %copy-start.17 = (s32[256]{0:T(256)S(1)}, s32[256]{0:T(256)}, u32[]{:S(2)}) copy-start(s32[256]{0:T(256)} %param.40) | copy-start | bytes 3076
  8.6 0.8 %copy-start.18 = (s32[256]{0:T(256)S(1)}, s32[256]{0:T(256)}, u32[]{:S(2)}) copy-start(s32[256]{0:T(256)} %param.39) | copy-start | bytes 3076
  9.3 0.8 %copy-start.12 = (f32[8,8,128]{2,1,0:T(8,128)S(1)}, f32[8,8,128]{2,1,0:T(8,128)}, u32[]{:S(2)}) copy-start(f32[8,8,128]{2,1,0:T(8,128)} %param.33) | copy-start | bytes 98308
  9.3 0.8 %copy-start.13 = (f32[8,8,128]{2,1,0:T(8,128)S(1)}, f32[8,8,128]{2,1,0:T(8,128)}, u32[]{:S(2)}) copy-start(f32[8,8,128]{2,1,0:T(8,128)} %param.32) | copy-start | bytes 98308
  11.7 9.9 %all-to-all-start = ((f32[32,1,192]{2,1,0:T(1,128)}), f32[32,1,192]{2,1,0:T(1,128)S(1)}, u32[]{:S(2)}, u32[]{:S(2)}) async-start(f32[32,1,192]{2,1,0:T(1,128)} %copy.42), calls=%async_computation | async-start | bytes 65536 | tf_op jit(solution)/shard_map/all_to_all | solution.py:208
  16.6 4.8 %collective-permute-start.3 = (f32[2,8,8,4]{3,2,1,0:T(8,128)S(1)}, f32[2,8,8,4]{3,2,1,0:T(8,128)S(1)}, u32[]{:S(2)}, u32[]{:S(2)}) collective-permute-start(f32[2,8,8,4]{3,2,1,0:T(8,128)S(1)} %fusion.161), channel_id=1, source_target_pairs={{0,4},{4,0},{1,5},{5,1},{2,6},{6,2},{3,7},{7,3},{8,12},{12,8},{9,1... | collective-permute-start | bytes 6152 | tf_op jit(solution)/shard_map/ppermute | solution.py:14
  18.1 4.5 %collective-permute-start.4 = (f32[2,4,16,136]{3,2,1,0:T(8,128)S(1)}, f32[2,4,16,136]{3,2,1,0:T(8,128)S(1)}, u32[]{:S(2)}, u32[]{:S(2)}) collective-permute-start(f32[2,4,16,136]{3,2,1,0:T(8,128)S(1)} %get-tuple-element.76), channel_id=1, source_target_pairs={{0,1},{1,0},{2,3},{3,2},{4,5},{5,4},{6,7},{7,6},{8,9},{9,8},{10,11... | collective-permute-start | bytes 208904 | tf_op jit(solution)/shard_map/ppermute | solution.py:21
  19.4 5.7 %collective-permute-start.5 = (f32[2,4,16,136]{3,2,1,0:T(8,128)S(1)}, f32[2,4,16,136]{3,2,1,0:T(8,128)S(1)}, u32[]{:S(2)}, u32[]{:S(2)}) collective-permute-start(f32[2,4,16,136]{3,2,1,0:T(8,128)S(1)} %get-tuple-element.77), channel_id=1, source_target_pairs={{1,2},{2,1},{5,6},{6,5},{9,10},{10,9},{13,14},{14,13},{17,18},{18,... | collective-permute-start | bytes 208904 | tf_op jit(solution)/shard_map/ppermute | solution.py:22
  25.9 0.8 %copy-start.5 = (f32[8,8,128]{2,1,0:T(8,128)S(1)}, f32[8,8,128]{2,1,0:T(8,128)}, u32[]{:S(2)}) copy-start(f32[8,8,128]{2,1,0:T(8,128)} %param.29) | copy-start | bytes 98308
  25.9 0.8 %copy-start.6 = (f32[8,8,128]{2,1,0:T(8,128)S(1)}, f32[8,8,128]{2,1,0:T(8,128)}, u32[]{:S(2)}) copy-start(f32[8,8,128]{2,1,0:T(8,128)} %param.34) | copy-start | bytes 98308
  25.9 0.8 %copy-start.7 = (f32[8,8,128]{2,1,0:T(8,128)S(1)}, f32[8,8,128]{2,1,0:T(8,128)}, u32[]{:S(2)}) copy-start(f32[8,8,128]{2,1,0:T(8,128)} %param.35) | copy-start | bytes 98308
  25.9 0.8 %copy-start.8 = (f32[8,8,128]{2,1,0:T(8,128)S(1)}, f32[8,8,128]{2,1,0:T(8,128)}, u32[]{:S(2)}) copy-start(f32[8,8,128]{2,1,0:T(8,128)} %param.31) | copy-start | bytes 98308
  26.0 0.8 %copy-start.9 = (f32[8,8,128]{2,1,0:T(8,128)S(1)}, f32[8,8,128]{2,1,0:T(8,128)}, u32[]{:S(2)}) copy-start(f32[8,8,128]{2,1,0:T(8,128)} %param.30) | copy-start | bytes 98308
  26.0 0.8 %copy-start.14 = (f32[8,8,128]{2,1,0:T(8,128)S(1)}, f32[8,8,128]{2,1,0:T(8,128)}, u32[]{:S(2)}) copy-start(f32[8,8,128]{2,1,0:T(8,128)} %param.28) | copy-start | bytes 98308
  26.0 0.8 %copy-start.15 = (f32[8,8,128]{2,1,0:T(8,128)S(1)}, f32[8,8,128]{2,1,0:T(8,128)}, u32[]{:S(2)}) copy-start(f32[8,8,128]{2,1,0:T(8,128)} %param.26) | copy-start | bytes 98308
  26.8 17.6 %copy-start.1 = (f32[8,8,128]{2,1,0:T(8,128)}, f32[8,8,128]{2,1,0:T(8,128)S(1)}, u32[]{:S(2)}) copy-start(f32[8,8,128]{2,1,0:T(8,128)S(1)} %get-tuple-element.126) | copy-start | bytes 98308
  26.8 17.6 %copy-start.2 = (f32[8,8,128]{2,1,0:T(8,128)}, f32[8,8,128]{2,1,0:T(8,128)S(1)}, u32[]{:S(2)}) copy-start(f32[8,8,128]{2,1,0:T(8,128)S(1)} %get-tuple-element.127) | copy-start | bytes 98308
  26.9 5.8 %collective-permute-start.9 = (f32[2,8,8,4]{3,2,1,0:T(8,128)S(1)}, f32[2,8,8,4]{3,2,1,0:T(8,128)S(1)}, u32[]{:S(2)}, u32[]{:S(2)}) collective-permute-start(f32[2,8,8,4]{3,2,1,0:T(8,128)S(1)} %fusion.49), channel_id=1, source_target_pairs={{0,4},{4,0},{1,5},{5,1},{2,6},{6,2},{3,7},{7,3},{8,12},{12,8},{9,1... | collective-permute-start | bytes 6152 | tf_op jit(solution)/shard_map/ppermute | solution.py:14
  27.3 7.0 %collective-permute-start.7 = (f32[2,8,4,128]{3,2,1,0:T(4,128)S(1)}, f32[2,8,4,128]{3,2,1,0:T(4,128)S(1)}, u32[]{:S(2)}, u32[]{:S(2)}) collective-permute-start(f32[2,8,4,128]{3,2,1,0:T(4,128)S(1)} %get-tuple-element.96), channel_id=1, source_target_pairs={{8,16},{16,8},{9,17},{17,9},{10,18},{18,10},{11,19},{19,11},{12,20... | collective-permute-start | bytes 98312 | tf_op jit(solution)/shard_map/ppermute | solution.py:22
  32.7 1.6 %collective-permute-start.6 = (f32[2,8,4,128]{3,2,1,0:T(4,128)S(1)}, f32[2,8,4,128]{3,2,1,0:T(4,128)S(1)}, u32[]{:S(2)}, u32[]{:S(2)}) collective-permute-start(f32[2,8,4,128]{3,2,1,0:T(4,128)S(1)} %get-tuple-element.97), channel_id=1, source_target_pairs={{0,8},{8,0},{16,24},{24,16},{1,9},{9,1},{17,25},{25,17},{2,10},{10... | collective-permute-start | bytes 98312 | tf_op jit(solution)/shard_map/ppermute | solution.py:21
  34.4 3.9 %collective-permute-start.8 = (f32[2,8,8,4]{3,2,1,0:T(8,128)S(1)}, f32[2,8,8,4]{3,2,1,0:T(8,128)S(1)}, u32[]{:S(2)}, u32[]{:S(2)}) collective-permute-start(f32[2,8,8,4]{3,2,1,0:T(8,128)S(1)} %fusion.104), channel_id=1, source_target_pairs={{0,4},{4,0},{1,5},{5,1},{2,6},{6,2},{3,7},{7,3},{8,12},{12,8},{9,1... | collective-permute-start | bytes 6152 | tf_op jit(solution)/shard_map/ppermute | solution.py:14
  36.0 5.0 %collective-permute-start.10 = (f32[2,4,16,136]{3,2,1,0:T(8,128)S(1)}, f32[2,4,16,136]{3,2,1,0:T(8,128)S(1)}, u32[]{:S(2)}, u32[]{:S(2)}) collective-permute-start(f32[2,4,16,136]{3,2,1,0:T(8,128)S(1)} %get-tuple-element.72), channel_id=1, source_target_pairs={{0,1},{1,0},{2,3},{3,2},{4,5},{5,4},{6,7},{7,6},{8,9},{9,8},{10,11... | collective-permute-start | bytes 208904 | tf_op jit(solution)/shard_map/ppermute | solution.py:21
  36.0 6.9 %collective-permute-start.11 = (f32[2,4,16,136]{3,2,1,0:T(8,128)S(1)}, f32[2,4,16,136]{3,2,1,0:T(8,128)S(1)}, u32[]{:S(2)}, u32[]{:S(2)}) collective-permute-start(f32[2,4,16,136]{3,2,1,0:T(8,128)S(1)} %get-tuple-element.73), channel_id=1, source_target_pairs={{1,2},{2,1},{5,6},{6,5},{9,10},{10,9},{13,14},{14,13},{17,18},{18,... | collective-permute-start | bytes 208904 | tf_op jit(solution)/shard_map/ppermute | solution.py:22
  44.5 0.6 %copy-start.10 = (f32[8,8,128]{2,1,0:T(8,128)}, f32[8,8,128]{2,1,0:T(8,128)S(1)}, u32[]{:S(2)}) copy-start(f32[8,8,128]{2,1,0:T(8,128)S(1)} %get-tuple-element.124) | copy-start | bytes 98308
  44.5 0.6 %copy-start.11 = (f32[8,8,128]{2,1,0:T(8,128)}, f32[8,8,128]{2,1,0:T(8,128)S(1)}, u32[]{:S(2)}) copy-start(f32[8,8,128]{2,1,0:T(8,128)S(1)} %get-tuple-element.125) | copy-start | bytes 98308

commit v10 on v9

--- a/solution.py
+++ b/solution.py
@@ -191,13 +191,16 @@
     order = jnp.arange(traces, dtype=jnp.int32)
     earlier = (order[:, None] > order[None, :]).astype(jnp.float32)
     rank = jnp.sum(jnp.dot(earlier, in_column, precision=highest) * in_column, axis=1)
-    lane = jnp.arange(3 * capacity, dtype=jnp.int32)[None, :]
+    lanes = 128 if 3 * capacity > 128 else 3 * capacity
+    rows = -(-3 * capacity // lanes)
+    lane = jnp.arange(rows * lanes, dtype=jnp.int32)[None, :]
     value = jnp.where(
         lane < capacity,
         payload[:, 0:1],
         jnp.where(lane < 2 * capacity, payload[:, 1:2], local_cell.astype(jnp.float32)[:, None]),
     )
-    spread = jnp.where(rank.astype(jnp.int32)[:, None] == lane % capacity, value, 0.0)
+    hit = (rank.astype(jnp.int32)[:, None] == lane % capacity) & (lane < 3 * capacity)
+    spread = jnp.where(hit, value, 0.0)
     to_device = (
         (owner * gz_count)[:, None] == jnp.arange(devices, dtype=jnp.int32)[None, :]
     ).astype(jnp.float32)
@@ -205,9 +208,11 @@
     current = jnp.stack([wave_p, wave_q])
     faces = first_round(current, 4)
     send, faces = lax.optimization_barrier((send, faces))
+    send = send.reshape(devices, rows, lanes)
     arrived = lax.all_to_all(send, ("inl", "xl", "gz"), split_axis=0, concat_axis=0, tiled=True)
+    arrived = arrived.reshape(devices, rows * lanes)
     amp = arrived[:, : steps * capacity].reshape(devices, steps, capacity)
-    cell = (arrived[:, steps * capacity :] + 0.5).astype(jnp.int32)
+    cell = (arrived[:, steps * capacity : 3 * capacity] + 0.5).astype(jnp.int32)
     row_hit = (
         cell[None, :, :] // cross_cells
         == jnp.arange(inline_cells, dtype=jnp.int32)[:, None, None]

time: 45.9 us -> 45.8 us (level)
    all_to_all x1 -> x0, local copies, waits for them, and re-layouts: 0.65 us -> none  [local(): lax.all_to_all(send, ('inl', 'xl', 'gz'), split_axis=0, concat_axis=0, ti...]
    reshape x0 -> x1, local copies, waits for them, and re-layouts: none -> 0.63 us  [local(): send = send.reshape(devices, rows, lanes)]
where the time goes in v10:
time: 45.8 us; the launch traced here: 45.1 us
  starting transfers between devices  23.3 us (51%)
  waiting for transfers between devices  8.83 us (19%)
  other arithmetic  5.65 us (12%)
  local copies, waits for them, and re-layouts  4.44 us (10%)
  matrix products  1.53 us (3%)
  between operations  1.32 us (3%)
    ppermute x4, starting transfers between devices, shift_pair(): got_outer = lax.ppermute(jnp.where(even, bottom, top), axis, outer)  12.3 us
    ppermute x4, waiting for transfers between devices, shift_pair(): got_outer = lax.ppermute(jnp.where(even, bottom, top), axis, outer)  5.92 us
    all_to_all x1, starting transfers between devices, local(): lax.all_to_all(send, ('inl', 'xl', 'gz'), split_axis=0, concat_axis=0, ti...  4.74 us
    ppermute x4, starting transfers between devices, shift_pair(): got = lax.ppermute(jnp.where(first, top, bottom), axis, [(0, 1), (1, 0)])  4.12 us
    unnamed x43, local copies, waits for them, and re-layouts  3.42 us
    ppermute x4, waiting for transfers between devices, shift_pair(): got_inner = lax.ppermute(jnp.where(even, top, bottom), axis, inner)  2.61 us
    ppermute x4, starting transfers between devices, shift_pair(): got_inner = lax.ppermute(jnp.where(even, top, bottom), axis, inner)  2.19 us
    sub x2, other arithmetic, advance(): h_two = u_xx + u_yy + u_zz - h_one  1.39 us
  transfers between devices with their start and end apart: 13, of which 6 were waited for; matrix products, arithmetic and copies ran while one was open for 7% of the time, Pallas kernels for 0%

profile of v10, /device:TPU:17, one launch (start us, length us, event | category | flops | bytes accessed | tf_op | source)
XLA Modules:
  0.0 45.1 jit_solution(12719740136229599688)
XLA Ops:
  0.6 0.0 copy-start
  0.7 0.8 %copy-done.3 = f32[8,8,128]{2,1,0:T(8,128)S(1)} copy-done((f32[8,8,128]{2,1,0:T(8,128)S(1)}, f32[8,8,128]{2,1,0:T(8,128)}, u32[]{:S(2)}) %copy-start.3) | copy-done | bytes 32792
  1.4 1.0 %broadcast_select_fusion.18 = (f32[2,8,4,128]{3,2,1,0:T(4,128)S(1)}, f32[2,8,4,128]{3,2,1,0:T(4,128)S(1)}) fusion(pred[]{:T(512)S(6)} %eq.120, f32[1,8,8,128]{3,2,1,0:T(8,128)} %bitcast.139, f32[1,8,8,128]{3,2,1,0:T(8,128)S(1)} %bitcast.132), kind=kLoop, calls=%fused_computation.390 | loop fusion | flops 49152 | bytes 131073 | tf_op jit(solution)/shard_map/jit(_where)/select_n | solution.py:21
  2.4 0.7 %collective-permute-start.1 = (f32[2,8,4,128]{3,2,1,0:T(4,128)S(1)}, f32[2,8,4,128]{3,2,1,0:T(4,128)S(1)}, u32[]{:S(2)}, u32[]{:S(2)}) collective-permute-start(f32[2,8,4,128]{3,2,1,0:T(4,128)S(1)} %get-tuple-element.117), channel_id=1, source_target_pairs={{0,8},{8,0},{16,24},{24,16},{1,9},{9,1},{17,25},{25,17},{2,10},{10... | collective-permute-start | bytes 98312 | tf_op jit(solution)/shard_map/ppermute | solution.py:21
  3.1 3.0 %collective-permute-start = (f32[2,8,4,128]{3,2,1,0:T(4,128)S(1)}, f32[2,8,4,128]{3,2,1,0:T(4,128)S(1)}, u32[]{:S(2)}, u32[]{:S(2)}) collective-permute-start(f32[2,8,4,128]{3,2,1,0:T(4,128)S(1)} %get-tuple-element.118), channel_id=1, source_target_pairs={{8,16},{16,8},{9,17},{17,9},{10,18},{18,10},{11,19},{19,11},{12,20... | collective-permute-start | bytes 98312 | tf_op jit(solution)/shard_map/ppermute | solution.py:22
  6.2 0.1 fusion.55
  6.3 1.3 %collective-permute-start.2 = (f32[2,8,8,4]{3,2,1,0:T(8,128)S(1)}, f32[2,8,8,4]{3,2,1,0:T(8,128)S(1)}, u32[]{:S(2)}, u32[]{:S(2)}) collective-permute-start(f32[2,8,8,4]{3,2,1,0:T(8,128)S(1)} %fusion.55), channel_id=1, source_target_pairs={{0,4},{4,0},{1,5},{5,1},{2,6},{6,2},{3,7},{7,3},{8,12},{12,8},{9,1... | collective-permute-start | bytes 6152 | tf_op jit(solution)/shard_map/ppermute | solution.py:14
  7.6 0.0 copy-start.16
  7.6 0.6 %copy-done.19 = s32[256]{0:T(256)S(1)} copy-done((s32[256]{0:T(256)S(1)}, s32[256]{0:T(256)}, u32[]{:S(2)}) %copy-start.19) | copy-done | bytes 1048
  8.3 0.1 select_reduce_fusion
  8.4 0.3 convolution_multiply_fusion
  8.6 0.1 copy-start.18
  8.7 0.7 %copy-done.17 = s32[256]{0:T(256)S(1)} copy-done((s32[256]{0:T(256)S(1)}, s32[256]{0:T(256)}, u32[]{:S(2)}) %copy-start.17) | copy-done | bytes 1048
  9.4 0.0 copy-done.18
  9.4 0.0 copy-start.12
  9.4 0.2 fusion
  9.7 0.5 %copy-done.12 = f32[8,8,128]{2,1,0:T(8,128)S(1)} copy-done((f32[8,8,128]{2,1,0:T(8,128)S(1)}, f32[8,8,128]{2,1,0:T(8,128)}, u32[]{:S(2)}) %copy-start.12) | copy-done | bytes 32792
  10.2 0.0 copy-done.13
  10.2 0.2 fusion.226
  10.5 0.4 fusion.18
  11.0 0.1 fusion.163
  11.1 0.6 %reshape.214 = f32[32,2,128]{2,1,0:T(2,128)} reshape(f32[32,256]{1,0:T(8,128)S(1)} %fusion.18) | data formatting | bytes 65536 | tf_op jit(solution)/shard_map/reshape | solution.py:211
  11.8 4.7 %all-to-all-start = ((f32[32,2,128]{2,1,0:T(2,128)}), f32[32,2,128]{2,1,0:T(2,128)S(1)}, u32[]{:S(2)}, u32[]{:S(2)}) async-start(f32[32,2,128]{2,1,0:T(2,128)} %reshape.214), calls=%async_computation | async-start | bytes 65536 | tf_op jit(solution)/shard_map/all_to_all | solution.py:212
  16.5 1.2 %collective-permute-start.3 = (f32[2,8,8,4]{3,2,1,0:T(8,128)S(1)}, f32[2,8,8,4]{3,2,1,0:T(8,128)S(1)}, u32[]{:S(2)}, u32[]{:S(2)}) collective-permute-start(f32[2,8,8,4]{3,2,1,0:T(8,128)S(1)} %fusion.163), channel_id=1, source_target_pairs={{0,4},{4,0},{1,5},{5,1},{2,6},{6,2},{3,7},{7,3},{8,12},{12,8},{9,1... | collective-permute-start | bytes 6152 | tf_op jit(solution)/shard_map/ppermute | solution.py:14
  17.8 0.2 select_maximum_fusion.2
  18.0 1.3 %collective-permute-start.4 = (f32[2,4,16,136]{3,2,1,0:T(8,128)S(1)}, f32[2,4,16,136]{3,2,1,0:T(8,128)S(1)}, u32[]{:S(2)}, u32[]{:S(2)}) collective-permute-start(f32[2,4,16,136]{3,2,1,0:T(8,128)S(1)} %get-tuple-element.76), channel_id=1, source_target_pairs={{0,1},{1,0},{2,3},{3,2},{4,5},{5,4},{6,7},{7,6},{8,9},{9,8},{10,11... | collective-permute-start | bytes 208904 | tf_op jit(solution)/shard_map/ppermute | solution.py:21
  19.3 1.9 %collective-permute-start.5 = (f32[2,4,16,136]{3,2,1,0:T(8,128)S(1)}, f32[2,4,16,136]{3,2,1,0:T(8,128)S(1)}, u32[]{:S(2)}, u32[]{:S(2)}) collective-permute-start(f32[2,4,16,136]{3,2,1,0:T(8,128)S(1)} %get-tuple-element.77), channel_id=1, source_target_pairs={{1,2},{2,1},{5,6},{6,5},{9,10},{10,9},{13,14},{14,13},{17,18},{18,... | collective-permute-start | bytes 208904 | tf_op jit(solution)/shard_map/ppermute | solution.py:22
  21.3 0.2 maximum_maximum_fusion
  21.6 0.1 reshape.216
  21.7 0.6 %convolution_bitcast_fusion = f32[16,128]{1,0:T(8,128)S(1)} fusion(s32[32,64]{1,0:T(8,128)S(1)} %add_select_fusion, f32[8,32,64]{2,0,1:T(8,128)S(1)} %fusion.46, f32[2,32,64]{2,0,1:T(2,128)S(1)} %bitcast.174), kind=kOutput, calls=%fused_computation.1 | convolution fusion | flops 50626560 | bytes 98304 | tf_op jit(solution)/shard_map/dot_general | solution.py:226
  22.4 0.1 collective-permute-done.4
  22.5 2.5 %collective-permute-done.5 = f32[2,4,16,136]{3,2,1,0:T(8,128)S(1)} collective-permute-done((f32[2,4,16,136]{3,2,1,0:T(8,128)S(1)}, f32[2,4,16,136]{3,2,1,0:T(8,128)S(1)}, u32[]{:S(2)}, u32[]{:S(2)}) %collective-permute-start.5) | collective-permute-done | bytes 69664 | tf_op jit(solution)/shard_map/ppermute | solution.py:22
  25.1 0.3 pad_maximum_fusion
  25.4 0.3 fusion.32
  25.7 0.2 fusion.10
  25.9 0.0 copy-start.5
  25.9 0.0 copy-start.8
  25.9 0.0 copy-start.9
  26.0 0.7 %add_subtract_fusion.1 = (f32[2,8,8,128]{3,2,1,0:T(8,128)S(1)}, f32[2,8,8,128]{3,2,1,0:T(8,128)S(1)}) fusion(f32[2,16,8,128]{3,2,1,0:T(8,128)S(1)} %fusion.32, f32[8,8,128]{2,1,0:T(8,128)S(1)} %get-tuple-element.102, f32[2,16,8,136]{3,2,1,0:T(8,128)S(1)} %fusion.10, f32[8,8,128]{2,1,0:T(8,128)S(1)} %get-tuple-element.103, ...), kind=kLoop, calls=%fused_computation.314 | loop fusion | flops 2703360 | bytes 3227648 | tf_op jit(solution)/shard_map/sub | solution.py:129
  26.7 0.0 copy-done.14
  26.7 0.0 copy-done.15
  26.8 0.0 copy-start.2
  26.8 0.1 fusion.51
  26.9 0.3 collective-permute-start.9
  27.3 5.4 %collective-permute-start.7 = (f32[2,8,4,128]{3,2,1,0:T(4,128)S(1)}, f32[2,8,4,128]{3,2,1,0:T(4,128)S(1)}, u32[]{:S(2)}, u32[]{:S(2)}) collective-permute-start(f32[2,8,4,128]{3,2,1,0:T(4,128)S(1)} %get-tuple-element.96), channel_id=1, source_target_pairs={{8,16},{16,8},{9,17},{17,9},{10,18},{18,10},{11,19},{19,11},{12,20... | collective-permute-start | bytes 98312 | tf_op jit(solution)/shard_map/ppermute | solution.py:22
  32.6 0.1 collective-permute-start.6
  32.8 1.5 %collective-permute-done.7 = f32[2,8,4,128]{3,2,1,0:T(4,128)S(1)} collective-permute-done((f32[2,8,4,128]{3,2,1,0:T(4,128)S(1)}, f32[2,8,4,128]{3,2,1,0:T(4,128)S(1)}, u32[]{:S(2)}, u32[]{:S(2)}) %collective-permute-start.7) | collective-permute-done | bytes 32800 | tf_op jit(solution)/shard_map/ppermute | solution.py:22
  34.2 0.1 fusion.106
  34.4 1.3 %collective-permute-start.8 = (f32[2,8,8,4]{3,2,1,0:T(8,128)S(1)}, f32[2,8,8,4]{3,2,1,0:T(8,128)S(1)}, u32[]{:S(2)}, u32[]{:S(2)}) collective-permute-start(f32[2,8,8,4]{3,2,1,0:T(8,128)S(1)} %fusion.106), channel_id=1, source_target_pairs={{0,4},{4,0},{1,5},{5,1},{2,6},{6,2},{3,7},{7,3},{8,12},{12,8},{9,1... | collective-permute-start | bytes 6152 | tf_op jit(solution)/shard_map/ppermute | solution.py:14
  35.6 0.2 select_maximum_fusion
  35.9 0.1 collective-permute-start.10
  36.0 1.9 %collective-permute-start.11 = (f32[2,4,16,136]{3,2,1,0:T(8,128)S(1)}, f32[2,4,16,136]{3,2,1,0:T(8,128)S(1)}, u32[]{:S(2)}, u32[]{:S(2)}) collective-permute-start(f32[2,4,16,136]{3,2,1,0:T(8,128)S(1)} %get-tuple-element.73), channel_id=1, source_target_pairs={{1,2},{2,1},{5,6},{6,5},{9,10},{10,9},{13,14},{14,13},{17,18},{18,... | collective-permute-start | bytes 208904 | tf_op jit(solution)/shard_map/ppermute | solution.py:22
  37.9 0.3 collective-permute-done.8
  38.3 0.2 maximum_maximum_fusion.2
  38.5 2.5 %collective-permute-done.10 = f32[2,4,16,136]{3,2,1,0:T(8,128)S(1)} collective-permute-done((f32[2,4,16,136]{3,2,1,0:T(8,128)S(1)}, f32[2,4,16,136]{3,2,1,0:T(8,128)S(1)}, u32[]{:S(2)}, u32[]{:S(2)}) %collective-permute-start.10) | collective-permute-done | bytes 69664 | tf_op jit(solution)/shard_map/ppermute | solution.py:21
  41.0 1.9 %collective-permute-done.11 = f32[2,4,16,136]{3,2,1,0:T(8,128)S(1)} collective-permute-done((f32[2,4,16,136]{3,2,1,0:T(8,128)S(1)}, f32[2,4,16,136]{3,2,1,0:T(8,128)S(1)}, u32[]{:S(2)}, u32[]{:S(2)}) %collective-permute-start.11) | collective-permute-done | bytes 69664 | tf_op jit(solution)/shard_map/ppermute | solution.py:22
  42.9 0.3 pad_maximum_fusion.1
  43.2 0.3 fusion.25
  43.5 0.2 fusion.3
  43.7 0.7 %add_subtract_fusion = (f32[2,8,8,128]{3,2,1,0:T(8,128)S(1)}, f32[2,8,8,128]{3,2,1,0:T(8,128)S(1)}) fusion(f32[2,16,8,128]{3,2,1,0:T(8,128)S(1)} %fusion.25, f32[8,8,128]{2,1,0:T(8,128)S(1)} %get-tuple-element.102, f32[2,16,8,136]{3,2,1,0:T(8,128)S(1)} %fusion.3, f32[8,8,128]{2,1,0:T(8,128)S(1)} %get-tuple-element.103, ...), kind=kLoop, calls=%fused_computation.313 | loop fusion | flops 2703360 | bytes 3227648 | tf_op jit(solution)/shard_map/sub | solution.py:129
  44.4 0.0 copy-start.10
  44.5 0.0 copy-start.11
  44.5 0.6 %copy-done.10 = f32[8,8,128]{2,1,0:T(8,128)} copy-done((f32[8,8,128]{2,1,0:T(8,128)}, f32[8,8,128]{2,1,0:T(8,128)S(1)}, u32[]{:S(2)}) %copy-start.10) | copy-done | bytes 32792
  45.1 0.0 copy-done.11
  (62 shorter events, 0.6 us)
Async XLA Ops:
  0.6 7.7 %copy-start = (f32[256,256]{1,0:T(8,128)S(1)}, f32[256,256]{1,0:T(8,128)}, u32[]{:S(2)}) copy-start(f32[256,256]{1,0:T(8,128)} %param.36) | copy-start | bytes 786436
  0.6 0.8 %copy-start.3 = (f32[8,8,128]{2,1,0:T(8,128)S(1)}, f32[8,8,128]{2,1,0:T(8,128)}, u32[]{:S(2)}) copy-start(f32[8,8,128]{2,1,0:T(8,128)} %param.25) | copy-start | bytes 98308
  1.4 4.8 %copy-start.4 = (f32[8,8,128]{2,1,0:T(8,128)S(1)}, f32[8,8,128]{2,1,0:T(8,128)}, u32[]{:S(2)}) copy-start(f32[8,8,128]{2,1,0:T(8,128)} %param.27) | copy-start | bytes 98308
  2.4 8.6 %collective-permute-start.1 = (f32[2,8,4,128]{3,2,1,0:T(4,128)S(1)}, f32[2,8,4,128]{3,2,1,0:T(4,128)S(1)}, u32[]{:S(2)}, u32[]{:S(2)}) collective-permute-start(f32[2,8,4,128]{3,2,1,0:T(4,128)S(1)} %get-tuple-element.117), channel_id=1, source_target_pairs={{0,8},{8,0},{16,24},{24,16},{1,9},{9,1},{17,25},{25,17},{2,10},{10... | collective-permute-start | bytes 98312 | tf_op jit(solution)/shard_map/ppermute | solution.py:21
  3.1 7.8 %collective-permute-start = (f32[2,8,4,128]{3,2,1,0:T(4,128)S(1)}, f32[2,8,4,128]{3,2,1,0:T(4,128)S(1)}, u32[]{:S(2)}, u32[]{:S(2)}) collective-permute-start(f32[2,8,4,128]{3,2,1,0:T(4,128)S(1)} %get-tuple-element.118), channel_id=1, source_target_pairs={{8,16},{16,8},{9,17},{17,9},{10,18},{18,10},{11,19},{19,11},{12,20... | collective-permute-start | bytes 98312 | tf_op jit(solution)/shard_map/ppermute | solution.py:22
  6.3 4.6 %collective-permute-start.2 = (f32[2,8,8,4]{3,2,1,0:T(8,128)S(1)}, f32[2,8,8,4]{3,2,1,0:T(8,128)S(1)}, u32[]{:S(2)}, u32[]{:S(2)}) collective-permute-start(f32[2,8,8,4]{3,2,1,0:T(8,128)S(1)} %fusion.55), channel_id=1, source_target_pairs={{0,4},{4,0},{1,5},{5,1},{2,6},{6,2},{3,7},{7,3},{8,12},{12,8},{9,1... | collective-permute-start | bytes 6152 | tf_op jit(solution)/shard_map/ppermute | solution.py:14
  7.6 0.7 %copy-start.19 = (s32[256]{0:T(256)S(1)}, s32[256]{0:T(256)}, u32[]{:S(2)}) copy-start(s32[256]{0:T(256)} %param.41) | copy-start | bytes 3076
  7.6 0.7 %copy-start.20 = (f32[64]{0:T(128)S(1)}, f32[64]{0:T(128)}, u32[]{:S(2)}) copy-start(f32[64]{0:T(128)} %param.38) | copy-start | bytes 772
  7.6 0.8 %copy-start.16 = (f32[2,256]{1,0:T(2,128)S(1)}, f32[2,256]{1,0:T(2,128)}, u32[]{:S(2)}) copy-start(f32[2,256]{1,0:T(2,128)} %param.37) | copy-start | bytes 6148
  8.6 0.7 %copy-start.17 = (s32[256]{0:T(256)S(1)}, s32[256]{0:T(256)}, u32[]{:S(2)}) copy-start(s32[256]{0:T(256)} %param.40) | copy-start | bytes 3076
  8.6 0.8 %copy-start.18 = (s32[256]{0:T(256)S(1)}, s32[256]{0:T(256)}, u32[]{:S(2)}) copy-start(s32[256]{0:T(256)} %param.39) | copy-start | bytes 3076
  9.4 0.8 %copy-start.12 = (f32[8,8,128]{2,1,0:T(8,128)S(1)}, f32[8,8,128]{2,1,0:T(8,128)}, u32[]{:S(2)}) copy-start(f32[8,8,128]{2,1,0:T(8,128)} %param.33) | copy-start | bytes 98308
  9.4 0.8 %copy-start.13 = (f32[8,8,128]{2,1,0:T(8,128)S(1)}, f32[8,8,128]{2,1,0:T(8,128)}, u32[]{:S(2)}) copy-start(f32[8,8,128]{2,1,0:T(8,128)} %param.32) | copy-start | bytes 98308
  11.8 9.8 %all-to-all-start = ((f32[32,2,128]{2,1,0:T(2,128)}), f32[32,2,128]{2,1,0:T(2,128)S(1)}, u32[]{:S(2)}, u32[]{:S(2)}) async-start(f32[32,2,128]{2,1,0:T(2,128)} %reshape.214), calls=%async_computation | async-start | bytes 65536 | tf_op jit(solution)/shard_map/all_to_all | solution.py:212
  16.5 4.8 %collective-permute-start.3 = (f32[2,8,8,4]{3,2,1,0:T(8,128)S(1)}, f32[2,8,8,4]{3,2,1,0:T(8,128)S(1)}, u32[]{:S(2)}, u32[]{:S(2)}) collective-permute-start(f32[2,8,8,4]{3,2,1,0:T(8,128)S(1)} %fusion.163), channel_id=1, source_target_pairs={{0,4},{4,0},{1,5},{5,1},{2,6},{6,2},{3,7},{7,3},{8,12},{12,8},{9,1... | collective-permute-start | bytes 6152 | tf_op jit(solution)/shard_map/ppermute | solution.py:14
  18.0 4.5 %collective-permute-start.4 = (f32[2,4,16,136]{3,2,1,0:T(8,128)S(1)}, f32[2,4,16,136]{3,2,1,0:T(8,128)S(1)}, u32[]{:S(2)}, u32[]{:S(2)}) collective-permute-start(f32[2,4,16,136]{3,2,1,0:T(8,128)S(1)} %get-tuple-element.76), channel_id=1, source_target_pairs={{0,1},{1,0},{2,3},{3,2},{4,5},{5,4},{6,7},{7,6},{8,9},{9,8},{10,11... | collective-permute-start | bytes 208904 | tf_op jit(solution)/shard_map/ppermute | solution.py:21
  19.3 5.7 %collective-permute-start.5 = (f32[2,4,16,136]{3,2,1,0:T(8,128)S(1)}, f32[2,4,16,136]{3,2,1,0:T(8,128)S(1)}, u32[]{:S(2)}, u32[]{:S(2)}) collective-permute-start(f32[2,4,16,136]{3,2,1,0:T(8,128)S(1)} %get-tuple-element.77), channel_id=1, source_target_pairs={{1,2},{2,1},{5,6},{6,5},{9,10},{10,9},{13,14},{14,13},{17,18},{18,... | collective-permute-start | bytes 208904 | tf_op jit(solution)/shard_map/ppermute | solution.py:22
  25.9 0.8 %copy-start.5 = (f32[8,8,128]{2,1,0:T(8,128)S(1)}, f32[8,8,128]{2,1,0:T(8,128)}, u32[]{:S(2)}) copy-start(f32[8,8,128]{2,1,0:T(8,128)} %param.29) | copy-start | bytes 98308
  25.9 0.8 %copy-start.6 = (f32[8,8,128]{2,1,0:T(8,128)S(1)}, f32[8,8,128]{2,1,0:T(8,128)}, u32[]{:S(2)}) copy-start(f32[8,8,128]{2,1,0:T(8,128)} %param.34) | copy-start | bytes 98308
  25.9 0.8 %copy-start.7 = (f32[8,8,128]{2,1,0:T(8,128)S(1)}, f32[8,8,128]{2,1,0:T(8,128)}, u32[]{:S(2)}) copy-start(f32[8,8,128]{2,1,0:T(8,128)} %param.35) | copy-start | bytes 98308
  25.9 0.8 %copy-start.8 = (f32[8,8,128]{2,1,0:T(8,128)S(1)}, f32[8,8,128]{2,1,0:T(8,128)}, u32[]{:S(2)}) copy-start(f32[8,8,128]{2,1,0:T(8,128)} %param.31) | copy-start | bytes 98308
  25.9 0.8 %copy-start.9 = (f32[8,8,128]{2,1,0:T(8,128)S(1)}, f32[8,8,128]{2,1,0:T(8,128)}, u32[]{:S(2)}) copy-start(f32[8,8,128]{2,1,0:T(8,128)} %param.30) | copy-start | bytes 98308
  25.9 0.8 %copy-start.14 = (f32[8,8,128]{2,1,0:T(8,128)S(1)}, f32[8,8,128]{2,1,0:T(8,128)}, u32[]{:S(2)}) copy-start(f32[8,8,128]{2,1,0:T(8,128)} %param.28) | copy-start | bytes 98308
  25.9 0.8 %copy-start.15 = (f32[8,8,128]{2,1,0:T(8,128)S(1)}, f32[8,8,128]{2,1,0:T(8,128)}, u32[]{:S(2)}) copy-start(f32[8,8,128]{2,1,0:T(8,128)} %param.26) | copy-start | bytes 98308
  26.8 17.6 %copy-start.1 = (f32[8,8,128]{2,1,0:T(8,128)}, f32[8,8,128]{2,1,0:T(8,128)S(1)}, u32[]{:S(2)}) copy-start(f32[8,8,128]{2,1,0:T(8,128)S(1)} %get-tuple-element.126) | copy-start | bytes 98308
  26.8 17.6 %copy-start.2 = (f32[8,8,128]{2,1,0:T(8,128)}, f32[8,8,128]{2,1,0:T(8,128)S(1)}, u32[]{:S(2)}) copy-start(f32[8,8,128]{2,1,0:T(8,128)S(1)} %get-tuple-element.127) | copy-start | bytes 98308
  26.9 5.8 %collective-permute-start.9 = (f32[2,8,8,4]{3,2,1,0:T(8,128)S(1)}, f32[2,8,8,4]{3,2,1,0:T(8,128)S(1)}, u32[]{:S(2)}, u32[]{:S(2)}) collective-permute-start(f32[2,8,8,4]{3,2,1,0:T(8,128)S(1)} %fusion.51), channel_id=1, source_target_pairs={{0,4},{4,0},{1,5},{5,1},{2,6},{6,2},{3,7},{7,3},{8,12},{12,8},{9,1... | collective-permute-start | bytes 6152 | tf_op jit(solution)/shard_map/ppermute | solution.py:14
  27.3 7.0 %collective-permute-start.7 = (f32[2,8,4,128]{3,2,1,0:T(4,128)S(1)}, f32[2,8,4,128]{3,2,1,0:T(4,128)S(1)}, u32[]{:S(2)}, u32[]{:S(2)}) collective-permute-start(f32[2,8,4,128]{3,2,1,0:T(4,128)S(1)} %get-tuple-element.96), channel_id=1, source_target_pairs={{8,16},{16,8},{9,17},{17,9},{10,18},{18,10},{11,19},{19,11},{12,20... | collective-permute-start | bytes 98312 | tf_op jit(solution)/shard_map/ppermute | solution.py:22
  32.6 1.6 %collective-permute-start.6 = (f32[2,8,4,128]{3,2,1,0:T(4,128)S(1)}, f32[2,8,4,128]{3,2,1,0:T(4,128)S(1)}, u32[]{:S(2)}, u32[]{:S(2)}) collective-permute-start(f32[2,8,4,128]{3,2,1,0:T(4,128)S(1)} %get-tuple-element.97), channel_id=1, source_target_pairs={{0,8},{8,0},{16,24},{24,16},{1,9},{9,1},{17,25},{25,17},{2,10},{10... | collective-permute-start | bytes 98312 | tf_op jit(solution)/shard_map/ppermute | solution.py:21
  34.4 3.9 %collective-permute-start.8 = (f32[2,8,8,4]{3,2,1,0:T(8,128)S(1)}, f32[2,8,8,4]{3,2,1,0:T(8,128)S(1)}, u32[]{:S(2)}, u32[]{:S(2)}) collective-permute-start(f32[2,8,8,4]{3,2,1,0:T(8,128)S(1)} %fusion.106), channel_id=1, source_target_pairs={{0,4},{4,0},{1,5},{5,1},{2,6},{6,2},{3,7},{7,3},{8,12},{12,8},{9,1... | collective-permute-start | bytes 6152 | tf_op jit(solution)/shard_map/ppermute | solution.py:14
  35.9 5.0 %collective-permute-start.10 = (f32[2,4,16,136]{3,2,1,0:T(8,128)S(1)}, f32[2,4,16,136]{3,2,1,0:T(8,128)S(1)}, u32[]{:S(2)}, u32[]{:S(2)}) collective-permute-start(f32[2,4,16,136]{3,2,1,0:T(8,128)S(1)} %get-tuple-element.72), channel_id=1, source_target_pairs={{0,1},{1,0},{2,3},{3,2},{4,5},{5,4},{6,7},{7,6},{8,9},{9,8},{10,11... | collective-permute-start | bytes 208904 | tf_op jit(solution)/shard_map/ppermute | solution.py:21
  36.0 6.9 %collective-permute-start.11 = (f32[2,4,16,136]{3,2,1,0:T(8,128)S(1)}, f32[2,4,16,136]{3,2,1,0:T(8,128)S(1)}, u32[]{:S(2)}, u32[]{:S(2)}) collective-permute-start(f32[2,4,16,136]{3,2,1,0:T(8,128)S(1)} %get-tuple-element.73), channel_id=1, source_target_pairs={{1,2},{2,1},{5,6},{6,5},{9,10},{10,9},{13,14},{14,13},{17,18},{18,... | collective-permute-start | bytes 208904 | tf_op jit(solution)/shard_map/ppermute | solution.py:22
  44.4 0.6 %copy-start.10 = (f32[8,8,128]{2,1,0:T(8,128)}, f32[8,8,128]{2,1,0:T(8,128)S(1)}, u32[]{:S(2)}) copy-start(f32[8,8,128]{2,1,0:T(8,128)S(1)} %get-tuple-element.124) | copy-start | bytes 98308
  44.5 0.6 %copy-start.11 = (f32[8,8,128]{2,1,0:T(8,128)}, f32[8,8,128]{2,1,0:T(8,128)S(1)}, u32[]{:S(2)}) copy-start(f32[8,8,128]{2,1,0:T(8,128)S(1)} %get-tuple-element.125) | copy-start | bytes 98308

commit v11 on v9

--- a/solution.py
+++ b/solution.py
@@ -7,43 +7,49 @@
 first_coef = (0.0, 4.0 / 5.0, -1.0 / 5.0, 4.0 / 105.0, -1.0 / 280.0)
 
 
-def shift_pair(top, bottom, axis):
+def shift_pair(block, dim, width, axis):
     count = lax.axis_size(axis)
-    if count == 2:
-        first = lax.axis_index(axis) == 0
-        got = lax.ppermute(jnp.where(first, top, bottom), axis, [(0, 1), (1, 0)])
-        empty = jnp.zeros_like(got)
-        return jnp.where(first, empty, got), jnp.where(first, got, empty)
+    size = block.shape[dim]
+    index = lax.axis_index(axis)
     if count % 2 == 0:
-        even = lax.axis_index(axis) % 2 == 0
+        even = index % 2 == 0
         inner = [(i, i ^ 1) for i in range(count)]
         outer = [(i, i + 1 if i % 2 else i - 1) for i in range(1, count - 1)]
-        got_inner = lax.ppermute(jnp.where(even, top, bottom), axis, inner)
-        got_outer = lax.ppermute(jnp.where(even, bottom, top), axis, outer)
+        got_inner = lax.ppermute(
+            lax.dynamic_slice_in_dim(block, jnp.where(even, size - width, 0), width, axis=dim),
+            axis,
+            inner,
+        )
+        if count == 2:
+            empty = jnp.zeros_like(got_inner)
+            return jnp.where(even, empty, got_inner), jnp.where(even, got_inner, empty)
+        got_outer = lax.ppermute(
+            lax.dynamic_slice_in_dim(block, jnp.where(even, 0, size - width), width, axis=dim),
+            axis,
+            outer,
+        )
         return jnp.where(even, got_outer, got_inner), jnp.where(even, got_inner, got_outer)
     forward = [(i, i + 1) for i in range(count - 1)]
     backward = [(target, source) for source, target in forward]
+    top = lax.slice_in_dim(block, size - width, None, axis=dim)
+    bottom = lax.slice_in_dim(block, 0, width, axis=dim)
     return lax.ppermute(top, axis, forward), lax.ppermute(bottom, axis, backward)
 
 
 def first_round(block, width):
-    cut = lambda a, dim, lo, hi: lax.slice_in_dim(a, lo, hi, axis=dim)
-    across, along = block.shape[2:]
-    low_x, high_x = shift_pair(cut(block, 2, across - width, None), cut(block, 2, 0, width), "inl")
-    low_y, high_y = shift_pair(cut(block, 3, along - width, None), cut(block, 3, 0, width), "xl")
+    low_x, high_x = shift_pair(block, 2, width, "inl")
+    low_y, high_y = shift_pair(block, 3, width, "xl")
     return low_x, high_x, low_y, high_y
 
 
 def second_round(block, width, faces):
-    cut = lambda a, dim, lo, hi: lax.slice_in_dim(a, lo, hi, axis=dim)
-    depth, along = block.shape[1], block.shape[3]
     low_x, high_x, low_y, high_y = faces
     strips = jnp.concatenate([low_x, high_x], axis=2)
-    low_c, high_c = shift_pair(cut(strips, 3, along - width, None), cut(strips, 3, 0, width), "xl")
+    low_c, high_c = shift_pair(strips, 3, width, "xl")
     wide_x = jnp.concatenate([low_x, block, high_x], axis=2)
     pad_x = ((0, 0), (0, 0), (width, width), (0, 0))
     bare = jnp.concatenate([jnp.pad(low_y, pad_x), wide_x, jnp.pad(high_y, pad_x)], axis=3)
-    low_z, high_z = shift_pair(cut(bare, 1, depth - width, None), cut(bare, 1, 0, width), "gz")
+    low_z, high_z = shift_pair(bare, 1, width, "gz")
     side_low = jnp.concatenate([low_c[:, :, :width], low_y, low_c[:, :, width:]], axis=2)
     side_high = jnp.concatenate([high_c[:, :, :width], high_y, high_c[:, :, width:]], axis=2)
     full = jnp.concatenate([side_low, wide_x, side_high], axis=3)

time: 45.9 us -> 45.8 us (level)
    select_n x12 -> x4, other arithmetic: 1.42 us -> 0.05 us  [the longest x3 0.04 us: shift_pair(): jnp.where(even, empty, got_inner)]
    another operation x0 -> x4, other arithmetic: none -> 1.02 us  [the longest x2 0.93 us: local(): current = jnp.stack([wave_p, wave_q])]
where the time goes in v11:
time: 45.8 us; the launch traced here: 45 us
  starting transfers between devices  23.4 us (51%)
  waiting for transfers between devices  8.83 us (19%)
  other arithmetic  5.5 us (12%)
  local copies, waits for them, and re-layouts  4.43 us (10%)
  matrix products  1.52 us (3%)
  between operations  1.33 us (3%)
    ppermute x4, starting transfers between devices, shift_pair(): lax.ppermute(lax.dynamic_slice_in_dim(block, jnp.where(even, 0, size - wi...  12.3 us
    ppermute x8, starting transfers between devices, shift_pair(): lax.ppermute(lax.dynamic_slice_in_dim(block, jnp.where(even, size - width...  6.26 us
    ppermute x4, waiting for transfers between devices, shift_pair(): lax.ppermute(lax.dynamic_slice_in_dim(block, jnp.where(even, 0, size - wi...  5.92 us
    all_to_all x1, starting transfers between devices, local(): lax.all_to_all(send, ('inl', 'xl', 'gz'), split_axis=0, concat_axis=0, ti...  4.84 us
    unnamed x43, local copies, waits for them, and re-layouts  3.34 us
    ppermute x8, waiting for transfers between devices, shift_pair(): lax.ppermute(lax.dynamic_slice_in_dim(block, jnp.where(even, size - width...  2.91 us
    sub x2, other arithmetic, advance(): h_two = u_xx + u_yy + u_zz - h_one  1.39 us
    another operation x2, other arithmetic, local(): current = jnp.stack([wave_p, wave_q])  0.93 us
  transfers between devices with their start and end apart: 13, of which 6 were waited for; matrix products, arithmetic and copies ran while one was open for 7% of the time, Pallas kernels for 0%

profile of v11, /device:TPU:17, one launch (start us, length us, event | category | flops | bytes accessed | tf_op | source)
XLA Modules:
  0.0 45.0 jit_solution(16918315713886721598)
XLA Ops:
  0.6 0.0 copy-start
  0.7 0.8 %copy-done.3 = f32[8,8,128]{2,1,0:T(8,128)S(1)} copy-done((f32[8,8,128]{2,1,0:T(8,128)S(1)}, f32[8,8,128]{2,1,0:T(8,128)}, u32[]{:S(2)}) %copy-start.3) | copy-done | bytes 32792
  1.4 0.8 %fusion.170 = (f32[2,8,4,128]{3,2,1,0:T(4,128)S(1)}, f32[2,8,4,128]{3,2,1,0:T(4,128)S(1)}) fusion(s32[]{:T(128)S(6)} %select_n.206, f32[1,8,8,128]{3,2,1,0:T(8,128)S(1)} %bitcast.132, f32[1,8,8,128]{3,2,1,0:T(8,128)} %bitcast.139, s32[]{:T(128)S(6)} %select_n.205), kind=kLoop, calls=%fused_computation.315 | loop fusion | flops 16384 | bytes 131080 | tf_op jit(solution)/shard_map/stack | solution.py:231
  2.3 0.7 %collective-permute-start.1 = (f32[2,8,4,128]{3,2,1,0:T(4,128)S(1)}, f32[2,8,4,128]{3,2,1,0:T(4,128)S(1)}, u32[]{:S(2)}, u32[]{:S(2)}) collective-permute-start(f32[2,8,4,128]{3,2,1,0:T(4,128)S(1)} %get-tuple-element.117), channel_id=1, source_target_pairs={{0,8},{8,0},{16,24},{24,16},{1,9},{9,1},{17,25},{25,17},{2,10},{10... | collective-permute-start | bytes 98312 | tf_op jit(solution)/shard_map/ppermute | solution.py:18
  3.0 3.0 %collective-permute-start = (f32[2,8,4,128]{3,2,1,0:T(4,128)S(1)}, f32[2,8,4,128]{3,2,1,0:T(4,128)S(1)}, u32[]{:S(2)}, u32[]{:S(2)}) collective-permute-start(f32[2,8,4,128]{3,2,1,0:T(4,128)S(1)} %get-tuple-element.118), channel_id=1, source_target_pairs={{8,16},{16,8},{9,17},{17,9},{10,18},{18,10},{11,19},{19,11},{12,20... | collective-permute-start | bytes 98312 | tf_op jit(solution)/shard_map/ppermute | solution.py:26
  6.1 0.0 copy-start.19
  6.2 0.1 fusion.50
  6.2 1.2 %collective-permute-start.2 = (f32[2,8,8,4]{3,2,1,0:T(8,128)S(1)}, f32[2,8,8,4]{3,2,1,0:T(8,128)S(1)}, u32[]{:S(2)}, u32[]{:S(2)}) collective-permute-start(f32[2,8,8,4]{3,2,1,0:T(8,128)S(1)} %fusion.50), channel_id=1, source_target_pairs={{0,4},{4,0},{1,5},{5,1},{2,6},{6,2},{3,7},{7,3},{8,12},{12,8},{9,1... | collective-permute-start | bytes 6152 | tf_op jit(solution)/shard_map/ppermute | solution.py:18
  7.5 0.1 select_reduce_fusion
  7.6 0.6 %copy-done.16 = f32[2,256]{1,0:T(2,128)S(1)} copy-done((f32[2,256]{1,0:T(2,128)S(1)}, f32[2,256]{1,0:T(2,128)}, u32[]{:S(2)}) %copy-start.16) | copy-done | bytes 2072
  8.2 0.3 convolution_multiply_fusion
  8.4 0.1 copy-start.18
  8.5 0.7 %copy-done.17 = s32[256]{0:T(256)S(1)} copy-done((s32[256]{0:T(256)S(1)}, s32[256]{0:T(256)}, u32[]{:S(2)}) %copy-start.17) | copy-done | bytes 1048
  9.2 0.0 copy-done.18
  9.2 0.2 fusion
  9.4 0.5 %copy-done.12 = f32[8,8,128]{2,1,0:T(8,128)S(1)} copy-done((f32[8,8,128]{2,1,0:T(8,128)S(1)}, f32[8,8,128]{2,1,0:T(8,128)}, u32[]{:S(2)}) %copy-start.12) | copy-done | bytes 32792
  10.0 0.0 copy-done.13
  10.0 0.2 fusion.214
  10.3 0.4 fusion.18
  10.8 0.1 dynamic-slice_maximum_fusion.1
  10.9 0.6 %copy.42 = f32[32,1,192]{2,1,0:T(1,128)} copy(f32[32,1,192]{2,0,1:T(8,128)S(1)} %bitcast.174) | data formatting | bytes 49152 | tf_op jit(solution)/shard_map/all_to_all | solution.py:214
  11.6 4.8 %all-to-all-start = ((f32[32,1,192]{2,1,0:T(1,128)}), f32[32,1,192]{2,1,0:T(1,128)S(1)}, u32[]{:S(2)}, u32[]{:S(2)}) async-start(f32[32,1,192]{2,1,0:T(1,128)} %copy.42), calls=%async_computation | async-start | bytes 65536 | tf_op jit(solution)/shard_map/all_to_all | solution.py:214
  16.4 1.2 %collective-permute-start.3 = (f32[2,8,8,4]{3,2,1,0:T(8,128)S(1)}, f32[2,8,8,4]{3,2,1,0:T(8,128)S(1)}, u32[]{:S(2)}, u32[]{:S(2)}) collective-permute-start(f32[2,8,8,4]{3,2,1,0:T(8,128)S(1)} %dynamic-slice_maximum_fusion.1), channel_id=1, source_target_pairs={{0,4},{4,0},{1,5},{5,1},{2,6},{6,2},{3,7},{7,3},{8,12},{12,8},{9,1... | collective-permute-start | bytes 6152 | tf_op jit(solution)/shard_map/ppermute | solution.py:18
  17.7 0.2 select_maximum_fusion.2
  18.0 1.3 %collective-permute-start.4 = (f32[2,4,16,136]{3,2,1,0:T(8,128)S(1)}, f32[2,4,16,136]{3,2,1,0:T(8,128)S(1)}, u32[]{:S(2)}, u32[]{:S(2)}) collective-permute-start(f32[2,4,16,136]{3,2,1,0:T(8,128)S(1)} %get-tuple-element.76), channel_id=1, source_target_pairs={{0,1},{1,0},{2,3},{3,2},{4,5},{5,4},{6,7},{7,6},{8,9},{9,8},{10,11... | collective-permute-start | bytes 208904 | tf_op jit(solution)/shard_map/ppermute | solution.py:18
  19.3 1.9 %collective-permute-start.5 = (f32[2,4,16,136]{3,2,1,0:T(8,128)S(1)}, f32[2,4,16,136]{3,2,1,0:T(8,128)S(1)}, u32[]{:S(2)}, u32[]{:S(2)}) collective-permute-start(f32[2,4,16,136]{3,2,1,0:T(8,128)S(1)} %get-tuple-element.77), channel_id=1, source_target_pairs={{1,2},{2,1},{5,6},{6,5},{9,10},{10,9},{13,14},{14,13},{17,18},{18,... | collective-permute-start | bytes 208904 | tf_op jit(solution)/shard_map/ppermute | solution.py:26
  21.3 0.2 maximum_maximum_fusion
  21.5 0.1 reshape.205
  21.7 0.6 %convolution_bitcast_fusion = f32[16,128]{1,0:T(8,128)S(1)} fusion(s32[32,64]{1,0:T(8,128)S(1)} %add_select_fusion, f32[8,32,64]{2,0,1:T(8,128)S(1)} %fusion.45, f32[2,32,64]{2,0,1:T(2,128)S(1)} %bitcast.173), kind=kOutput, calls=%fused_computation.1 | convolution fusion | flops 50626560 | bytes 98304 | tf_op jit(solution)/shard_map/dot_general | solution.py:227
  22.3 0.1 collective-permute-done.4
  22.4 2.5 %collective-permute-done.5 = f32[2,4,16,136]{3,2,1,0:T(8,128)S(1)} collective-permute-done((f32[2,4,16,136]{3,2,1,0:T(8,128)S(1)}, f32[2,4,16,136]{3,2,1,0:T(8,128)S(1)}, u32[]{:S(2)}, u32[]{:S(2)}) %collective-permute-start.5) | collective-permute-done | bytes 69664 | tf_op jit(solution)/shard_map/ppermute | solution.py:26
  25.0 0.3 pad_maximum_fusion
  25.3 0.3 fusion.31
  25.6 0.2 fusion.10
  25.8 0.0 copy-start.6
  25.8 0.0 copy-start.7
  25.9 0.0 copy-start.14
  25.9 0.0 copy-start.15
  25.9 0.7 %add_subtract_fusion.1 = (f32[2,8,8,128]{3,2,1,0:T(8,128)S(1)}, f32[2,8,8,128]{3,2,1,0:T(8,128)S(1)}) fusion(f32[2,16,8,128]{3,2,1,0:T(8,128)S(1)} %fusion.31, f32[8,8,128]{2,1,0:T(8,128)S(1)} %get-tuple-element.102, f32[2,16,8,136]{3,2,1,0:T(8,128)S(1)} %fusion.10, f32[8,8,128]{2,1,0:T(8,128)S(1)} %get-tuple-element.103, ...), kind=kLoop, calls=%fused_computation.298 | loop fusion | flops 2703360 | bytes 3227648 | tf_op jit(solution)/shard_map/sub | solution.py:135
  26.6 0.0 copy-done.14
  26.6 0.0 copy-done.15
  26.7 0.0 copy-start.2
  26.7 0.1 fusion.48
  26.8 0.3 collective-permute-start.9
  27.2 5.4 %collective-permute-start.7 = (f32[2,8,4,128]{3,2,1,0:T(4,128)S(1)}, f32[2,8,4,128]{3,2,1,0:T(4,128)S(1)}, u32[]{:S(2)}, u32[]{:S(2)}) collective-permute-start(f32[2,8,4,128]{3,2,1,0:T(4,128)S(1)} %get-tuple-element.96), channel_id=1, source_target_pairs={{8,16},{16,8},{9,17},{17,9},{10,18},{18,10},{11,19},{19,11},{12,20... | collective-permute-start | bytes 98312 | tf_op jit(solution)/shard_map/ppermute | solution.py:26
  32.5 0.1 collective-permute-start.6
  32.7 1.5 %collective-permute-done.7 = f32[2,8,4,128]{3,2,1,0:T(4,128)S(1)} collective-permute-done((f32[2,8,4,128]{3,2,1,0:T(4,128)S(1)}, f32[2,8,4,128]{3,2,1,0:T(4,128)S(1)}, u32[]{:S(2)}, u32[]{:S(2)}) %collective-permute-start.7) | collective-permute-done | bytes 32800 | tf_op jit(solution)/shard_map/ppermute | solution.py:26
  34.1 0.1 dynamic-slice_maximum_fusion
  34.3 1.3 %collective-permute-start.8 = (f32[2,8,8,4]{3,2,1,0:T(8,128)S(1)}, f32[2,8,8,4]{3,2,1,0:T(8,128)S(1)}, u32[]{:S(2)}, u32[]{:S(2)}) collective-permute-start(f32[2,8,8,4]{3,2,1,0:T(8,128)S(1)} %dynamic-slice_maximum_fusion), channel_id=1, source_target_pairs={{0,4},{4,0},{1,5},{5,1},{2,6},{6,2},{3,7},{7,3},{8,12},{12,8},{9,1... | collective-permute-start | bytes 6152 | tf_op jit(solution)/shard_map/ppermute | solution.py:18
  35.5 0.2 select_maximum_fusion
  35.8 0.1 collective-permute-start.10
  35.9 1.9 %collective-permute-start.11 = (f32[2,4,16,136]{3,2,1,0:T(8,128)S(1)}, f32[2,4,16,136]{3,2,1,0:T(8,128)S(1)}, u32[]{:S(2)}, u32[]{:S(2)}) collective-permute-start(f32[2,4,16,136]{3,2,1,0:T(8,128)S(1)} %get-tuple-element.73), channel_id=1, source_target_pairs={{1,2},{2,1},{5,6},{6,5},{9,10},{10,9},{13,14},{14,13},{17,18},{18,... | collective-permute-start | bytes 208904 | tf_op jit(solution)/shard_map/ppermute | solution.py:26
  37.8 0.3 collective-permute-done.8
  38.2 0.2 maximum_maximum_fusion.2
  38.4 2.4 %collective-permute-done.10 = f32[2,4,16,136]{3,2,1,0:T(8,128)S(1)} collective-permute-done((f32[2,4,16,136]{3,2,1,0:T(8,128)S(1)}, f32[2,4,16,136]{3,2,1,0:T(8,128)S(1)}, u32[]{:S(2)}, u32[]{:S(2)}) %collective-permute-start.10) | collective-permute-done | bytes 69664 | tf_op jit(solution)/shard_map/ppermute | solution.py:18
  40.9 1.9 %collective-permute-done.11 = f32[2,4,16,136]{3,2,1,0:T(8,128)S(1)} collective-permute-done((f32[2,4,16,136]{3,2,1,0:T(8,128)S(1)}, f32[2,4,16,136]{3,2,1,0:T(8,128)S(1)}, u32[]{:S(2)}, u32[]{:S(2)}) %collective-permute-start.11) | collective-permute-done | bytes 69664 | tf_op jit(solution)/shard_map/ppermute | solution.py:26
  42.8 0.3 pad_maximum_fusion.1
  43.1 0.3 fusion.24
  43.4 0.2 fusion.3
  43.6 0.7 %add_subtract_fusion = (f32[2,8,8,128]{3,2,1,0:T(8,128)S(1)}, f32[2,8,8,128]{3,2,1,0:T(8,128)S(1)}) fusion(f32[2,16,8,128]{3,2,1,0:T(8,128)S(1)} %fusion.24, f32[8,8,128]{2,1,0:T(8,128)S(1)} %get-tuple-element.102, f32[2,16,8,136]{3,2,1,0:T(8,128)S(1)} %fusion.3, f32[8,8,128]{2,1,0:T(8,128)S(1)} %get-tuple-element.103, ...), kind=kLoop, calls=%fused_computation.297 | loop fusion | flops 2703360 | bytes 3227648 | tf_op jit(solution)/shard_map/sub | solution.py:135
  44.4 0.0 copy-start.10
  44.4 0.0 copy-start.11
  44.4 0.6 %copy-done.10 = f32[8,8,128]{2,1,0:T(8,128)} copy-done((f32[8,8,128]{2,1,0:T(8,128)}, f32[8,8,128]{2,1,0:T(8,128)S(1)}, u32[]{:S(2)}) %copy-start.10) | copy-done | bytes 32792
  45.0 0.0 copy-done.11
  (61 shorter events, 0.6 us)
Async XLA Ops:
  0.6 7.0 %copy-start = (f32[256,256]{1,0:T(8,128)S(1)}, f32[256,256]{1,0:T(8,128)}, u32[]{:S(2)}) copy-start(f32[256,256]{1,0:T(8,128)} %param.36) | copy-start | bytes 786436
  0.6 0.8 %copy-start.3 = (f32[8,8,128]{2,1,0:T(8,128)S(1)}, f32[8,8,128]{2,1,0:T(8,128)}, u32[]{:S(2)}) copy-start(f32[8,8,128]{2,1,0:T(8,128)} %param.25) | copy-start | bytes 98308
  2.3 3.8 %copy-start.4 = (f32[8,8,128]{2,1,0:T(8,128)S(1)}, f32[8,8,128]{2,1,0:T(8,128)}, u32[]{:S(2)}) copy-start(f32[8,8,128]{2,1,0:T(8,128)} %param.27) | copy-start | bytes 98308
  2.3 8.5 %collective-permute-start.1 = (f32[2,8,4,128]{3,2,1,0:T(4,128)S(1)}, f32[2,8,4,128]{3,2,1,0:T(4,128)S(1)}, u32[]{:S(2)}, u32[]{:S(2)}) collective-permute-start(f32[2,8,4,128]{3,2,1,0:T(4,128)S(1)} %get-tuple-element.117), channel_id=1, source_target_pairs={{0,8},{8,0},{16,24},{24,16},{1,9},{9,1},{17,25},{25,17},{2,10},{10... | collective-permute-start | bytes 98312 | tf_op jit(solution)/shard_map/ppermute | solution.py:18
  3.0 7.7 %collective-permute-start = (f32[2,8,4,128]{3,2,1,0:T(4,128)S(1)}, f32[2,8,4,128]{3,2,1,0:T(4,128)S(1)}, u32[]{:S(2)}, u32[]{:S(2)}) collective-permute-start(f32[2,8,4,128]{3,2,1,0:T(4,128)S(1)} %get-tuple-element.118), channel_id=1, source_target_pairs={{8,16},{16,8},{9,17},{17,9},{10,18},{18,10},{11,19},{19,11},{12,20... | collective-permute-start | bytes 98312 | tf_op jit(solution)/shard_map/ppermute | solution.py:26
  6.1 1.4 %copy-start.19 = (s32[256]{0:T(256)S(1)}, s32[256]{0:T(256)}, u32[]{:S(2)}) copy-start(s32[256]{0:T(256)} %param.41) | copy-start | bytes 3076
  6.1 1.4 %copy-start.20 = (f32[64]{0:T(128)S(1)}, f32[64]{0:T(128)}, u32[]{:S(2)}) copy-start(f32[64]{0:T(128)} %param.38) | copy-start | bytes 772
  6.2 4.5 %collective-permute-start.2 = (f32[2,8,8,4]{3,2,1,0:T(8,128)S(1)}, f32[2,8,8,4]{3,2,1,0:T(8,128)S(1)}, u32[]{:S(2)}, u32[]{:S(2)}) collective-permute-start(f32[2,8,8,4]{3,2,1,0:T(8,128)S(1)} %fusion.50), channel_id=1, source_target_pairs={{0,4},{4,0},{1,5},{5,1},{2,6},{6,2},{3,7},{7,3},{8,12},{12,8},{9,1... | collective-permute-start | bytes 6152 | tf_op jit(solution)/shard_map/ppermute | solution.py:18
  7.5 0.7 %copy-start.16 = (f32[2,256]{1,0:T(2,128)S(1)}, f32[2,256]{1,0:T(2,128)}, u32[]{:S(2)}) copy-start(f32[2,256]{1,0:T(2,128)} %param.37) | copy-start | bytes 6148
  8.4 0.7 %copy-start.17 = (s32[256]{0:T(256)S(1)}, s32[256]{0:T(256)}, u32[]{:S(2)}) copy-start(s32[256]{0:T(256)} %param.40) | copy-start | bytes 3076
  8.4 0.8 %copy-start.18 = (s32[256]{0:T(256)S(1)}, s32[256]{0:T(256)}, u32[]{:S(2)}) copy-start(s32[256]{0:T(256)} %param.39) | copy-start | bytes 3076
  9.2 0.8 %copy-start.12 = (f32[8,8,128]{2,1,0:T(8,128)S(1)}, f32[8,8,128]{2,1,0:T(8,128)}, u32[]{:S(2)}) copy-start(f32[8,8,128]{2,1,0:T(8,128)} %param.33) | copy-start | bytes 98308
  9.2 0.8 %copy-start.13 = (f32[8,8,128]{2,1,0:T(8,128)S(1)}, f32[8,8,128]{2,1,0:T(8,128)}, u32[]{:S(2)}) copy-start(f32[8,8,128]{2,1,0:T(8,128)} %param.32) | copy-start | bytes 98308
  11.6 9.9 %all-to-all-start = ((f32[32,1,192]{2,1,0:T(1,128)}), f32[32,1,192]{2,1,0:T(1,128)S(1)}, u32[]{:S(2)}, u32[]{:S(2)}) async-start(f32[32,1,192]{2,1,0:T(1,128)} %copy.42), calls=%async_computation | async-start | bytes 65536 | tf_op jit(solution)/shard_map/all_to_all | solution.py:214
  16.4 4.8 %collective-permute-start.3 = (f32[2,8,8,4]{3,2,1,0:T(8,128)S(1)}, f32[2,8,8,4]{3,2,1,0:T(8,128)S(1)}, u32[]{:S(2)}, u32[]{:S(2)}) collective-permute-start(f32[2,8,8,4]{3,2,1,0:T(8,128)S(1)} %dynamic-slice_maximum_fusion.1), channel_id=1, source_target_pairs={{0,4},{4,0},{1,5},{5,1},{2,6},{6,2},{3,7},{7,3},{8,12},{12,8},{9,1... | collective-permute-start | bytes 6152 | tf_op jit(solution)/shard_map/ppermute | solution.py:18
  18.0 4.5 %collective-permute-start.4 = (f32[2,4,16,136]{3,2,1,0:T(8,128)S(1)}, f32[2,4,16,136]{3,2,1,0:T(8,128)S(1)}, u32[]{:S(2)}, u32[]{:S(2)}) collective-permute-start(f32[2,4,16,136]{3,2,1,0:T(8,128)S(1)} %get-tuple-element.76), channel_id=1, source_target_pairs={{0,1},{1,0},{2,3},{3,2},{4,5},{5,4},{6,7},{7,6},{8,9},{9,8},{10,11... | collective-permute-start | bytes 208904 | tf_op jit(solution)/shard_map/ppermute | solution.py:18
  19.3 5.7 %collective-permute-start.5 = (f32[2,4,16,136]{3,2,1,0:T(8,128)S(1)}, f32[2,4,16,136]{3,2,1,0:T(8,128)S(1)}, u32[]{:S(2)}, u32[]{:S(2)}) collective-permute-start(f32[2,4,16,136]{3,2,1,0:T(8,128)S(1)} %get-tuple-element.77), channel_id=1, source_target_pairs={{1,2},{2,1},{5,6},{6,5},{9,10},{10,9},{13,14},{14,13},{17,18},{18,... | collective-permute-start | bytes 208904 | tf_op jit(solution)/shard_map/ppermute | solution.py:26
  25.8 0.8 %copy-start.5 = (f32[8,8,128]{2,1,0:T(8,128)S(1)}, f32[8,8,128]{2,1,0:T(8,128)}, u32[]{:S(2)}) copy-start(f32[8,8,128]{2,1,0:T(8,128)} %param.29) | copy-start | bytes 98308
  25.8 0.8 %copy-start.6 = (f32[8,8,128]{2,1,0:T(8,128)S(1)}, f32[8,8,128]{2,1,0:T(8,128)}, u32[]{:S(2)}) copy-start(f32[8,8,128]{2,1,0:T(8,128)} %param.34) | copy-start | bytes 98308
  25.8 0.8 %copy-start.7 = (f32[8,8,128]{2,1,0:T(8,128)S(1)}, f32[8,8,128]{2,1,0:T(8,128)}, u32[]{:S(2)}) copy-start(f32[8,8,128]{2,1,0:T(8,128)} %param.35) | copy-start | bytes 98308
  25.8 0.8 %copy-start.8 = (f32[8,8,128]{2,1,0:T(8,128)S(1)}, f32[8,8,128]{2,1,0:T(8,128)}, u32[]{:S(2)}) copy-start(f32[8,8,128]{2,1,0:T(8,128)} %param.31) | copy-start | bytes 98308
  25.8 0.8 %copy-start.9 = (f32[8,8,128]{2,1,0:T(8,128)S(1)}, f32[8,8,128]{2,1,0:T(8,128)}, u32[]{:S(2)}) copy-start(f32[8,8,128]{2,1,0:T(8,128)} %param.30) | copy-start | bytes 98308
  25.9 0.8 %copy-start.14 = (f32[8,8,128]{2,1,0:T(8,128)S(1)}, f32[8,8,128]{2,1,0:T(8,128)}, u32[]{:S(2)}) copy-start(f32[8,8,128]{2,1,0:T(8,128)} %param.28) | copy-start | bytes 98308
  25.9 0.8 %copy-start.15 = (f32[8,8,128]{2,1,0:T(8,128)S(1)}, f32[8,8,128]{2,1,0:T(8,128)}, u32[]{:S(2)}) copy-start(f32[8,8,128]{2,1,0:T(8,128)} %param.26) | copy-start | bytes 98308
  26.7 17.6 %copy-start.1 = (f32[8,8,128]{2,1,0:T(8,128)}, f32[8,8,128]{2,1,0:T(8,128)S(1)}, u32[]{:S(2)}) copy-start(f32[8,8,128]{2,1,0:T(8,128)S(1)} %get-tuple-element.126) | copy-start | bytes 98308
  26.7 17.6 %copy-start.2 = (f32[8,8,128]{2,1,0:T(8,128)}, f32[8,8,128]{2,1,0:T(8,128)S(1)}, u32[]{:S(2)}) copy-start(f32[8,8,128]{2,1,0:T(8,128)S(1)} %get-tuple-element.127) | copy-start | bytes 98308
  26.8 5.8 %collective-permute-start.9 = (f32[2,8,8,4]{3,2,1,0:T(8,128)S(1)}, f32[2,8,8,4]{3,2,1,0:T(8,128)S(1)}, u32[]{:S(2)}, u32[]{:S(2)}) collective-permute-start(f32[2,8,8,4]{3,2,1,0:T(8,128)S(1)} %fusion.48), channel_id=1, source_target_pairs={{0,4},{4,0},{1,5},{5,1},{2,6},{6,2},{3,7},{7,3},{8,12},{12,8},{9,1... | collective-permute-start | bytes 6152 | tf_op jit(solution)/shard_map/ppermute | solution.py:18
  27.2 7.0 %collective-permute-start.7 = (f32[2,8,4,128]{3,2,1,0:T(4,128)S(1)}, f32[2,8,4,128]{3,2,1,0:T(4,128)S(1)}, u32[]{:S(2)}, u32[]{:S(2)}) collective-permute-start(f32[2,8,4,128]{3,2,1,0:T(4,128)S(1)} %get-tuple-element.96), channel_id=1, source_target_pairs={{8,16},{16,8},{9,17},{17,9},{10,18},{18,10},{11,19},{19,11},{12,20... | collective-permute-start | bytes 98312 | tf_op jit(solution)/shard_map/ppermute | solution.py:26
  32.5 1.6 %collective-permute-start.6 = (f32[2,8,4,128]{3,2,1,0:T(4,128)S(1)}, f32[2,8,4,128]{3,2,1,0:T(4,128)S(1)}, u32[]{:S(2)}, u32[]{:S(2)}) collective-permute-start(f32[2,8,4,128]{3,2,1,0:T(4,128)S(1)} %get-tuple-element.97), channel_id=1, source_target_pairs={{0,8},{8,0},{16,24},{24,16},{1,9},{9,1},{17,25},{25,17},{2,10},{10... | collective-permute-start | bytes 98312 | tf_op jit(solution)/shard_map/ppermute | solution.py:18
  34.3 3.9 %collective-permute-start.8 = (f32[2,8,8,4]{3,2,1,0:T(8,128)S(1)}, f32[2,8,8,4]{3,2,1,0:T(8,128)S(1)}, u32[]{:S(2)}, u32[]{:S(2)}) collective-permute-start(f32[2,8,8,4]{3,2,1,0:T(8,128)S(1)} %dynamic-slice_maximum_fusion), channel_id=1, source_target_pairs={{0,4},{4,0},{1,5},{5,1},{2,6},{6,2},{3,7},{7,3},{8,12},{12,8},{9,1... | collective-permute-start | bytes 6152 | tf_op jit(solution)/shard_map/ppermute | solution.py:18
  35.8 5.0 %collective-permute-start.10 = (f32[2,4,16,136]{3,2,1,0:T(8,128)S(1)}, f32[2,4,16,136]{3,2,1,0:T(8,128)S(1)}, u32[]{:S(2)}, u32[]{:S(2)}) collective-permute-start(f32[2,4,16,136]{3,2,1,0:T(8,128)S(1)} %get-tuple-element.72), channel_id=1, source_target_pairs={{0,1},{1,0},{2,3},{3,2},{4,5},{5,4},{6,7},{7,6},{8,9},{9,8},{10,11... | collective-permute-start | bytes 208904 | tf_op jit(solution)/shard_map/ppermute | solution.py:18
  35.9 6.9 %collective-permute-start.11 = (f32[2,4,16,136]{3,2,1,0:T(8,128)S(1)}, f32[2,4,16,136]{3,2,1,0:T(8,128)S(1)}, u32[]{:S(2)}, u32[]{:S(2)}) collective-permute-start(f32[2,4,16,136]{3,2,1,0:T(8,128)S(1)} %get-tuple-element.73), channel_id=1, source_target_pairs={{1,2},{2,1},{5,6},{6,5},{9,10},{10,9},{13,14},{14,13},{17,18},{18,... | collective-permute-start | bytes 208904 | tf_op jit(solution)/shard_map/ppermute | solution.py:26
  44.4 0.6 %copy-start.10 = (f32[8,8,128]{2,1,0:T(8,128)}, f32[8,8,128]{2,1,0:T(8,128)S(1)}, u32[]{:S(2)}) copy-start(f32[8,8,128]{2,1,0:T(8,128)S(1)} %get-tuple-element.124) | copy-start | bytes 98308
  44.4 0.6 %copy-start.11 = (f32[8,8,128]{2,1,0:T(8,128)}, f32[8,8,128]{2,1,0:T(8,128)S(1)}, u32[]{:S(2)}) copy-start(f32[8,8,128]{2,1,0:T(8,128)S(1)} %get-tuple-element.125) | copy-start | bytes 98308

commit v12 on v11

--- a/solution.py
+++ b/solution.py
@@ -37,23 +37,23 @@
 
 
 def first_round(block, width):
-    low_x, high_x = shift_pair(block, 2, width, "inl")
+    low_z, high_z = shift_pair(block, 1, width, "gz")
     low_y, high_y = shift_pair(block, 3, width, "xl")
-    return low_x, high_x, low_y, high_y
+    return low_z, high_z, low_y, high_y
 
 
 def second_round(block, width, faces):
-    low_x, high_x, low_y, high_y = faces
-    strips = jnp.concatenate([low_x, high_x], axis=2)
+    low_z, high_z, low_y, high_y = faces
+    strips = jnp.concatenate([low_z, high_z], axis=1)
     low_c, high_c = shift_pair(strips, 3, width, "xl")
-    wide_x = jnp.concatenate([low_x, block, high_x], axis=2)
-    pad_x = ((0, 0), (0, 0), (width, width), (0, 0))
-    bare = jnp.concatenate([jnp.pad(low_y, pad_x), wide_x, jnp.pad(high_y, pad_x)], axis=3)
-    low_z, high_z = shift_pair(bare, 1, width, "gz")
-    side_low = jnp.concatenate([low_c[:, :, :width], low_y, low_c[:, :, width:]], axis=2)
-    side_high = jnp.concatenate([high_c[:, :, :width], high_y, high_c[:, :, width:]], axis=2)
-    full = jnp.concatenate([side_low, wide_x, side_high], axis=3)
-    return jnp.concatenate([low_z, full, high_z], axis=1)
+    wide_z = jnp.concatenate([low_z, block, high_z], axis=1)
+    pad_z = ((0, 0), (width, width), (0, 0), (0, 0))
+    bare = jnp.concatenate([jnp.pad(low_y, pad_z), wide_z, jnp.pad(high_y, pad_z)], axis=3)
+    low_x, high_x = shift_pair(bare, 2, width, "inl")
+    side_low = jnp.concatenate([low_c[:, :width], low_y, low_c[:, width:]], axis=1)
+    side_high = jnp.concatenate([high_c[:, :width], high_y, high_c[:, width:]], axis=1)
+    full = jnp.concatenate([side_low, wide_z, side_high], axis=3)
+    return jnp.concatenate([low_x, full, high_x], axis=2)
 
 
 def with_halo(block, width):

time: 45.8 us -> 45 us (0.983)
  waiting for transfers between devices: 8.83 us -> 6.74 us
  starting transfers between devices: 23.4 us -> 25.1 us
    ppermute x8, waiting for transfers between devices: 2.91 us -> 0.02 us  [shift_pair(): lax.ppermute(lax.dynamic_slice_in_dim(block, jnp.where(even, size - width...]
    ppermute x8, starting transfers between devices: 6.26 us -> 7.42 us  [shift_pair(): lax.ppermute(lax.dynamic_slice_in_dim(block, jnp.where(even, size - width...]
    all_to_all x1, starting transfers between devices: 4.84 us -> 5.86 us  [local(): lax.all_to_all(send, ('inl', 'xl', 'gz'), split_axis=0, concat_axis=0, ti...]
    ppermute x4, waiting for transfers between devices: 5.92 us -> 6.72 us  [shift_pair(): lax.ppermute(lax.dynamic_slice_in_dim(block, jnp.where(even, 0, size - wi...]
    concatenate x10 -> x12, other arithmetic: 1.69 us -> 1.68 us  [the longest x4 0.91 us: second_round(): return jnp.concatenate([low_x, full, high_x], axis=2)]
  transfers between devices with their start and end apart: 13 -> 13, of which waited for: 6 -> 3; matrix products, arithmetic and copies ran while one was open for 7% -> 8% of each run, Pallas kernels for 0% -> 0%
where the time goes in v12:
time: 45 us; the launch traced here: 44.5 us
  starting transfers between devices  25.1 us (56%)
  waiting for transfers between devices  6.74 us (15%)
  other arithmetic  5.21 us (12%)
  local copies, waits for them, and re-layouts  4.61 us (10%)
  matrix products  1.52 us (3%)
  between operations  1.3 us (3%)
    ppermute x4, starting transfers between devices, shift_pair(): lax.ppermute(lax.dynamic_slice_in_dim(block, jnp.where(even, 0, size - wi...  11.9 us
    ppermute x8, starting transfers between devices, shift_pair(): lax.ppermute(lax.dynamic_slice_in_dim(block, jnp.where(even, size - width...  7.42 us
    ppermute x4, waiting for transfers between devices, shift_pair(): lax.ppermute(lax.dynamic_slice_in_dim(block, jnp.where(even, 0, size - wi...  6.72 us
    all_to_all x1, starting transfers between devices, local(): lax.all_to_all(send, ('inl', 'xl', 'gz'), split_axis=0, concat_axis=0, ti...  5.86 us
    unnamed x43, local copies, waits for them, and re-layouts  3.49 us
    sub x2, other arithmetic, advance(): h_two = u_xx + u_yy + u_zz - h_one  1.18 us
    concatenate x4, other arithmetic, second_round(): return jnp.concatenate([low_x, full, high_x], axis=2)  0.91 us
  transfers between devices with their start and end apart: 13, of which 3 were waited for; matrix products, arithmetic and copies ran while one was open for 8% of the time, Pallas kernels for 0%

profile of v12, /device:TPU:17, one launch (start us, length us, event | category | flops | bytes accessed | tf_op | source)
XLA Modules:
  0.0 44.5 jit_solution(4947390092573912090)
XLA Ops:
  0.6 0.0 copy-start
  0.7 0.8 %copy-done.3 = f32[8,8,128]{2,1,0:T(8,128)S(1)} copy-done((f32[8,8,128]{2,1,0:T(8,128)S(1)}, f32[8,8,128]{2,1,0:T(8,128)}, u32[]{:S(2)}) %copy-start.3) | copy-done | bytes 32792
  1.4 0.7 %fusion.160 = (f32[2,4,8,128]{3,2,1,0:T(8,128)S(1)}, f32[2,4,8,128]{3,2,1,0:T(8,128)S(1)}) fusion(s32[]{:T(128)S(6)} %select_n.208, f32[1,8,8,128]{3,2,1,0:T(8,128)S(1)} %bitcast.134, f32[1,8,8,128]{3,2,1,0:T(8,128)} %bitcast.142, s32[]{:T(128)S(6)} %select_n.207), kind=kLoop, calls=%fused_computation.277 | loop fusion | flops 16384 | bytes 131080 | tf_op jit(solution)/shard_map/stack | solution.py:231
  2.2 1.4 %collective-permute-start.1 = (f32[2,4,8,128]{3,2,1,0:T(8,128)S(1)}, f32[2,4,8,128]{3,2,1,0:T(8,128)S(1)}, u32[]{:S(2)}, u32[]{:S(2)}) collective-permute-start(f32[2,4,8,128]{3,2,1,0:T(8,128)S(1)} %get-tuple-element.117), channel_id=1, source_target_pairs={{0,1},{1,0},{2,3},{3,2},{4,5},{5,4},{6,7},{7,6},{8,9},{9,8},{10,11... | collective-permute-start | bytes 98312 | tf_op jit(solution)/shard_map/ppermute | solution.py:18
  3.5 1.9 %collective-permute-start = (f32[2,4,8,128]{3,2,1,0:T(8,128)S(1)}, f32[2,4,8,128]{3,2,1,0:T(8,128)S(1)}, u32[]{:S(2)}, u32[]{:S(2)}) collective-permute-start(f32[2,4,8,128]{3,2,1,0:T(8,128)S(1)} %get-tuple-element.118), channel_id=1, source_target_pairs={{1,2},{2,1},{5,6},{6,5},{9,10},{10,9},{13,14},{14,13},{17,18},{18,... | collective-permute-start | bytes 98312 | tf_op jit(solution)/shard_map/ppermute | solution.py:26
  5.5 0.1 fusion.50
  5.6 1.2 %collective-permute-start.2 = (f32[2,8,8,4]{3,2,1,0:T(8,128)S(1)}, f32[2,8,8,4]{3,2,1,0:T(8,128)S(1)}, u32[]{:S(2)}, u32[]{:S(2)}) collective-permute-start(f32[2,8,8,4]{3,2,1,0:T(8,128)S(1)} %fusion.50), channel_id=1, source_target_pairs={{0,4},{4,0},{1,5},{5,1},{2,6},{6,2},{3,7},{7,3},{8,12},{12,8},{9,1... | collective-permute-start | bytes 6152 | tf_op jit(solution)/shard_map/ppermute | solution.py:18
  6.9 0.1 select_reduce_fusion
  7.0 0.6 %copy-done.16 = f32[2,256]{1,0:T(2,128)S(1)} copy-done((f32[2,256]{1,0:T(2,128)S(1)}, f32[2,256]{1,0:T(2,128)}, u32[]{:S(2)}) %copy-start.16) | copy-done | bytes 2072
  7.5 0.3 convolution_multiply_fusion
  7.8 0.1 copy-start.18
  7.9 0.7 %copy-done.17 = s32[256]{0:T(256)S(1)} copy-done((s32[256]{0:T(256)S(1)}, s32[256]{0:T(256)}, u32[]{:S(2)}) %copy-start.17) | copy-done | bytes 1048
  8.5 0.0 copy-done.18
  8.6 0.2 fusion
  8.8 0.5 %copy-done.12 = f32[8,8,128]{2,1,0:T(8,128)S(1)} copy-done((f32[8,8,128]{2,1,0:T(8,128)S(1)}, f32[8,8,128]{2,1,0:T(8,128)}, u32[]{:S(2)}) %copy-start.12) | copy-done | bytes 32792
  9.3 0.0 copy-done.13
  9.3 0.2 fusion.204
  9.6 0.4 fusion.18
  10.2 0.1 dynamic-slice_maximum_fusion.1
  10.3 0.6 %copy.42 = f32[32,1,192]{2,1,0:T(1,128)} copy(f32[32,1,192]{2,0,1:T(8,128)S(1)} %bitcast.162) | data formatting | bytes 49152 | tf_op jit(solution)/shard_map/all_to_all | solution.py:214
  10.9 5.9 %all-to-all-start = ((f32[32,1,192]{2,1,0:T(1,128)}), f32[32,1,192]{2,1,0:T(1,128)S(1)}, u32[]{:S(2)}, u32[]{:S(2)}) async-start(f32[32,1,192]{2,1,0:T(1,128)} %copy.42), calls=%async_computation | async-start | bytes 65536 | tf_op jit(solution)/shard_map/all_to_all | solution.py:214
  16.8 1.2 %collective-permute-start.3 = (f32[2,8,8,4]{3,2,1,0:T(8,128)S(1)}, f32[2,8,8,4]{3,2,1,0:T(8,128)S(1)}, u32[]{:S(2)}, u32[]{:S(2)}) collective-permute-start(f32[2,8,8,4]{3,2,1,0:T(8,128)S(1)} %dynamic-slice_maximum_fusion.1), channel_id=1, source_target_pairs={{0,4},{4,0},{1,5},{5,1},{2,6},{6,2},{3,7},{7,3},{8,12},{12,8},{9,1... | collective-permute-start | bytes 6152 | tf_op jit(solution)/shard_map/ppermute | solution.py:18
  18.0 0.1 select_maximum_fusion.2
  18.2 0.1 constant_dynamic-slice_fusion.3
  18.2 0.7 %collective-permute-start.4 = (f32[2,16,4,136]{3,2,1,0:T(4,128)S(1)}, f32[2,16,4,136]{3,2,1,0:T(4,128)S(1)}, u32[]{:S(2)}, u32[]{:S(2)}) collective-permute-start(f32[2,16,4,136]{3,2,1,0:T(4,128)S(1)} %get-tuple-element.76), channel_id=1, source_target_pairs={{0,8},{8,0},{16,24},{24,16},{1,9},{9,1},{17,25},{25,17},{2,10},{10... | collective-permute-start | bytes 208904 | tf_op jit(solution)/shard_map/ppermute | solution.py:18
  19.0 3.0 %collective-permute-start.5 = (f32[2,16,4,136]{3,2,1,0:T(4,128)S(1)}, f32[2,16,4,136]{3,2,1,0:T(4,128)S(1)}, u32[]{:S(2)}, u32[]{:S(2)}) collective-permute-start(f32[2,16,4,136]{3,2,1,0:T(4,128)S(1)} %get-tuple-element.77), channel_id=1, source_target_pairs={{8,16},{16,8},{9,17},{17,9},{10,18},{18,10},{11,19},{19,11},{12,20... | collective-permute-start | bytes 208904 | tf_op jit(solution)/shard_map/ppermute | solution.py:26
  22.0 0.1 maximum_maximum_fusion.2
  22.2 0.3 fusion.31
  22.6 0.1 reshape.205
  22.7 0.6 %convolution_bitcast_fusion = f32[16,128]{1,0:T(8,128)S(1)} fusion(s32[32,64]{1,0:T(8,128)S(1)} %add_select_fusion, f32[8,32,64]{2,0,1:T(8,128)S(1)} %fusion.45, f32[2,32,64]{2,0,1:T(2,128)S(1)} %bitcast.161), kind=kOutput, calls=%fused_computation.1 | convolution fusion | flops 50626560 | bytes 98304 | tf_op jit(solution)/shard_map/dot_general | solution.py:227
  23.3 1.9 %collective-permute-done.5 = f32[2,16,4,136]{3,2,1,0:T(4,128)S(1)} collective-permute-done((f32[2,16,4,136]{3,2,1,0:T(4,128)S(1)}, f32[2,16,4,136]{3,2,1,0:T(4,128)S(1)}, u32[]{:S(2)}, u32[]{:S(2)}) %collective-permute-start.5) | collective-permute-done | bytes 69664 | tf_op jit(solution)/shard_map/ppermute | solution.py:26
  25.3 0.2 pad_maximum_fusion
  25.4 0.3 maximum_maximum_fusion
  25.7 0.2 fusion.10
  26.0 0.6 %add_subtract_fusion.1 = (f32[2,8,8,128]{3,2,1,0:T(8,128)S(1)}, f32[2,8,8,128]{3,2,1,0:T(8,128)S(1)}) fusion(f32[2,16,8,128]{3,2,1,0:T(8,128)S(1)} %fusion.31, f32[8,8,128]{2,1,0:T(8,128)S(1)} %get-tuple-element.102, f32[2,16,8,136]{3,2,1,0:T(8,128)S(1)} %fusion.10, f32[8,8,128]{2,1,0:T(8,128)S(1)} %get-tuple-element.103, ...), kind=kLoop, calls=%fused_computation.260 | loop fusion | flops 1392640 | bytes 3538944 | tf_op jit(solution)/shard_map/sub | solution.py:135
  26.6 0.1 copy-done.5
  26.7 0.0 copy-done.6
  26.7 0.0 copy-done.7
  26.7 0.0 copy-done.8
  26.8 0.0 copy-done.9
  26.8 0.0 copy-done.14
  26.8 0.0 copy-done.15
  26.9 0.0 copy-start.1
  26.9 0.1 fusion.48
  27.0 0.3 collective-permute-start.9
  27.3 1.2 %collective-permute-start.7 = (f32[2,4,8,128]{3,2,1,0:T(8,128)S(1)}, f32[2,4,8,128]{3,2,1,0:T(8,128)S(1)}, u32[]{:S(2)}, u32[]{:S(2)}) collective-permute-start(f32[2,4,8,128]{3,2,1,0:T(8,128)S(1)} %get-tuple-element.98), channel_id=1, source_target_pairs={{0,1},{1,0},{2,3},{3,2},{4,5},{5,4},{6,7},{7,6},{8,9},{9,8},{10,11... | collective-permute-start | bytes 98312 | tf_op jit(solution)/shard_map/ppermute | solution.py:18
  28.5 1.9 %collective-permute-start.6 = (f32[2,4,8,128]{3,2,1,0:T(8,128)S(1)}, f32[2,4,8,128]{3,2,1,0:T(8,128)S(1)}, u32[]{:S(2)}, u32[]{:S(2)}) collective-permute-start(f32[2,4,8,128]{3,2,1,0:T(8,128)S(1)} %get-tuple-element.99), channel_id=1, source_target_pairs={{1,2},{2,1},{5,6},{6,5},{9,10},{10,9},{13,14},{14,13},{17,18},{18,... | collective-permute-start | bytes 98312 | tf_op jit(solution)/shard_map/ppermute | solution.py:26
  30.5 2.7 %collective-permute-done.6 = f32[2,4,8,128]{3,2,1,0:T(8,128)S(1)} collective-permute-done((f32[2,4,8,128]{3,2,1,0:T(8,128)S(1)}, f32[2,4,8,128]{3,2,1,0:T(8,128)S(1)}, u32[]{:S(2)}, u32[]{:S(2)}) %collective-permute-start.6) | collective-permute-done | bytes 32800 | tf_op jit(solution)/shard_map/ppermute | solution.py:26
  33.2 0.1 dynamic-slice_maximum_fusion
  33.3 1.2 %collective-permute-start.8 = (f32[2,8,8,4]{3,2,1,0:T(8,128)S(1)}, f32[2,8,8,4]{3,2,1,0:T(8,128)S(1)}, u32[]{:S(2)}, u32[]{:S(2)}) collective-permute-start(f32[2,8,8,4]{3,2,1,0:T(8,128)S(1)} %dynamic-slice_maximum_fusion), channel_id=1, source_target_pairs={{0,4},{4,0},{1,5},{5,1},{2,6},{6,2},{3,7},{7,3},{8,12},{12,8},{9,1... | collective-permute-start | bytes 6152 | tf_op jit(solution)/shard_map/ppermute | solution.py:18
  34.5 0.1 select_maximum_fusion
  34.7 0.1 constant_dynamic-slice_fusion.1
  34.8 0.1 collective-permute-start.10
  34.8 5.0 %collective-permute-start.11 = (f32[2,16,4,136]{3,2,1,0:T(4,128)S(1)}, f32[2,16,4,136]{3,2,1,0:T(4,128)S(1)}, u32[]{:S(2)}, u32[]{:S(2)}) collective-permute-start(f32[2,16,4,136]{3,2,1,0:T(4,128)S(1)} %get-tuple-element.73), channel_id=1, source_target_pairs={{8,16},{16,8},{9,17},{17,9},{10,18},{18,10},{11,19},{19,11},{12,20... | collective-permute-start | bytes 208904 | tf_op jit(solution)/shard_map/ppermute | solution.py:26
  39.9 0.1 maximum_maximum_fusion.4
  40.1 0.3 fusion.24
  40.4 2.1 %collective-permute-done.11 = f32[2,16,4,136]{3,2,1,0:T(4,128)S(1)} collective-permute-done((f32[2,16,4,136]{3,2,1,0:T(4,128)S(1)}, f32[2,16,4,136]{3,2,1,0:T(4,128)S(1)}, u32[]{:S(2)}, u32[]{:S(2)}) %collective-permute-start.11) | collective-permute-done | bytes 69664 | tf_op jit(solution)/shard_map/ppermute | solution.py:26
  42.5 0.2 pad_maximum_fusion.1
  42.7 0.3 maximum_maximum_fusion.1
  43.0 0.2 fusion.3
  43.2 0.6 %add_subtract_fusion = (f32[2,8,8,128]{3,2,1,0:T(8,128)S(1)}, f32[2,8,8,128]{3,2,1,0:T(8,128)S(1)}) fusion(f32[2,16,8,128]{3,2,1,0:T(8,128)S(1)} %fusion.24, f32[8,8,128]{2,1,0:T(8,128)S(1)} %get-tuple-element.102, f32[2,16,8,136]{3,2,1,0:T(8,128)S(1)} %fusion.3, f32[8,8,128]{2,1,0:T(8,128)S(1)} %get-tuple-element.103, ...), kind=kLoop, calls=%fused_computation.259 | loop fusion | flops 1392640 | bytes 3538944 | tf_op jit(solution)/shard_map/sub | solution.py:135
  43.9 0.0 copy-start.10
  43.9 0.6 %copy-done.10 = f32[8,8,128]{2,1,0:T(8,128)} copy-done((f32[8,8,128]{2,1,0:T(8,128)}, f32[8,8,128]{2,1,0:T(8,128)S(1)}, u32[]{:S(2)}) %copy-start.10) | copy-done | bytes 32792
  44.5 0.0 copy-done.11
  (63 shorter events, 0.5 us)
Async XLA Ops:
  0.6 6.3 %copy-start = (f32[256,256]{1,0:T(8,128)S(1)}, f32[256,256]{1,0:T(8,128)}, u32[]{:S(2)}) copy-start(f32[256,256]{1,0:T(8,128)} %param.36) | copy-start | bytes 786436
  0.6 0.8 %copy-start.3 = (f32[8,8,128]{2,1,0:T(8,128)S(1)}, f32[8,8,128]{2,1,0:T(8,128)}, u32[]{:S(2)}) copy-start(f32[8,8,128]{2,1,0:T(8,128)} %param.25) | copy-start | bytes 98308
  2.2 3.3 %copy-start.4 = (f32[8,8,128]{2,1,0:T(8,128)S(1)}, f32[8,8,128]{2,1,0:T(8,128)}, u32[]{:S(2)}) copy-start(f32[8,8,128]{2,1,0:T(8,128)} %param.27) | copy-start | bytes 98308
  2.2 7.9 %collective-permute-start.1 = (f32[2,4,8,128]{3,2,1,0:T(8,128)S(1)}, f32[2,4,8,128]{3,2,1,0:T(8,128)S(1)}, u32[]{:S(2)}, u32[]{:S(2)}) collective-permute-start(f32[2,4,8,128]{3,2,1,0:T(8,128)S(1)} %get-tuple-element.117), channel_id=1, source_target_pairs={{0,1},{1,0},{2,3},{3,2},{4,5},{5,4},{6,7},{7,6},{8,9},{9,8},{10,11... | collective-permute-start | bytes 98312 | tf_op jit(solution)/shard_map/ppermute | solution.py:18
  3.5 6.6 %collective-permute-start = (f32[2,4,8,128]{3,2,1,0:T(8,128)S(1)}, f32[2,4,8,128]{3,2,1,0:T(8,128)S(1)}, u32[]{:S(2)}, u32[]{:S(2)}) collective-permute-start(f32[2,4,8,128]{3,2,1,0:T(8,128)S(1)} %get-tuple-element.118), channel_id=1, source_target_pairs={{1,2},{2,1},{5,6},{6,5},{9,10},{10,9},{13,14},{14,13},{17,18},{18,... | collective-permute-start | bytes 98312 | tf_op jit(solution)/shard_map/ppermute | solution.py:26
  5.5 1.4 %copy-start.19 = (s32[256]{0:T(256)S(1)}, s32[256]{0:T(256)}, u32[]{:S(2)}) copy-start(s32[256]{0:T(256)} %param.41) | copy-start | bytes 3076
  5.5 1.4 %copy-start.20 = (f32[64]{0:T(128)S(1)}, f32[64]{0:T(128)}, u32[]{:S(2)}) copy-start(f32[64]{0:T(128)} %param.38) | copy-start | bytes 772
  5.6 4.5 %collective-permute-start.2 = (f32[2,8,8,4]{3,2,1,0:T(8,128)S(1)}, f32[2,8,8,4]{3,2,1,0:T(8,128)S(1)}, u32[]{:S(2)}, u32[]{:S(2)}) collective-permute-start(f32[2,8,8,4]{3,2,1,0:T(8,128)S(1)} %fusion.50), channel_id=1, source_target_pairs={{0,4},{4,0},{1,5},{5,1},{2,6},{6,2},{3,7},{7,3},{8,12},{12,8},{9,1... | collective-permute-start | bytes 6152 | tf_op jit(solution)/shard_map/ppermute | solution.py:18
  6.8 0.7 %copy-start.16 = (f32[2,256]{1,0:T(2,128)S(1)}, f32[2,256]{1,0:T(2,128)}, u32[]{:S(2)}) copy-start(f32[2,256]{1,0:T(2,128)} %param.37) | copy-start | bytes 6148
  7.8 0.7 %copy-start.17 = (s32[256]{0:T(256)S(1)}, s32[256]{0:T(256)}, u32[]{:S(2)}) copy-start(s32[256]{0:T(256)} %param.40) | copy-start | bytes 3076
  7.8 0.8 %copy-start.18 = (s32[256]{0:T(256)S(1)}, s32[256]{0:T(256)}, u32[]{:S(2)}) copy-start(s32[256]{0:T(256)} %param.39) | copy-start | bytes 3076
  8.6 0.8 %copy-start.12 = (f32[8,8,128]{2,1,0:T(8,128)S(1)}, f32[8,8,128]{2,1,0:T(8,128)}, u32[]{:S(2)}) copy-start(f32[8,8,128]{2,1,0:T(8,128)} %param.33) | copy-start | bytes 98308
  8.6 0.8 %copy-start.13 = (f32[8,8,128]{2,1,0:T(8,128)S(1)}, f32[8,8,128]{2,1,0:T(8,128)}, u32[]{:S(2)}) copy-start(f32[8,8,128]{2,1,0:T(8,128)} %param.32) | copy-start | bytes 98308
  10.9 11.6 %all-to-all-start = ((f32[32,1,192]{2,1,0:T(1,128)}), f32[32,1,192]{2,1,0:T(1,128)S(1)}, u32[]{:S(2)}, u32[]{:S(2)}) async-start(f32[32,1,192]{2,1,0:T(1,128)} %copy.42), calls=%async_computation | async-start | bytes 65536 | tf_op jit(solution)/shard_map/all_to_all | solution.py:214
  16.8 5.2 %collective-permute-start.3 = (f32[2,8,8,4]{3,2,1,0:T(8,128)S(1)}, f32[2,8,8,4]{3,2,1,0:T(8,128)S(1)}, u32[]{:S(2)}, u32[]{:S(2)}) collective-permute-start(f32[2,8,8,4]{3,2,1,0:T(8,128)S(1)} %dynamic-slice_maximum_fusion.1), channel_id=1, source_target_pairs={{0,4},{4,0},{1,5},{5,1},{2,6},{6,2},{3,7},{7,3},{8,12},{12,8},{9,1... | collective-permute-start | bytes 6152 | tf_op jit(solution)/shard_map/ppermute | solution.py:18
  18.2 5.1 %collective-permute-start.4 = (f32[2,16,4,136]{3,2,1,0:T(4,128)S(1)}, f32[2,16,4,136]{3,2,1,0:T(4,128)S(1)}, u32[]{:S(2)}, u32[]{:S(2)}) collective-permute-start(f32[2,16,4,136]{3,2,1,0:T(4,128)S(1)} %get-tuple-element.76), channel_id=1, source_target_pairs={{0,8},{8,0},{16,24},{24,16},{1,9},{9,1},{17,25},{25,17},{2,10},{10... | collective-permute-start | bytes 208904 | tf_op jit(solution)/shard_map/ppermute | solution.py:18
  19.0 6.3 %collective-permute-start.5 = (f32[2,16,4,136]{3,2,1,0:T(4,128)S(1)}, f32[2,16,4,136]{3,2,1,0:T(4,128)S(1)}, u32[]{:S(2)}, u32[]{:S(2)}) collective-permute-start(f32[2,16,4,136]{3,2,1,0:T(4,128)S(1)} %get-tuple-element.77), channel_id=1, source_target_pairs={{8,16},{16,8},{9,17},{17,9},{10,18},{18,10},{11,19},{19,11},{12,20... | collective-permute-start | bytes 208904 | tf_op jit(solution)/shard_map/ppermute | solution.py:26
  25.9 0.8 %copy-start.5 = (f32[8,8,128]{2,1,0:T(8,128)S(1)}, f32[8,8,128]{2,1,0:T(8,128)}, u32[]{:S(2)}) copy-start(f32[8,8,128]{2,1,0:T(8,128)} %param.29) | copy-start | bytes 98308
  26.0 0.8 %copy-start.6 = (f32[8,8,128]{2,1,0:T(8,128)S(1)}, f32[8,8,128]{2,1,0:T(8,128)}, u32[]{:S(2)}) copy-start(f32[8,8,128]{2,1,0:T(8,128)} %param.34) | copy-start | bytes 98308
  26.0 0.8 %copy-start.7 = (f32[8,8,128]{2,1,0:T(8,128)S(1)}, f32[8,8,128]{2,1,0:T(8,128)}, u32[]{:S(2)}) copy-start(f32[8,8,128]{2,1,0:T(8,128)} %param.35) | copy-start | bytes 98308
  26.0 0.8 %copy-start.8 = (f32[8,8,128]{2,1,0:T(8,128)S(1)}, f32[8,8,128]{2,1,0:T(8,128)}, u32[]{:S(2)}) copy-start(f32[8,8,128]{2,1,0:T(8,128)} %param.30) | copy-start | bytes 98308
  26.0 0.8 %copy-start.9 = (f32[8,8,128]{2,1,0:T(8,128)S(1)}, f32[8,8,128]{2,1,0:T(8,128)}, u32[]{:S(2)}) copy-start(f32[8,8,128]{2,1,0:T(8,128)} %param.31) | copy-start | bytes 98308
  26.0 0.8 %copy-start.14 = (f32[8,8,128]{2,1,0:T(8,128)S(1)}, f32[8,8,128]{2,1,0:T(8,128)}, u32[]{:S(2)}) copy-start(f32[8,8,128]{2,1,0:T(8,128)} %param.26) | copy-start | bytes 98308
  26.0 0.8 %copy-start.15 = (f32[8,8,128]{2,1,0:T(8,128)S(1)}, f32[8,8,128]{2,1,0:T(8,128)}, u32[]{:S(2)}) copy-start(f32[8,8,128]{2,1,0:T(8,128)} %param.28) | copy-start | bytes 98308
  26.9 16.9 %copy-start.1 = (f32[8,8,128]{2,1,0:T(8,128)}, f32[8,8,128]{2,1,0:T(8,128)S(1)}, u32[]{:S(2)}) copy-start(f32[8,8,128]{2,1,0:T(8,128)S(1)} %get-tuple-element.126) | copy-start | bytes 98308
  26.9 16.9 %copy-start.2 = (f32[8,8,128]{2,1,0:T(8,128)}, f32[8,8,128]{2,1,0:T(8,128)S(1)}, u32[]{:S(2)}) copy-start(f32[8,8,128]{2,1,0:T(8,128)S(1)} %get-tuple-element.127) | copy-start | bytes 98308
  27.0 3.5 %collective-permute-start.9 = (f32[2,8,8,4]{3,2,1,0:T(8,128)S(1)}, f32[2,8,8,4]{3,2,1,0:T(8,128)S(1)}, u32[]{:S(2)}, u32[]{:S(2)}) collective-permute-start(f32[2,8,8,4]{3,2,1,0:T(8,128)S(1)} %fusion.48), channel_id=1, source_target_pairs={{0,4},{4,0},{1,5},{5,1},{2,6},{6,2},{3,7},{7,3},{8,12},{12,8},{9,1... | collective-permute-start | bytes 6152 | tf_op jit(solution)/shard_map/ppermute | solution.py:18
  27.3 3.2 %collective-permute-start.7 = (f32[2,4,8,128]{3,2,1,0:T(8,128)S(1)}, f32[2,4,8,128]{3,2,1,0:T(8,128)S(1)}, u32[]{:S(2)}, u32[]{:S(2)}) collective-permute-start(f32[2,4,8,128]{3,2,1,0:T(8,128)S(1)} %get-tuple-element.98), channel_id=1, source_target_pairs={{0,1},{1,0},{2,3},{3,2},{4,5},{5,4},{6,7},{7,6},{8,9},{9,8},{10,11... | collective-permute-start | bytes 98312 | tf_op jit(solution)/shard_map/ppermute | solution.py:18
  28.5 4.6 %collective-permute-start.6 = (f32[2,4,8,128]{3,2,1,0:T(8,128)S(1)}, f32[2,4,8,128]{3,2,1,0:T(8,128)S(1)}, u32[]{:S(2)}, u32[]{:S(2)}) collective-permute-start(f32[2,4,8,128]{3,2,1,0:T(8,128)S(1)} %get-tuple-element.99), channel_id=1, source_target_pairs={{1,2},{2,1},{5,6},{6,5},{9,10},{10,9},{13,14},{14,13},{17,18},{18,... | collective-permute-start | bytes 98312 | tf_op jit(solution)/shard_map/ppermute | solution.py:26
  33.3 6.6 %collective-permute-start.8 = (f32[2,8,8,4]{3,2,1,0:T(8,128)S(1)}, f32[2,8,8,4]{3,2,1,0:T(8,128)S(1)}, u32[]{:S(2)}, u32[]{:S(2)}) collective-permute-start(f32[2,8,8,4]{3,2,1,0:T(8,128)S(1)} %dynamic-slice_maximum_fusion), channel_id=1, source_target_pairs={{0,4},{4,0},{1,5},{5,1},{2,6},{6,2},{3,7},{7,3},{8,12},{12,8},{9,1... | collective-permute-start | bytes 6152 | tf_op jit(solution)/shard_map/ppermute | solution.py:18
  34.8 5.6 %collective-permute-start.10 = (f32[2,16,4,136]{3,2,1,0:T(4,128)S(1)}, f32[2,16,4,136]{3,2,1,0:T(4,128)S(1)}, u32[]{:S(2)}, u32[]{:S(2)}) collective-permute-start(f32[2,16,4,136]{3,2,1,0:T(4,128)S(1)} %get-tuple-element.72), channel_id=1, source_target_pairs={{0,8},{8,0},{16,24},{24,16},{1,9},{9,1},{17,25},{25,17},{2,10},{10... | collective-permute-start | bytes 208904 | tf_op jit(solution)/shard_map/ppermute | solution.py:18
  34.8 7.7 %collective-permute-start.11 = (f32[2,16,4,136]{3,2,1,0:T(4,128)S(1)}, f32[2,16,4,136]{3,2,1,0:T(4,128)S(1)}, u32[]{:S(2)}, u32[]{:S(2)}) collective-permute-start(f32[2,16,4,136]{3,2,1,0:T(4,128)S(1)} %get-tuple-element.73), channel_id=1, source_target_pairs={{8,16},{16,8},{9,17},{17,9},{10,18},{18,10},{11,19},{19,11},{12,20... | collective-permute-start | bytes 208904 | tf_op jit(solution)/shard_map/ppermute | solution.py:26
  43.9 0.6 %copy-start.10 = (f32[8,8,128]{2,1,0:T(8,128)}, f32[8,8,128]{2,1,0:T(8,128)S(1)}, u32[]{:S(2)}) copy-start(f32[8,8,128]{2,1,0:T(8,128)S(1)} %get-tuple-element.124) | copy-start | bytes 98308
  43.9 0.6 %copy-start.11 = (f32[8,8,128]{2,1,0:T(8,128)}, f32[8,8,128]{2,1,0:T(8,128)S(1)}, u32[]{:S(2)}) copy-start(f32[8,8,128]{2,1,0:T(8,128)S(1)} %get-tuple-element.125) | copy-start | bytes 98308

commit v13 on v12

--- a/solution.py
+++ b/solution.py
@@ -208,7 +208,7 @@
         (owner * gz_count)[:, None] == jnp.arange(devices, dtype=jnp.int32)[None, :]
     ).astype(jnp.float32)
     send = lax.dot_general(to_device, spread, (((0,), (0,)), ((), ())), precision=highest)
-    current = jnp.stack([wave_p, wave_q])
+    current, send = lax.optimization_barrier((jnp.stack([wave_p, wave_q]), send))
     faces = first_round(current, 4)
     send, faces = lax.optimization_barrier((send, faces))
     arrived = lax.all_to_all(send, ("inl", "xl", "gz"), split_axis=0, concat_axis=0, tiled=True)

time: 45 us -> 46.7 us (1.038)
  waiting for transfers between devices: 6.74 us -> 8.35 us
  starting transfers between devices: 25.1 us -> 26.5 us
  other arithmetic: 5.21 us -> 4.4 us
    ppermute x8, waiting for transfers between devices: 0.02 us -> 1.63 us  [shift_pair(): lax.ppermute(lax.dynamic_slice_in_dim(block, jnp.where(even, size - width...]
    all_to_all x1, starting transfers between devices: 5.86 us -> 7.22 us  [local(): lax.all_to_all(send, ('inl', 'xl', 'gz'), split_axis=0, concat_axis=0, ti...]
    another operation x2 -> x1, other arithmetic: 0.82 us -> 0.01 us  [local(): current = jnp.stack([wave_p, wave_q])]
    unnamed x43, local copies, waits for them, and re-layouts: 3.49 us -> 2.97 us
  transfers between devices with their start and end apart: 13 -> 13, of which waited for: 3 -> 4; matrix products, arithmetic and copies ran while one was open for 8% -> 5% of each run, Pallas kernels for 0% -> 0%
where the time goes in v13:
time: 46.7 us; the launch traced here: 46.3 us
  starting transfers between devices  26.5 us (57%)
  waiting for transfers between devices  8.35 us (18%)
  other arithmetic  4.4 us (9%)
  local copies, waits for them, and re-layouts  4.18 us (9%)
  matrix products  1.52 us (3%)
  between operations  1.31 us (3%)
    ppermute x4, starting transfers between devices, shift_pair(): lax.ppermute(lax.dynamic_slice_in_dim(block, jnp.where(even, 0, size - wi...  11.9 us
    ppermute x8, starting transfers between devices, shift_pair(): lax.ppermute(lax.dynamic_slice_in_dim(block, jnp.where(even, size - width...  7.43 us
    all_to_all x1, starting transfers between devices, local(): lax.all_to_all(send, ('inl', 'xl', 'gz'), split_axis=0, concat_axis=0, ti...  7.22 us
    ppermute x4, waiting for transfers between devices, shift_pair(): lax.ppermute(lax.dynamic_slice_in_dim(block, jnp.where(even, 0, size - wi...  6.72 us
    unnamed x43, local copies, waits for them, and re-layouts  2.97 us
    ppermute x8, waiting for transfers between devices, shift_pair(): lax.ppermute(lax.dynamic_slice_in_dim(block, jnp.where(even, size - width...  1.63 us
    sub x2, other arithmetic, advance(): h_two = u_xx + u_yy + u_zz - h_one  1.18 us
  transfers between devices with their start and end apart: 13, of which 4 were waited for; matrix products, arithmetic and copies ran while one was open for 5% of the time, Pallas kernels for 0%

profile of v13, /device:TPU:17, one launch (start us, length us, event | category | flops | bytes accessed | tf_op | source)
XLA Modules:
  0.0 46.3 jit_solution(11579630328043136510)
XLA Ops:
  0.6 0.0 copy-start
  0.7 0.7 %copy-done.19 = s32[256]{0:T(256)S(1)} copy-done((s32[256]{0:T(256)S(1)}, s32[256]{0:T(256)}, u32[]{:S(2)}) %copy-start.19) | copy-done | bytes 1048
  1.4 0.1 select_reduce_fusion
  1.5 0.1 copy-done
  1.6 0.3 convolution_multiply_fusion
  1.9 0.1 copy-start.18
  2.0 0.7 %copy-done.17 = s32[256]{0:T(256)S(1)} copy-done((s32[256]{0:T(256)S(1)}, s32[256]{0:T(256)}, u32[]{:S(2)}) %copy-start.17) | copy-done | bytes 1048
  2.6 0.0 copy-done.18
  2.7 0.2 fusion
  2.9 0.5 %copy-done.3 = f32[8,8,128]{2,1,0:T(8,128)S(1)} copy-done((f32[8,8,128]{2,1,0:T(8,128)S(1)}, f32[8,8,128]{2,1,0:T(8,128)}, u32[]{:S(2)}) %copy-start.3) | copy-done | bytes 32792
  3.4 0.0 copy-done.4
  3.5 0.4 fusion.18
  3.9 1.4 %collective-permute-start.1 = (f32[2,4,8,128]{3,2,1,0:T(8,128)S(1)}, f32[2,4,8,128]{3,2,1,0:T(8,128)S(1)}, u32[]{:S(2)}, u32[]{:S(2)}) collective-permute-start(f32[2,4,8,128]{3,2,1,0:T(8,128)S(1)} %get-tuple-element.121), channel_id=1, source_target_pairs={{0,1},{1,0},{2,3},{3,2},{4,5},{5,4},{6,7},{7,6},{8,9},{9,8},{10,11... | collective-permute-start | bytes 98312 | tf_op jit(solution)/shard_map/ppermute | solution.py:18
  5.3 1.9 %collective-permute-start = (f32[2,4,8,128]{3,2,1,0:T(8,128)S(1)}, f32[2,4,8,128]{3,2,1,0:T(8,128)S(1)}, u32[]{:S(2)}, u32[]{:S(2)}) collective-permute-start(f32[2,4,8,128]{3,2,1,0:T(8,128)S(1)} %get-tuple-element.122), channel_id=1, source_target_pairs={{1,2},{2,1},{5,6},{6,5},{9,10},{10,9},{13,14},{14,13},{17,18},{18,... | collective-permute-start | bytes 98312 | tf_op jit(solution)/shard_map/ppermute | solution.py:26
  7.2 0.1 constant_dynamic-slice_fusion.4
  7.3 1.2 %collective-permute-start.2 = (f32[2,8,8,4]{3,2,1,0:T(8,128)S(1)}, f32[2,8,8,4]{3,2,1,0:T(8,128)S(1)}, u32[]{:S(2)}, u32[]{:S(2)}) collective-permute-start(f32[2,8,8,4]{3,2,1,0:T(8,128)S(1)} %constant_dynamic-slice_fusion.4), channel_id=1, source_target_pairs={{0,4},{4,0},{1,5},{5,1},{2,6},{6,2},{3,7},{7,3},{8,12},{12,8},{9,1... | collective-permute-start | bytes 6152 | tf_op jit(solution)/shard_map/ppermute | solution.py:18
  8.6 0.2 fusion.200
  8.9 1.6 %collective-permute-done.2 = f32[2,8,8,4]{3,2,1,0:T(8,128)S(1)} collective-permute-done((f32[2,8,8,4]{3,2,1,0:T(8,128)S(1)}, f32[2,8,8,4]{3,2,1,0:T(8,128)S(1)}, u32[]{:S(2)}, u32[]{:S(2)}) %collective-permute-start.2) | collective-permute-done | bytes 2080 | tf_op jit(solution)/shard_map/ppermute | solution.py:18
  10.5 0.1 dynamic-slice_maximum_fusion.1
  10.6 0.6 %copy.42 = f32[32,1,192]{2,1,0:T(1,128)} copy(f32[32,1,192]{2,0,1:T(8,128)S(1)} %bitcast.160) | data formatting | bytes 49152 | tf_op jit(solution)/shard_map/all_to_all | solution.py:214
  11.3 7.2 %all-to-all-start = ((f32[32,1,192]{2,1,0:T(1,128)}), f32[32,1,192]{2,1,0:T(1,128)S(1)}, u32[]{:S(2)}, u32[]{:S(2)}) async-start(f32[32,1,192]{2,1,0:T(1,128)} %copy.42), calls=%async_computation | async-start | bytes 65536 | tf_op jit(solution)/shard_map/all_to_all | solution.py:214
  18.5 1.2 %collective-permute-start.3 = (f32[2,8,8,4]{3,2,1,0:T(8,128)S(1)}, f32[2,8,8,4]{3,2,1,0:T(8,128)S(1)}, u32[]{:S(2)}, u32[]{:S(2)}) collective-permute-start(f32[2,8,8,4]{3,2,1,0:T(8,128)S(1)} %dynamic-slice_maximum_fusion.1), channel_id=1, source_target_pairs={{0,4},{4,0},{1,5},{5,1},{2,6},{6,2},{3,7},{7,3},{8,12},{12,8},{9,1... | collective-permute-start | bytes 6152 | tf_op jit(solution)/shard_map/ppermute | solution.py:18
  19.8 0.1 select_maximum_fusion.2
  19.9 0.1 constant_dynamic-slice_fusion.3
  20.0 0.7 %collective-permute-start.4 = (f32[2,16,4,136]{3,2,1,0:T(4,128)S(1)}, f32[2,16,4,136]{3,2,1,0:T(4,128)S(1)}, u32[]{:S(2)}, u32[]{:S(2)}) collective-permute-start(f32[2,16,4,136]{3,2,1,0:T(4,128)S(1)} %get-tuple-element.80), channel_id=1, source_target_pairs={{0,8},{8,0},{16,24},{24,16},{1,9},{9,1},{17,25},{25,17},{2,10},{10... | collective-permute-start | bytes 208904 | tf_op jit(solution)/shard_map/ppermute | solution.py:18
  20.7 3.0 %collective-permute-start.5 = (f32[2,16,4,136]{3,2,1,0:T(4,128)S(1)}, f32[2,16,4,136]{3,2,1,0:T(4,128)S(1)}, u32[]{:S(2)}, u32[]{:S(2)}) collective-permute-start(f32[2,16,4,136]{3,2,1,0:T(4,128)S(1)} %get-tuple-element.81), channel_id=1, source_target_pairs={{8,16},{16,8},{9,17},{17,9},{10,18},{18,10},{11,19},{19,11},{12,20... | collective-permute-start | bytes 208904 | tf_op jit(solution)/shard_map/ppermute | solution.py:26
  23.8 0.1 maximum_maximum_fusion.2
  23.9 0.3 fusion.31
  24.3 0.1 reshape.205
  24.4 0.6 %convolution_bitcast_fusion = f32[16,128]{1,0:T(8,128)S(1)} fusion(s32[32,64]{1,0:T(8,128)S(1)} %add_select_fusion, f32[8,32,64]{2,0,1:T(8,128)S(1)} %fusion.45, f32[2,32,64]{2,0,1:T(2,128)S(1)} %bitcast.159), kind=kOutput, calls=%fused_computation.1 | convolution fusion | flops 50626560 | bytes 98304 | tf_op jit(solution)/shard_map/dot_general | solution.py:227
  25.0 1.9 %collective-permute-done.5 = f32[2,16,4,136]{3,2,1,0:T(4,128)S(1)} collective-permute-done((f32[2,16,4,136]{3,2,1,0:T(4,128)S(1)}, f32[2,16,4,136]{3,2,1,0:T(4,128)S(1)}, u32[]{:S(2)}, u32[]{:S(2)}) %collective-permute-start.5) | collective-permute-done | bytes 69664 | tf_op jit(solution)/shard_map/ppermute | solution.py:26
  27.0 0.2 pad_maximum_fusion
  27.2 0.3 maximum_maximum_fusion
  27.4 0.2 fusion.10
  27.8 0.6 %add_subtract_fusion.1 = (f32[2,8,8,128]{3,2,1,0:T(8,128)S(1)}, f32[2,8,8,128]{3,2,1,0:T(8,128)S(1)}) fusion(f32[2,16,8,128]{3,2,1,0:T(8,128)S(1)} %fusion.31, f32[8,8,128]{2,1,0:T(8,128)S(1)} %get-tuple-element.106, f32[2,16,8,136]{3,2,1,0:T(8,128)S(1)} %fusion.10, f32[8,8,128]{2,1,0:T(8,128)S(1)} %get-tuple-element.107, ...), kind=kLoop, calls=%fused_computation.252 | loop fusion | flops 1392640 | bytes 3538944 | tf_op jit(solution)/shard_map/sub | solution.py:135
  28.4 0.1 copy-done.5
  28.4 0.0 copy-done.6
  28.5 0.0 copy-done.7
  28.5 0.0 copy-done.8
  28.5 0.0 copy-done.9
  28.5 0.0 copy-done.14
  28.5 0.0 copy-done.15
  28.6 0.0 copy-start.1
  28.6 0.1 fusion.48
  28.7 0.3 collective-permute-start.9
  29.0 1.2 %collective-permute-start.7 = (f32[2,4,8,128]{3,2,1,0:T(8,128)S(1)}, f32[2,4,8,128]{3,2,1,0:T(8,128)S(1)}, u32[]{:S(2)}, u32[]{:S(2)}) collective-permute-start(f32[2,4,8,128]{3,2,1,0:T(8,128)S(1)} %get-tuple-element.102), channel_id=1, source_target_pairs={{0,1},{1,0},{2,3},{3,2},{4,5},{5,4},{6,7},{7,6},{8,9},{9,8},{10,11... | collective-permute-start | bytes 98312 | tf_op jit(solution)/shard_map/ppermute | solution.py:18
  30.3 1.9 %collective-permute-start.6 = (f32[2,4,8,128]{3,2,1,0:T(8,128)S(1)}, f32[2,4,8,128]{3,2,1,0:T(8,128)S(1)}, u32[]{:S(2)}, u32[]{:S(2)}) collective-permute-start(f32[2,4,8,128]{3,2,1,0:T(8,128)S(1)} %get-tuple-element.103), channel_id=1, source_target_pairs={{1,2},{2,1},{5,6},{6,5},{9,10},{10,9},{13,14},{14,13},{17,18},{18,... | collective-permute-start | bytes 98312 | tf_op jit(solution)/shard_map/ppermute | solution.py:26
  32.2 2.7 %collective-permute-done.6 = f32[2,4,8,128]{3,2,1,0:T(8,128)S(1)} collective-permute-done((f32[2,4,8,128]{3,2,1,0:T(8,128)S(1)}, f32[2,4,8,128]{3,2,1,0:T(8,128)S(1)}, u32[]{:S(2)}, u32[]{:S(2)}) %collective-permute-start.6) | collective-permute-done | bytes 32800 | tf_op jit(solution)/shard_map/ppermute | solution.py:26
  34.9 0.1 dynamic-slice_maximum_fusion
  35.0 1.2 %collective-permute-start.8 = (f32[2,8,8,4]{3,2,1,0:T(8,128)S(1)}, f32[2,8,8,4]{3,2,1,0:T(8,128)S(1)}, u32[]{:S(2)}, u32[]{:S(2)}) collective-permute-start(f32[2,8,8,4]{3,2,1,0:T(8,128)S(1)} %dynamic-slice_maximum_fusion), channel_id=1, source_target_pairs={{0,4},{4,0},{1,5},{5,1},{2,6},{6,2},{3,7},{7,3},{8,12},{12,8},{9,1... | collective-permute-start | bytes 6152 | tf_op jit(solution)/shard_map/ppermute | solution.py:18
  36.2 0.1 select_maximum_fusion
  36.4 0.1 constant_dynamic-slice_fusion.1
  36.5 0.1 collective-permute-start.10
  36.6 5.0 %collective-permute-start.11 = (f32[2,16,4,136]{3,2,1,0:T(4,128)S(1)}, f32[2,16,4,136]{3,2,1,0:T(4,128)S(1)}, u32[]{:S(2)}, u32[]{:S(2)}) collective-permute-start(f32[2,16,4,136]{3,2,1,0:T(4,128)S(1)} %get-tuple-element.77), channel_id=1, source_target_pairs={{8,16},{16,8},{9,17},{17,9},{10,18},{18,10},{11,19},{19,11},{12,20... | collective-permute-start | bytes 208904 | tf_op jit(solution)/shard_map/ppermute | solution.py:26
  41.7 0.1 maximum_maximum_fusion.4
  41.8 0.3 fusion.24
  42.1 2.1 %collective-permute-done.11 = f32[2,16,4,136]{3,2,1,0:T(4,128)S(1)} collective-permute-done((f32[2,16,4,136]{3,2,1,0:T(4,128)S(1)}, f32[2,16,4,136]{3,2,1,0:T(4,128)S(1)}, u32[]{:S(2)}, u32[]{:S(2)}) %collective-permute-start.11) | collective-permute-done | bytes 69664 | tf_op jit(solution)/shard_map/ppermute | solution.py:26
  44.3 0.2 pad_maximum_fusion.1
  44.4 0.3 maximum_maximum_fusion.1
  44.7 0.2 fusion.3
  44.9 0.6 %add_subtract_fusion = (f32[2,8,8,128]{3,2,1,0:T(8,128)S(1)}, f32[2,8,8,128]{3,2,1,0:T(8,128)S(1)}) fusion(f32[2,16,8,128]{3,2,1,0:T(8,128)S(1)} %fusion.24, f32[8,8,128]{2,1,0:T(8,128)S(1)} %get-tuple-element.106, f32[2,16,8,136]{3,2,1,0:T(8,128)S(1)} %fusion.3, f32[8,8,128]{2,1,0:T(8,128)S(1)} %get-tuple-element.107, ...), kind=kLoop, calls=%fused_computation.251 | loop fusion | flops 1392640 | bytes 3538944 | tf_op jit(solution)/shard_map/sub | solution.py:135
  45.6 0.0 copy-start.10
  45.6 0.6 %copy-done.10 = f32[8,8,128]{2,1,0:T(8,128)} copy-done((f32[8,8,128]{2,1,0:T(8,128)}, f32[8,8,128]{2,1,0:T(8,128)S(1)}, u32[]{:S(2)}) %copy-start.10) | copy-done | bytes 32792
  46.2 0.0 copy-done.11
  (64 shorter events, 0.5 us)
Async XLA Ops:
  0.6 1.0 %copy-start = (f32[256,256]{1,0:T(8,128)S(1)}, f32[256,256]{1,0:T(8,128)}, u32[]{:S(2)}) copy-start(f32[256,256]{1,0:T(8,128)} %param.36) | copy-start | bytes 786436
  0.7 0.7 %copy-start.19 = (s32[256]{0:T(256)S(1)}, s32[256]{0:T(256)}, u32[]{:S(2)}) copy-start(s32[256]{0:T(256)} %param.41) | copy-start | bytes 3076
  0.7 0.7 %copy-start.20 = (f32[64]{0:T(128)S(1)}, f32[64]{0:T(128)}, u32[]{:S(2)}) copy-start(f32[64]{0:T(128)} %param.38) | copy-start | bytes 772
  0.7 0.9 %copy-start.16 = (f32[2,256]{1,0:T(2,128)S(1)}, f32[2,256]{1,0:T(2,128)}, u32[]{:S(2)}) copy-start(f32[2,256]{1,0:T(2,128)} %param.37) | copy-start | bytes 6148
  1.9 0.7 %copy-start.17 = (s32[256]{0:T(256)S(1)}, s32[256]{0:T(256)}, u32[]{:S(2)}) copy-start(s32[256]{0:T(256)} %param.40) | copy-start | bytes 3076
  1.9 0.8 %copy-start.18 = (s32[256]{0:T(256)S(1)}, s32[256]{0:T(256)}, u32[]{:S(2)}) copy-start(s32[256]{0:T(256)} %param.39) | copy-start | bytes 3076
  2.7 0.8 %copy-start.3 = (f32[8,8,128]{2,1,0:T(8,128)S(1)}, f32[8,8,128]{2,1,0:T(8,128)}, u32[]{:S(2)}) copy-start(f32[8,8,128]{2,1,0:T(8,128)} %param.27) | copy-start | bytes 98308
  2.7 0.8 %copy-start.4 = (f32[8,8,128]{2,1,0:T(8,128)S(1)}, f32[8,8,128]{2,1,0:T(8,128)}, u32[]{:S(2)}) copy-start(f32[8,8,128]{2,1,0:T(8,128)} %param.25) | copy-start | bytes 98308
  3.9 6.6 %collective-permute-start.1 = (f32[2,4,8,128]{3,2,1,0:T(8,128)S(1)}, f32[2,4,8,128]{3,2,1,0:T(8,128)S(1)}, u32[]{:S(2)}, u32[]{:S(2)}) collective-permute-start(f32[2,4,8,128]{3,2,1,0:T(8,128)S(1)} %get-tuple-element.121), channel_id=1, source_target_pairs={{0,1},{1,0},{2,3},{3,2},{4,5},{5,4},{6,7},{7,6},{8,9},{9,8},{10,11... | collective-permute-start | bytes 98312 | tf_op jit(solution)/shard_map/ppermute | solution.py:18
  5.3 5.2 %collective-permute-start = (f32[2,4,8,128]{3,2,1,0:T(8,128)S(1)}, f32[2,4,8,128]{3,2,1,0:T(8,128)S(1)}, u32[]{:S(2)}, u32[]{:S(2)}) collective-permute-start(f32[2,4,8,128]{3,2,1,0:T(8,128)S(1)} %get-tuple-element.122), channel_id=1, source_target_pairs={{1,2},{2,1},{5,6},{6,5},{9,10},{10,9},{13,14},{14,13},{17,18},{18,... | collective-permute-start | bytes 98312 | tf_op jit(solution)/shard_map/ppermute | solution.py:26
  7.2 1.4 %copy-start.12 = (f32[8,8,128]{2,1,0:T(8,128)S(1)}, f32[8,8,128]{2,1,0:T(8,128)}, u32[]{:S(2)}) copy-start(f32[8,8,128]{2,1,0:T(8,128)} %param.33) | copy-start | bytes 98308
  7.2 1.3 %copy-start.13 = (f32[8,8,128]{2,1,0:T(8,128)S(1)}, f32[8,8,128]{2,1,0:T(8,128)}, u32[]{:S(2)}) copy-start(f32[8,8,128]{2,1,0:T(8,128)} %param.32) | copy-start | bytes 98308
  7.3 3.2 %collective-permute-start.2 = (f32[2,8,8,4]{3,2,1,0:T(8,128)S(1)}, f32[2,8,8,4]{3,2,1,0:T(8,128)S(1)}, u32[]{:S(2)}, u32[]{:S(2)}) collective-permute-start(f32[2,8,8,4]{3,2,1,0:T(8,128)S(1)} %constant_dynamic-slice_fusion.4), channel_id=1, source_target_pairs={{0,4},{4,0},{1,5},{5,1},{2,6},{6,2},{3,7},{7,3},{8,12},{12,8},{9,1... | collective-permute-start | bytes 6152 | tf_op jit(solution)/shard_map/ppermute | solution.py:18
  11.3 12.9 %all-to-all-start = ((f32[32,1,192]{2,1,0:T(1,128)}), f32[32,1,192]{2,1,0:T(1,128)S(1)}, u32[]{:S(2)}, u32[]{:S(2)}) async-start(f32[32,1,192]{2,1,0:T(1,128)} %copy.42), calls=%async_computation | async-start | bytes 65536 | tf_op jit(solution)/shard_map/all_to_all | solution.py:214
  18.5 5.2 %collective-permute-start.3 = (f32[2,8,8,4]{3,2,1,0:T(8,128)S(1)}, f32[2,8,8,4]{3,2,1,0:T(8,128)S(1)}, u32[]{:S(2)}, u32[]{:S(2)}) collective-permute-start(f32[2,8,8,4]{3,2,1,0:T(8,128)S(1)} %dynamic-slice_maximum_fusion.1), channel_id=1, source_target_pairs={{0,4},{4,0},{1,5},{5,1},{2,6},{6,2},{3,7},{7,3},{8,12},{12,8},{9,1... | collective-permute-start | bytes 6152 | tf_op jit(solution)/shard_map/ppermute | solution.py:18
  20.0 5.1 %collective-permute-start.4 = (f32[2,16,4,136]{3,2,1,0:T(4,128)S(1)}, f32[2,16,4,136]{3,2,1,0:T(4,128)S(1)}, u32[]{:S(2)}, u32[]{:S(2)}) collective-permute-start(f32[2,16,4,136]{3,2,1,0:T(4,128)S(1)} %get-tuple-element.80), channel_id=1, source_target_pairs={{0,8},{8,0},{16,24},{24,16},{1,9},{9,1},{17,25},{25,17},{2,10},{10... | collective-permute-start | bytes 208904 | tf_op jit(solution)/shard_map/ppermute | solution.py:18
  20.7 6.3 %collective-permute-start.5 = (f32[2,16,4,136]{3,2,1,0:T(4,128)S(1)}, f32[2,16,4,136]{3,2,1,0:T(4,128)S(1)}, u32[]{:S(2)}, u32[]{:S(2)}) collective-permute-start(f32[2,16,4,136]{3,2,1,0:T(4,128)S(1)} %get-tuple-element.81), channel_id=1, source_target_pairs={{8,16},{16,8},{9,17},{17,9},{10,18},{18,10},{11,19},{19,11},{12,20... | collective-permute-start | bytes 208904 | tf_op jit(solution)/shard_map/ppermute | solution.py:26
  27.7 0.8 %copy-start.5 = (f32[8,8,128]{2,1,0:T(8,128)S(1)}, f32[8,8,128]{2,1,0:T(8,128)}, u32[]{:S(2)}) copy-start(f32[8,8,128]{2,1,0:T(8,128)} %param.29) | copy-start | bytes 98308
  27.7 0.8 %copy-start.6 = (f32[8,8,128]{2,1,0:T(8,128)S(1)}, f32[8,8,128]{2,1,0:T(8,128)}, u32[]{:S(2)}) copy-start(f32[8,8,128]{2,1,0:T(8,128)} %param.34) | copy-start | bytes 98308
  27.7 0.8 %copy-start.7 = (f32[8,8,128]{2,1,0:T(8,128)S(1)}, f32[8,8,128]{2,1,0:T(8,128)}, u32[]{:S(2)}) copy-start(f32[8,8,128]{2,1,0:T(8,128)} %param.35) | copy-start | bytes 98308
  27.7 0.8 %copy-start.8 = (f32[8,8,128]{2,1,0:T(8,128)S(1)}, f32[8,8,128]{2,1,0:T(8,128)}, u32[]{:S(2)}) copy-start(f32[8,8,128]{2,1,0:T(8,128)} %param.30) | copy-start | bytes 98308
  27.7 0.8 %copy-start.9 = (f32[8,8,128]{2,1,0:T(8,128)S(1)}, f32[8,8,128]{2,1,0:T(8,128)}, u32[]{:S(2)}) copy-start(f32[8,8,128]{2,1,0:T(8,128)} %param.31) | copy-start | bytes 98308
  27.7 0.8 %copy-start.14 = (f32[8,8,128]{2,1,0:T(8,128)S(1)}, f32[8,8,128]{2,1,0:T(8,128)}, u32[]{:S(2)}) copy-start(f32[8,8,128]{2,1,0:T(8,128)} %param.26) | copy-start | bytes 98308
  27.7 0.8 %copy-start.15 = (f32[8,8,128]{2,1,0:T(8,128)S(1)}, f32[8,8,128]{2,1,0:T(8,128)}, u32[]{:S(2)}) copy-start(f32[8,8,128]{2,1,0:T(8,128)} %param.28) | copy-start | bytes 98308
  28.6 16.9 %copy-start.1 = (f32[8,8,128]{2,1,0:T(8,128)}, f32[8,8,128]{2,1,0:T(8,128)S(1)}, u32[]{:S(2)}) copy-start(f32[8,8,128]{2,1,0:T(8,128)S(1)} %get-tuple-element.130) | copy-start | bytes 98308
  28.6 16.9 %copy-start.2 = (f32[8,8,128]{2,1,0:T(8,128)}, f32[8,8,128]{2,1,0:T(8,128)S(1)}, u32[]{:S(2)}) copy-start(f32[8,8,128]{2,1,0:T(8,128)S(1)} %get-tuple-element.131) | copy-start | bytes 98308
  28.7 3.5 %collective-permute-start.9 = (f32[2,8,8,4]{3,2,1,0:T(8,128)S(1)}, f32[2,8,8,4]{3,2,1,0:T(8,128)S(1)}, u32[]{:S(2)}, u32[]{:S(2)}) collective-permute-start(f32[2,8,8,4]{3,2,1,0:T(8,128)S(1)} %fusion.48), channel_id=1, source_target_pairs={{0,4},{4,0},{1,5},{5,1},{2,6},{6,2},{3,7},{7,3},{8,12},{12,8},{9,1... | collective-permute-start | bytes 6152 | tf_op jit(solution)/shard_map/ppermute | solution.py:18
  29.0 3.2 %collective-permute-start.7 = (f32[2,4,8,128]{3,2,1,0:T(8,128)S(1)}, f32[2,4,8,128]{3,2,1,0:T(8,128)S(1)}, u32[]{:S(2)}, u32[]{:S(2)}) collective-permute-start(f32[2,4,8,128]{3,2,1,0:T(8,128)S(1)} %get-tuple-element.102), channel_id=1, source_target_pairs={{0,1},{1,0},{2,3},{3,2},{4,5},{5,4},{6,7},{7,6},{8,9},{9,8},{10,11... | collective-permute-start | bytes 98312 | tf_op jit(solution)/shard_map/ppermute | solution.py:18
  30.3 4.6 %collective-permute-start.6 = (f32[2,4,8,128]{3,2,1,0:T(8,128)S(1)}, f32[2,4,8,128]{3,2,1,0:T(8,128)S(1)}, u32[]{:S(2)}, u32[]{:S(2)}) collective-permute-start(f32[2,4,8,128]{3,2,1,0:T(8,128)S(1)} %get-tuple-element.103), channel_id=1, source_target_pairs={{1,2},{2,1},{5,6},{6,5},{9,10},{10,9},{13,14},{14,13},{17,18},{18,... | collective-permute-start | bytes 98312 | tf_op jit(solution)/shard_map/ppermute | solution.py:26
  35.0 6.6 %collective-permute-start.8 = (f32[2,8,8,4]{3,2,1,0:T(8,128)S(1)}, f32[2,8,8,4]{3,2,1,0:T(8,128)S(1)}, u32[]{:S(2)}, u32[]{:S(2)}) collective-permute-start(f32[2,8,8,4]{3,2,1,0:T(8,128)S(1)} %dynamic-slice_maximum_fusion), channel_id=1, source_target_pairs={{0,4},{4,0},{1,5},{5,1},{2,6},{6,2},{3,7},{7,3},{8,12},{12,8},{9,1... | collective-permute-start | bytes 6152 | tf_op jit(solution)/shard_map/ppermute | solution.py:18
  36.5 5.6 %collective-permute-start.10 = (f32[2,16,4,136]{3,2,1,0:T(4,128)S(1)}, f32[2,16,4,136]{3,2,1,0:T(4,128)S(1)}, u32[]{:S(2)}, u32[]{:S(2)}) collective-permute-start(f32[2,16,4,136]{3,2,1,0:T(4,128)S(1)} %get-tuple-element.76), channel_id=1, source_target_pairs={{0,8},{8,0},{16,24},{24,16},{1,9},{9,1},{17,25},{25,17},{2,10},{10... | collective-permute-start | bytes 208904 | tf_op jit(solution)/shard_map/ppermute | solution.py:18
  36.6 7.7 %collective-permute-start.11 = (f32[2,16,4,136]{3,2,1,0:T(4,128)S(1)}, f32[2,16,4,136]{3,2,1,0:T(4,128)S(1)}, u32[]{:S(2)}, u32[]{:S(2)}) collective-permute-start(f32[2,16,4,136]{3,2,1,0:T(4,128)S(1)} %get-tuple-element.77), channel_id=1, source_target_pairs={{8,16},{16,8},{9,17},{17,9},{10,18},{18,10},{11,19},{19,11},{12,20... | collective-permute-start | bytes 208904 | tf_op jit(solution)/shard_map/ppermute | solution.py:26
  45.6 0.6 %copy-start.10 = (f32[8,8,128]{2,1,0:T(8,128)}, f32[8,8,128]{2,1,0:T(8,128)S(1)}, u32[]{:S(2)}) copy-start(f32[8,8,128]{2,1,0:T(8,128)S(1)} %get-tuple-element.128) | copy-start | bytes 98308
  45.6 0.6 %copy-start.11 = (f32[8,8,128]{2,1,0:T(8,128)}, f32[8,8,128]{2,1,0:T(8,128)S(1)}, u32[]{:S(2)}) copy-start(f32[8,8,128]{2,1,0:T(8,128)S(1)} %get-tuple-element.129) | copy-start | bytes 98308

commit v14 on v12

--- a/solution.py
+++ b/solution.py
@@ -212,21 +212,30 @@
     faces = first_round(current, 4)
     send, faces = lax.optimization_barrier((send, faces))
     arrived = lax.all_to_all(send, ("inl", "xl", "gz"), split_axis=0, concat_axis=0, tiled=True)
-    amp = arrived[:, : steps * capacity].reshape(devices, steps, capacity)
-    cell = (arrived[:, steps * capacity :] + 0.5).astype(jnp.int32)
-    row_hit = (
-        cell[None, :, :] // cross_cells
-        == jnp.arange(inline_cells, dtype=jnp.int32)[:, None, None]
-    ).astype(jnp.float32)
-    col_hit = (
-        cell[None, :, :] % cross_cells == jnp.arange(cross_cells, dtype=jnp.int32)[:, None, None]
-    ).astype(jnp.float32)
-    weighted = (jnp.transpose(amp, (1, 0, 2))[:, None] * row_hit[None]).reshape(
-        steps * inline_cells, devices, capacity
-    )
-    planes = lax.dot_general(
-        weighted, col_hit, (((1, 2), (1, 2)), ((), ())), precision=highest
-    ).reshape(steps, inline_cells, cross_cells)
+    def surface_planes(arrived):
+        amp = arrived[:, : steps * capacity].reshape(devices, steps, capacity)
+        cell = (arrived[:, steps * capacity :] + 0.5).astype(jnp.int32)
+        row_hit = (
+            cell[None, :, :] // cross_cells
+            == jnp.arange(inline_cells, dtype=jnp.int32)[:, None, None]
+        ).astype(jnp.float32)
+        col_hit = (
+            cell[None, :, :] % cross_cells == jnp.arange(cross_cells, dtype=jnp.int32)[:, None, None]
+        ).astype(jnp.float32)
+        weighted = (jnp.transpose(amp, (1, 0, 2))[:, None] * row_hit[None]).reshape(
+            steps * inline_cells, devices, capacity
+        )
+        planes = lax.dot_general(
+            weighted, col_hit, (((1, 2), (1, 2)), ((), ())), precision=highest
+        ).reshape(steps, inline_cells, cross_cells)
+        return planes
+
+    planes = lax.cond(
+        lax.axis_index("gz") == 0,
+        surface_planes,
+        lambda arrived: jnp.zeros((steps, inline_cells, cross_cells), jnp.float32),
+        arrived,
+    )
     fields = (courant_square, thomsen_epsilon, thomsen_delta, shear_ratio, damping)
     current = jnp.stack([wave_p, wave_q])
     previous = jnp.stack([wave_p_old, wave_q_old])

time: 45 us -> 45.4 us (level)
  matrix products: 1.52 us -> 0.91 us
  waiting for transfers between devices: 6.74 us -> 7.28 us
    ppermute x4, starting transfers between devices: 11.9 us -> 12.6 us  [shift_pair(): lax.ppermute(lax.dynamic_slice_in_dim(block, jnp.where(even, 0, size - wi...]
    ppermute x8, starting transfers between devices: 7.42 us -> 6.79 us  [shift_pair(): lax.ppermute(lax.dynamic_slice_in_dim(block, jnp.where(even, size - width...]
    dot_general x1 -> x0, matrix products: 0.62 us -> none  [local(): lax.dot_general(weighted, col_hit, (((1, 2), (1, 2)), ((), ())), precisio...]
    ppermute x4, waiting for transfers between devices: 6.72 us -> 7.26 us  [shift_pair(): lax.ppermute(lax.dynamic_slice_in_dim(block, jnp.where(even, 0, size - wi...]
    unnamed x43 -> x46, local copies, waits for them, and re-layouts: 3.49 us -> 3.6 us
  transfers between devices with their start and end apart: 13 -> 13, of which waited for: 3 -> 3; matrix products, arithmetic and copies ran while one was open for 8% -> 6% of each run, Pallas kernels for 0% -> 0%
where the time goes in v14:
time: 45.4 us; the launch traced here: 44.9 us
  starting transfers between devices  25.2 us (56%)
  waiting for transfers between devices  7.28 us (16%)
  other arithmetic  5.17 us (11%)
  local copies, waits for them, and re-layouts  4.98 us (11%)
  between operations  1.32 us (3%)
  matrix products  0.91 us (2%)
    ppermute x4, starting transfers between devices, shift_pair(): lax.ppermute(lax.dynamic_slice_in_dim(block, jnp.where(even, 0, size - wi...  12.6 us
    ppermute x4, waiting for transfers between devices, shift_pair(): lax.ppermute(lax.dynamic_slice_in_dim(block, jnp.where(even, 0, size - wi...  7.26 us
    ppermute x8, starting transfers between devices, shift_pair(): lax.ppermute(lax.dynamic_slice_in_dim(block, jnp.where(even, size - width...  6.79 us
    all_to_all x1, starting transfers between devices, local(): lax.all_to_all(send, ('inl', 'xl', 'gz'), split_axis=0, concat_axis=0, ti...  5.86 us
    unnamed x46, local copies, waits for them, and re-layouts  3.6 us
    sub x2, other arithmetic, advance(): h_two = u_xx + u_yy + u_zz - h_one  1.18 us
    concatenate x4, other arithmetic, second_round(): return jnp.concatenate([low_x, full, high_x], axis=2)  0.91 us
  transfers between devices with their start and end apart: 13, of which 3 were waited for; matrix products, arithmetic and copies ran while one was open for 6% of the time, Pallas kernels for 0%

profile of v14, /device:TPU:17, one launch (start us, length us, event | category | flops | bytes accessed | tf_op | source)
XLA Modules:
  0.0 44.9 jit_solution(4347991224572017858)
XLA Ops:
  0.6 0.0 copy-start
  0.7 0.8 %copy-done.3 = f32[8,8,128]{2,1,0:T(8,128)S(1)} copy-done((f32[8,8,128]{2,1,0:T(8,128)S(1)}, f32[8,8,128]{2,1,0:T(8,128)}, u32[]{:S(2)}) %copy-start.3) | copy-done | bytes 32792
  1.4 0.7 %fusion.164 = (f32[2,4,8,128]{3,2,1,0:T(8,128)S(1)}, f32[2,4,8,128]{3,2,1,0:T(8,128)S(1)}) fusion(s32[]{:T(128)S(6)} %select_n.210, f32[1,8,8,128]{3,2,1,0:T(8,128)S(1)} %bitcast.115, f32[1,8,8,128]{3,2,1,0:T(8,128)} %bitcast.123, s32[]{:T(128)S(6)} %select_n.209), kind=kLoop, calls=%fused_computation.289 | loop fusion | flops 16384 | bytes 131080 | tf_op jit(solution)/shard_map/stack | solution.py:240
  2.2 1.4 %collective-permute-start.1 = (f32[2,4,8,128]{3,2,1,0:T(8,128)S(1)}, f32[2,4,8,128]{3,2,1,0:T(8,128)S(1)}, u32[]{:S(2)}, u32[]{:S(2)}) collective-permute-start(f32[2,4,8,128]{3,2,1,0:T(8,128)S(1)} %get-tuple-element.137), channel_id=1, source_target_pairs={{0,1},{1,0},{2,3},{3,2},{4,5},{5,4},{6,7},{7,6},{8,9},{9,8},{10,11... | collective-permute-start | bytes 98312 | tf_op jit(solution)/shard_map/ppermute | solution.py:18
  3.5 1.9 %collective-permute-start = (f32[2,4,8,128]{3,2,1,0:T(8,128)S(1)}, f32[2,4,8,128]{3,2,1,0:T(8,128)S(1)}, u32[]{:S(2)}, u32[]{:S(2)}) collective-permute-start(f32[2,4,8,128]{3,2,1,0:T(8,128)S(1)} %get-tuple-element.138), channel_id=1, source_target_pairs={{1,2},{2,1},{5,6},{6,5},{9,10},{10,9},{13,14},{14,13},{17,18},{18,... | collective-permute-start | bytes 98312 | tf_op jit(solution)/shard_map/ppermute | solution.py:26
  5.5 0.1 fusion.54
  5.6 1.2 %collective-permute-start.2 = (f32[2,8,8,4]{3,2,1,0:T(8,128)S(1)}, f32[2,8,8,4]{3,2,1,0:T(8,128)S(1)}, u32[]{:S(2)}, u32[]{:S(2)}) collective-permute-start(f32[2,8,8,4]{3,2,1,0:T(8,128)S(1)} %fusion.54), channel_id=1, source_target_pairs={{0,4},{4,0},{1,5},{5,1},{2,6},{6,2},{3,7},{7,3},{8,12},{12,8},{9,1... | collective-permute-start | bytes 6152 | tf_op jit(solution)/shard_map/ppermute | solution.py:18
  6.9 0.1 select_reduce_fusion
  7.0 0.6 %copy-done.16 = f32[2,256]{1,0:T(2,128)S(1)} copy-done((f32[2,256]{1,0:T(2,128)S(1)}, f32[2,256]{1,0:T(2,128)}, u32[]{:S(2)}) %copy-start.16) | copy-done | bytes 2072
  7.5 0.3 convolution_multiply_fusion
  7.8 0.1 copy-start.18
  7.9 0.7 %copy-done.17 = s32[256]{0:T(256)S(1)} copy-done((s32[256]{0:T(256)S(1)}, s32[256]{0:T(256)}, u32[]{:S(2)}) %copy-start.17) | copy-done | bytes 1048
  8.5 0.0 copy-done.18
  8.6 0.2 fusion.10
  8.8 0.5 %copy-done.12 = f32[8,8,128]{2,1,0:T(8,128)S(1)} copy-done((f32[8,8,128]{2,1,0:T(8,128)S(1)}, f32[8,8,128]{2,1,0:T(8,128)}, u32[]{:S(2)}) %copy-start.12) | copy-done | bytes 32792
  9.3 0.0 copy-done.13
  9.3 0.2 fusion.206
  9.6 0.4 fusion.25
  10.2 0.1 dynamic-slice_maximum_fusion.1
  10.3 0.6 %copy.147 = f32[32,1,192]{2,1,0:T(1,128)} copy(f32[32,1,192]{2,0,1:T(8,128)S(1)} %bitcast.135) | data formatting | bytes 49152 | tf_op jit(solution)/shard_map/all_to_all | solution.py:214
  10.9 5.9 %all-to-all-start = ((f32[32,1,192]{2,1,0:T(1,128)}), f32[32,1,192]{2,1,0:T(1,128)S(1)}, u32[]{:S(2)}, u32[]{:S(2)}) async-start(f32[32,1,192]{2,1,0:T(1,128)} %copy.147), calls=%async_computation | async-start | bytes 65536 | tf_op jit(solution)/shard_map/all_to_all | solution.py:214
  16.8 1.2 %collective-permute-start.3 = (f32[2,8,8,4]{3,2,1,0:T(8,128)S(1)}, f32[2,8,8,4]{3,2,1,0:T(8,128)S(1)}, u32[]{:S(2)}, u32[]{:S(2)}) collective-permute-start(f32[2,8,8,4]{3,2,1,0:T(8,128)S(1)} %dynamic-slice_maximum_fusion.1), channel_id=1, source_target_pairs={{0,4},{4,0},{1,5},{5,1},{2,6},{6,2},{3,7},{7,3},{8,12},{12,8},{9,1... | collective-permute-start | bytes 6152 | tf_op jit(solution)/shard_map/ppermute | solution.py:18
  18.0 0.1 select_maximum_fusion.2
  18.2 0.1 constant_dynamic-slice_fusion.3
  18.3 3.6 %collective-permute-start.5 = (f32[2,16,4,136]{3,1,2,0:T(8,128)S(1)}, f32[2,16,4,136]{3,1,2,0:T(8,128)S(1)}, u32[]{:S(2)}, u32[]{:S(2)}) collective-permute-start(f32[2,16,4,136]{3,1,2,0:T(8,128)S(1)} %copy.155), channel_id=1, source_target_pairs={{8,16},{16,8},{9,17},{17,9},{10,18},{18,10},{11,19},{19,11},{12,20... | collective-permute-start | bytes 208904 | tf_op jit(solution)/shard_map/ppermute | solution.py:26
  22.0 0.1 collective-permute-start.4
  22.1 0.1 maximum_maximum_fusion.2
  22.2 0.3 fusion.38
  22.6 2.0 %collective-permute-done.5 = f32[2,16,4,136]{3,1,2,0:T(8,128)S(1)} collective-permute-done((f32[2,16,4,136]{3,1,2,0:T(8,128)S(1)}, f32[2,16,4,136]{3,1,2,0:T(8,128)S(1)}, u32[]{:S(2)}, u32[]{:S(2)}) %collective-permute-start.5) | collective-permute-done | bytes 69664 | tf_op jit(solution)/shard_map/ppermute | solution.py:26
  24.6 0.1 copy.145
  24.7 0.1 copy.146
  24.8 0.3 maximum_maximum_fusion
  25.1 0.2 pad_maximum_fusion
  25.3 0.2 fusion.19
  25.6 0.6 %add_subtract_fusion.1 = (f32[2,8,8,128]{3,2,1,0:T(8,128)S(1)}, f32[2,8,8,128]{3,2,1,0:T(8,128)S(1)}) fusion(f32[2,16,8,128]{3,2,1,0:T(8,128)S(1)} %fusion.38, f32[8,8,128]{2,1,0:T(8,128)S(1)} %get-tuple-element.122, f32[2,16,8,136]{3,2,1,0:T(8,128)S(1)} %fusion.19, f32[8,8,128]{2,1,0:T(8,128)S(1)} %get-tuple-element.123, ...), kind=kLoop, calls=%fused_computation.272 | loop fusion | flops 1392640 | bytes 3538944 | tf_op jit(solution)/shard_map/sub | solution.py:135
  26.2 0.1 copy-done.5
  26.3 0.0 copy-done.6
  26.3 0.0 copy-done.7
  26.3 0.0 copy-done.8
  26.3 0.0 copy-done.9
  26.4 0.0 copy-done.14
  26.4 0.0 copy-done.15
  26.5 0.1 fusion.52
  26.6 0.3 collective-permute-start.9
  26.9 1.2 %collective-permute-start.7 = (f32[2,4,8,128]{3,2,1,0:T(8,128)S(1)}, f32[2,4,8,128]{3,2,1,0:T(8,128)S(1)}, u32[]{:S(2)}, u32[]{:S(2)}) collective-permute-start(f32[2,4,8,128]{3,2,1,0:T(8,128)S(1)} %get-tuple-element.118), channel_id=1, source_target_pairs={{0,1},{1,0},{2,3},{3,2},{4,5},{5,4},{6,7},{7,6},{8,9},{9,8},{10,11... | collective-permute-start | bytes 98312 | tf_op jit(solution)/shard_map/ppermute | solution.py:18
  28.1 1.9 %collective-permute-start.6 = (f32[2,4,8,128]{3,2,1,0:T(8,128)S(1)}, f32[2,4,8,128]{3,2,1,0:T(8,128)S(1)}, u32[]{:S(2)}, u32[]{:S(2)}) collective-permute-start(f32[2,4,8,128]{3,2,1,0:T(8,128)S(1)} %get-tuple-element.119), channel_id=1, source_target_pairs={{1,2},{2,1},{5,6},{6,5},{9,10},{10,9},{13,14},{14,13},{17,18},{18,... | collective-permute-start | bytes 98312 | tf_op jit(solution)/shard_map/ppermute | solution.py:26
  30.1 3.2 %collective-permute-done.6 = f32[2,4,8,128]{3,2,1,0:T(8,128)S(1)} collective-permute-done((f32[2,4,8,128]{3,2,1,0:T(8,128)S(1)}, f32[2,4,8,128]{3,2,1,0:T(8,128)S(1)}, u32[]{:S(2)}, u32[]{:S(2)}) %collective-permute-start.6) | collective-permute-done | bytes 32800 | tf_op jit(solution)/shard_map/ppermute | solution.py:26
  33.3 0.1 dynamic-slice_maximum_fusion
  33.4 1.2 %collective-permute-start.8 = (f32[2,8,8,4]{3,2,1,0:T(8,128)S(1)}, f32[2,8,8,4]{3,2,1,0:T(8,128)S(1)}, u32[]{:S(2)}, u32[]{:S(2)}) collective-permute-start(f32[2,8,8,4]{3,2,1,0:T(8,128)S(1)} %dynamic-slice_maximum_fusion), channel_id=1, source_target_pairs={{0,4},{4,0},{1,5},{5,1},{2,6},{6,2},{3,7},{7,3},{8,12},{12,8},{9,1... | collective-permute-start | bytes 6152 | tf_op jit(solution)/shard_map/ppermute | solution.py:18
  34.6 0.1 select_maximum_fusion
  34.8 0.1 constant_dynamic-slice_fusion.1
  34.9 5.1 %collective-permute-start.11 = (f32[2,16,4,136]{3,1,2,0:T(8,128)S(1)}, f32[2,16,4,136]{3,1,2,0:T(8,128)S(1)}, u32[]{:S(2)}, u32[]{:S(2)}) collective-permute-start(f32[2,16,4,136]{3,1,2,0:T(8,128)S(1)} %copy.157), channel_id=1, source_target_pairs={{8,16},{16,8},{9,17},{17,9},{10,18},{18,10},{11,19},{19,11},{12,20... | collective-permute-start | bytes 208904 | tf_op jit(solution)/shard_map/ppermute | solution.py:26
  40.0 0.1 collective-permute-start.10
  40.2 0.1 maximum_maximum_fusion.4
  40.3 0.3 fusion.31
  40.6 2.0 %collective-permute-done.11 = f32[2,16,4,136]{3,1,2,0:T(8,128)S(1)} collective-permute-done((f32[2,16,4,136]{3,1,2,0:T(8,128)S(1)}, f32[2,16,4,136]{3,1,2,0:T(8,128)S(1)}, u32[]{:S(2)}, u32[]{:S(2)}) %collective-permute-start.11) | collective-permute-done | bytes 69664 | tf_op jit(solution)/shard_map/ppermute | solution.py:26
  42.7 0.1 copy.151
  42.8 0.1 copy.152
  42.9 0.3 maximum_maximum_fusion.1
  43.2 0.2 pad_maximum_fusion.1
  43.4 0.2 fusion.12
  43.6 0.6 %add_subtract_fusion = (f32[2,8,8,128]{3,2,1,0:T(8,128)S(1)}, f32[2,8,8,128]{3,2,1,0:T(8,128)S(1)}) fusion(f32[2,16,8,128]{3,2,1,0:T(8,128)S(1)} %fusion.31, f32[8,8,128]{2,1,0:T(8,128)S(1)} %get-tuple-element.122, f32[2,16,8,136]{3,2,1,0:T(8,128)S(1)} %fusion.12, f32[8,8,128]{2,1,0:T(8,128)S(1)} %get-tuple-element.123, ...), kind=kLoop, calls=%fused_computation.271 | loop fusion | flops 1392640 | bytes 3538944 | tf_op jit(solution)/shard_map/sub | solution.py:135
  44.3 0.6 %copy-done.10 = f32[8,8,128]{2,1,0:T(8,128)} copy-done((f32[8,8,128]{2,1,0:T(8,128)}, f32[8,8,128]{2,1,0:T(8,128)S(1)}, u32[]{:S(2)}) %copy-start.10) | copy-done | bytes 32792
  44.9 0.0 copy-done.11
  (67 shorter events, 0.6 us)
Async XLA Ops:
  0.6 6.3 %copy-start = (f32[256,256]{1,0:T(8,128)S(1)}, f32[256,256]{1,0:T(8,128)}, u32[]{:S(2)}) copy-start(f32[256,256]{1,0:T(8,128)} %param.38) | copy-start | bytes 786436
  0.6 0.8 %copy-start.3 = (f32[8,8,128]{2,1,0:T(8,128)S(1)}, f32[8,8,128]{2,1,0:T(8,128)}, u32[]{:S(2)}) copy-start(f32[8,8,128]{2,1,0:T(8,128)} %param.27) | copy-start | bytes 98308
  2.2 3.3 %copy-start.4 = (f32[8,8,128]{2,1,0:T(8,128)S(1)}, f32[8,8,128]{2,1,0:T(8,128)}, u32[]{:S(2)}) copy-start(f32[8,8,128]{2,1,0:T(8,128)} %param.29) | copy-start | bytes 98308
  2.2 7.9 %collective-permute-start.1 = (f32[2,4,8,128]{3,2,1,0:T(8,128)S(1)}, f32[2,4,8,128]{3,2,1,0:T(8,128)S(1)}, u32[]{:S(2)}, u32[]{:S(2)}) collective-permute-start(f32[2,4,8,128]{3,2,1,0:T(8,128)S(1)} %get-tuple-element.137), channel_id=1, source_target_pairs={{0,1},{1,0},{2,3},{3,2},{4,5},{5,4},{6,7},{7,6},{8,9},{9,8},{10,11... | collective-permute-start | bytes 98312 | tf_op jit(solution)/shard_map/ppermute | solution.py:18
  3.5 6.6 %collective-permute-start = (f32[2,4,8,128]{3,2,1,0:T(8,128)S(1)}, f32[2,4,8,128]{3,2,1,0:T(8,128)S(1)}, u32[]{:S(2)}, u32[]{:S(2)}) collective-permute-start(f32[2,4,8,128]{3,2,1,0:T(8,128)S(1)} %get-tuple-element.138), channel_id=1, source_target_pairs={{1,2},{2,1},{5,6},{6,5},{9,10},{10,9},{13,14},{14,13},{17,18},{18,... | collective-permute-start | bytes 98312 | tf_op jit(solution)/shard_map/ppermute | solution.py:26
  5.5 1.4 %copy-start.19 = (s32[256]{0:T(256)S(1)}, s32[256]{0:T(256)}, u32[]{:S(2)}) copy-start(s32[256]{0:T(256)} %param.43) | copy-start | bytes 3076
  5.5 1.4 %copy-start.20 = (f32[64]{0:T(128)S(1)}, f32[64]{0:T(128)}, u32[]{:S(2)}) copy-start(f32[64]{0:T(128)} %param.40) | copy-start | bytes 772
  5.6 4.5 %collective-permute-start.2 = (f32[2,8,8,4]{3,2,1,0:T(8,128)S(1)}, f32[2,8,8,4]{3,2,1,0:T(8,128)S(1)}, u32[]{:S(2)}, u32[]{:S(2)}) collective-permute-start(f32[2,8,8,4]{3,2,1,0:T(8,128)S(1)} %fusion.54), channel_id=1, source_target_pairs={{0,4},{4,0},{1,5},{5,1},{2,6},{6,2},{3,7},{7,3},{8,12},{12,8},{9,1... | collective-permute-start | bytes 6152 | tf_op jit(solution)/shard_map/ppermute | solution.py:18
  6.8 0.7 %copy-start.16 = (f32[2,256]{1,0:T(2,128)S(1)}, f32[2,256]{1,0:T(2,128)}, u32[]{:S(2)}) copy-start(f32[2,256]{1,0:T(2,128)} %param.39) | copy-start | bytes 6148
  7.8 0.7 %copy-start.17 = (s32[256]{0:T(256)S(1)}, s32[256]{0:T(256)}, u32[]{:S(2)}) copy-start(s32[256]{0:T(256)} %param.42) | copy-start | bytes 3076
  7.8 0.8 %copy-start.18 = (s32[256]{0:T(256)S(1)}, s32[256]{0:T(256)}, u32[]{:S(2)}) copy-start(s32[256]{0:T(256)} %param.41) | copy-start | bytes 3076
  8.6 0.8 %copy-start.12 = (f32[8,8,128]{2,1,0:T(8,128)S(1)}, f32[8,8,128]{2,1,0:T(8,128)}, u32[]{:S(2)}) copy-start(f32[8,8,128]{2,1,0:T(8,128)} %param.35) | copy-start | bytes 98308
  8.6 0.8 %copy-start.13 = (f32[8,8,128]{2,1,0:T(8,128)S(1)}, f32[8,8,128]{2,1,0:T(8,128)}, u32[]{:S(2)}) copy-start(f32[8,8,128]{2,1,0:T(8,128)} %param.34) | copy-start | bytes 98308
  10.9 11.6 %all-to-all-start = ((f32[32,1,192]{2,1,0:T(1,128)}), f32[32,1,192]{2,1,0:T(1,128)S(1)}, u32[]{:S(2)}, u32[]{:S(2)}) async-start(f32[32,1,192]{2,1,0:T(1,128)} %copy.147), calls=%async_computation | async-start | bytes 65536 | tf_op jit(solution)/shard_map/all_to_all | solution.py:214
  16.8 5.3 %collective-permute-start.3 = (f32[2,8,8,4]{3,2,1,0:T(8,128)S(1)}, f32[2,8,8,4]{3,2,1,0:T(8,128)S(1)}, u32[]{:S(2)}, u32[]{:S(2)}) collective-permute-start(f32[2,8,8,4]{3,2,1,0:T(8,128)S(1)} %dynamic-slice_maximum_fusion.1), channel_id=1, source_target_pairs={{0,4},{4,0},{1,5},{5,1},{2,6},{6,2},{3,7},{7,3},{8,12},{12,8},{9,1... | collective-permute-start | bytes 6152 | tf_op jit(solution)/shard_map/ppermute | solution.py:18
  18.3 6.3 %collective-permute-start.5 = (f32[2,16,4,136]{3,1,2,0:T(8,128)S(1)}, f32[2,16,4,136]{3,1,2,0:T(8,128)S(1)}, u32[]{:S(2)}, u32[]{:S(2)}) collective-permute-start(f32[2,16,4,136]{3,1,2,0:T(8,128)S(1)} %copy.155), channel_id=1, source_target_pairs={{8,16},{16,8},{9,17},{17,9},{10,18},{18,10},{11,19},{19,11},{12,20... | collective-permute-start | bytes 208904 | tf_op jit(solution)/shard_map/ppermute | solution.py:26
  22.0 2.6 %collective-permute-start.4 = (f32[2,16,4,136]{3,1,2,0:T(8,128)S(1)}, f32[2,16,4,136]{3,1,2,0:T(8,128)S(1)}, u32[]{:S(2)}, u32[]{:S(2)}) collective-permute-start(f32[2,16,4,136]{3,1,2,0:T(8,128)S(1)} %copy.154), channel_id=1, source_target_pairs={{0,8},{8,0},{16,24},{24,16},{1,9},{9,1},{17,25},{25,17},{2,10},{10... | collective-permute-start | bytes 208904 | tf_op jit(solution)/shard_map/ppermute | solution.py:18
  25.5 0.8 %copy-start.5 = (f32[8,8,128]{2,1,0:T(8,128)S(1)}, f32[8,8,128]{2,1,0:T(8,128)}, u32[]{:S(2)}) copy-start(f32[8,8,128]{2,1,0:T(8,128)} %param.31) | copy-start | bytes 98308
  25.5 0.8 %copy-start.6 = (f32[8,8,128]{2,1,0:T(8,128)S(1)}, f32[8,8,128]{2,1,0:T(8,128)}, u32[]{:S(2)}) copy-start(f32[8,8,128]{2,1,0:T(8,128)} %param.36) | copy-start | bytes 98308
  25.5 0.8 %copy-start.7 = (f32[8,8,128]{2,1,0:T(8,128)S(1)}, f32[8,8,128]{2,1,0:T(8,128)}, u32[]{:S(2)}) copy-start(f32[8,8,128]{2,1,0:T(8,128)} %param.37) | copy-start | bytes 98308
  25.6 0.8 %copy-start.8 = (f32[8,8,128]{2,1,0:T(8,128)S(1)}, f32[8,8,128]{2,1,0:T(8,128)}, u32[]{:S(2)}) copy-start(f32[8,8,128]{2,1,0:T(8,128)} %param.32) | copy-start | bytes 98308
  25.6 0.8 %copy-start.9 = (f32[8,8,128]{2,1,0:T(8,128)S(1)}, f32[8,8,128]{2,1,0:T(8,128)}, u32[]{:S(2)}) copy-start(f32[8,8,128]{2,1,0:T(8,128)} %param.33) | copy-start | bytes 98308
  25.6 0.8 %copy-start.14 = (f32[8,8,128]{2,1,0:T(8,128)S(1)}, f32[8,8,128]{2,1,0:T(8,128)}, u32[]{:S(2)}) copy-start(f32[8,8,128]{2,1,0:T(8,128)} %param.28) | copy-start | bytes 98308
  25.6 0.8 %copy-start.15 = (f32[8,8,128]{2,1,0:T(8,128)S(1)}, f32[8,8,128]{2,1,0:T(8,128)}, u32[]{:S(2)}) copy-start(f32[8,8,128]{2,1,0:T(8,128)} %param.30) | copy-start | bytes 98308
  26.5 17.7 %copy-start.1 = (f32[8,8,128]{2,1,0:T(8,128)}, f32[8,8,128]{2,1,0:T(8,128)S(1)}, u32[]{:S(2)}) copy-start(f32[8,8,128]{2,1,0:T(8,128)S(1)} %get-tuple-element.146) | copy-start | bytes 98308
  26.5 17.7 %copy-start.2 = (f32[8,8,128]{2,1,0:T(8,128)}, f32[8,8,128]{2,1,0:T(8,128)S(1)}, u32[]{:S(2)}) copy-start(f32[8,8,128]{2,1,0:T(8,128)S(1)} %get-tuple-element.147) | copy-start | bytes 98308
  26.6 3.5 %collective-permute-start.9 = (f32[2,8,8,4]{3,2,1,0:T(8,128)S(1)}, f32[2,8,8,4]{3,2,1,0:T(8,128)S(1)}, u32[]{:S(2)}, u32[]{:S(2)}) collective-permute-start(f32[2,8,8,4]{3,2,1,0:T(8,128)S(1)} %fusion.52), channel_id=1, source_target_pairs={{0,4},{4,0},{1,5},{5,1},{2,6},{6,2},{3,7},{7,3},{8,12},{12,8},{9,1... | collective-permute-start | bytes 6152 | tf_op jit(solution)/shard_map/ppermute | solution.py:18
  26.9 3.2 %collective-permute-start.7 = (f32[2,4,8,128]{3,2,1,0:T(8,128)S(1)}, f32[2,4,8,128]{3,2,1,0:T(8,128)S(1)}, u32[]{:S(2)}, u32[]{:S(2)}) collective-permute-start(f32[2,4,8,128]{3,2,1,0:T(8,128)S(1)} %get-tuple-element.118), channel_id=1, source_target_pairs={{0,1},{1,0},{2,3},{3,2},{4,5},{5,4},{6,7},{7,6},{8,9},{9,8},{10,11... | collective-permute-start | bytes 98312 | tf_op jit(solution)/shard_map/ppermute | solution.py:18
  28.1 5.2 %collective-permute-start.6 = (f32[2,4,8,128]{3,2,1,0:T(8,128)S(1)}, f32[2,4,8,128]{3,2,1,0:T(8,128)S(1)}, u32[]{:S(2)}, u32[]{:S(2)}) collective-permute-start(f32[2,4,8,128]{3,2,1,0:T(8,128)S(1)} %get-tuple-element.119), channel_id=1, source_target_pairs={{1,2},{2,1},{5,6},{6,5},{9,10},{10,9},{13,14},{14,13},{17,18},{18,... | collective-permute-start | bytes 98312 | tf_op jit(solution)/shard_map/ppermute | solution.py:26
  33.4 6.7 %collective-permute-start.8 = (f32[2,8,8,4]{3,2,1,0:T(8,128)S(1)}, f32[2,8,8,4]{3,2,1,0:T(8,128)S(1)}, u32[]{:S(2)}, u32[]{:S(2)}) collective-permute-start(f32[2,8,8,4]{3,2,1,0:T(8,128)S(1)} %dynamic-slice_maximum_fusion), channel_id=1, source_target_pairs={{0,4},{4,0},{1,5},{5,1},{2,6},{6,2},{3,7},{7,3},{8,12},{12,8},{9,1... | collective-permute-start | bytes 6152 | tf_op jit(solution)/shard_map/ppermute | solution.py:18
  34.9 7.8 %collective-permute-start.11 = (f32[2,16,4,136]{3,1,2,0:T(8,128)S(1)}, f32[2,16,4,136]{3,1,2,0:T(8,128)S(1)}, u32[]{:S(2)}, u32[]{:S(2)}) collective-permute-start(f32[2,16,4,136]{3,1,2,0:T(8,128)S(1)} %copy.157), channel_id=1, source_target_pairs={{8,16},{16,8},{9,17},{17,9},{10,18},{18,10},{11,19},{19,11},{12,20... | collective-permute-start | bytes 208904 | tf_op jit(solution)/shard_map/ppermute | solution.py:26
  40.0 2.6 %collective-permute-start.10 = (f32[2,16,4,136]{3,1,2,0:T(8,128)S(1)}, f32[2,16,4,136]{3,1,2,0:T(8,128)S(1)}, u32[]{:S(2)}, u32[]{:S(2)}) collective-permute-start(f32[2,16,4,136]{3,1,2,0:T(8,128)S(1)} %copy.156), channel_id=1, source_target_pairs={{0,8},{8,0},{16,24},{24,16},{1,9},{9,1},{17,25},{25,17},{2,10},{10... | collective-permute-start | bytes 208904 | tf_op jit(solution)/shard_map/ppermute | solution.py:18
  44.3 0.6 %copy-start.10 = (f32[8,8,128]{2,1,0:T(8,128)}, f32[8,8,128]{2,1,0:T(8,128)S(1)}, u32[]{:S(2)}) copy-start(f32[8,8,128]{2,1,0:T(8,128)S(1)} %get-tuple-element.144) | copy-start | bytes 98308
  44.3 0.6 %copy-start.11 = (f32[8,8,128]{2,1,0:T(8,128)}, f32[8,8,128]{2,1,0:T(8,128)S(1)}, u32[]{:S(2)}) copy-start(f32[8,8,128]{2,1,0:T(8,128)S(1)} %get-tuple-element.145) | copy-start | bytes 98308

commit v15 on v12

--- a/solution.py
+++ b/solution.py
@@ -195,8 +195,9 @@
     highest = lax.Precision.HIGHEST
     in_column = (owner[:, None] == jnp.arange(columns, dtype=jnp.int32)[None, :]).astype(jnp.float32)
     order = jnp.arange(traces, dtype=jnp.int32)
-    earlier = (order[:, None] > order[None, :]).astype(jnp.float32)
-    rank = jnp.sum(jnp.dot(earlier, in_column, precision=highest) * in_column, axis=1)
+    earlier = (order[:, None] > order[None, :]).astype(jnp.bfloat16)
+    before = jnp.dot(earlier, in_column.astype(jnp.bfloat16), preferred_element_type=jnp.float32)
+    rank = jnp.sum(before * in_column, axis=1)
     lane = jnp.arange(3 * capacity, dtype=jnp.int32)[None, :]
     value = jnp.where(
         lane < capacity,

time: 45 us -> 45 us (level)
  no operation moved by 1% of the time
where the time goes in v15:
time: 45 us; the launch traced here: 44.5 us
  starting transfers between devices  25.1 us (56%)
  waiting for transfers between devices  6.74 us (15%)
  other arithmetic  5.21 us (12%)
  local copies, waits for them, and re-layouts  4.61 us (10%)
  matrix products  1.52 us (3%)
  between operations  1.3 us (3%)
    ppermute x4, starting transfers between devices, shift_pair(): lax.ppermute(lax.dynamic_slice_in_dim(block, jnp.where(even, 0, size - wi...  11.9 us
    ppermute x8, starting transfers between devices, shift_pair(): lax.ppermute(lax.dynamic_slice_in_dim(block, jnp.where(even, size - width...  7.42 us
    ppermute x4, waiting for transfers between devices, shift_pair(): lax.ppermute(lax.dynamic_slice_in_dim(block, jnp.where(even, 0, size - wi...  6.72 us
    all_to_all x1, starting transfers between devices, local(): lax.all_to_all(send, ('inl', 'xl', 'gz'), split_axis=0, concat_axis=0, ti...  5.86 us
    unnamed x43, local copies, waits for them, and re-layouts  3.49 us
    sub x2, other arithmetic, advance(): h_two = u_xx + u_yy + u_zz - h_one  1.18 us
    concatenate x4, other arithmetic, second_round(): return jnp.concatenate([low_x, full, high_x], axis=2)  0.91 us
  transfers between devices with their start and end apart: 13, of which 3 were waited for; matrix products, arithmetic and copies ran while one was open for 8% of the time, Pallas kernels for 0%

profile of v15, /device:TPU:17, one launch (start us, length us, event | category | flops | bytes accessed | tf_op | source)
XLA Modules:
  0.0 44.5 jit_solution(10833530992534459222)
XLA Ops:
  0.6 0.0 copy-start
  0.7 0.8 %copy-done.3 = f32[8,8,128]{2,1,0:T(8,128)S(1)} copy-done((f32[8,8,128]{2,1,0:T(8,128)S(1)}, f32[8,8,128]{2,1,0:T(8,128)}, u32[]{:S(2)}) %copy-start.3) | copy-done | bytes 32792
  1.4 0.7 %fusion.160 = (f32[2,4,8,128]{3,2,1,0:T(8,128)S(1)}, f32[2,4,8,128]{3,2,1,0:T(8,128)S(1)}) fusion(s32[]{:T(128)S(6)} %select_n.208, f32[1,8,8,128]{3,2,1,0:T(8,128)S(1)} %bitcast.134, f32[1,8,8,128]{3,2,1,0:T(8,128)} %bitcast.142, s32[]{:T(128)S(6)} %select_n.207), kind=kLoop, calls=%fused_computation.277 | loop fusion | flops 16384 | bytes 131080 | tf_op jit(solution)/shard_map/stack | solution.py:232
  2.2 1.4 %collective-permute-start.1 = (f32[2,4,8,128]{3,2,1,0:T(8,128)S(1)}, f32[2,4,8,128]{3,2,1,0:T(8,128)S(1)}, u32[]{:S(2)}, u32[]{:S(2)}) collective-permute-start(f32[2,4,8,128]{3,2,1,0:T(8,128)S(1)} %get-tuple-element.117), channel_id=1, source_target_pairs={{0,1},{1,0},{2,3},{3,2},{4,5},{5,4},{6,7},{7,6},{8,9},{9,8},{10,11... | collective-permute-start | bytes 98312 | tf_op jit(solution)/shard_map/ppermute | solution.py:18
  3.5 1.9 %collective-permute-start = (f32[2,4,8,128]{3,2,1,0:T(8,128)S(1)}, f32[2,4,8,128]{3,2,1,0:T(8,128)S(1)}, u32[]{:S(2)}, u32[]{:S(2)}) collective-permute-start(f32[2,4,8,128]{3,2,1,0:T(8,128)S(1)} %get-tuple-element.118), channel_id=1, source_target_pairs={{1,2},{2,1},{5,6},{6,5},{9,10},{10,9},{13,14},{14,13},{17,18},{18,... | collective-permute-start | bytes 98312 | tf_op jit(solution)/shard_map/ppermute | solution.py:26
  5.5 0.1 fusion.50
  5.6 1.2 %collective-permute-start.2 = (f32[2,8,8,4]{3,2,1,0:T(8,128)S(1)}, f32[2,8,8,4]{3,2,1,0:T(8,128)S(1)}, u32[]{:S(2)}, u32[]{:S(2)}) collective-permute-start(f32[2,8,8,4]{3,2,1,0:T(8,128)S(1)} %fusion.50), channel_id=1, source_target_pairs={{0,4},{4,0},{1,5},{5,1},{2,6},{6,2},{3,7},{7,3},{8,12},{12,8},{9,1... | collective-permute-start | bytes 6152 | tf_op jit(solution)/shard_map/ppermute | solution.py:18
  6.9 0.1 select_reduce_fusion
  7.0 0.6 %copy-done.16 = f32[2,256]{1,0:T(2,128)S(1)} copy-done((f32[2,256]{1,0:T(2,128)S(1)}, f32[2,256]{1,0:T(2,128)}, u32[]{:S(2)}) %copy-start.16) | copy-done | bytes 2072
  7.5 0.3 convolution_multiply_fusion
  7.8 0.1 copy-start.18
  7.9 0.7 %copy-done.17 = s32[256]{0:T(256)S(1)} copy-done((s32[256]{0:T(256)S(1)}, s32[256]{0:T(256)}, u32[]{:S(2)}) %copy-start.17) | copy-done | bytes 1048
  8.5 0.0 copy-done.18
  8.6 0.2 fusion
  8.8 0.5 %copy-done.12 = f32[8,8,128]{2,1,0:T(8,128)S(1)} copy-done((f32[8,8,128]{2,1,0:T(8,128)S(1)}, f32[8,8,128]{2,1,0:T(8,128)}, u32[]{:S(2)}) %copy-start.12) | copy-done | bytes 32792
  9.3 0.0 copy-done.13
  9.3 0.2 fusion.204
  9.6 0.4 fusion.18
  10.2 0.1 dynamic-slice_maximum_fusion.1
  10.3 0.6 %copy.42 = f32[32,1,192]{2,1,0:T(1,128)} copy(f32[32,1,192]{2,0,1:T(8,128)S(1)} %bitcast.162) | data formatting | bytes 49152 | tf_op jit(solution)/shard_map/all_to_all | solution.py:215
  10.9 5.9 %all-to-all-start = ((f32[32,1,192]{2,1,0:T(1,128)}), f32[32,1,192]{2,1,0:T(1,128)S(1)}, u32[]{:S(2)}, u32[]{:S(2)}) async-start(f32[32,1,192]{2,1,0:T(1,128)} %copy.42), calls=%async_computation | async-start | bytes 65536 | tf_op jit(solution)/shard_map/all_to_all | solution.py:215
  16.8 1.2 %collective-permute-start.3 = (f32[2,8,8,4]{3,2,1,0:T(8,128)S(1)}, f32[2,8,8,4]{3,2,1,0:T(8,128)S(1)}, u32[]{:S(2)}, u32[]{:S(2)}) collective-permute-start(f32[2,8,8,4]{3,2,1,0:T(8,128)S(1)} %dynamic-slice_maximum_fusion.1), channel_id=1, source_target_pairs={{0,4},{4,0},{1,5},{5,1},{2,6},{6,2},{3,7},{7,3},{8,12},{12,8},{9,1... | collective-permute-start | bytes 6152 | tf_op jit(solution)/shard_map/ppermute | solution.py:18
  18.0 0.1 select_maximum_fusion.2
  18.2 0.1 constant_dynamic-slice_fusion.3
  18.2 0.7 %collective-permute-start.4 = (f32[2,16,4,136]{3,2,1,0:T(4,128)S(1)}, f32[2,16,4,136]{3,2,1,0:T(4,128)S(1)}, u32[]{:S(2)}, u32[]{:S(2)}) collective-permute-start(f32[2,16,4,136]{3,2,1,0:T(4,128)S(1)} %get-tuple-element.76), channel_id=1, source_target_pairs={{0,8},{8,0},{16,24},{24,16},{1,9},{9,1},{17,25},{25,17},{2,10},{10... | collective-permute-start | bytes 208904 | tf_op jit(solution)/shard_map/ppermute | solution.py:18
  19.0 3.0 %collective-permute-start.5 = (f32[2,16,4,136]{3,2,1,0:T(4,128)S(1)}, f32[2,16,4,136]{3,2,1,0:T(4,128)S(1)}, u32[]{:S(2)}, u32[]{:S(2)}) collective-permute-start(f32[2,16,4,136]{3,2,1,0:T(4,128)S(1)} %get-tuple-element.77), channel_id=1, source_target_pairs={{8,16},{16,8},{9,17},{17,9},{10,18},{18,10},{11,19},{19,11},{12,20... | collective-permute-start | bytes 208904 | tf_op jit(solution)/shard_map/ppermute | solution.py:26
  22.0 0.1 maximum_maximum_fusion.2
  22.2 0.3 fusion.31
  22.6 0.1 reshape.205
  22.7 0.6 %convolution_bitcast_fusion = f32[16,128]{1,0:T(8,128)S(1)} fusion(s32[32,64]{1,0:T(8,128)S(1)} %add_select_fusion, f32[8,32,64]{2,0,1:T(8,128)S(1)} %fusion.45, f32[2,32,64]{2,0,1:T(2,128)S(1)} %bitcast.161), kind=kOutput, calls=%fused_computation.1 | convolution fusion | flops 50626560 | bytes 98304 | tf_op jit(solution)/shard_map/dot_general | solution.py:228
  23.3 1.9 %collective-permute-done.5 = f32[2,16,4,136]{3,2,1,0:T(4,128)S(1)} collective-permute-done((f32[2,16,4,136]{3,2,1,0:T(4,128)S(1)}, f32[2,16,4,136]{3,2,1,0:T(4,128)S(1)}, u32[]{:S(2)}, u32[]{:S(2)}) %collective-permute-start.5) | collective-permute-done | bytes 69664 | tf_op jit(solution)/shard_map/ppermute | solution.py:26
  25.3 0.2 pad_maximum_fusion
  25.4 0.3 maximum_maximum_fusion
  25.7 0.2 fusion.10
  26.0 0.6 %add_subtract_fusion.1 = (f32[2,8,8,128]{3,2,1,0:T(8,128)S(1)}, f32[2,8,8,128]{3,2,1,0:T(8,128)S(1)}) fusion(f32[2,16,8,128]{3,2,1,0:T(8,128)S(1)} %fusion.31, f32[8,8,128]{2,1,0:T(8,128)S(1)} %get-tuple-element.102, f32[2,16,8,136]{3,2,1,0:T(8,128)S(1)} %fusion.10, f32[8,8,128]{2,1,0:T(8,128)S(1)} %get-tuple-element.103, ...), kind=kLoop, calls=%fused_computation.260 | loop fusion | flops 1392640 | bytes 3538944 | tf_op jit(solution)/shard_map/sub | solution.py:135
  26.6 0.1 copy-done.5
  26.7 0.0 copy-done.6
  26.7 0.0 copy-done.7
  26.7 0.0 copy-done.8
  26.8 0.0 copy-done.9
  26.8 0.0 copy-done.14
  26.8 0.0 copy-done.15
  26.9 0.0 copy-start.1
  26.9 0.1 fusion.48
  27.0 0.3 collective-permute-start.9
  27.3 1.2 %collective-permute-start.7 = (f32[2,4,8,128]{3,2,1,0:T(8,128)S(1)}, f32[2,4,8,128]{3,2,1,0:T(8,128)S(1)}, u32[]{:S(2)}, u32[]{:S(2)}) collective-permute-start(f32[2,4,8,128]{3,2,1,0:T(8,128)S(1)} %get-tuple-element.98), channel_id=1, source_target_pairs={{0,1},{1,0},{2,3},{3,2},{4,5},{5,4},{6,7},{7,6},{8,9},{9,8},{10,11... | collective-permute-start | bytes 98312 | tf_op jit(solution)/shard_map/ppermute | solution.py:18
  28.5 1.9 %collective-permute-start.6 = (f32[2,4,8,128]{3,2,1,0:T(8,128)S(1)}, f32[2,4,8,128]{3,2,1,0:T(8,128)S(1)}, u32[]{:S(2)}, u32[]{:S(2)}) collective-permute-start(f32[2,4,8,128]{3,2,1,0:T(8,128)S(1)} %get-tuple-element.99), channel_id=1, source_target_pairs={{1,2},{2,1},{5,6},{6,5},{9,10},{10,9},{13,14},{14,13},{17,18},{18,... | collective-permute-start | bytes 98312 | tf_op jit(solution)/shard_map/ppermute | solution.py:26
  30.5 2.7 %collective-permute-done.6 = f32[2,4,8,128]{3,2,1,0:T(8,128)S(1)} collective-permute-done((f32[2,4,8,128]{3,2,1,0:T(8,128)S(1)}, f32[2,4,8,128]{3,2,1,0:T(8,128)S(1)}, u32[]{:S(2)}, u32[]{:S(2)}) %collective-permute-start.6) | collective-permute-done | bytes 32800 | tf_op jit(solution)/shard_map/ppermute | solution.py:26
  33.2 0.1 dynamic-slice_maximum_fusion
  33.3 1.2 %collective-permute-start.8 = (f32[2,8,8,4]{3,2,1,0:T(8,128)S(1)}, f32[2,8,8,4]{3,2,1,0:T(8,128)S(1)}, u32[]{:S(2)}, u32[]{:S(2)}) collective-permute-start(f32[2,8,8,4]{3,2,1,0:T(8,128)S(1)} %dynamic-slice_maximum_fusion), channel_id=1, source_target_pairs={{0,4},{4,0},{1,5},{5,1},{2,6},{6,2},{3,7},{7,3},{8,12},{12,8},{9,1... | collective-permute-start | bytes 6152 | tf_op jit(solution)/shard_map/ppermute | solution.py:18
  34.5 0.1 select_maximum_fusion
  34.7 0.1 constant_dynamic-slice_fusion.1
  34.8 0.1 collective-permute-start.10
  34.8 5.0 %collective-permute-start.11 = (f32[2,16,4,136]{3,2,1,0:T(4,128)S(1)}, f32[2,16,4,136]{3,2,1,0:T(4,128)S(1)}, u32[]{:S(2)}, u32[]{:S(2)}) collective-permute-start(f32[2,16,4,136]{3,2,1,0:T(4,128)S(1)} %get-tuple-element.73), channel_id=1, source_target_pairs={{8,16},{16,8},{9,17},{17,9},{10,18},{18,10},{11,19},{19,11},{12,20... | collective-permute-start | bytes 208904 | tf_op jit(solution)/shard_map/ppermute | solution.py:26
  39.9 0.1 maximum_maximum_fusion.4
  40.1 0.3 fusion.24
  40.4 2.1 %collective-permute-done.11 = f32[2,16,4,136]{3,2,1,0:T(4,128)S(1)} collective-permute-done((f32[2,16,4,136]{3,2,1,0:T(4,128)S(1)}, f32[2,16,4,136]{3,2,1,0:T(4,128)S(1)}, u32[]{:S(2)}, u32[]{:S(2)}) %collective-permute-start.11) | collective-permute-done | bytes 69664 | tf_op jit(solution)/shard_map/ppermute | solution.py:26
  42.5 0.2 pad_maximum_fusion.1
  42.7 0.3 maximum_maximum_fusion.1
  43.0 0.2 fusion.3
  43.2 0.6 %add_subtract_fusion = (f32[2,8,8,128]{3,2,1,0:T(8,128)S(1)}, f32[2,8,8,128]{3,2,1,0:T(8,128)S(1)}) fusion(f32[2,16,8,128]{3,2,1,0:T(8,128)S(1)} %fusion.24, f32[8,8,128]{2,1,0:T(8,128)S(1)} %get-tuple-element.102, f32[2,16,8,136]{3,2,1,0:T(8,128)S(1)} %fusion.3, f32[8,8,128]{2,1,0:T(8,128)S(1)} %get-tuple-element.103, ...), kind=kLoop, calls=%fused_computation.259 | loop fusion | flops 1392640 | bytes 3538944 | tf_op jit(solution)/shard_map/sub | solution.py:135
  43.9 0.0 copy-start.10
  43.9 0.6 %copy-done.10 = f32[8,8,128]{2,1,0:T(8,128)} copy-done((f32[8,8,128]{2,1,0:T(8,128)}, f32[8,8,128]{2,1,0:T(8,128)S(1)}, u32[]{:S(2)}) %copy-start.10) | copy-done | bytes 32792
  44.5 0.0 copy-done.11
  (63 shorter events, 0.5 us)
Async XLA Ops:
  0.6 6.3 %copy-start = (f32[256,256]{1,0:T(8,128)S(1)}, f32[256,256]{1,0:T(8,128)}, u32[]{:S(2)}) copy-start(f32[256,256]{1,0:T(8,128)} %param.36) | copy-start | bytes 786436
  0.6 0.8 %copy-start.3 = (f32[8,8,128]{2,1,0:T(8,128)S(1)}, f32[8,8,128]{2,1,0:T(8,128)}, u32[]{:S(2)}) copy-start(f32[8,8,128]{2,1,0:T(8,128)} %param.25) | copy-start | bytes 98308
  2.2 3.3 %copy-start.4 = (f32[8,8,128]{2,1,0:T(8,128)S(1)}, f32[8,8,128]{2,1,0:T(8,128)}, u32[]{:S(2)}) copy-start(f32[8,8,128]{2,1,0:T(8,128)} %param.27) | copy-start | bytes 98308
  2.2 7.9 %collective-permute-start.1 = (f32[2,4,8,128]{3,2,1,0:T(8,128)S(1)}, f32[2,4,8,128]{3,2,1,0:T(8,128)S(1)}, u32[]{:S(2)}, u32[]{:S(2)}) collective-permute-start(f32[2,4,8,128]{3,2,1,0:T(8,128)S(1)} %get-tuple-element.117), channel_id=1, source_target_pairs={{0,1},{1,0},{2,3},{3,2},{4,5},{5,4},{6,7},{7,6},{8,9},{9,8},{10,11... | collective-permute-start | bytes 98312 | tf_op jit(solution)/shard_map/ppermute | solution.py:18
  3.5 6.6 %collective-permute-start = (f32[2,4,8,128]{3,2,1,0:T(8,128)S(1)}, f32[2,4,8,128]{3,2,1,0:T(8,128)S(1)}, u32[]{:S(2)}, u32[]{:S(2)}) collective-permute-start(f32[2,4,8,128]{3,2,1,0:T(8,128)S(1)} %get-tuple-element.118), channel_id=1, source_target_pairs={{1,2},{2,1},{5,6},{6,5},{9,10},{10,9},{13,14},{14,13},{17,18},{18,... | collective-permute-start | bytes 98312 | tf_op jit(solution)/shard_map/ppermute | solution.py:26
  5.5 1.4 %copy-start.19 = (s32[256]{0:T(256)S(1)}, s32[256]{0:T(256)}, u32[]{:S(2)}) copy-start(s32[256]{0:T(256)} %param.41) | copy-start | bytes 3076
  5.5 1.4 %copy-start.20 = (f32[64]{0:T(128)S(1)}, f32[64]{0:T(128)}, u32[]{:S(2)}) copy-start(f32[64]{0:T(128)} %param.38) | copy-start | bytes 772
  5.6 4.5 %collective-permute-start.2 = (f32[2,8,8,4]{3,2,1,0:T(8,128)S(1)}, f32[2,8,8,4]{3,2,1,0:T(8,128)S(1)}, u32[]{:S(2)}, u32[]{:S(2)}) collective-permute-start(f32[2,8,8,4]{3,2,1,0:T(8,128)S(1)} %fusion.50), channel_id=1, source_target_pairs={{0,4},{4,0},{1,5},{5,1},{2,6},{6,2},{3,7},{7,3},{8,12},{12,8},{9,1... | collective-permute-start | bytes 6152 | tf_op jit(solution)/shard_map/ppermute | solution.py:18
  6.8 0.7 %copy-start.16 = (f32[2,256]{1,0:T(2,128)S(1)}, f32[2,256]{1,0:T(2,128)}, u32[]{:S(2)}) copy-start(f32[2,256]{1,0:T(2,128)} %param.37) | copy-start | bytes 6148
  7.8 0.7 %copy-start.17 = (s32[256]{0:T(256)S(1)}, s32[256]{0:T(256)}, u32[]{:S(2)}) copy-start(s32[256]{0:T(256)} %param.40) | copy-start | bytes 3076
  7.8 0.8 %copy-start.18 = (s32[256]{0:T(256)S(1)}, s32[256]{0:T(256)}, u32[]{:S(2)}) copy-start(s32[256]{0:T(256)} %param.39) | copy-start | bytes 3076
  8.6 0.8 %copy-start.12 = (f32[8,8,128]{2,1,0:T(8,128)S(1)}, f32[8,8,128]{2,1,0:T(8,128)}, u32[]{:S(2)}) copy-start(f32[8,8,128]{2,1,0:T(8,128)} %param.33) | copy-start | bytes 98308
  8.6 0.8 %copy-start.13 = (f32[8,8,128]{2,1,0:T(8,128)S(1)}, f32[8,8,128]{2,1,0:T(8,128)}, u32[]{:S(2)}) copy-start(f32[8,8,128]{2,1,0:T(8,128)} %param.32) | copy-start | bytes 98308
  10.9 11.6 %all-to-all-start = ((f32[32,1,192]{2,1,0:T(1,128)}), f32[32,1,192]{2,1,0:T(1,128)S(1)}, u32[]{:S(2)}, u32[]{:S(2)}) async-start(f32[32,1,192]{2,1,0:T(1,128)} %copy.42), calls=%async_computation | async-start | bytes 65536 | tf_op jit(solution)/shard_map/all_to_all | solution.py:215
  16.8 5.2 %collective-permute-start.3 = (f32[2,8,8,4]{3,2,1,0:T(8,128)S(1)}, f32[2,8,8,4]{3,2,1,0:T(8,128)S(1)}, u32[]{:S(2)}, u32[]{:S(2)}) collective-permute-start(f32[2,8,8,4]{3,2,1,0:T(8,128)S(1)} %dynamic-slice_maximum_fusion.1), channel_id=1, source_target_pairs={{0,4},{4,0},{1,5},{5,1},{2,6},{6,2},{3,7},{7,3},{8,12},{12,8},{9,1... | collective-permute-start | bytes 6152 | tf_op jit(solution)/shard_map/ppermute | solution.py:18
  18.2 5.1 %collective-permute-start.4 = (f32[2,16,4,136]{3,2,1,0:T(4,128)S(1)}, f32[2,16,4,136]{3,2,1,0:T(4,128)S(1)}, u32[]{:S(2)}, u32[]{:S(2)}) collective-permute-start(f32[2,16,4,136]{3,2,1,0:T(4,128)S(1)} %get-tuple-element.76), channel_id=1, source_target_pairs={{0,8},{8,0},{16,24},{24,16},{1,9},{9,1},{17,25},{25,17},{2,10},{10... | collective-permute-start | bytes 208904 | tf_op jit(solution)/shard_map/ppermute | solution.py:18
  19.0 6.3 %collective-permute-start.5 = (f32[2,16,4,136]{3,2,1,0:T(4,128)S(1)}, f32[2,16,4,136]{3,2,1,0:T(4,128)S(1)}, u32[]{:S(2)}, u32[]{:S(2)}) collective-permute-start(f32[2,16,4,136]{3,2,1,0:T(4,128)S(1)} %get-tuple-element.77), channel_id=1, source_target_pairs={{8,16},{16,8},{9,17},{17,9},{10,18},{18,10},{11,19},{19,11},{12,20... | collective-permute-start | bytes 208904 | tf_op jit(solution)/shard_map/ppermute | solution.py:26
  25.9 0.8 %copy-start.5 = (f32[8,8,128]{2,1,0:T(8,128)S(1)}, f32[8,8,128]{2,1,0:T(8,128)}, u32[]{:S(2)}) copy-start(f32[8,8,128]{2,1,0:T(8,128)} %param.29) | copy-start | bytes 98308
  26.0 0.8 %copy-start.6 = (f32[8,8,128]{2,1,0:T(8,128)S(1)}, f32[8,8,128]{2,1,0:T(8,128)}, u32[]{:S(2)}) copy-start(f32[8,8,128]{2,1,0:T(8,128)} %param.34) | copy-start | bytes 98308
  26.0 0.8 %copy-start.7 = (f32[8,8,128]{2,1,0:T(8,128)S(1)}, f32[8,8,128]{2,1,0:T(8,128)}, u32[]{:S(2)}) copy-start(f32[8,8,128]{2,1,0:T(8,128)} %param.35) | copy-start | bytes 98308
  26.0 0.8 %copy-start.8 = (f32[8,8,128]{2,1,0:T(8,128)S(1)}, f32[8,8,128]{2,1,0:T(8,128)}, u32[]{:S(2)}) copy-start(f32[8,8,128]{2,1,0:T(8,128)} %param.30) | copy-start | bytes 98308
  26.0 0.8 %copy-start.9 = (f32[8,8,128]{2,1,0:T(8,128)S(1)}, f32[8,8,128]{2,1,0:T(8,128)}, u32[]{:S(2)}) copy-start(f32[8,8,128]{2,1,0:T(8,128)} %param.31) | copy-start | bytes 98308
  26.0 0.8 %copy-start.14 = (f32[8,8,128]{2,1,0:T(8,128)S(1)}, f32[8,8,128]{2,1,0:T(8,128)}, u32[]{:S(2)}) copy-start(f32[8,8,128]{2,1,0:T(8,128)} %param.26) | copy-start | bytes 98308
  26.0 0.8 %copy-start.15 = (f32[8,8,128]{2,1,0:T(8,128)S(1)}, f32[8,8,128]{2,1,0:T(8,128)}, u32[]{:S(2)}) copy-start(f32[8,8,128]{2,1,0:T(8,128)} %param.28) | copy-start | bytes 98308
  26.9 16.9 %copy-start.1 = (f32[8,8,128]{2,1,0:T(8,128)}, f32[8,8,128]{2,1,0:T(8,128)S(1)}, u32[]{:S(2)}) copy-start(f32[8,8,128]{2,1,0:T(8,128)S(1)} %get-tuple-element.126) | copy-start | bytes 98308
  26.9 16.9 %copy-start.2 = (f32[8,8,128]{2,1,0:T(8,128)}, f32[8,8,128]{2,1,0:T(8,128)S(1)}, u32[]{:S(2)}) copy-start(f32[8,8,128]{2,1,0:T(8,128)S(1)} %get-tuple-element.127) | copy-start | bytes 98308
  27.0 3.5 %collective-permute-start.9 = (f32[2,8,8,4]{3,2,1,0:T(8,128)S(1)}, f32[2,8,8,4]{3,2,1,0:T(8,128)S(1)}, u32[]{:S(2)}, u32[]{:S(2)}) collective-permute-start(f32[2,8,8,4]{3,2,1,0:T(8,128)S(1)} %fusion.48), channel_id=1, source_target_pairs={{0,4},{4,0},{1,5},{5,1},{2,6},{6,2},{3,7},{7,3},{8,12},{12,8},{9,1... | collective-permute-start | bytes 6152 | tf_op jit(solution)/shard_map/ppermute | solution.py:18
  27.3 3.2 %collective-permute-start.7 = (f32[2,4,8,128]{3,2,1,0:T(8,128)S(1)}, f32[2,4,8,128]{3,2,1,0:T(8,128)S(1)}, u32[]{:S(2)}, u32[]{:S(2)}) collective-permute-start(f32[2,4,8,128]{3,2,1,0:T(8,128)S(1)} %get-tuple-element.98), channel_id=1, source_target_pairs={{0,1},{1,0},{2,3},{3,2},{4,5},{5,4},{6,7},{7,6},{8,9},{9,8},{10,11... | collective-permute-start | bytes 98312 | tf_op jit(solution)/shard_map/ppermute | solution.py:18
  28.5 4.6 %collective-permute-start.6 = (f32[2,4,8,128]{3,2,1,0:T(8,128)S(1)}, f32[2,4,8,128]{3,2,1,0:T(8,128)S(1)}, u32[]{:S(2)}, u32[]{:S(2)}) collective-permute-start(f32[2,4,8,128]{3,2,1,0:T(8,128)S(1)} %get-tuple-element.99), channel_id=1, source_target_pairs={{1,2},{2,1},{5,6},{6,5},{9,10},{10,9},{13,14},{14,13},{17,18},{18,... | collective-permute-start | bytes 98312 | tf_op jit(solution)/shard_map/ppermute | solution.py:26
  33.3 6.6 %collective-permute-start.8 = (f32[2,8,8,4]{3,2,1,0:T(8,128)S(1)}, f32[2,8,8,4]{3,2,1,0:T(8,128)S(1)}, u32[]{:S(2)}, u32[]{:S(2)}) collective-permute-start(f32[2,8,8,4]{3,2,1,0:T(8,128)S(1)} %dynamic-slice_maximum_fusion), channel_id=1, source_target_pairs={{0,4},{4,0},{1,5},{5,1},{2,6},{6,2},{3,7},{7,3},{8,12},{12,8},{9,1... | collective-permute-start | bytes 6152 | tf_op jit(solution)/shard_map/ppermute | solution.py:18
  34.8 5.6 %collective-permute-start.10 = (f32[2,16,4,136]{3,2,1,0:T(4,128)S(1)}, f32[2,16,4,136]{3,2,1,0:T(4,128)S(1)}, u32[]{:S(2)}, u32[]{:S(2)}) collective-permute-start(f32[2,16,4,136]{3,2,1,0:T(4,128)S(1)} %get-tuple-element.72), channel_id=1, source_target_pairs={{0,8},{8,0},{16,24},{24,16},{1,9},{9,1},{17,25},{25,17},{2,10},{10... | collective-permute-start | bytes 208904 | tf_op jit(solution)/shard_map/ppermute | solution.py:18
  34.8 7.7 %collective-permute-start.11 = (f32[2,16,4,136]{3,2,1,0:T(4,128)S(1)}, f32[2,16,4,136]{3,2,1,0:T(4,128)S(1)}, u32[]{:S(2)}, u32[]{:S(2)}) collective-permute-start(f32[2,16,4,136]{3,2,1,0:T(4,128)S(1)} %get-tuple-element.73), channel_id=1, source_target_pairs={{8,16},{16,8},{9,17},{17,9},{10,18},{18,10},{11,19},{19,11},{12,20... | collective-permute-start | bytes 208904 | tf_op jit(solution)/shard_map/ppermute | solution.py:26
  43.9 0.6 %copy-start.10 = (f32[8,8,128]{2,1,0:T(8,128)}, f32[8,8,128]{2,1,0:T(8,128)S(1)}, u32[]{:S(2)}) copy-start(f32[8,8,128]{2,1,0:T(8,128)S(1)} %get-tuple-element.124) | copy-start | bytes 98308
  43.9 0.6 %copy-start.11 = (f32[8,8,128]{2,1,0:T(8,128)}, f32[8,8,128]{2,1,0:T(8,128)S(1)}, u32[]{:S(2)}) copy-start(f32[8,8,128]{2,1,0:T(8,128)S(1)} %get-tuple-element.125) | copy-start | bytes 98308

commit v16 on v15

--- a/solution.py
+++ b/solution.py
@@ -1,4 +1,5 @@
 import jax
+import numpy as np
 import jax.numpy as jnp
 from jax import lax
 from jax.sharding import PartitionSpec as P
@@ -194,8 +195,7 @@
     traces = owner.shape[0]
     highest = lax.Precision.HIGHEST
     in_column = (owner[:, None] == jnp.arange(columns, dtype=jnp.int32)[None, :]).astype(jnp.float32)
-    order = jnp.arange(traces, dtype=jnp.int32)
-    earlier = (order[:, None] > order[None, :]).astype(jnp.bfloat16)
+    earlier = jnp.asarray(np.tri(traces, traces, -1), dtype=jnp.bfloat16)
     before = jnp.dot(earlier, in_column.astype(jnp.bfloat16), preferred_element_type=jnp.float32)
     rank = jnp.sum(before * in_column, axis=1)
     lane = jnp.arange(3 * capacity, dtype=jnp.int32)[None, :]

time: 45 us -> 45 us (level)
    unnamed x43 -> x45, local copies, waits for them, and re-layouts: 3.49 us -> 3.5 us
where the time goes in v16:
time: 45 us; the launch traced here: 44.5 us
  starting transfers between devices  25.1 us (56%)
  waiting for transfers between devices  6.74 us (15%)
  other arithmetic  5.21 us (12%)
  local copies, waits for them, and re-layouts  4.62 us (10%)
  matrix products  1.52 us (3%)
  between operations  1.31 us (3%)
    ppermute x4, starting transfers between devices, shift_pair(): lax.ppermute(lax.dynamic_slice_in_dim(block, jnp.where(even, 0, size - wi...  11.9 us
    ppermute x8, starting transfers between devices, shift_pair(): lax.ppermute(lax.dynamic_slice_in_dim(block, jnp.where(even, size - width...  7.42 us
    ppermute x4, waiting for transfers between devices, shift_pair(): lax.ppermute(lax.dynamic_slice_in_dim(block, jnp.where(even, 0, size - wi...  6.72 us
    all_to_all x1, starting transfers between devices, local(): lax.all_to_all(send, ('inl', 'xl', 'gz'), split_axis=0, concat_axis=0, ti...  5.85 us
    unnamed x45, local copies, waits for them, and re-layouts  3.5 us
    sub x2, other arithmetic, advance(): h_two = u_xx + u_yy + u_zz - h_one  1.18 us
    concatenate x4, other arithmetic, second_round(): return jnp.concatenate([low_x, full, high_x], axis=2)  0.91 us
  transfers between devices with their start and end apart: 13, of which 3 were waited for; matrix products, arithmetic and copies ran while one was open for 8% of the time, Pallas kernels for 0%

profile of v16, /device:TPU:17, one launch (start us, length us, event | category | flops | bytes accessed | tf_op | source)
XLA Modules:
  0.0 44.5 jit_solution(10072409001073085052)
XLA Ops:
  0.6 0.0 copy-start
  0.7 0.8 %copy-done.3 = f32[8,8,128]{2,1,0:T(8,128)S(1)} copy-done((f32[8,8,128]{2,1,0:T(8,128)S(1)}, f32[8,8,128]{2,1,0:T(8,128)}, u32[]{:S(2)}) %copy-start.3) | copy-done | bytes 32792
  1.4 0.7 %fusion.160 = (f32[2,4,8,128]{3,2,1,0:T(8,128)S(1)}, f32[2,4,8,128]{3,2,1,0:T(8,128)S(1)}) fusion(s32[]{:T(128)S(6)} %select_n.208, f32[1,8,8,128]{3,2,1,0:T(8,128)S(1)} %bitcast.135, f32[1,8,8,128]{3,2,1,0:T(8,128)} %bitcast.143, s32[]{:T(128)S(6)} %select_n.207), kind=kLoop, calls=%fused_computation.276 | loop fusion | flops 16384 | bytes 131080 | tf_op jit(solution)/shard_map/stack | solution.py:232
  2.2 1.4 %collective-permute-start.1 = (f32[2,4,8,128]{3,2,1,0:T(8,128)S(1)}, f32[2,4,8,128]{3,2,1,0:T(8,128)S(1)}, u32[]{:S(2)}, u32[]{:S(2)}) collective-permute-start(f32[2,4,8,128]{3,2,1,0:T(8,128)S(1)} %get-tuple-element.117), channel_id=1, source_target_pairs={{0,1},{1,0},{2,3},{3,2},{4,5},{5,4},{6,7},{7,6},{8,9},{9,8},{10,11... | collective-permute-start | bytes 98312 | tf_op jit(solution)/shard_map/ppermute | solution.py:19
  3.5 1.9 %collective-permute-start = (f32[2,4,8,128]{3,2,1,0:T(8,128)S(1)}, f32[2,4,8,128]{3,2,1,0:T(8,128)S(1)}, u32[]{:S(2)}, u32[]{:S(2)}) collective-permute-start(f32[2,4,8,128]{3,2,1,0:T(8,128)S(1)} %get-tuple-element.118), channel_id=1, source_target_pairs={{1,2},{2,1},{5,6},{6,5},{9,10},{10,9},{13,14},{14,13},{17,18},{18,... | collective-permute-start | bytes 98312 | tf_op jit(solution)/shard_map/ppermute | solution.py:27
  5.5 0.1 fusion.50
  5.6 1.2 %collective-permute-start.2 = (f32[2,8,8,4]{3,2,1,0:T(8,128)S(1)}, f32[2,8,8,4]{3,2,1,0:T(8,128)S(1)}, u32[]{:S(2)}, u32[]{:S(2)}) collective-permute-start(f32[2,8,8,4]{3,2,1,0:T(8,128)S(1)} %fusion.50), channel_id=1, source_target_pairs={{0,4},{4,0},{1,5},{5,1},{2,6},{6,2},{3,7},{7,3},{8,12},{12,8},{9,1... | collective-permute-start | bytes 6152 | tf_op jit(solution)/shard_map/ppermute | solution.py:19
  6.9 0.1 select_reduce_fusion
  7.0 0.6 %copy-done.17 = f32[2,256]{1,0:T(2,128)S(1)} copy-done((f32[2,256]{1,0:T(2,128)S(1)}, f32[2,256]{1,0:T(2,128)}, u32[]{:S(2)}) %copy-start.17) | copy-done | bytes 2072
  7.5 0.3 convolution_multiply_fusion
  7.8 0.1 copy-start.19
  7.9 0.7 %copy-done.18 = s32[256]{0:T(256)S(1)} copy-done((s32[256]{0:T(256)S(1)}, s32[256]{0:T(256)}, u32[]{:S(2)}) %copy-start.18) | copy-done | bytes 1048
  8.5 0.0 copy-done.19
  8.6 0.2 fusion
  8.8 0.5 %copy-done.13 = f32[8,8,128]{2,1,0:T(8,128)S(1)} copy-done((f32[8,8,128]{2,1,0:T(8,128)S(1)}, f32[8,8,128]{2,1,0:T(8,128)}, u32[]{:S(2)}) %copy-start.13) | copy-done | bytes 32792
  9.3 0.0 copy-done.14
  9.4 0.2 fusion.204
  9.6 0.4 fusion.18
  10.2 0.1 dynamic-slice_maximum_fusion.1
  10.3 0.6 %copy.43 = f32[32,1,192]{2,1,0:T(1,128)} copy(f32[32,1,192]{2,0,1:T(8,128)S(1)} %bitcast.163) | data formatting | bytes 49152 | tf_op jit(solution)/shard_map/all_to_all | solution.py:215
  10.9 5.8 %all-to-all-start = ((f32[32,1,192]{2,1,0:T(1,128)}), f32[32,1,192]{2,1,0:T(1,128)S(1)}, u32[]{:S(2)}, u32[]{:S(2)}) async-start(f32[32,1,192]{2,1,0:T(1,128)} %copy.43), calls=%async_computation | async-start | bytes 65536 | tf_op jit(solution)/shard_map/all_to_all | solution.py:215
  16.8 1.2 %collective-permute-start.3 = (f32[2,8,8,4]{3,2,1,0:T(8,128)S(1)}, f32[2,8,8,4]{3,2,1,0:T(8,128)S(1)}, u32[]{:S(2)}, u32[]{:S(2)}) collective-permute-start(f32[2,8,8,4]{3,2,1,0:T(8,128)S(1)} %dynamic-slice_maximum_fusion.1), channel_id=1, source_target_pairs={{0,4},{4,0},{1,5},{5,1},{2,6},{6,2},{3,7},{7,3},{8,12},{12,8},{9,1... | collective-permute-start | bytes 6152 | tf_op jit(solution)/shard_map/ppermute | solution.py:19
  18.0 0.1 select_maximum_fusion.2
  18.2 0.1 constant_dynamic-slice_fusion.3
  18.2 0.7 %collective-permute-start.4 = (f32[2,16,4,136]{3,2,1,0:T(4,128)S(1)}, f32[2,16,4,136]{3,2,1,0:T(4,128)S(1)}, u32[]{:S(2)}, u32[]{:S(2)}) collective-permute-start(f32[2,16,4,136]{3,2,1,0:T(4,128)S(1)} %get-tuple-element.76), channel_id=1, source_target_pairs={{0,8},{8,0},{16,24},{24,16},{1,9},{9,1},{17,25},{25,17},{2,10},{10... | collective-permute-start | bytes 208904 | tf_op jit(solution)/shard_map/ppermute | solution.py:19
  19.0 3.0 %collective-permute-start.5 = (f32[2,16,4,136]{3,2,1,0:T(4,128)S(1)}, f32[2,16,4,136]{3,2,1,0:T(4,128)S(1)}, u32[]{:S(2)}, u32[]{:S(2)}) collective-permute-start(f32[2,16,4,136]{3,2,1,0:T(4,128)S(1)} %get-tuple-element.77), channel_id=1, source_target_pairs={{8,16},{16,8},{9,17},{17,9},{10,18},{18,10},{11,19},{19,11},{12,20... | collective-permute-start | bytes 208904 | tf_op jit(solution)/shard_map/ppermute | solution.py:27
  22.0 0.1 maximum_maximum_fusion.2
  22.2 0.3 fusion.31
  22.6 0.1 reshape.205
  22.7 0.6 %convolution_bitcast_fusion = f32[16,128]{1,0:T(8,128)S(1)} fusion(s32[32,64]{1,0:T(8,128)S(1)} %add_select_fusion, f32[8,32,64]{2,0,1:T(8,128)S(1)} %fusion.45, f32[2,32,64]{2,0,1:T(2,128)S(1)} %bitcast.162), kind=kOutput, calls=%fused_computation.1 | convolution fusion | flops 50626560 | bytes 98304 | tf_op jit(solution)/shard_map/dot_general | solution.py:228
  23.3 1.9 %collective-permute-done.5 = f32[2,16,4,136]{3,2,1,0:T(4,128)S(1)} collective-permute-done((f32[2,16,4,136]{3,2,1,0:T(4,128)S(1)}, f32[2,16,4,136]{3,2,1,0:T(4,128)S(1)}, u32[]{:S(2)}, u32[]{:S(2)}) %collective-permute-start.5) | collective-permute-done | bytes 69664 | tf_op jit(solution)/shard_map/ppermute | solution.py:27
  25.3 0.2 pad_maximum_fusion
  25.4 0.3 maximum_maximum_fusion
  25.7 0.2 fusion.10
  26.0 0.6 %add_subtract_fusion.1 = (f32[2,8,8,128]{3,2,1,0:T(8,128)S(1)}, f32[2,8,8,128]{3,2,1,0:T(8,128)S(1)}) fusion(f32[2,16,8,128]{3,2,1,0:T(8,128)S(1)} %fusion.31, f32[8,8,128]{2,1,0:T(8,128)S(1)} %get-tuple-element.102, f32[2,16,8,136]{3,2,1,0:T(8,128)S(1)} %fusion.10, f32[8,8,128]{2,1,0:T(8,128)S(1)} %get-tuple-element.103, ...), kind=kLoop, calls=%fused_computation.259 | loop fusion | flops 1392640 | bytes 3538944 | tf_op jit(solution)/shard_map/sub | solution.py:136
  26.6 0.1 copy-done.6
  26.7 0.0 copy-done.7
  26.7 0.0 copy-done.8
  26.7 0.0 copy-done.9
  26.8 0.0 copy-done.10
  26.8 0.0 copy-done.15
  26.8 0.0 copy-done.16
  26.9 0.0 copy-start.1
  26.9 0.1 fusion.48
  27.0 0.3 collective-permute-start.9
  27.3 1.2 %collective-permute-start.7 = (f32[2,4,8,128]{3,2,1,0:T(8,128)S(1)}, f32[2,4,8,128]{3,2,1,0:T(8,128)S(1)}, u32[]{:S(2)}, u32[]{:S(2)}) collective-permute-start(f32[2,4,8,128]{3,2,1,0:T(8,128)S(1)} %get-tuple-element.98), channel_id=1, source_target_pairs={{0,1},{1,0},{2,3},{3,2},{4,5},{5,4},{6,7},{7,6},{8,9},{9,8},{10,11... | collective-permute-start | bytes 98312 | tf_op jit(solution)/shard_map/ppermute | solution.py:19
  28.5 1.9 %collective-permute-start.6 = (f32[2,4,8,128]{3,2,1,0:T(8,128)S(1)}, f32[2,4,8,128]{3,2,1,0:T(8,128)S(1)}, u32[]{:S(2)}, u32[]{:S(2)}) collective-permute-start(f32[2,4,8,128]{3,2,1,0:T(8,128)S(1)} %get-tuple-element.99), channel_id=1, source_target_pairs={{1,2},{2,1},{5,6},{6,5},{9,10},{10,9},{13,14},{14,13},{17,18},{18,... | collective-permute-start | bytes 98312 | tf_op jit(solution)/shard_map/ppermute | solution.py:27
  30.5 2.7 %collective-permute-done.6 = f32[2,4,8,128]{3,2,1,0:T(8,128)S(1)} collective-permute-done((f32[2,4,8,128]{3,2,1,0:T(8,128)S(1)}, f32[2,4,8,128]{3,2,1,0:T(8,128)S(1)}, u32[]{:S(2)}, u32[]{:S(2)}) %collective-permute-start.6) | collective-permute-done | bytes 32800 | tf_op jit(solution)/shard_map/ppermute | solution.py:27
  33.2 0.1 dynamic-slice_maximum_fusion
  33.3 1.2 %collective-permute-start.8 = (f32[2,8,8,4]{3,2,1,0:T(8,128)S(1)}, f32[2,8,8,4]{3,2,1,0:T(8,128)S(1)}, u32[]{:S(2)}, u32[]{:S(2)}) collective-permute-start(f32[2,8,8,4]{3,2,1,0:T(8,128)S(1)} %dynamic-slice_maximum_fusion), channel_id=1, source_target_pairs={{0,4},{4,0},{1,5},{5,1},{2,6},{6,2},{3,7},{7,3},{8,12},{12,8},{9,1... | collective-permute-start | bytes 6152 | tf_op jit(solution)/shard_map/ppermute | solution.py:19
  34.5 0.1 select_maximum_fusion
  34.7 0.1 constant_dynamic-slice_fusion.1
  34.8 0.1 collective-permute-start.10
  34.8 5.0 %collective-permute-start.11 = (f32[2,16,4,136]{3,2,1,0:T(4,128)S(1)}, f32[2,16,4,136]{3,2,1,0:T(4,128)S(1)}, u32[]{:S(2)}, u32[]{:S(2)}) collective-permute-start(f32[2,16,4,136]{3,2,1,0:T(4,128)S(1)} %get-tuple-element.73), channel_id=1, source_target_pairs={{8,16},{16,8},{9,17},{17,9},{10,18},{18,10},{11,19},{19,11},{12,20... | collective-permute-start | bytes 208904 | tf_op jit(solution)/shard_map/ppermute | solution.py:27
  39.9 0.1 maximum_maximum_fusion.4
  40.1 0.3 fusion.24
  40.4 2.1 %collective-permute-done.11 = f32[2,16,4,136]{3,2,1,0:T(4,128)S(1)} collective-permute-done((f32[2,16,4,136]{3,2,1,0:T(4,128)S(1)}, f32[2,16,4,136]{3,2,1,0:T(4,128)S(1)}, u32[]{:S(2)}, u32[]{:S(2)}) %collective-permute-start.11) | collective-permute-done | bytes 69664 | tf_op jit(solution)/shard_map/ppermute | solution.py:27
  42.5 0.2 pad_maximum_fusion.1
  42.7 0.3 maximum_maximum_fusion.1
  43.0 0.2 fusion.3
  43.2 0.6 %add_subtract_fusion = (f32[2,8,8,128]{3,2,1,0:T(8,128)S(1)}, f32[2,8,8,128]{3,2,1,0:T(8,128)S(1)}) fusion(f32[2,16,8,128]{3,2,1,0:T(8,128)S(1)} %fusion.24, f32[8,8,128]{2,1,0:T(8,128)S(1)} %get-tuple-element.102, f32[2,16,8,136]{3,2,1,0:T(8,128)S(1)} %fusion.3, f32[8,8,128]{2,1,0:T(8,128)S(1)} %get-tuple-element.103, ...), kind=kLoop, calls=%fused_computation.258 | loop fusion | flops 1392640 | bytes 3538944 | tf_op jit(solution)/shard_map/sub | solution.py:136
  43.9 0.0 copy-start.11
  43.9 0.6 %copy-done.11 = f32[8,8,128]{2,1,0:T(8,128)} copy-done((f32[8,8,128]{2,1,0:T(8,128)}, f32[8,8,128]{2,1,0:T(8,128)S(1)}, u32[]{:S(2)}) %copy-start.11) | copy-done | bytes 32792
  44.5 0.0 copy-done.12
  (65 shorter events, 0.5 us)
Async XLA Ops:
  0.6 6.3 %copy-start = (f32[256,256]{1,0:T(8,128)S(1)}, f32[256,256]{1,0:T(8,128)}, u32[]{:S(2)}) copy-start(f32[256,256]{1,0:T(8,128)} %param.37) | copy-start | bytes 786436
  0.6 0.8 %copy-start.3 = (f32[8,8,128]{2,1,0:T(8,128)S(1)}, f32[8,8,128]{2,1,0:T(8,128)}, u32[]{:S(2)}) copy-start(f32[8,8,128]{2,1,0:T(8,128)} %param.26) | copy-start | bytes 98308
  2.2 3.3 %copy-start.4 = (f32[8,8,128]{2,1,0:T(8,128)S(1)}, f32[8,8,128]{2,1,0:T(8,128)}, u32[]{:S(2)}) copy-start(f32[8,8,128]{2,1,0:T(8,128)} %param.28) | copy-start | bytes 98308
  2.2 7.9 %collective-permute-start.1 = (f32[2,4,8,128]{3,2,1,0:T(8,128)S(1)}, f32[2,4,8,128]{3,2,1,0:T(8,128)S(1)}, u32[]{:S(2)}, u32[]{:S(2)}) collective-permute-start(f32[2,4,8,128]{3,2,1,0:T(8,128)S(1)} %get-tuple-element.117), channel_id=1, source_target_pairs={{0,1},{1,0},{2,3},{3,2},{4,5},{5,4},{6,7},{7,6},{8,9},{9,8},{10,11... | collective-permute-start | bytes 98312 | tf_op jit(solution)/shard_map/ppermute | solution.py:19
  3.5 6.6 %collective-permute-start = (f32[2,4,8,128]{3,2,1,0:T(8,128)S(1)}, f32[2,4,8,128]{3,2,1,0:T(8,128)S(1)}, u32[]{:S(2)}, u32[]{:S(2)}) collective-permute-start(f32[2,4,8,128]{3,2,1,0:T(8,128)S(1)} %get-tuple-element.118), channel_id=1, source_target_pairs={{1,2},{2,1},{5,6},{6,5},{9,10},{10,9},{13,14},{14,13},{17,18},{18,... | collective-permute-start | bytes 98312 | tf_op jit(solution)/shard_map/ppermute | solution.py:27
  5.5 1.4 %copy-start.20 = (s32[256]{0:T(256)S(1)}, s32[256]{0:T(256)}, u32[]{:S(2)}) copy-start(s32[256]{0:T(256)} %param.42) | copy-start | bytes 3076
  5.5 1.4 %copy-start.21 = (f32[64]{0:T(128)S(1)}, f32[64]{0:T(128)}, u32[]{:S(2)}) copy-start(f32[64]{0:T(128)} %param.39) | copy-start | bytes 772
  5.6 4.5 %collective-permute-start.2 = (f32[2,8,8,4]{3,2,1,0:T(8,128)S(1)}, f32[2,8,8,4]{3,2,1,0:T(8,128)S(1)}, u32[]{:S(2)}, u32[]{:S(2)}) collective-permute-start(f32[2,8,8,4]{3,2,1,0:T(8,128)S(1)} %fusion.50), channel_id=1, source_target_pairs={{0,4},{4,0},{1,5},{5,1},{2,6},{6,2},{3,7},{7,3},{8,12},{12,8},{9,1... | collective-permute-start | bytes 6152 | tf_op jit(solution)/shard_map/ppermute | solution.py:19
  6.8 0.7 %copy-start.17 = (f32[2,256]{1,0:T(2,128)S(1)}, f32[2,256]{1,0:T(2,128)}, u32[]{:S(2)}) copy-start(f32[2,256]{1,0:T(2,128)} %param.38) | copy-start | bytes 6148
  7.5 1.0 %copy-start.5 = (bf16[256,256]{1,0:T(8,128)(2,1)S(1)}, bf16[256,256]{1,0:T(8,128)(2,1)}, u32[]{:S(2)}) copy-start(bf16[256,256]{1,0:T(8,128)(2,1)} %constant.258.clone) | copy-start | bytes 393220
  7.8 0.7 %copy-start.18 = (s32[256]{0:T(256)S(1)}, s32[256]{0:T(256)}, u32[]{:S(2)}) copy-start(s32[256]{0:T(256)} %param.41) | copy-start | bytes 3076
  7.8 0.8 %copy-start.19 = (s32[256]{0:T(256)S(1)}, s32[256]{0:T(256)}, u32[]{:S(2)}) copy-start(s32[256]{0:T(256)} %param.40) | copy-start | bytes 3076
  8.6 0.8 %copy-start.13 = (f32[8,8,128]{2,1,0:T(8,128)S(1)}, f32[8,8,128]{2,1,0:T(8,128)}, u32[]{:S(2)}) copy-start(f32[8,8,128]{2,1,0:T(8,128)} %param.34) | copy-start | bytes 98308
  8.6 0.8 %copy-start.14 = (f32[8,8,128]{2,1,0:T(8,128)S(1)}, f32[8,8,128]{2,1,0:T(8,128)}, u32[]{:S(2)}) copy-start(f32[8,8,128]{2,1,0:T(8,128)} %param.33) | copy-start | bytes 98308
  10.9 11.6 %all-to-all-start = ((f32[32,1,192]{2,1,0:T(1,128)}), f32[32,1,192]{2,1,0:T(1,128)S(1)}, u32[]{:S(2)}, u32[]{:S(2)}) async-start(f32[32,1,192]{2,1,0:T(1,128)} %copy.43), calls=%async_computation | async-start | bytes 65536 | tf_op jit(solution)/shard_map/all_to_all | solution.py:215
  16.8 5.2 %collective-permute-start.3 = (f32[2,8,8,4]{3,2,1,0:T(8,128)S(1)}, f32[2,8,8,4]{3,2,1,0:T(8,128)S(1)}, u32[]{:S(2)}, u32[]{:S(2)}) collective-permute-start(f32[2,8,8,4]{3,2,1,0:T(8,128)S(1)} %dynamic-slice_maximum_fusion.1), channel_id=1, source_target_pairs={{0,4},{4,0},{1,5},{5,1},{2,6},{6,2},{3,7},{7,3},{8,12},{12,8},{9,1... | collective-permute-start | bytes 6152 | tf_op jit(solution)/shard_map/ppermute | solution.py:19
  18.2 5.1 %collective-permute-start.4 = (f32[2,16,4,136]{3,2,1,0:T(4,128)S(1)}, f32[2,16,4,136]{3,2,1,0:T(4,128)S(1)}, u32[]{:S(2)}, u32[]{:S(2)}) collective-permute-start(f32[2,16,4,136]{3,2,1,0:T(4,128)S(1)} %get-tuple-element.76), channel_id=1, source_target_pairs={{0,8},{8,0},{16,24},{24,16},{1,9},{9,1},{17,25},{25,17},{2,10},{10... | collective-permute-start | bytes 208904 | tf_op jit(solution)/shard_map/ppermute | solution.py:19
  19.0 6.3 %collective-permute-start.5 = (f32[2,16,4,136]{3,2,1,0:T(4,128)S(1)}, f32[2,16,4,136]{3,2,1,0:T(4,128)S(1)}, u32[]{:S(2)}, u32[]{:S(2)}) collective-permute-start(f32[2,16,4,136]{3,2,1,0:T(4,128)S(1)} %get-tuple-element.77), channel_id=1, source_target_pairs={{8,16},{16,8},{9,17},{17,9},{10,18},{18,10},{11,19},{19,11},{12,20... | collective-permute-start | bytes 208904 | tf_op jit(solution)/shard_map/ppermute | solution.py:27
  25.9 0.8 %copy-start.6 = (f32[8,8,128]{2,1,0:T(8,128)S(1)}, f32[8,8,128]{2,1,0:T(8,128)}, u32[]{:S(2)}) copy-start(f32[8,8,128]{2,1,0:T(8,128)} %param.30) | copy-start | bytes 98308
  26.0 0.8 %copy-start.7 = (f32[8,8,128]{2,1,0:T(8,128)S(1)}, f32[8,8,128]{2,1,0:T(8,128)}, u32[]{:S(2)}) copy-start(f32[8,8,128]{2,1,0:T(8,128)} %param.35) | copy-start | bytes 98308
  26.0 0.8 %copy-start.8 = (f32[8,8,128]{2,1,0:T(8,128)S(1)}, f32[8,8,128]{2,1,0:T(8,128)}, u32[]{:S(2)}) copy-start(f32[8,8,128]{2,1,0:T(8,128)} %param.36) | copy-start | bytes 98308
  26.0 0.8 %copy-start.9 = (f32[8,8,128]{2,1,0:T(8,128)S(1)}, f32[8,8,128]{2,1,0:T(8,128)}, u32[]{:S(2)}) copy-start(f32[8,8,128]{2,1,0:T(8,128)} %param.31) | copy-start | bytes 98308
  26.0 0.8 %copy-start.10 = (f32[8,8,128]{2,1,0:T(8,128)S(1)}, f32[8,8,128]{2,1,0:T(8,128)}, u32[]{:S(2)}) copy-start(f32[8,8,128]{2,1,0:T(8,128)} %param.32) | copy-start | bytes 98308
  26.0 0.8 %copy-start.15 = (f32[8,8,128]{2,1,0:T(8,128)S(1)}, f32[8,8,128]{2,1,0:T(8,128)}, u32[]{:S(2)}) copy-start(f32[8,8,128]{2,1,0:T(8,128)} %param.27) | copy-start | bytes 98308
  26.0 0.8 %copy-start.16 = (f32[8,8,128]{2,1,0:T(8,128)S(1)}, f32[8,8,128]{2,1,0:T(8,128)}, u32[]{:S(2)}) copy-start(f32[8,8,128]{2,1,0:T(8,128)} %param.29) | copy-start | bytes 98308
  26.9 16.9 %copy-start.1 = (f32[8,8,128]{2,1,0:T(8,128)}, f32[8,8,128]{2,1,0:T(8,128)S(1)}, u32[]{:S(2)}) copy-start(f32[8,8,128]{2,1,0:T(8,128)S(1)} %get-tuple-element.126) | copy-start | bytes 98308
  26.9 16.9 %copy-start.2 = (f32[8,8,128]{2,1,0:T(8,128)}, f32[8,8,128]{2,1,0:T(8,128)S(1)}, u32[]{:S(2)}) copy-start(f32[8,8,128]{2,1,0:T(8,128)S(1)} %get-tuple-element.127) | copy-start | bytes 98308
  27.0 3.5 %collective-permute-start.9 = (f32[2,8,8,4]{3,2,1,0:T(8,128)S(1)}, f32[2,8,8,4]{3,2,1,0:T(8,128)S(1)}, u32[]{:S(2)}, u32[]{:S(2)}) collective-permute-start(f32[2,8,8,4]{3,2,1,0:T(8,128)S(1)} %fusion.48), channel_id=1, source_target_pairs={{0,4},{4,0},{1,5},{5,1},{2,6},{6,2},{3,7},{7,3},{8,12},{12,8},{9,1... | collective-permute-start | bytes 6152 | tf_op jit(solution)/shard_map/ppermute | solution.py:19
  27.3 3.2 %collective-permute-start.7 = (f32[2,4,8,128]{3,2,1,0:T(8,128)S(1)}, f32[2,4,8,128]{3,2,1,0:T(8,128)S(1)}, u32[]{:S(2)}, u32[]{:S(2)}) collective-permute-start(f32[2,4,8,128]{3,2,1,0:T(8,128)S(1)} %get-tuple-element.98), channel_id=1, source_target_pairs={{0,1},{1,0},{2,3},{3,2},{4,5},{5,4},{6,7},{7,6},{8,9},{9,8},{10,11... | collective-permute-start | bytes 98312 | tf_op jit(solution)/shard_map/ppermute | solution.py:19
  28.5 4.6 %collective-permute-start.6 = (f32[2,4,8,128]{3,2,1,0:T(8,128)S(1)}, f32[2,4,8,128]{3,2,1,0:T(8,128)S(1)}, u32[]{:S(2)}, u32[]{:S(2)}) collective-permute-start(f32[2,4,8,128]{3,2,1,0:T(8,128)S(1)} %get-tuple-element.99), channel_id=1, source_target_pairs={{1,2},{2,1},{5,6},{6,5},{9,10},{10,9},{13,14},{14,13},{17,18},{18,... | collective-permute-start | bytes 98312 | tf_op jit(solution)/shard_map/ppermute | solution.py:27
  33.3 6.6 %collective-permute-start.8 = (f32[2,8,8,4]{3,2,1,0:T(8,128)S(1)}, f32[2,8,8,4]{3,2,1,0:T(8,128)S(1)}, u32[]{:S(2)}, u32[]{:S(2)}) collective-permute-start(f32[2,8,8,4]{3,2,1,0:T(8,128)S(1)} %dynamic-slice_maximum_fusion), channel_id=1, source_target_pairs={{0,4},{4,0},{1,5},{5,1},{2,6},{6,2},{3,7},{7,3},{8,12},{12,8},{9,1... | collective-permute-start | bytes 6152 | tf_op jit(solution)/shard_map/ppermute | solution.py:19
  34.8 5.6 %collective-permute-start.10 = (f32[2,16,4,136]{3,2,1,0:T(4,128)S(1)}, f32[2,16,4,136]{3,2,1,0:T(4,128)S(1)}, u32[]{:S(2)}, u32[]{:S(2)}) collective-permute-start(f32[2,16,4,136]{3,2,1,0:T(4,128)S(1)} %get-tuple-element.72), channel_id=1, source_target_pairs={{0,8},{8,0},{16,24},{24,16},{1,9},{9,1},{17,25},{25,17},{2,10},{10... | collective-permute-start | bytes 208904 | tf_op jit(solution)/shard_map/ppermute | solution.py:19
  34.8 7.7 %collective-permute-start.11 = (f32[2,16,4,136]{3,2,1,0:T(4,128)S(1)}, f32[2,16,4,136]{3,2,1,0:T(4,128)S(1)}, u32[]{:S(2)}, u32[]{:S(2)}) collective-permute-start(f32[2,16,4,136]{3,2,1,0:T(4,128)S(1)} %get-tuple-element.73), channel_id=1, source_target_pairs={{8,16},{16,8},{9,17},{17,9},{10,18},{18,10},{11,19},{19,11},{12,20... | collective-permute-start | bytes 208904 | tf_op jit(solution)/shard_map/ppermute | solution.py:27
  43.9 0.6 %copy-start.11 = (f32[8,8,128]{2,1,0:T(8,128)}, f32[8,8,128]{2,1,0:T(8,128)S(1)}, u32[]{:S(2)}) copy-start(f32[8,8,128]{2,1,0:T(8,128)S(1)} %get-tuple-element.124) | copy-start | bytes 98308
  43.9 0.6 %copy-start.12 = (f32[8,8,128]{2,1,0:T(8,128)}, f32[8,8,128]{2,1,0:T(8,128)S(1)}, u32[]{:S(2)}) copy-start(f32[8,8,128]{2,1,0:T(8,128)S(1)} %get-tuple-element.125) | copy-start | bytes 98308
